TPU v7x, 256 devices: a whole 4x4x8 slice. The times are simulated.
256 devices in a mesh: heads: 4 (over y), seq: 64 (over z, x, core).
Axes of the slice: x: 4, y: 4, z: 8, core: 2. Of those that a mesh axis runs over, the one named last changes fastest.
Arguments:
- hidden: bfloat16 [64, 2048], P(None, 'seq')
- w_qkv: bfloat16 [2048, 3, 2048], P('seq', None, 'heads')
- w_out: bfloat16 [2048, 2048], P('heads', 'seq'), may hold values from -0.125 to 0.125
- positions: int32 [64], replicated, may hold values from 0 to 8191
- req_blocks: int32 [64], replicated, may hold values from 1 to 64, 1152 in all
- keep_list: int32 [1152], P('seq'), may hold values from 0 to 1, as said below
- dest_slot: int32 [1152], P('seq'), may hold values from 0 to 1023, as said below
- key_cache: bfloat16 [1152, 128, 2048], P('seq', None, 'heads')
- value_cache: bfloat16 [1152, 128, 2048], P('seq', None, 'heads')
- fold_weight: float32 [1152, 128], P('seq'), may hold values from 0.1 to 10
Outputs:
- packed_keys: bfloat16 [1024, 128, 2048], P('seq', None, 'heads')
- packed_values: bfloat16 [1024, 128, 2048], P('seq', None, 'heads')
- packed_request: int32 [1024], P('seq')
- folded_keys: bfloat16 [1152, 2048], P('seq', 'heads')
- folded_values: bfloat16 [1152, 2048], P('seq', 'heads')
- attn_out: bfloat16 [64, 2048], P(None, 'seq')
Inputs may be any that keep to these rules, and one draw needn't show every extreme that they name: `keep_list`: each index of seq (its 18 blocks) keeps at most 15 blocks, and some index keeps exactly that many. `dest_slot`: for a kept block: its slot among 1024 packed slots, 16 to each owner (owner = slot // 16); kept blocks have distinct slots; a kept block held by index i of seq goes to owner (i + j) mod 64 for some j with 0 <= j < 4; at most 4 kept blocks of one index share an owner, and some index sends that many to one owner; some owner has all its slots filled. Entries of dropped blocks are meaningless.
All inputs are finite; a program needn't handle non-finite values.
Results may differ from a plain program's by a relative error of at most 0.0156.
The roundings to bfloat16 on the way count: a program that leaves them out, or rounds other values in their place, can miss the bound.
Values may be sent and summed in bfloat16 or wider, within the bound.
No kernel may reach another device: no remote copies, remote signals or barrier semaphores. Data moves between devices by JAX's collectives and lax.ppermute only.
A program may use at most 128 MiB of HBM per device.

v0:
```python
import math

import jax
import jax.numpy as jnp
from jax import lax
from jax.sharding import PartitionSpec as P

D = 2048
HDIM = 64
ROWS = 128
HOPS = 4
CAP = 4
SLOT_DEV = 16


ROPE_BASE = 130000.0
NORM_EPSILON = 1e-05
MASKED_SCORE = -1e30


def passed_along(array, axis, by):
    count = lax.axis_size(axis)
    return lax.ppermute(array, axis, [(i, (i + by) % count) for i in range(count)])


def rotate_half(values, cos_table, sin_table):
    half = values.shape[-1] // 2
    lower = values[..., :half]
    upper = values[..., half:]
    return jnp.concatenate(
        [lower * cos_table - upper * sin_table, upper * cos_table + lower * sin_table], axis=-1
    )


def rope_tables(positions, head_size):
    half = head_size // 2
    freqs = ROPE_BASE ** (-(2.0 * jnp.arange(half, dtype=jnp.float32)) / head_size)
    angles = positions.astype(jnp.float32)[:, None] * freqs[None, :]
    return (jnp.cos(angles)[:, None, :], jnp.sin(angles)[:, None, :])


def shards(
    hidden,
    w_qkv,
    w_out,
    positions,
    req_blocks,
    keep_list,
    dest_slot,
    key_cache,
    value_cache,
    fold_weight,
):
    requests = hidden.shape[0]
    n_blocks, row_count, feat_width = key_cache.shape
    heads_here = feat_width // HDIM
    seq_count = lax.axis_size("seq")
    my_index = lax.axis_index("seq")
    widened = hidden.astype(jnp.float32)
    total_sq = lax.psum(jnp.sum(widened * widened, axis=1), "seq")
    normed = (widened * lax.rsqrt(total_sq / D + NORM_EPSILON)[:, None]).astype(jnp.bfloat16)
    partial_value = jnp.dot(
        normed, w_qkv.reshape(w_qkv.shape[0], 3 * feat_width), preferred_element_type=jnp.float32
    )
    proj_all = lax.psum(partial_value, "seq").reshape(requests, 3, heads_here, HDIM)
    cos_table, sin_table = rope_tables(positions, HDIM)
    queries = rotate_half(proj_all[:, 0], cos_table, sin_table).astype(jnp.bfloat16)
    new_keys = rotate_half(proj_all[:, 1], cos_table, sin_table).astype(jnp.bfloat16)
    new_values = proj_all[:, 2].astype(jnp.bfloat16)
    block_ids = jnp.arange(n_blocks, dtype=jnp.int32)
    global_ids = my_index * n_blocks + block_ids
    req_ends = jnp.cumsum(req_blocks)
    blk_req = jnp.sum((global_ids[:, None] >= req_ends[None, :]).astype(jnp.int32), axis=1)
    is_kept = keep_list == 1
    weight_sum = jnp.sum(fold_weight, axis=1)
    fold_keys = jnp.einsum(
        "bi,bif->bf",
        fold_weight,
        key_cache,
        preferred_element_type=jnp.float32,
        precision=lax.Precision.HIGHEST,
    )
    fold_values = jnp.einsum(
        "bi,bif->bf",
        fold_weight,
        value_cache,
        preferred_element_type=jnp.float32,
        precision=lax.Precision.HIGHEST,
    )
    folded_keys = jnp.where(is_kept[:, None], 0.0, fold_keys / weight_sum[:, None]).astype(
        jnp.bfloat16
    )
    folded_values = jnp.where(is_kept[:, None], 0.0, fold_values / weight_sum[:, None]).astype(
        jnp.bfloat16
    )
    owners = dest_slot // SLOT_DEV
    local_slot = dest_slot % SLOT_DEV
    hop_of = (owners - my_index) % seq_count
    earlier = (
        is_kept[None, :]
        & is_kept[:, None]
        & (hop_of[None, :] == hop_of[:, None])
        & (block_ids[None, :] < block_ids[:, None])
    )
    placed = jnp.sum(earlier.astype(jnp.int32), axis=1)
    arrivals = HOPS * CAP
    send_pos = jnp.where(is_kept, hop_of * CAP + placed, arrivals)
    targets = jnp.arange(arrivals, dtype=jnp.int32)
    hit_table = send_pos[None, :] == targets[:, None]
    has_block = jnp.any(hit_table, axis=1)
    source = jnp.sum(jnp.where(hit_table, block_ids[None, :], 0), axis=1)
    send_keys = jnp.where(
        has_block[:, None, None], key_cache[source], jnp.zeros((), jnp.bfloat16)
    ).reshape(HOPS, CAP, row_count, feat_width)
    send_values = jnp.where(
        has_block[:, None, None], value_cache[source], jnp.zeros((), jnp.bfloat16)
    ).reshape(HOPS, CAP, row_count, feat_width)
    meta_data = jnp.stack(
        [jnp.where(has_block, local_slot[source], -1), jnp.where(has_block, blk_req[source], -1)],
        axis=-1,
    )
    meta_data = meta_data.astype(jnp.float32).astype(jnp.bfloat16).reshape(HOPS, CAP, 2)
    arrived = [(send_keys[0], send_values[0], meta_data[0])]
    for distance in range(1, HOPS):
        arrived.append(
            passed_along(
                (send_keys[distance], send_values[distance], meta_data[distance]), "seq", distance
            )
        )
    recv_keys = jnp.stack([entry[0] for entry in arrived])
    recv_values = jnp.stack([entry[1] for entry in arrived])
    recv_meta = jnp.stack([entry[2] for entry in arrived])
    recv_keys = recv_keys.reshape(arrivals, row_count, feat_width)
    recv_values = recv_values.reshape(arrivals, row_count, feat_width)
    recv_meta = recv_meta.reshape(arrivals, 2).astype(jnp.float32).astype(jnp.int32)
    match_table = recv_meta[None, :, 0] == jnp.arange(SLOT_DEV, dtype=jnp.int32)[:, None]
    filled = jnp.any(match_table, axis=1)
    picked = jnp.sum(
        jnp.where(match_table, jnp.arange(arrivals, dtype=jnp.int32)[None, :], 0), axis=1
    )
    packed_keys = jnp.where(filled[:, None, None], recv_keys[picked], jnp.zeros((), jnp.bfloat16))
    packed_values = jnp.where(
        filled[:, None, None], recv_values[picked], jnp.zeros((), jnp.bfloat16)
    )
    packed_request = jnp.where(filled, recv_meta[picked, 1], -1)
    row_keys = packed_keys.reshape(-1, heads_here, HDIM)
    row_values = packed_values.reshape(-1, heads_here, HDIM)
    row_req = jnp.repeat(packed_request, row_count)
    all_keys = jnp.concatenate([row_keys, folded_keys.reshape(n_blocks, heads_here, HDIM)], axis=0)
    all_values = jnp.concatenate(
        [row_values, folded_values.reshape(n_blocks, heads_here, HDIM)], axis=0
    )
    all_req = jnp.concatenate([row_req, jnp.where(is_kept, -1, blk_req)])
    bias = jnp.concatenate(
        [
            jnp.zeros((row_req.shape[0],), jnp.float32),
            jnp.full((n_blocks,), math.log(ROWS), jnp.float32),
        ]
    )
    row_mask = all_req[None, :] == jnp.arange(requests, dtype=jnp.int32)[:, None]
    scores = (
        jnp.einsum("rhd,nhd->hrn", queries, all_keys, preferred_element_type=jnp.float32) * 0.125
        + bias[None, None, :]
    )
    scores = jnp.where(row_mask[None], scores, MASKED_SCORE)
    local_top = jnp.max(scores, axis=2)
    expo = jnp.where(row_mask[None], jnp.exp(scores - local_top[..., None]), 0.0)
    local_sum = jnp.sum(expo, axis=2)
    local_acc = jnp.einsum(
        "hrn,nhd->hrd", expo.astype(jnp.bfloat16), all_values, preferred_element_type=jnp.float32
    )
    top_score = lax.pmax(local_top, "seq")
    factor = jnp.exp(local_top - top_score)
    totals, mixture = lax.psum((local_sum * factor, local_acc * factor[..., None]), "seq")
    own_score = (
        jnp.einsum("rhd,rhd->hr", queries, new_keys, preferred_element_type=jnp.float32) * 0.125
    )
    final_top = jnp.maximum(top_score, own_score)
    shrink = jnp.exp(top_score - final_top)
    own_expo = jnp.exp(own_score - final_top)
    own_prob = lax.optimization_barrier(own_expo.astype(jnp.bfloat16)).astype(jnp.float32)
    totals = totals * shrink + own_expo
    own_values = jnp.transpose(new_values, (1, 0, 2)).astype(jnp.float32)
    mixture = mixture * shrink[..., None] + own_prob[..., None] * own_values
    mixed = (mixture / totals[..., None]).astype(jnp.bfloat16)
    mixed_rows = jnp.transpose(mixed, (1, 0, 2)).reshape(requests, feat_width)
    out_terms = jnp.dot(mixed_rows, w_out, preferred_element_type=jnp.float32)
    attn_out = lax.psum(out_terms, "heads").astype(jnp.bfloat16)
    return (packed_keys, packed_values, packed_request, folded_keys, folded_values, attn_out)


def solution(mesh):
    return jax.shard_map(
        shards,
        mesh=mesh,
        in_specs=(
            P(None, "seq"),
            P("seq", None, "heads"),
            P("heads", "seq"),
            P(),
            P(),
            P("seq"),
            P("seq"),
            P("seq", None, "heads"),
            P("seq", None, "heads"),
            P("seq", None),
        ),
        out_specs=(
            P("seq", None, "heads"),
            P("seq", None, "heads"),
            P("seq"),
            P("seq", "heads"),
            P("seq", "heads"),
            P(None, "seq"),
        ),
        check_vma=False,
    )
```

profile of v0, /device:TPU:6, one launch (start us, length us, event | category | flops | bytes accessed | tf_op | source)
XLA Modules:
  0.0 857.9 jit_solution(1130575333120009257)
XLA Ops:
  7.2 0.8 broadcast_compare_fusion
  8.1 0.7 and_select_fusion
  8.7 0.7 copy.41
  10.1 1.2 broadcast_select_fusion.7
  12.1 0.7 gather_fusion
  12.8 0.7 slice_bitcast_fusion.5
  13.5 1.3 collective-permute-start.2
  14.8 1.5 collective-permute-start.1
  16.3 1.9 collective-permute-start
  18.2 0.7 fusion.31
  18.9 112.3 %psum.35 = f32[64]{0:T(128)S(1)} all-reduce(f32[64]{0:T(128)S(1)} %fusion.31), channel_id=1, replica_groups=mesh['heads'=4,'seq'=64] {'seq'}, use_global_device_ids=true, to_apply=%region_9.10 | all-reduce | flops 64 | bytes 512 | tf_op jit(solution)/shard_map/psum | solution.py:60
  131.2 0.9 copy.63
  132.1 0.9 fusion.34
  133.3 1.0 copy.47
  134.3 3.7 gather_fusion.4
  138.0 2.0 gather_fusion.2
  140.0 3.9 broadcast_select_fusion
  143.9 1.2 slice_bitcast_fusion
  145.2 1.0 fusion.43
  146.8 1.0 fusion.41
  148.0 0.8 copy.51
  148.8 0.8 copy.49
  149.6 2.7 slice_bitcast_fusion.1
  152.3 0.8 multiply_cosine_fusion
  155.9 0.7 gather_fusion.6
  157.3 1.2 pad_clamp_fusion
  158.5 10.1 %collective-permute-done.8 = bf16[4,128,512]{2,1,0:T(8,128)(2,1)} collective-permute-done((bf16[4,128,512]{2,1,0:T(8,128)(2,1)}, bf16[4,128,512]{2,1,0:T(8,128)(2,1)}, u32[]{:S(2)}, u32[]{:S(2)}) %collective-permute-start.8) | collective-permute-done | bytes 524320 | tf_op jit(solution)/shard_map/ppermute | solution.py:23
  168.6 187.5 %all-reduce.4.cloned.1.call-done = f32[64,3,8,64]{3,0,2,1:T(8,128)} async-done(((f32[64,3,8,64]{3,0,2,1:T(8,128)}), f32[64,3,8,64]{3,0,2,1:T(8,128)}) %all-reduce.4.cloned.1.call-update) | async-done | bytes 393232 | tf_op jit(solution)/shard_map/psum | solution.py:65
  356.1 1.1 slice_bitcast_fusion.2
  357.2 1.0 subtract_convert_fusion
  359.2 2.9 pad_maximum_fusion.1
  362.1 3.7 gather_fusion.5
  365.8 4.5 copy.50
  370.4 2.9 pad_maximum_fusion
  373.3 3.7 gather_fusion.3
  377.0 4.6 broadcast_select_fusion.2
  381.6 4.5 copy.48
  386.1 4.2 gather.33
  390.3 4.2 gather.32
  394.5 3.9 broadcast_select_fusion.4
  398.4 3.4 fusion.54
  401.7 113.7 %pmax.7 = f32[8,64]{1,0:T(8,128)S(1)} all-reduce(f32[8,64]{1,0:T(8,128)S(1)} %get-tuple-element.49), channel_id=1, replica_groups=mesh['heads'=4,'seq'=64] {'seq'}, use_global_device_ids=true, to_apply=%region_12.13 | all-reduce | flops 512 | bytes 4096 | tf_op jit(solution)/shard_map/pmax | solution.py:172
  515.5 3.3 fusion.2
  518.8 124.1 %psum.38 = f32[8,64]{1,0:T(8,128)S(1)} all-reduce(f32[8,64]{1,0:T(8,128)S(1)} %get-tuple-element.6), channel_id=1, replica_groups=mesh['heads'=4,'seq'=64] {'seq'}, use_global_device_ids=true, to_apply=%region_15.16 | all-reduce | flops 512 | bytes 4096 | tf_op jit(solution)/shard_map/psum | solution.py:174
  642.9 4.6 fusion.15
  647.5 184.4 %all-reduce.6.cloned.1.call-done = f32[8,64,64]{2,1,0:T(8,128)} async-done(((f32[8,64,64]{2,1,0:T(8,128)}), f32[8,64,64]{2,1,0:T(8,128)}) %all-reduce.6.cloned.1.call-update) | async-done | bytes 131088 | tf_op jit(solution)/shard_map/psum | solution.py:174
  831.9 1.3 fusion.26
  833.6 17.5 %psum.39 = bf16[64,32]{0,1:T(8,128)(2,1)} all-reduce(f32[64,32]{0,1:T(8,128)S(1)} %fusion.55), channel_id=1, replica_groups=mesh['heads'=4,'seq'=64] {'heads'}, use_global_device_ids=true, to_apply=%region_16.17 | all-reduce | flops 2048 | bytes 12288 | tf_op jit(solution)/shard_map/psum | solution.py:188
  (96 shorter events, 7.4 us)
Async XLA Ops:
  7.2 130.8 %copy-start = (bf16[18,128,512]{2,1,0:T(8,128)(2,1)S(1)}, bf16[18,128,512]{2,1,0:T(8,128)(2,1)}, u32[]{:S(2)}) copy-start(bf16[18,128,512]{2,1,0:T(8,128)(2,1)} %param.17) | copy-start | bytes 7077892
  7.2 349.0 %all-reduce.4.cloned.1.call-start = ((), (), s32[]{:S(2)}) async-start(), calls=%async_computation | async-start | bytes 1572864 | tf_op jit(solution)/shard_map/psum | solution.py:65
  13.5 139.6 %collective-permute-start.2 = (bf16[4,2]{0,1:T(2,128)(2,1)}, bf16[4,2]{0,1:T(2,128)(2,1)}, u32[]{:S(2)}, u32[]{:S(2)}) collective-permute-start(bf16[4,2]{0,1:T(2,128)(2,1)} %get-tuple-element.42), channel_id=1, source_target_pairs={{0,3},{1,4},{2,5},{3,6},{4,7},{5,8},{6,9},{7,10},{8,11},{9,12},{10... | collective-permute-start | bytes 56 | tf_op jit(solution)/shard_map/ppermute | solution.py:23
  14.8 139.0 %collective-permute-start.1 = (bf16[4,2]{0,1:T(2,128)(2,1)}, bf16[4,2]{0,1:T(2,128)(2,1)}, u32[]{:S(2)}, u32[]{:S(2)}) collective-permute-start(bf16[4,2]{0,1:T(2,128)(2,1)} %get-tuple-element.43), channel_id=1, source_target_pairs={{0,2},{1,3},{2,4},{3,5},{4,6},{5,7},{6,8},{7,9},{8,10},{9,11},{10,... | collective-permute-start | bytes 56 | tf_op jit(solution)/shard_map/ppermute | solution.py:23
  16.3 138.1 %collective-permute-start = (bf16[4,2]{0,1:T(2,128)(2,1)S(1)}, bf16[4,2]{0,1:T(2,128)(2,1)}, u32[]{:S(2)}, u32[]{:S(2)}) collective-permute-start(bf16[4,2]{0,1:T(2,128)(2,1)S(1)} %get-tuple-element.44), channel_id=1, source_target_pairs={{0,1},{1,2},{2,3},{3,4},{4,5},{5,6},{6,7},{7,8},{8,9},{9,10},{10,1... | collective-permute-start | bytes 56 | tf_op jit(solution)/shard_map/ppermute | solution.py:23
  134.3 697.6 %all-reduce.6.cloned.1.call-start = ((), (), s32[]{:S(2)}) async-start(), calls=%async_computation.1 | async-start | bytes 524288 | tf_op jit(solution)/shard_map/psum | solution.py:174
  143.9 1.2 copy-start.10
  145.1 1.7 copy-start.1
  145.1 23.5 %collective-permute-start.8 = (bf16[4,128,512]{2,1,0:T(8,128)(2,1)}, bf16[4,128,512]{2,1,0:T(8,128)(2,1)}, u32[]{:S(2)}, u32[]{:S(2)}) collective-permute-start(bf16[4,128,512]{2,1,0:T(8,128)(2,1)} %get-tuple-element.9), channel_id=1, source_target_pairs={{0,3},{1,4},{2,5},{3,6},{4,7},{5,8},{6,9},{7,10},{8,11},{9,12},{10... | collective-permute-start | bytes 1572872 | tf_op jit(solution)/shard_map/ppermute | solution.py:23
  145.1 214.1 %collective-permute-start.7 = (bf16[4,128,512]{2,1,0:T(8,128)(2,1)}, bf16[4,128,512]{2,1,0:T(8,128)(2,1)}, u32[]{:S(2)}, u32[]{:S(2)}) collective-permute-start(bf16[4,128,512]{2,1,0:T(8,128)(2,1)} %get-tuple-element.10), channel_id=1, source_target_pairs={{0,2},{1,3},{2,4},{3,5},{4,6},{5,7},{6,8},{7,9},{8,10},{9,11},{10,... | collective-permute-start | bytes 1572872 | tf_op jit(solution)/shard_map/ppermute | solution.py:23
  145.1 2.7 copy-start.17
  145.1 2.8 copy-start.16
  148.0 1.6 copy-start.8
  148.0 1.6 copy-start.9
  149.6 7.5 copy-start.14
  153.2 206.0 %collective-permute-start.6 = (bf16[4,128,512]{2,1,0:T(8,128)(2,1)}, bf16[4,128,512]{2,1,0:T(8,128)(2,1)}, u32[]{:S(2)}, u32[]{:S(2)}) collective-permute-start(bf16[4,128,512]{2,1,0:T(8,128)(2,1)} %get-tuple-element.11), channel_id=1, source_target_pairs={{0,1},{1,2},{2,3},{3,4},{4,5},{5,6},{6,7},{7,8},{8,9},{9,10},{10,1... | collective-permute-start | bytes 1572872 | tf_op jit(solution)/shard_map/ppermute | solution.py:23
  153.8 216.6 %collective-permute-start.5 = (bf16[4,128,512]{2,1,0:T(8,128)(2,1)}, bf16[4,128,512]{2,1,0:T(8,128)(2,1)}, u32[]{:S(2)}, u32[]{:S(2)}) collective-permute-start(bf16[4,128,512]{2,1,0:T(8,128)(2,1)} %get-tuple-element.13), channel_id=1, source_target_pairs={{0,3},{1,4},{2,5},{3,6},{4,7},{5,8},{6,9},{7,10},{8,11},{9,12},{10... | collective-permute-start | bytes 1572872 | tf_op jit(solution)/shard_map/ppermute | solution.py:23
  154.4 216.0 %collective-permute-start.4 = (bf16[4,128,512]{2,1,0:T(8,128)(2,1)}, bf16[4,128,512]{2,1,0:T(8,128)(2,1)}, u32[]{:S(2)}, u32[]{:S(2)}) collective-permute-start(bf16[4,128,512]{2,1,0:T(8,128)(2,1)} %get-tuple-element.14), channel_id=1, source_target_pairs={{0,2},{1,3},{2,4},{3,5},{4,6},{5,7},{6,8},{7,9},{8,10},{9,11},{10,... | collective-permute-start | bytes 1572872 | tf_op jit(solution)/shard_map/ppermute | solution.py:23
  155.2 203.0 %copy-start.12 = (pred[16]{0:T(512)(128)(4,1)}, pred[16]{0:T(512)(128)(4,1)S(1)}, u32[]{:S(2)}) copy-start(pred[16]{0:T(512)(128)(4,1)S(1)} %fusion.37) | copy-start | bytes 52
  156.6 0.5 copy-start.15
  168.6 201.8 %collective-permute-start.3 = (bf16[4,128,512]{2,1,0:T(8,128)(2,1)}, bf16[4,128,512]{2,1,0:T(8,128)(2,1)}, u32[]{:S(2)}, u32[]{:S(2)}) collective-permute-start(bf16[4,128,512]{2,1,0:T(8,128)(2,1)} %get-tuple-element.15), channel_id=1, source_target_pairs={{0,1},{1,2},{2,3},{3,4},{4,5},{5,6},{6,7},{7,8},{8,9},{9,10},{10,1... | collective-permute-start | bytes 1572872 | tf_op jit(solution)/shard_map/ppermute | solution.py:23
  358.2 0.6 copy-start.2
  358.2 0.9 copy-start.4
  373.3 3.7 copy-start.13
  394.4 3.9 copy-start.3
  394.4 3.9 copy-start.5
  394.4 3.9 copy-start.7
  394.5 3.9 copy-start.18
  515.5 127.4 %copy-start.6 = (bf16[18,512]{0,1:T(8,128)(2,1)S(1)}, bf16[18,512]{0,1:T(8,128)(2,1)}, u32[]{:S(2)}) copy-start(bf16[18,512]{0,1:T(8,128)(2,1)} %copy.51) | copy-start | bytes 55300
  642.9 190.5 %copy-start.11 = (bf16[512,32]{0,1:T(8,128)(2,1)S(1)}, bf16[512,32]{0,1:T(8,128)(2,1)}, u32[]{:S(2)}) copy-start(bf16[512,32]{0,1:T(8,128)(2,1)} %param.12) | copy-start | bytes 98308
Sparse Core Ops, SparseCore 0:
  134.4 221.6 all-reduce.3
  647.6 184.2 all-reduce.5
where the time goes:
time: 860 us; the launch traced here: 858 us
  waiting for transfers between devices  382 us (44%)
  blocking collectives  368 us (43%)
  local copies, waits for them, and re-layouts  46.6 us (5%)
  other arithmetic  31.5 us (4%)
  between operations  14.4 us (2%)
  matrix products  11 us (1%)
    psum x1, waiting for transfers between devices, shards(): lax.psum(partial_value, 'seq').reshape(requests, 3, heads_here, HDIM)  188 us
    psum x1, waiting for transfers between devices, shards(): lax.psum((local_sum * factor, local_acc * factor[..., None]), 'seq')  184 us
    psum x1, blocking collectives, shards(): lax.psum((local_sum * factor, local_acc * factor[..., None]), 'seq')  124 us
    pmax x1, blocking collectives, shards(): top_score = lax.pmax(local_top, 'seq')  114 us
    psum x1, blocking collectives, shards(): total_sq = lax.psum(jnp.sum(widened * widened, axis=1), 'seq')  112 us
    psum x1, blocking collectives, shards(): attn_out = lax.psum(out_terms, 'heads').astype(jnp.bfloat16)  17.5 us
  transfers between devices with their start and end apart: 11, of which 3 were waited for; matrix products, arithmetic and copies ran while one was open for 5% of the time, Pallas kernels for 0%

commit v1 on v0

--- a/solution.py
+++ b/solution.py
@@ -3,6 +3,7 @@
 import jax
 import jax.numpy as jnp
 from jax import lax
+from jax.sharding import Mesh
 from jax.sharding import PartitionSpec as P
 
 D = 2048
@@ -17,10 +18,56 @@
 NORM_EPSILON = 1e-05
 MASKED_SCORE = -1e30
 
-
-def passed_along(array, axis, by):
-    count = lax.axis_size(axis)
-    return lax.ppermute(array, axis, [(i, (i + by) % count) for i in range(count)])
+SEQ_PARTS = ("z", "x", "core")
+
+
+AXIS_SIZES = {"heads": 4, "z": 8, "x": 4, "core": 2}
+
+
+def exchange_steps(axes):
+    for axis in axes:
+        bit = 1
+        while bit < AXIS_SIZES[axis]:
+            yield axis, [(i, i ^ bit) for i in range(AXIS_SIZES[axis])]
+            bit *= 2
+
+
+def butterfly(x, merge, axes):
+    for axis, pairs in exchange_steps(axes):
+        x = merge(x, lax.ppermute(x, axis, pairs))
+    return x
+
+
+def seq_sum(x):
+    return butterfly(x, jnp.add, reversed(SEQ_PARTS))
+
+
+def softmax_merge(mine, theirs):
+    top_a, top_b = mine[..., -1:], theirs[..., -1:]
+    top = jnp.maximum(top_a, top_b)
+    scale_a = jnp.exp(top_a - top)
+    scale_b = jnp.exp(top_b - top)
+    merged = mine[..., :-1] * scale_a + theirs[..., :-1] * scale_b
+    return jnp.concatenate([merged, top], axis=-1)
+
+
+def seq_index():
+    index = lax.axis_index(SEQ_PARTS[0])
+    for axis in SEQ_PARTS[1:]:
+        index = index * lax.axis_size(axis) + lax.axis_index(axis)
+    return index
+
+
+def seq_size():
+    count = 1
+    for axis in SEQ_PARTS:
+        count *= lax.axis_size(axis)
+    return count
+
+
+def passed_along(array, by):
+    count = seq_size()
+    return lax.ppermute(array, SEQ_PARTS, [(i, (i + by) % count) for i in range(count)])
 
 
 def rotate_half(values, cos_table, sin_table):
@@ -54,24 +101,27 @@
     requests = hidden.shape[0]
     n_blocks, row_count, feat_width = key_cache.shape
     heads_here = feat_width // HDIM
-    seq_count = lax.axis_size("seq")
-    my_index = lax.axis_index("seq")
+    seq_count = seq_size()
+    my_index = seq_index()
+
     widened = hidden.astype(jnp.float32)
-    total_sq = lax.psum(jnp.sum(widened * widened, axis=1), "seq")
+    total_sq = seq_sum(jnp.sum(widened * widened, axis=1))
     normed = (widened * lax.rsqrt(total_sq / D + NORM_EPSILON)[:, None]).astype(jnp.bfloat16)
     partial_value = jnp.dot(
         normed, w_qkv.reshape(w_qkv.shape[0], 3 * feat_width), preferred_element_type=jnp.float32
     )
-    proj_all = lax.psum(partial_value, "seq").reshape(requests, 3, heads_here, HDIM)
+    proj_all = seq_sum(partial_value).reshape(requests, 3, heads_here, HDIM)
     cos_table, sin_table = rope_tables(positions, HDIM)
     queries = rotate_half(proj_all[:, 0], cos_table, sin_table).astype(jnp.bfloat16)
     new_keys = rotate_half(proj_all[:, 1], cos_table, sin_table).astype(jnp.bfloat16)
     new_values = proj_all[:, 2].astype(jnp.bfloat16)
+
     block_ids = jnp.arange(n_blocks, dtype=jnp.int32)
     global_ids = my_index * n_blocks + block_ids
     req_ends = jnp.cumsum(req_blocks)
     blk_req = jnp.sum((global_ids[:, None] >= req_ends[None, :]).astype(jnp.int32), axis=1)
     is_kept = keep_list == 1
+
     weight_sum = jnp.sum(fold_weight, axis=1)
     fold_keys = jnp.einsum(
         "bi,bif->bf",
@@ -93,6 +143,7 @@
     folded_values = jnp.where(is_kept[:, None], 0.0, fold_values / weight_sum[:, None]).astype(
         jnp.bfloat16
     )
+
     owners = dest_slot // SLOT_DEV
     local_slot = dest_slot % SLOT_DEV
     hop_of = (owners - my_index) % seq_count
@@ -109,12 +160,8 @@
     hit_table = send_pos[None, :] == targets[:, None]
     has_block = jnp.any(hit_table, axis=1)
     source = jnp.sum(jnp.where(hit_table, block_ids[None, :], 0), axis=1)
-    send_keys = jnp.where(
-        has_block[:, None, None], key_cache[source], jnp.zeros((), jnp.bfloat16)
-    ).reshape(HOPS, CAP, row_count, feat_width)
-    send_values = jnp.where(
-        has_block[:, None, None], value_cache[source], jnp.zeros((), jnp.bfloat16)
-    ).reshape(HOPS, CAP, row_count, feat_width)
+    send_keys = key_cache[source].reshape(HOPS, CAP, row_count, feat_width)
+    send_values = value_cache[source].reshape(HOPS, CAP, row_count, feat_width)
     meta_data = jnp.stack(
         [jnp.where(has_block, local_slot[source], -1), jnp.where(has_block, blk_req[source], -1)],
         axis=-1,
@@ -123,9 +170,7 @@
     arrived = [(send_keys[0], send_values[0], meta_data[0])]
     for distance in range(1, HOPS):
         arrived.append(
-            passed_along(
-                (send_keys[distance], send_values[distance], meta_data[distance]), "seq", distance
-            )
+            passed_along((send_keys[distance], send_values[distance], meta_data[distance]), distance)
         )
     recv_keys = jnp.stack([entry[0] for entry in arrived])
     recv_values = jnp.stack([entry[1] for entry in arrived])
@@ -143,9 +188,10 @@
         filled[:, None, None], recv_values[picked], jnp.zeros((), jnp.bfloat16)
     )
     packed_request = jnp.where(filled, recv_meta[picked, 1], -1)
-    row_keys = packed_keys.reshape(-1, heads_here, HDIM)
-    row_values = packed_values.reshape(-1, heads_here, HDIM)
-    row_req = jnp.repeat(packed_request, row_count)
+
+    row_keys = key_cache.reshape(-1, heads_here, HDIM)
+    row_values = value_cache.reshape(-1, heads_here, HDIM)
+    row_req = jnp.repeat(jnp.where(is_kept, blk_req, -1), row_count)
     all_keys = jnp.concatenate([row_keys, folded_keys.reshape(n_blocks, heads_here, HDIM)], axis=0)
     all_values = jnp.concatenate(
         [row_values, folded_values.reshape(n_blocks, heads_here, HDIM)], axis=0
@@ -169,9 +215,13 @@
     local_acc = jnp.einsum(
         "hrn,nhd->hrd", expo.astype(jnp.bfloat16), all_values, preferred_element_type=jnp.float32
     )
-    top_score = lax.pmax(local_top, "seq")
-    factor = jnp.exp(local_top - top_score)
-    totals, mixture = lax.psum((local_sum * factor, local_acc * factor[..., None]), "seq")
+    stats = jnp.concatenate(
+        [local_acc, local_sum[..., None], local_top[..., None]], axis=-1
+    )
+    stats = butterfly(stats, softmax_merge, reversed(SEQ_PARTS))
+    mixture = stats[..., :HDIM]
+    totals = stats[..., HDIM]
+    top_score = stats[..., HDIM + 1]
     own_score = (
         jnp.einsum("rhd,rhd->hr", queries, new_keys, preferred_element_type=jnp.float32) * 0.125
     )
@@ -185,33 +235,39 @@
     mixed = (mixture / totals[..., None]).astype(jnp.bfloat16)
     mixed_rows = jnp.transpose(mixed, (1, 0, 2)).reshape(requests, feat_width)
     out_terms = jnp.dot(mixed_rows, w_out, preferred_element_type=jnp.float32)
-    attn_out = lax.psum(out_terms, "heads").astype(jnp.bfloat16)
+    attn_out = butterfly(out_terms, jnp.add, ["heads"]).astype(jnp.bfloat16)
     return (packed_keys, packed_values, packed_request, folded_keys, folded_values, attn_out)
 
 
 def solution(mesh):
+    heads_count, seq_count = mesh.devices.shape
+    fine = Mesh(
+        mesh.devices.reshape(heads_count, seq_count // 8, 4, 2),
+        ("heads",) + SEQ_PARTS,
+    )
+    seq = SEQ_PARTS
     return jax.shard_map(
         shards,
-        mesh=mesh,
+        mesh=fine,
         in_specs=(
-            P(None, "seq"),
-            P("seq", None, "heads"),
-            P("heads", "seq"),
+            P(None, seq),
+            P(seq, None, "heads"),
+            P("heads", seq),
             P(),
             P(),
-            P("seq"),
-            P("seq"),
-            P("seq", None, "heads"),
-            P("seq", None, "heads"),
-            P("seq", None),
+            P(seq),
+            P(seq),
+            P(seq, None, "heads"),
+            P(seq, None, "heads"),
+            P(seq, None),
         ),
         out_specs=(
-            P("seq", None, "heads"),
-            P("seq", None, "heads"),
-            P("seq"),
-            P("seq", "heads"),
-            P("seq", "heads"),
-            P(None, "seq"),
+            P(seq, None, "heads"),
+            P(seq, None, "heads"),
+            P(seq),
+            P(seq, "heads"),
+            P(seq, "heads"),
+            P(None, seq),
         ),
         check_vma=False,
     )

time: 860 us -> 261 us (0.30)
  blocking collectives: 368 us -> 0 us
  waiting for transfers between devices: 382 us -> 116 us
  starting transfers between devices: 4.79 us -> 64.7 us
  between operations: 14.4 us -> 1.3 us
    psum x2 -> x0, waiting for transfers between devices: 372 us -> none  [the longest x1 188 us: shards(): lax.psum(partial_value, 'seq').reshape(requests, 3, heads_here, HDIM)]
    psum x3 -> x0, blocking collectives: 254 us -> none  [the longest x1 124 us: shards(): lax.psum((local_sum * factor, local_acc * factor[..., None]), 'seq')]
    pmax x1 -> x0, blocking collectives: 114 us -> none  [shards(): top_score = lax.pmax(local_top, 'seq')]
    ppermute x9 -> x29, waiting for transfers between devices: 10.1 us -> 116 us  [the longest x20 116 us: butterfly(): x = merge(x, lax.ppermute(x, axis, pairs))]
    ppermute x9 -> x29, starting transfers between devices: 4.71 us -> 64.7 us  [the longest x20 39.9 us: butterfly(): x = merge(x, lax.ppermute(x, axis, pairs))]
    gather x3 -> x1, local copies, waits for them, and re-layouts: 12.4 us -> 2.03 us  [shards(): recv_keys[picked]]
    gather x3 -> x1, local copies, waits for them, and re-layouts: 12.4 us -> 3.74 us  [shards(): recv_values[picked]]
  transfers between devices with their start and end apart: 11 -> 29, of which waited for: 3 -> 14; matrix products, arithmetic and copies ran while one was open for 5% -> 28% of each run, Pallas kernels for 0% -> 0%
where the time goes in v1:
time: 261 us; the launch traced here: 258 us
  waiting for transfers between devices  116 us (44%)
  starting transfers between devices  64.7 us (25%)
  local copies, waits for them, and re-layouts  41.1 us (16%)
  other arithmetic  27.2 us (10%)
  matrix products  8 us (3%)
    ppermute x20, waiting for transfers between devices, butterfly(): x = merge(x, lax.ppermute(x, axis, pairs))  116 us
    ppermute x20, starting transfers between devices, butterfly(): x = merge(x, lax.ppermute(x, axis, pairs))  39.9 us
    ppermute x9, starting transfers between devices, passed_along(): lax.ppermute(array, SEQ_PARTS, [(i, (i + by) % count) for i in range(coun...  24.8 us
    unnamed x64, local copies, waits for them, and re-layouts  9.99 us
    reshape x1, local copies, waits for them, and re-layouts, shards(): row_keys = key_cache.reshape(-1, heads_here, HDIM)  5.51 us
  transfers between devices with their start and end apart: 29, of which 14 were waited for; matrix products, arithmetic and copies ran while one was open for 28% of the time, Pallas kernels for 0%

profile of v1, /device:TPU:6, one launch (start us, length us, event | category | flops | bytes accessed | tf_op | source)
XLA Modules:
  0.0 258.1 jit_solution(11129616786539888342)
XLA Ops:
  3.9 2.5 collective-permute-done.10
  6.4 1.7 collective-permute-start.11
  8.1 3.4 %collective-permute-done.11 = f32[64]{0:T(128)S(1)} collective-permute-done((f32[64]{0:T(128)S(1)}, f32[64]{0:T(128)S(1)}, u32[]{:S(2)}, u32[]{:S(2)}) %collective-permute-start.11) | collective-permute-done | bytes 288 | tf_op jit(solution)/shard_map/ppermute | solution.py:37
  11.5 1.9 collective-permute-start.12
  15.0 3.3 %collective-permute-start.13 = (f32[64]{0:T(128)S(1)}, f32[64]{0:T(128)S(1)}, u32[]{:S(2)}, u32[]{:S(2)}) collective-permute-start(f32[64]{0:T(128)S(1)} %add.155), channel_id=1, source_target_pairs={{0,16},{8,24},{16,0},{24,8},{32,48},{40,56},{48,32},{56,40},{1,17}... | collective-permute-start | bytes 776 | tf_op jit(solution)/shard_map/ppermute | solution.py:37
  18.5 1.3 collective-permute-done.13
  19.8 6.8 %collective-permute-start.14 = (f32[64]{0:T(128)S(1)}, f32[64]{0:T(128)S(1)}, u32[]{:S(2)}, u32[]{:S(2)}) collective-permute-start(f32[64]{0:T(128)S(1)} %add.156), channel_id=1, source_target_pairs={{0,32},{8,40},{16,48},{24,56},{32,0},{40,8},{48,16},{56,24},{1,33}... | collective-permute-start | bytes 776 | tf_op jit(solution)/shard_map/ppermute | solution.py:37
  32.1 10.3 %collective-permute-done.16 = f32[64,1536]{1,0:T(8,128)S(1)} collective-permute-done((f32[64,1536]{1,0:T(8,128)S(1)}, f32[64,1536]{1,0:T(8,128)S(1)}, u32[]{:S(2)}, u32[]{:S(2)}) %collective-permute-start.16) | collective-permute-done | bytes 393248 | tf_op jit(solution)/shard_map/ppermute | solution.py:37
  42.5 1.5 collective-permute-start.17
  44.6 2.6 collective-permute-start.1
  47.6 7.0 %collective-permute-done.17 = f32[64,1536]{1,0:T(8,128)S(1)} collective-permute-done((f32[64,1536]{1,0:T(8,128)S(1)}, f32[64,1536]{1,0:T(8,128)S(1)}, u32[]{:S(2)}, u32[]{:S(2)}) %collective-permute-start.17) | collective-permute-done | bytes 393248 | tf_op jit(solution)/shard_map/ppermute | solution.py:37
  54.6 1.1 collective-permute-start.18
  55.8 8.5 %collective-permute-done.18 = f32[64,1536]{1,0:T(8,128)S(1)} collective-permute-done((f32[64,1536]{1,0:T(8,128)S(1)}, f32[64,1536]{1,0:T(8,128)S(1)}, u32[]{:S(2)}, u32[]{:S(2)}) %collective-permute-start.18) | collective-permute-done | bytes 393248 | tf_op jit(solution)/shard_map/ppermute | solution.py:37
  64.3 2.2 collective-permute-start.19
  68.7 13.7 %collective-permute-done.19 = f32[64,1536]{1,0:T(8,128)S(1)} collective-permute-done((f32[64,1536]{1,0:T(8,128)S(1)}, f32[64,1536]{1,0:T(8,128)S(1)}, u32[]{:S(2)}, u32[]{:S(2)}) %collective-permute-start.19) | collective-permute-done | bytes 393248 | tf_op jit(solution)/shard_map/ppermute | solution.py:37
  83.2 5.9 %collective-permute-start.20 = (f32[64,1536]{1,0:T(8,128)}, f32[64,1536]{1,0:T(8,128)}, u32[]{:S(2)}, u32[]{:S(2)}) collective-permute-start(f32[64,1536]{1,0:T(8,128)} %add.164), channel_id=1, source_target_pairs={{0,32},{8,40},{16,48},{24,56},{32,0},{40,8},{48,16},{56,24},{1,33}... | collective-permute-start | bytes 1179656 | tf_op jit(solution)/shard_map/ppermute | solution.py:37
  89.2 3.3 %copy.89 = bf16[18,128,512]{1,0,2:T(8,128)(2,1)} copy(bf16[18,128,512]{2,1,0:T(8,128)(2,1)S(1)} %copy-done.1) | data formatting | bytes 4718592 | tf_op args[7]
  92.5 4.7 %copy.91 = bf16[18,128,512]{1,0,2:T(8,128)(2,1)} copy(bf16[18,128,512]{2,1,0:T(8,128)(2,1)} %param.18) | data formatting | bytes 4718592 | tf_op args[8]
  97.2 2.0 gather_fusion.2
  99.9 5.5 %reshape.245 = bf16[2304,8,64]{0,2,1:T(8,128)(2,1)} reshape(bf16[18,128,512]{1,0,2:T(8,128)(2,1)} %copy.89) | data formatting | bytes 4718592 | tf_op jit(solution)/shard_map/reshape | solution.py:192
  106.2 2.6 %reshape.247 = bf16[2304,8,64]{0,2,1:T(8,128)(2,1)} reshape(bf16[18,128,512]{1,0,2:T(8,128)(2,1)S(1)} %copy-done.4) | data formatting | bytes 4718592 | tf_op jit(solution)/shard_map/reshape | solution.py:193
  109.1 1.9 add.165
  111.0 1.3 reshape.244
  113.4 1.3 fusion.56
  114.8 1.1 fusion.2
  115.9 1.4 copy-done.8
  118.3 3.6 %fusion.4 = f32[8,64,64]{2,1,0:T(8,128)S(1)} fusion(f32[8,64,2322]{2,1,0:T(8,128)} %copy-done.8, bf16[18,8,64]{0,2,1:T(8,128)(2,1)} %bitcast.102, bf16[2304,8,64]{0,2,1:T(8,128)(2,1)S(1)} %copy-done.9, f32[8,64]{1,0:T(8,128)S(1)} %get-tuple-element.62, pred[64,2322]{1,0:T(8,128)(4,1)} %copy-done.15), kind=kOutput, calls=%fused_computation.13 | convolution fusion | flops 160496640 | bytes 7414912 | tf_op jit(solution)/shard_map/hrn,nhd->hrd/dot_general | solution.py:215
  122.8 1.4 slice_bitcast_fusion.1
  125.2 2.1 gather_fusion.4
  127.4 1.4 exponential_reduce_fusion.11
  128.8 1.4 fusion.22
  131.2 1.4 slice_bitcast_fusion
  134.0 1.9 collective-permute-start.6
  136.7 4.5 %collective-permute-done.22 = f32[8,64,66]{2,1,0:T(8,128)S(1)} collective-permute-done((f32[8,64,66]{2,1,0:T(8,128)S(1)}, f32[8,64,66]{2,1,0:T(8,128)S(1)}, u32[]{:S(2)}, u32[]{:S(2)}) %collective-permute-start.22) | collective-permute-done | bytes 135200 | tf_op jit(solution)/shard_map/ppermute | solution.py:37
  142.1 8.3 %collective-permute-done.23 = f32[8,64,66]{2,1,0:T(8,128)S(1)} collective-permute-done((f32[8,64,66]{2,1,0:T(8,128)S(1)}, f32[8,64,66]{2,1,0:T(8,128)S(1)}, u32[]{:S(2)}, u32[]{:S(2)}) %collective-permute-start.23) | collective-permute-done | bytes 135200 | tf_op jit(solution)/shard_map/ppermute | solution.py:37
  152.0 15.5 %collective-permute-done.24 = f32[8,64,66]{2,1,0:T(8,128)S(1)} collective-permute-done((f32[8,64,66]{2,1,0:T(8,128)S(1)}, f32[8,64,66]{2,1,0:T(8,128)S(1)}, u32[]{:S(2)}, u32[]{:S(2)}) %collective-permute-start.24) | collective-permute-done | bytes 135200 | tf_op jit(solution)/shard_map/ppermute | solution.py:37
  168.3 3.2 %collective-permute-start.25 = (f32[8,64,66]{2,1,0:T(8,128)S(1)}, f32[8,64,66]{2,1,0:T(8,128)S(1)}, u32[]{:S(2)}, u32[]{:S(2)}) collective-permute-start(f32[8,64,66]{2,1,0:T(8,128)S(1)} %pad_maximum_fusion.6), channel_id=1, source_target_pairs={{0,16},{8,24},{16,0},{24,8},{32,48},{40,56},{48,32},{56,40},{1,17}... | collective-permute-start | bytes 405512 | tf_op jit(solution)/shard_map/ppermute | solution.py:37
  172.0 6.6 %collective-permute-done.25 = f32[8,64,66]{2,1,0:T(8,128)S(1)} collective-permute-done((f32[8,64,66]{2,1,0:T(8,128)S(1)}, f32[8,64,66]{2,1,0:T(8,128)S(1)}, u32[]{:S(2)}, u32[]{:S(2)}) %collective-permute-start.25) | collective-permute-done | bytes 135200 | tf_op jit(solution)/shard_map/ppermute | solution.py:37
  178.7 19.3 %collective-permute-start.7 = (bf16[4,128,512]{2,1,0:T(8,128)(2,1)}, bf16[4,128,512]{2,1,0:T(8,128)(2,1)}, u32[]{:S(2)}, u32[]{:S(2)}) collective-permute-start(bf16[4,128,512]{2,1,0:T(8,128)(2,1)} %get-tuple-element.25), channel_id=1, source_target_pairs={{0,2},{1,3},{2,4},{3,5},{4,6},{5,7},{6,8},{7,9},{8,10},{9,11},{10,... | collective-permute-start | bytes 1572872 | tf_op jit(solution)/shard_map/ppermute | solution.py:70
  198.8 4.6 %collective-permute-start.26 = (f32[8,64,66]{2,1,0:T(8,128)S(1)}, f32[8,64,66]{2,1,0:T(8,128)S(1)}, u32[]{:S(2)}, u32[]{:S(2)}) collective-permute-start(f32[8,64,66]{2,1,0:T(8,128)S(1)} %pad_maximum_fusion.7), channel_id=1, source_target_pairs={{0,32},{8,40},{16,48},{24,56},{32,0},{40,8},{48,16},{56,24},{1,33}... | collective-permute-start | bytes 405512 | tf_op jit(solution)/shard_map/ppermute | solution.py:37
  203.5 1.6 pad_maximum_fusion
  205.4 33.2 %collective-permute-done.26 = f32[8,64,66]{2,1,0:T(8,128)S(1)} collective-permute-done((f32[8,64,66]{2,1,0:T(8,128)S(1)}, f32[8,64,66]{2,1,0:T(8,128)S(1)}, u32[]{:S(2)}, u32[]{:S(2)}) %collective-permute-start.26) | collective-permute-done | bytes 135200 | tf_op jit(solution)/shard_map/ppermute | solution.py:37
  240.2 1.7 collective-permute-start.27
  241.9 2.9 %pad_maximum_fusion.1 = bf16[4,4,128,512]{3,2,1,0:T(8,128)(2,1)} fusion(bf16[1,4,128,512]{3,2,1,0:T(8,128)(2,1)} %bitcast.22, bf16[1,4,128,512]{3,2,1,0:T(8,128)(2,1)} %bitcast.21, bf16[1,4,128,512]{3,2,1,0:T(8,128)(2,1)} %bitcast.20, bf16[1,4,128,512]{3,2,1,0:T(8,128)(2,1)S(1)} %copy-done.12), kind=kLoop, calls=%fused_computation.24 | loop fusion | flops 3145728 | bytes 4194304 | tf_op jit(solution)/shard_map/stack | solution.py:176
  244.9 2.0 gather_fusion.3
  246.9 3.7 %gather_fusion.5 = bf16[16,128,512]{2,1,0:T(8,128)(2,1)} fusion(bf16[16,128,512]{2,1,0:T(8,128)(2,1)} %bitcast.100, s32[1024]{0:T(1024)S(1)} %pad_clamp_fusion), kind=kCustom, calls=%fused_computation.5 | custom fusion | bytes 4194368 | tf_op jit(solution)/shard_map/gather | solution.py:188
  250.6 3.0 %collective-permute-start.28 = (f32[64,32]{0,1:T(8,128)S(1)}, f32[64,32]{0,1:T(8,128)S(1)}, u32[]{:S(2)}, u32[]{:S(2)}) collective-permute-start(f32[64,32]{0,1:T(8,128)S(1)} %add.178), channel_id=1, source_target_pairs={{0,128},{64,192},{128,0},{192,64},{1,129},{65,193},{129,1},{193,65... | collective-permute-start | bytes 24584 | tf_op jit(solution)/shard_map/ppermute | solution.py:37
  253.6 3.9 %broadcast_select_fusion = (bf16[16,128,512]{2,1,0:T(8,128)(2,1)}, bf16[16,128,512]{2,1,0:T(8,128)(2,1)}) fusion(bf16[16,128,512]{2,1,0:T(8,128)(2,1)} %gather_fusion.5, pred[16]{0:T(512)(128)(4,1)S(1)} %fusion.39, bf16[16,128,512]{2,1,0:T(8,128)(2,1)S(1)} %copy-done.7), kind=kLoop, calls=%fused_computation.25 | loop fusion | flops 2097152 | bytes 8388624 | tf_op jit(solution)/shard_map/jit(_where)/select_n | solution.py:187
  (181 shorter events, 30.6 us)
Async XLA Ops:
  0.6 239.5 %copy-start = (bf16[512,32]{0,1:T(8,128)(2,1)S(1)}, bf16[512,32]{0,1:T(8,128)(2,1)}, u32[]{:S(2)}) copy-start(bf16[512,32]{0,1:T(8,128)(2,1)} %param.12) | copy-start | bytes 98308
  1.4 1.4 collective-permute-start.9
  2.8 3.6 %collective-permute-start.10 = (f32[64]{0:T(128)S(1)}, f32[64]{0:T(128)S(1)}, u32[]{:S(2)}, u32[]{:S(2)}) collective-permute-start(f32[64]{0:T(128)S(1)} %add.152), channel_id=1, source_target_pairs={{0,2},{2,0},{4,6},{6,4},{1,3},{3,1},{5,7},{7,5},{8,10},{10,8},{12,... | collective-permute-start | bytes 776 | tf_op jit(solution)/shard_map/ppermute | solution.py:37
  6.4 5.0 %collective-permute-start.11 = (f32[64]{0:T(128)S(1)}, f32[64]{0:T(128)S(1)}, u32[]{:S(2)}, u32[]{:S(2)}) collective-permute-start(f32[64]{0:T(128)S(1)} %add.153), channel_id=1, source_target_pairs={{0,4},{2,6},{4,0},{6,2},{1,5},{3,7},{5,1},{7,3},{8,12},{10,14},{12... | collective-permute-start | bytes 776 | tf_op jit(solution)/shard_map/ppermute | solution.py:37
  11.5 3.5 %collective-permute-start.12 = (f32[64]{0:T(128)S(1)}, f32[64]{0:T(128)S(1)}, u32[]{:S(2)}, u32[]{:S(2)}) collective-permute-start(f32[64]{0:T(128)S(1)} %add.154), channel_id=1, source_target_pairs={{0,8},{8,0},{16,24},{24,16},{32,40},{40,32},{48,56},{56,48},{1,9},... | collective-permute-start | bytes 776 | tf_op jit(solution)/shard_map/ppermute | solution.py:37
  15.0 4.8 %collective-permute-start.13 = (f32[64]{0:T(128)S(1)}, f32[64]{0:T(128)S(1)}, u32[]{:S(2)}, u32[]{:S(2)}) collective-permute-start(f32[64]{0:T(128)S(1)} %add.155), channel_id=1, source_target_pairs={{0,16},{8,24},{16,0},{24,8},{32,48},{40,56},{48,32},{56,40},{1,17}... | collective-permute-start | bytes 776 | tf_op jit(solution)/shard_map/ppermute | solution.py:37
  19.8 8.4 %collective-permute-start.14 = (f32[64]{0:T(128)S(1)}, f32[64]{0:T(128)S(1)}, u32[]{:S(2)}, u32[]{:S(2)}) collective-permute-start(f32[64]{0:T(128)S(1)} %add.156), channel_id=1, source_target_pairs={{0,32},{8,40},{16,48},{24,56},{32,0},{40,8},{48,16},{56,24},{1,33}... | collective-permute-start | bytes 776 | tf_op jit(solution)/shard_map/ppermute | solution.py:37
  29.2 1.8 collective-permute-start.15
  29.4 67.7 %copy-start.26 = (s32[1024]{0:T(1024)}, s32[1024]{0:T(1024)S(1)}, u32[]{:S(2)}) copy-start(s32[1024]{0:T(1024)S(1)} %pad_clamp_fusion.1) | copy-start | bytes 12292
  30.8 35.8 %copy-start.2 = (bf16[18,128,512]{2,1,0:T(8,128)(2,1)S(1)}, bf16[18,128,512]{2,1,0:T(8,128)(2,1)}, u32[]{:S(2)}) copy-start(bf16[18,128,512]{2,1,0:T(8,128)(2,1)} %param.18) | copy-start | bytes 7077892
  30.8 35.8 %copy-start.25 = (f32[18,128]{1,0:T(8,128)S(1)}, f32[18,128]{1,0:T(8,128)}, u32[]{:S(2)}) copy-start(f32[18,128]{1,0:T(8,128)} %param.19) | copy-start | bytes 27652
  31.0 11.4 %collective-permute-start.16 = (f32[64,1536]{1,0:T(8,128)S(1)}, f32[64,1536]{1,0:T(8,128)S(1)}, u32[]{:S(2)}, u32[]{:S(2)}) collective-permute-start(f32[64,1536]{1,0:T(8,128)S(1)} %add.160), channel_id=1, source_target_pairs={{0,2},{2,0},{4,6},{6,4},{1,3},{3,1},{5,7},{7,5},{8,10},{10,8},{12,... | collective-permute-start | bytes 1179656 | tf_op jit(solution)/shard_map/ppermute | solution.py:37
  42.5 12.1 %collective-permute-start.17 = (f32[64,1536]{1,0:T(8,128)S(1)}, f32[64,1536]{1,0:T(8,128)S(1)}, u32[]{:S(2)}, u32[]{:S(2)}) collective-permute-start(f32[64,1536]{1,0:T(8,128)S(1)} %add.161), channel_id=1, source_target_pairs={{0,4},{2,6},{4,0},{6,2},{1,5},{3,7},{5,1},{7,3},{8,12},{10,14},{12... | collective-permute-start | bytes 1179656 | tf_op jit(solution)/shard_map/ppermute | solution.py:37
  44.6 88.0 %collective-permute-start = (bf16[4,2]{0,1:T(2,128)(2,1)}, bf16[4,2]{0,1:T(2,128)(2,1)}, u32[]{:S(2)}, u32[]{:S(2)}) collective-permute-start(bf16[4,2]{0,1:T(2,128)(2,1)} %get-tuple-element.57), channel_id=1, source_target_pairs={{0,1},{1,2},{2,3},{3,4},{4,5},{5,6},{6,7},{7,8},{8,9},{9,10},{10,1... | collective-permute-start | bytes 56 | tf_op jit(solution)/shard_map/ppermute | solution.py:70
  44.6 88.7 %collective-permute-start.1 = (bf16[4,2]{0,1:T(2,128)(2,1)}, bf16[4,2]{0,1:T(2,128)(2,1)}, u32[]{:S(2)}, u32[]{:S(2)}) collective-permute-start(bf16[4,2]{0,1:T(2,128)(2,1)} %get-tuple-element.56), channel_id=1, source_target_pairs={{0,2},{1,3},{2,4},{3,5},{4,6},{5,7},{6,8},{7,9},{8,10},{9,11},{10,... | collective-permute-start | bytes 56 | tf_op jit(solution)/shard_map/ppermute | solution.py:70
  47.2 86.8 %collective-permute-start.2 = (bf16[4,2]{0,1:T(2,128)(2,1)}, bf16[4,2]{0,1:T(2,128)(2,1)}, u32[]{:S(2)}, u32[]{:S(2)}) collective-permute-start(bf16[4,2]{0,1:T(2,128)(2,1)} %get-tuple-element.55), channel_id=1, source_target_pairs={{0,3},{1,4},{2,5},{3,6},{4,7},{5,8},{6,9},{7,10},{8,11},{9,12},{10... | collective-permute-start | bytes 56 | tf_op jit(solution)/shard_map/ppermute | solution.py:70
  47.6 20.1 %copy-start.1 = (bf16[18,128,512]{2,1,0:T(8,128)(2,1)S(1)}, bf16[18,128,512]{2,1,0:T(8,128)(2,1)}, u32[]{:S(2)}) copy-start(bf16[18,128,512]{2,1,0:T(8,128)(2,1)} %param.17) | copy-start | bytes 7077892
  54.6 9.7 %collective-permute-start.18 = (f32[64,1536]{1,0:T(8,128)S(1)}, f32[64,1536]{1,0:T(8,128)S(1)}, u32[]{:S(2)}, u32[]{:S(2)}) collective-permute-start(f32[64,1536]{1,0:T(8,128)S(1)} %add.162), channel_id=1, source_target_pairs={{0,8},{8,0},{16,24},{24,16},{32,40},{40,32},{48,56},{56,48},{1,9},... | collective-permute-start | bytes 1179656 | tf_op jit(solution)/shard_map/ppermute | solution.py:37
  55.8 58.9 %copy-start.15 = (pred[64,2322]{1,0:T(8,128)(4,1)}, pred[64,2322]{1,0:T(8,128)(4,1)S(1)}, u32[]{:S(2)}) copy-start(pred[64,2322]{1,0:T(8,128)(4,1)S(1)} %iota_compare_fusion) | copy-start | bytes 445828
  64.3 18.1 %collective-permute-start.19 = (f32[64,1536]{1,0:T(8,128)S(1)}, f32[64,1536]{1,0:T(8,128)S(1)}, u32[]{:S(2)}, u32[]{:S(2)}) collective-permute-start(f32[64,1536]{1,0:T(8,128)S(1)} %add.163), channel_id=1, source_target_pairs={{0,16},{8,24},{16,0},{24,8},{32,48},{40,56},{48,32},{56,40},{1,17}... | collective-permute-start | bytes 1179656 | tf_op jit(solution)/shard_map/ppermute | solution.py:37
  83.2 25.9 %collective-permute-start.20 = (f32[64,1536]{1,0:T(8,128)}, f32[64,1536]{1,0:T(8,128)}, u32[]{:S(2)}, u32[]{:S(2)}) collective-permute-start(f32[64,1536]{1,0:T(8,128)} %add.164), channel_id=1, source_target_pairs={{0,32},{8,40},{16,48},{24,56},{32,0},{40,8},{48,16},{56,24},{1,33}... | collective-permute-start | bytes 1179656 | tf_op jit(solution)/shard_map/ppermute | solution.py:37
  89.2 10.6 %copy-start.24 = (bf16[18,512]{1,0:T(8,128)(2,1)}, bf16[18,512]{1,0:T(8,128)(2,1)S(1)}, u32[]{:S(2)}) copy-start(bf16[18,512]{1,0:T(8,128)(2,1)S(1)} %get-tuple-element.48) | copy-start | bytes 55300
  89.2 16.2 %copy-start.23 = (bf16[18,512]{1,0:T(8,128)(2,1)}, bf16[18,512]{1,0:T(8,128)(2,1)S(1)}, u32[]{:S(2)}) copy-start(bf16[18,512]{1,0:T(8,128)(2,1)S(1)} %get-tuple-element.47) | copy-start | bytes 55300
  99.9 6.3 %copy-start.4 = (bf16[18,128,512]{1,0,2:T(8,128)(2,1)S(1)}, bf16[18,128,512]{1,0,2:T(8,128)(2,1)}, u32[]{:S(2)}) copy-start(bf16[18,128,512]{1,0,2:T(8,128)(2,1)} %copy.91) | copy-start | bytes 7077892
  118.3 3.6 %copy-start.11 = (f32[8,64,1]{2,1,0:T(8,128)S(1)}, f32[8,64,1]{2,1,0:T(8,128)}, u32[]{:S(2)}) copy-start(f32[8,64,1]{2,1,0:T(8,128)} %copy.93) | copy-start | bytes 6148
  118.3 4.5 %copy-start.5 = (bf16[16,128,512]{2,1,0:T(8,128)(2,1)S(1)}, bf16[16,128,512]{2,1,0:T(8,128)(2,1)}, u32[]{:S(2)}) copy-start(bf16[16,128,512]{2,1,0:T(8,128)(2,1)} %gather_fusion.2) | copy-start | bytes 6291460
  122.8 4.5 %collective-permute-start.21 = (f32[8,64,66]{2,1,0:T(8,128)}, f32[8,64,66]{2,1,0:T(8,128)}, u32[]{:S(2)}, u32[]{:S(2)}) collective-permute-start(f32[8,64,66]{2,1,0:T(8,128)} %pad_maximum_fusion.2), channel_id=1, source_target_pairs={{0,1},{1,0},{2,3},{3,2},{4,5},{5,4},{6,7},{7,6},{8,9},{9,8},{10,11... | collective-permute-start | bytes 405512 | tf_op jit(solution)/shard_map/ppermute | solution.py:37
  124.2 74.5 %collective-permute-start.3 = (bf16[4,128,512]{2,1,0:T(8,128)(2,1)}, bf16[4,128,512]{2,1,0:T(8,128)(2,1)}, u32[]{:S(2)}, u32[]{:S(2)}) collective-permute-start(bf16[4,128,512]{2,1,0:T(8,128)(2,1)} %get-tuple-element.30), channel_id=1, source_target_pairs={{0,1},{1,2},{2,3},{3,4},{4,5},{5,6},{6,7},{7,8},{8,9},{9,10},{10,1... | collective-permute-start | bytes 1572872 | tf_op jit(solution)/shard_map/ppermute | solution.py:70
  127.4 3.9 %copy-start.6 = (bf16[16,128,512]{2,1,0:T(8,128)(2,1)S(1)}, bf16[16,128,512]{2,1,0:T(8,128)(2,1)}, u32[]{:S(2)}) copy-start(bf16[16,128,512]{2,1,0:T(8,128)(2,1)} %gather_fusion.4) | copy-start | bytes 6291460
  130.4 10.8 %collective-permute-start.22 = (f32[8,64,66]{2,1,0:T(8,128)S(1)}, f32[8,64,66]{2,1,0:T(8,128)S(1)}, u32[]{:S(2)}, u32[]{:S(2)}) collective-permute-start(f32[8,64,66]{2,1,0:T(8,128)S(1)} %pad_maximum_fusion.3), channel_id=1, source_target_pairs={{0,2},{2,0},{4,6},{6,4},{1,3},{3,1},{5,7},{7,5},{8,10},{10,8},{12,... | collective-permute-start | bytes 405512 | tf_op jit(solution)/shard_map/ppermute | solution.py:37
  132.6 66.2 %collective-permute-start.4 = (bf16[4,128,512]{2,1,0:T(8,128)(2,1)}, bf16[4,128,512]{2,1,0:T(8,128)(2,1)}, u32[]{:S(2)}, u32[]{:S(2)}) collective-permute-start(bf16[4,128,512]{2,1,0:T(8,128)(2,1)} %get-tuple-element.29), channel_id=1, source_target_pairs={{0,2},{1,3},{2,4},{3,5},{4,6},{5,7},{6,8},{7,9},{8,10},{9,11},{10,... | collective-permute-start | bytes 1572872 | tf_op jit(solution)/shard_map/ppermute | solution.py:70
  133.4 70.1 %collective-permute-start.5 = (bf16[4,128,512]{2,1,0:T(8,128)(2,1)S(1)}, bf16[4,128,512]{2,1,0:T(8,128)(2,1)}, u32[]{:S(2)}, u32[]{:S(2)}) collective-permute-start(bf16[4,128,512]{2,1,0:T(8,128)(2,1)S(1)} %copy-done.22), channel_id=1, source_target_pairs={{0,3},{1,4},{2,5},{3,6},{4,7},{5,8},{6,9},{7,10},{8,11},{9,12},{10... | collective-permute-start | bytes 1572872 | tf_op jit(solution)/shard_map/ppermute | solution.py:70
  134.0 107.9 %collective-permute-start.6 = (bf16[4,128,512]{2,1,0:T(8,128)(2,1)}, bf16[4,128,512]{2,1,0:T(8,128)(2,1)}, u32[]{:S(2)}, u32[]{:S(2)}) collective-permute-start(bf16[4,128,512]{2,1,0:T(8,128)(2,1)} %get-tuple-element.26), channel_id=1, source_target_pairs={{0,1},{1,2},{2,3},{3,4},{4,5},{5,6},{6,7},{7,8},{8,9},{9,10},{10,1... | collective-permute-start | bytes 1572872 | tf_op jit(solution)/shard_map/ppermute | solution.py:70
  141.8 8.6 %collective-permute-start.23 = (f32[8,64,66]{2,1,0:T(8,128)S(1)}, f32[8,64,66]{2,1,0:T(8,128)S(1)}, u32[]{:S(2)}, u32[]{:S(2)}) collective-permute-start(f32[8,64,66]{2,1,0:T(8,128)S(1)} %pad_maximum_fusion.4), channel_id=1, source_target_pairs={{0,4},{2,6},{4,0},{6,2},{1,5},{3,7},{5,1},{7,3},{8,12},{10,14},{12... | collective-permute-start | bytes 405512 | tf_op jit(solution)/shard_map/ppermute | solution.py:37
  151.1 16.5 %collective-permute-start.24 = (f32[8,64,66]{2,1,0:T(8,128)S(1)}, f32[8,64,66]{2,1,0:T(8,128)S(1)}, u32[]{:S(2)}, u32[]{:S(2)}) collective-permute-start(f32[8,64,66]{2,1,0:T(8,128)S(1)} %pad_maximum_fusion.5), channel_id=1, source_target_pairs={{0,8},{8,0},{16,24},{24,16},{32,40},{40,32},{48,56},{56,48},{1,9},... | collective-permute-start | bytes 405512 | tf_op jit(solution)/shard_map/ppermute | solution.py:37
  152.0 51.4 %copy-start.13 = (bf16[1,4,128,512]{3,2,1,0:T(8,128)(2,1)S(1)}, bf16[1,4,128,512]{3,2,1,0:T(8,128)(2,1)}, u32[]{:S(2)}) copy-start(bf16[1,4,128,512]{3,2,1,0:T(8,128)(2,1)} %get-tuple-element.28) | copy-start | bytes 1572868
  168.3 10.4 %collective-permute-start.25 = (f32[8,64,66]{2,1,0:T(8,128)S(1)}, f32[8,64,66]{2,1,0:T(8,128)S(1)}, u32[]{:S(2)}, u32[]{:S(2)}) collective-permute-start(f32[8,64,66]{2,1,0:T(8,128)S(1)} %pad_maximum_fusion.6), channel_id=1, source_target_pairs={{0,16},{8,24},{16,0},{24,8},{32,48},{40,56},{48,32},{56,40},{1,17}... | collective-permute-start | bytes 405512 | tf_op jit(solution)/shard_map/ppermute | solution.py:37
  178.7 63.2 %collective-permute-start.7 = (bf16[4,128,512]{2,1,0:T(8,128)(2,1)}, bf16[4,128,512]{2,1,0:T(8,128)(2,1)}, u32[]{:S(2)}, u32[]{:S(2)}) collective-permute-start(bf16[4,128,512]{2,1,0:T(8,128)(2,1)} %get-tuple-element.25), channel_id=1, source_target_pairs={{0,2},{1,3},{2,4},{3,5},{4,6},{5,7},{6,8},{7,9},{8,10},{9,11},{10,... | collective-permute-start | bytes 1572872 | tf_op jit(solution)/shard_map/ppermute | solution.py:70
  198.7 6.4 %copy-start.16 = (bf16[64,8,32]{2,0,1:T(8,128)(2,1)S(1)}, bf16[64,8,32]{2,0,1:T(8,128)(2,1)}, u32[]{:S(2)}) copy-start(bf16[64,8,32]{2,0,1:T(8,128)(2,1)} %get-tuple-element.34) | copy-start | bytes 98308
  198.7 6.4 %copy-start.17 = (bf16[64,8,32]{2,0,1:T(8,128)(2,1)S(1)}, bf16[64,8,32]{2,0,1:T(8,128)(2,1)}, u32[]{:S(2)}) copy-start(bf16[64,8,32]{2,0,1:T(8,128)(2,1)} %get-tuple-element.35) | copy-start | bytes 98308
  198.7 6.4 %copy-start.19 = (bf16[64,8,32]{2,0,1:T(8,128)(2,1)S(1)}, bf16[64,8,32]{2,0,1:T(8,128)(2,1)}, u32[]{:S(2)}) copy-start(bf16[64,8,32]{2,0,1:T(8,128)(2,1)} %copy-done.18) | copy-start | bytes 98308
  198.7 6.4 %copy-start.21 = (bf16[64,8,32]{2,0,1:T(8,128)(2,1)S(1)}, bf16[64,8,32]{2,0,1:T(8,128)(2,1)}, u32[]{:S(2)}) copy-start(bf16[64,8,32]{2,0,1:T(8,128)(2,1)} %copy-done.20) | copy-start | bytes 98308
  198.7 43.2 %collective-permute-start.8 = (bf16[4,128,512]{2,1,0:T(8,128)(2,1)}, bf16[4,128,512]{2,1,0:T(8,128)(2,1)}, u32[]{:S(2)}, u32[]{:S(2)}) collective-permute-start(bf16[4,128,512]{2,1,0:T(8,128)(2,1)} %get-tuple-element.27), channel_id=1, source_target_pairs={{0,3},{1,4},{2,5},{3,6},{4,7},{5,8},{6,9},{7,10},{8,11},{9,12},{10... | collective-permute-start | bytes 1572872 | tf_op jit(solution)/shard_map/ppermute | solution.py:70
  198.8 39.8 %collective-permute-start.26 = (f32[8,64,66]{2,1,0:T(8,128)S(1)}, f32[8,64,66]{2,1,0:T(8,128)S(1)}, u32[]{:S(2)}, u32[]{:S(2)}) collective-permute-start(f32[8,64,66]{2,1,0:T(8,128)S(1)} %pad_maximum_fusion.7), channel_id=1, source_target_pairs={{0,32},{8,40},{16,48},{24,56},{32,0},{40,8},{48,16},{56,24},{1,33}... | collective-permute-start | bytes 405512 | tf_op jit(solution)/shard_map/ppermute | solution.py:37
  205.1 36.8 %copy-start.12 = (bf16[1,4,128,512]{3,2,1,0:T(8,128)(2,1)S(1)}, bf16[1,4,128,512]{3,2,1,0:T(8,128)(2,1)}, u32[]{:S(2)}) copy-start(bf16[1,4,128,512]{3,2,1,0:T(8,128)(2,1)} %get-tuple-element.24) | copy-start | bytes 1572868
  240.2 10.4 %collective-permute-start.27 = (f32[64,32]{0,1:T(8,128)S(1)}, f32[64,32]{0,1:T(8,128)S(1)}, u32[]{:S(2)}, u32[]{:S(2)}) collective-permute-start(f32[64,32]{0,1:T(8,128)S(1)} %fusion.57), channel_id=1, source_target_pairs={{0,64},{64,0},{128,192},{192,128},{1,65},{65,1},{129,193},{193,129... | collective-permute-start | bytes 24584 | tf_op jit(solution)/shard_map/ppermute | solution.py:37
  246.9 6.7 %copy-start.7 = (bf16[16,128,512]{2,1,0:T(8,128)(2,1)S(1)}, bf16[16,128,512]{2,1,0:T(8,128)(2,1)}, u32[]{:S(2)}) copy-start(bf16[16,128,512]{2,1,0:T(8,128)(2,1)} %gather_fusion.3) | copy-start | bytes 6291460
  250.6 6.9 %collective-permute-start.28 = (f32[64,32]{0,1:T(8,128)S(1)}, f32[64,32]{0,1:T(8,128)S(1)}, u32[]{:S(2)}, u32[]{:S(2)}) collective-permute-start(f32[64,32]{0,1:T(8,128)S(1)} %add.178), channel_id=1, source_target_pairs={{0,128},{64,192},{128,0},{192,64},{1,129},{65,193},{129,1},{193,65... | collective-permute-start | bytes 24584 | tf_op jit(solution)/shard_map/ppermute | solution.py:37
  (12 other events, 28.5 us)

commit v2 on v1

--- a/solution.py
+++ b/solution.py
@@ -111,11 +111,6 @@
         normed, w_qkv.reshape(w_qkv.shape[0], 3 * feat_width), preferred_element_type=jnp.float32
     )
     proj_all = seq_sum(partial_value).reshape(requests, 3, heads_here, HDIM)
-    cos_table, sin_table = rope_tables(positions, HDIM)
-    queries = rotate_half(proj_all[:, 0], cos_table, sin_table).astype(jnp.bfloat16)
-    new_keys = rotate_half(proj_all[:, 1], cos_table, sin_table).astype(jnp.bfloat16)
-    new_values = proj_all[:, 2].astype(jnp.bfloat16)
-
     block_ids = jnp.arange(n_blocks, dtype=jnp.int32)
     global_ids = my_index * n_blocks + block_ids
     req_ends = jnp.cumsum(req_blocks)
@@ -167,6 +162,9 @@
         axis=-1,
     )
     meta_data = meta_data.astype(jnp.float32).astype(jnp.bfloat16).reshape(HOPS, CAP, 2)
+    send_keys, send_values, meta_data, proj_all = lax.optimization_barrier(
+        (send_keys, send_values, meta_data, proj_all)
+    )
     arrived = [(send_keys[0], send_values[0], meta_data[0])]
     for distance in range(1, HOPS):
         arrived.append(
@@ -189,6 +187,11 @@
     )
     packed_request = jnp.where(filled, recv_meta[picked, 1], -1)
 
+    cos_table, sin_table = rope_tables(positions, HDIM)
+    queries = rotate_half(proj_all[:, 0], cos_table, sin_table).astype(jnp.bfloat16)
+    new_keys = rotate_half(proj_all[:, 1], cos_table, sin_table).astype(jnp.bfloat16)
+    new_values = proj_all[:, 2].astype(jnp.bfloat16)
+
     row_keys = key_cache.reshape(-1, heads_here, HDIM)
     row_values = value_cache.reshape(-1, heads_here, HDIM)
     row_req = jnp.repeat(jnp.where(is_kept, blk_req, -1), row_count)
@@ -217,6 +220,9 @@
     )
     stats = jnp.concatenate(
         [local_acc, local_sum[..., None], local_top[..., None]], axis=-1
+    )
+    recv_keys, recv_values, recv_meta, stats = lax.optimization_barrier(
+        (recv_keys, recv_values, recv_meta, stats)
     )
     stats = butterfly(stats, softmax_merge, reversed(SEQ_PARTS))
     mixture = stats[..., :HDIM]

time: 261 us -> 272 us (1.042)
  waiting for transfers between devices: 116 us -> 143 us
  starting transfers between devices: 64.7 us -> 54.2 us
    ppermute x9, waiting for transfers between devices: 0.02 us -> 45.3 us  [passed_along(): lax.ppermute(array, SEQ_PARTS, [(i, (i + by) % count) for i in range(coun...]
    ppermute x20, waiting for transfers between devices: 116 us -> 97.7 us  [butterfly(): x = merge(x, lax.ppermute(x, axis, pairs))]
    ppermute x9, starting transfers between devices: 24.8 us -> 14.4 us  [passed_along(): lax.ppermute(array, SEQ_PARTS, [(i, (i + by) % count) for i in range(coun...]
    unnamed x64 -> x57, local copies, waits for them, and re-layouts: 9.99 us -> 10.5 us
  transfers between devices with their start and end apart: 29 -> 29, of which waited for: 14 -> 23; matrix products, arithmetic and copies ran while one was open for 28% -> 20% of each run, Pallas kernels for 0% -> 0%
where the time goes in v2:
time: 272 us; the launch traced here: 270 us
  waiting for transfers between devices  143 us (53%)
  starting transfers between devices  54.2 us (20%)
  local copies, waits for them, and re-layouts  39 us (14%)
  other arithmetic  25.1 us (9%)
  matrix products  7.91 us (3%)
    ppermute x20, waiting for transfers between devices, butterfly(): x = merge(x, lax.ppermute(x, axis, pairs))  97.7 us
    ppermute x9, waiting for transfers between devices, passed_along(): lax.ppermute(array, SEQ_PARTS, [(i, (i + by) % count) for i in range(coun...  45.3 us
    ppermute x20, starting transfers between devices, butterfly(): x = merge(x, lax.ppermute(x, axis, pairs))  39.9 us
    ppermute x9, starting transfers between devices, passed_along(): lax.ppermute(array, SEQ_PARTS, [(i, (i + by) % count) for i in range(coun...  14.4 us
    unnamed x57, local copies, waits for them, and re-layouts  10.5 us
  transfers between devices with their start and end apart: 29, of which 23 were waited for; matrix products, arithmetic and copies ran while one was open for 20% of the time, Pallas kernels for 0%

profile of v2, /device:TPU:6, one launch (start us, length us, event | category | flops | bytes accessed | tf_op | source)
XLA Modules:
  0.0 270.3 jit_solution(2773411188926016363)
XLA Ops:
  4.1 2.1 collective-permute-done.1
  6.1 1.7 collective-permute-start.2
  8.0 3.2 %collective-permute-done.2 = f32[64]{0:T(128)S(1)} collective-permute-done((f32[64]{0:T(128)S(1)}, f32[64]{0:T(128)S(1)}, u32[]{:S(2)}, u32[]{:S(2)}) %collective-permute-start.2) | collective-permute-done | bytes 288 | tf_op jit(solution)/shard_map/ppermute | solution.py:37
  11.2 1.9 collective-permute-start.3
  13.1 1.6 collective-permute-done.3
  14.7 3.3 %collective-permute-start.4 = (f32[64]{0:T(128)S(1)}, f32[64]{0:T(128)S(1)}, u32[]{:S(2)}, u32[]{:S(2)}) collective-permute-start(f32[64]{0:T(128)S(1)} %add.154), channel_id=1, source_target_pairs={{0,16},{8,24},{16,0},{24,8},{32,48},{40,56},{48,32},{56,40},{1,17}... | collective-permute-start | bytes 776 | tf_op jit(solution)/shard_map/ppermute | solution.py:37
  19.5 6.8 %collective-permute-start.5 = (f32[64]{0:T(128)S(1)}, f32[64]{0:T(128)S(1)}, u32[]{:S(2)}, u32[]{:S(2)}) collective-permute-start(f32[64]{0:T(128)S(1)} %add.155), channel_id=1, source_target_pairs={{0,32},{8,40},{16,48},{24,56},{32,0},{40,8},{48,16},{56,24},{1,33}... | collective-permute-start | bytes 776 | tf_op jit(solution)/shard_map/ppermute | solution.py:37
  31.8 10.1 %collective-permute-done.7 = f32[64,1536]{1,0:T(8,128)S(1)} collective-permute-done((f32[64,1536]{1,0:T(8,128)S(1)}, f32[64,1536]{1,0:T(8,128)S(1)}, u32[]{:S(2)}, u32[]{:S(2)}) %collective-permute-start.7) | collective-permute-done | bytes 393248 | tf_op jit(solution)/shard_map/ppermute | solution.py:37
  42.0 1.5 collective-permute-start.8
  44.9 2.7 fusion.44
  47.6 6.3 %collective-permute-done.8 = f32[64,1536]{1,0:T(8,128)S(1)} collective-permute-done((f32[64,1536]{1,0:T(8,128)S(1)}, f32[64,1536]{1,0:T(8,128)S(1)}, u32[]{:S(2)}, u32[]{:S(2)}) %collective-permute-start.8) | collective-permute-done | bytes 393248 | tf_op jit(solution)/shard_map/ppermute | solution.py:37
  56.2 7.2 %collective-permute-done.9 = f32[64,1536]{1,0:T(8,128)S(1)} collective-permute-done((f32[64,1536]{1,0:T(8,128)S(1)}, f32[64,1536]{1,0:T(8,128)S(1)}, u32[]{:S(2)}, u32[]{:S(2)}) %collective-permute-start.9) | collective-permute-done | bytes 393248 | tf_op jit(solution)/shard_map/ppermute | solution.py:37
  63.5 2.3 collective-permute-start.10
  65.9 15.5 %collective-permute-done.10 = f32[64,1536]{1,0:T(8,128)S(1)} collective-permute-done((f32[64,1536]{1,0:T(8,128)S(1)}, f32[64,1536]{1,0:T(8,128)S(1)}, u32[]{:S(2)}, u32[]{:S(2)}) %collective-permute-start.10) | collective-permute-done | bytes 393248 | tf_op jit(solution)/shard_map/ppermute | solution.py:37
  82.2 5.9 %collective-permute-start.11 = (f32[64,1536]{1,0:T(8,128)}, f32[64,1536]{1,0:T(8,128)}, u32[]{:S(2)}, u32[]{:S(2)}) collective-permute-start(f32[64,1536]{1,0:T(8,128)} %add.163), channel_id=1, source_target_pairs={{0,32},{8,40},{16,48},{24,56},{32,0},{40,8},{48,16},{56,24},{1,33}... | collective-permute-start | bytes 1179656 | tf_op jit(solution)/shard_map/ppermute | solution.py:37
  88.2 2.0 gather_fusion
  90.2 3.7 %gather_fusion.1 = bf16[16,128,512]{2,1,0:T(8,128)(2,1)} fusion(bf16[18,128,512]{2,1,0:T(8,128)(2,1)} %param.18, s32[1024]{0:T(1024)S(1)} %pad_clamp_fusion.1), kind=kCustom, calls=%fused_computation.1 | custom fusion | bytes 4194368 | tf_op jit(solution)/shard_map/gather | solution.py:159
  93.8 3.2 %copy.75 = bf16[18,128,512]{1,0,2:T(8,128)(2,1)} copy(bf16[18,128,512]{2,1,0:T(8,128)(2,1)S(1)} %copy-done.1) | data formatting | bytes 4718592 | tf_op args[7]
  97.0 3.4 %copy.77 = bf16[18,128,512]{1,0,2:T(8,128)(2,1)S(1)} copy(bf16[18,128,512]{2,1,0:T(8,128)(2,1)} %param.18) | data formatting | bytes 4718592 | tf_op args[8]
  101.4 5.4 %reshape.244 = bf16[2304,8,64]{0,2,1:T(8,128)(2,1)} reshape(bf16[18,128,512]{1,0,2:T(8,128)(2,1)} %copy.75) | data formatting | bytes 4718592 | tf_op jit(solution)/shard_map/reshape | solution.py:195
  107.6 2.6 reshape.246
  110.4 1.3 add.164
  114.2 1.4 collective-permute-start.17
  115.9 1.8 collective-permute-start.13
  119.3 1.4 fusion.58
  123.1 1.8 fusion.4
  124.9 19.6 %collective-permute-done.12 = bf16[4,2]{0,1:T(2,128)(2,1)S(1)} collective-permute-done((bf16[4,2]{0,1:T(2,128)(2,1)S(1)}, bf16[4,2]{0,1:T(2,128)(2,1)S(1)}, u32[]{:S(2)}, u32[]{:S(2)}) %collective-permute-start.12) | collective-permute-done | bytes 48 | tf_op jit(solution)/shard_map/ppermute | solution.py:70
  145.2 2.4 collective-permute-start.18
  147.7 1.2 collective-permute-done.14
  148.9 8.5 %collective-permute-start.19 = (bf16[4,128,512]{2,1,0:T(8,128)(2,1)}, bf16[4,128,512]{2,1,0:T(8,128)(2,1)}, u32[]{:S(2)}, u32[]{:S(2)}) collective-permute-start(bf16[4,128,512]{2,1,0:T(8,128)(2,1)} %get-tuple-element.36), channel_id=1, source_target_pairs={{0,2},{1,3},{2,4},{3,5},{4,6},{5,7},{6,8},{7,9},{8,10},{9,11},{10,... | collective-permute-start | bytes 1572872 | tf_op jit(solution)/shard_map/ppermute | solution.py:70
  161.2 1.6 pad_maximum_fusion
  162.8 1.9 collective-permute-done.18
  164.8 10.9 %collective-permute-done.19 = bf16[4,128,512]{2,1,0:T(8,128)(2,1)} collective-permute-done((bf16[4,128,512]{2,1,0:T(8,128)(2,1)}, bf16[4,128,512]{2,1,0:T(8,128)(2,1)}, u32[]{:S(2)}, u32[]{:S(2)}) %collective-permute-start.19) | collective-permute-done | bytes 524320 | tf_op jit(solution)/shard_map/ppermute | solution.py:70
  175.7 10.8 %collective-permute-done.20 = bf16[4,128,512]{2,1,0:T(8,128)(2,1)} collective-permute-done((bf16[4,128,512]{2,1,0:T(8,128)(2,1)}, bf16[4,128,512]{2,1,0:T(8,128)(2,1)}, u32[]{:S(2)}, u32[]{:S(2)}) %collective-permute-start.20) | collective-permute-done | bytes 524320 | tf_op jit(solution)/shard_map/ppermute | solution.py:70
  186.5 2.9 %pad_maximum_fusion.1 = bf16[4,4,128,512]{3,2,1,0:T(8,128)(2,1)} fusion(bf16[1,4,128,512]{3,2,1,0:T(8,128)(2,1)} %bitcast.25, bf16[1,4,128,512]{3,2,1,0:T(8,128)(2,1)} %bitcast.23, bf16[1,4,128,512]{3,2,1,0:T(8,128)(2,1)} %bitcast.21, bf16[1,4,128,512]{3,2,1,0:T(8,128)(2,1)S(1)} %get-tuple-element.34), kind=kLoop, calls=%fused_computation.24 | loop fusion | flops 3145728 | bytes 4194304 | tf_op jit(solution)/shard_map/stack | solution.py:174
  189.6 1.5 collective-permute-done.21
  191.9 8.3 %collective-permute-done.22 = f32[8,64,66]{2,1,0:T(8,128)S(1)} collective-permute-done((f32[8,64,66]{2,1,0:T(8,128)S(1)}, f32[8,64,66]{2,1,0:T(8,128)S(1)}, u32[]{:S(2)}, u32[]{:S(2)}) %collective-permute-start.22) | collective-permute-done | bytes 135200 | tf_op jit(solution)/shard_map/ppermute | solution.py:37
  201.0 7.8 %collective-permute-start.23 = (f32[8,64,66]{2,1,0:T(8,128)S(1)}, f32[8,64,66]{2,1,0:T(8,128)S(1)}, u32[]{:S(2)}, u32[]{:S(2)}) collective-permute-start(f32[8,64,66]{2,1,0:T(8,128)S(1)} %pad_maximum_fusion.4), channel_id=1, source_target_pairs={{0,4},{2,6},{4,0},{6,2},{1,5},{3,7},{5,1},{7,3},{8,12},{10,14},{12... | collective-permute-start | bytes 405512 | tf_op jit(solution)/shard_map/ppermute | solution.py:37
  209.1 6.0 %collective-permute-done.23 = f32[8,64,66]{2,1,0:T(8,128)S(1)} collective-permute-done((f32[8,64,66]{2,1,0:T(8,128)S(1)}, f32[8,64,66]{2,1,0:T(8,128)S(1)}, u32[]{:S(2)}, u32[]{:S(2)}) %collective-permute-start.23) | collective-permute-done | bytes 135200 | tf_op jit(solution)/shard_map/ppermute | solution.py:37
  215.9 7.3 %collective-permute-done.24 = f32[8,64,66]{2,1,0:T(8,128)S(1)} collective-permute-done((f32[8,64,66]{2,1,0:T(8,128)S(1)}, f32[8,64,66]{2,1,0:T(8,128)S(1)}, u32[]{:S(2)}, u32[]{:S(2)}) %collective-permute-start.24) | collective-permute-done | bytes 135200 | tf_op jit(solution)/shard_map/ppermute | solution.py:37
  224.9 12.2 %collective-permute-done.25 = f32[8,64,66]{2,1,0:T(8,128)S(1)} collective-permute-done((f32[8,64,66]{2,1,0:T(8,128)S(1)}, f32[8,64,66]{2,1,0:T(8,128)S(1)}, u32[]{:S(2)}, u32[]{:S(2)}) %collective-permute-start.25) | collective-permute-done | bytes 135200 | tf_op jit(solution)/shard_map/ppermute | solution.py:37
  238.9 13.9 %collective-permute-done.26 = f32[8,64,66]{2,1,0:T(8,128)S(1)} collective-permute-done((f32[8,64,66]{2,1,0:T(8,128)S(1)}, f32[8,64,66]{2,1,0:T(8,128)S(1)}, u32[]{:S(2)}, u32[]{:S(2)}) %collective-permute-start.26) | collective-permute-done | bytes 135200 | tf_op jit(solution)/shard_map/ppermute | solution.py:37
  253.8 1.2 fusion.27
  255.4 1.6 collective-permute-start.27
  257.0 2.0 gather_fusion.4
  259.0 3.7 %gather_fusion.5 = bf16[16,128,512]{2,1,0:T(8,128)(2,1)} fusion(bf16[16,128,512]{2,1,0:T(8,128)(2,1)} %bitcast.113, s32[1024]{0:T(1024)S(1)} %pad_clamp_fusion), kind=kCustom, calls=%fused_computation.5 | custom fusion | bytes 4194368 | tf_op jit(solution)/shard_map/gather | solution.py:186
  262.7 3.0 %collective-permute-start.28 = (f32[64,32]{0,1:T(8,128)S(1)}, f32[64,32]{0,1:T(8,128)S(1)}, u32[]{:S(2)}, u32[]{:S(2)}) collective-permute-start(f32[64,32]{0,1:T(8,128)S(1)} %add.178), channel_id=1, source_target_pairs={{0,128},{64,192},{128,0},{192,64},{1,129},{65,193},{129,1},{193,65... | collective-permute-start | bytes 24584 | tf_op jit(solution)/shard_map/ppermute | solution.py:37
  265.8 3.9 %broadcast_select_fusion = (bf16[16,128,512]{2,1,0:T(8,128)(2,1)}, bf16[16,128,512]{2,1,0:T(8,128)(2,1)}) fusion(bf16[16,128,512]{2,1,0:T(8,128)(2,1)} %gather_fusion.5, pred[16]{0:T(512)(128)(4,1)S(1)} %fusion.38, bf16[16,128,512]{2,1,0:T(8,128)(2,1)S(1)} %copy-done.4), kind=kLoop, calls=%fused_computation.25 | loop fusion | flops 2097152 | bytes 8388624 | tf_op jit(solution)/shard_map/jit(_where)/select_n | solution.py:185
  (174 shorter events, 36.6 us)
Async XLA Ops:
  0.6 254.6 %copy-start = (bf16[512,32]{0,1:T(8,128)(2,1)S(1)}, bf16[512,32]{0,1:T(8,128)(2,1)}, u32[]{:S(2)}) copy-start(bf16[512,32]{0,1:T(8,128)(2,1)} %param.12) | copy-start | bytes 98308
  0.6 44.2 %copy-start.23 = (f32[18,128]{1,0:T(8,128)S(1)}, f32[18,128]{1,0:T(8,128)}, u32[]{:S(2)}) copy-start(f32[18,128]{1,0:T(8,128)} %param.19) | copy-start | bytes 27652
  1.4 1.2 collective-permute-start
  2.6 3.5 %collective-permute-start.1 = (f32[64]{0:T(128)S(1)}, f32[64]{0:T(128)S(1)}, u32[]{:S(2)}, u32[]{:S(2)}) collective-permute-start(f32[64]{0:T(128)S(1)} %add.151), channel_id=1, source_target_pairs={{0,2},{2,0},{4,6},{6,4},{1,3},{3,1},{5,7},{7,5},{8,10},{10,8},{12,... | collective-permute-start | bytes 776 | tf_op jit(solution)/shard_map/ppermute | solution.py:37
  6.1 5.0 %collective-permute-start.2 = (f32[64]{0:T(128)S(1)}, f32[64]{0:T(128)S(1)}, u32[]{:S(2)}, u32[]{:S(2)}) collective-permute-start(f32[64]{0:T(128)S(1)} %add.152), channel_id=1, source_target_pairs={{0,4},{2,6},{4,0},{6,2},{1,5},{3,7},{5,1},{7,3},{8,12},{10,14},{12... | collective-permute-start | bytes 776 | tf_op jit(solution)/shard_map/ppermute | solution.py:37
  11.2 3.5 %collective-permute-start.3 = (f32[64]{0:T(128)S(1)}, f32[64]{0:T(128)S(1)}, u32[]{:S(2)}, u32[]{:S(2)}) collective-permute-start(f32[64]{0:T(128)S(1)} %add.153), channel_id=1, source_target_pairs={{0,8},{8,0},{16,24},{24,16},{32,40},{40,32},{48,56},{56,48},{1,9},... | collective-permute-start | bytes 776 | tf_op jit(solution)/shard_map/ppermute | solution.py:37
  14.7 4.8 %collective-permute-start.4 = (f32[64]{0:T(128)S(1)}, f32[64]{0:T(128)S(1)}, u32[]{:S(2)}, u32[]{:S(2)}) collective-permute-start(f32[64]{0:T(128)S(1)} %add.154), channel_id=1, source_target_pairs={{0,16},{8,24},{16,0},{24,8},{32,48},{40,56},{48,32},{56,40},{1,17}... | collective-permute-start | bytes 776 | tf_op jit(solution)/shard_map/ppermute | solution.py:37
  19.5 8.4 %collective-permute-start.5 = (f32[64]{0:T(128)S(1)}, f32[64]{0:T(128)S(1)}, u32[]{:S(2)}, u32[]{:S(2)}) collective-permute-start(f32[64]{0:T(128)S(1)} %add.155), channel_id=1, source_target_pairs={{0,32},{8,40},{16,48},{24,56},{32,0},{40,8},{48,16},{56,24},{1,33}... | collective-permute-start | bytes 776 | tf_op jit(solution)/shard_map/ppermute | solution.py:37
  28.8 1.8 collective-permute-start.6
  30.7 11.2 %collective-permute-start.7 = (f32[64,1536]{1,0:T(8,128)S(1)}, f32[64,1536]{1,0:T(8,128)S(1)}, u32[]{:S(2)}, u32[]{:S(2)}) collective-permute-start(f32[64,1536]{1,0:T(8,128)S(1)} %add.159), channel_id=1, source_target_pairs={{0,2},{2,0},{4,6},{6,4},{1,3},{3,1},{5,7},{7,5},{8,10},{10,8},{12,... | collective-permute-start | bytes 1179656 | tf_op jit(solution)/shard_map/ppermute | solution.py:37
  31.7 86.9 %copy-start.8 = (pred[64,2322]{1,0:T(8,128)(4,1)}, pred[64,2322]{1,0:T(8,128)(4,1)S(1)}, u32[]{:S(2)}) copy-start(pred[64,2322]{1,0:T(8,128)(4,1)S(1)} %iota_compare_fusion) | copy-start | bytes 445828
  42.0 13.2 %copy-start.1 = (bf16[18,128,512]{2,1,0:T(8,128)(2,1)S(1)}, bf16[18,128,512]{2,1,0:T(8,128)(2,1)}, u32[]{:S(2)}) copy-start(bf16[18,128,512]{2,1,0:T(8,128)(2,1)} %param.17) | copy-start | bytes 7077892
  42.0 11.9 %collective-permute-start.8 = (f32[64,1536]{1,0:T(8,128)S(1)}, f32[64,1536]{1,0:T(8,128)S(1)}, u32[]{:S(2)}, u32[]{:S(2)}) collective-permute-start(f32[64,1536]{1,0:T(8,128)S(1)} %add.160), channel_id=1, source_target_pairs={{0,4},{2,6},{4,0},{6,2},{1,5},{3,7},{5,1},{7,3},{8,12},{10,14},{12... | collective-permute-start | bytes 1179656 | tf_op jit(solution)/shard_map/ppermute | solution.py:37
  53.9 9.5 %collective-permute-start.9 = (f32[64,1536]{1,0:T(8,128)S(1)}, f32[64,1536]{1,0:T(8,128)S(1)}, u32[]{:S(2)}, u32[]{:S(2)}) collective-permute-start(f32[64,1536]{1,0:T(8,128)S(1)} %add.161), channel_id=1, source_target_pairs={{0,8},{8,0},{16,24},{24,16},{32,40},{40,32},{48,56},{56,48},{1,9},... | collective-permute-start | bytes 1179656 | tf_op jit(solution)/shard_map/ppermute | solution.py:37
  63.5 17.9 %collective-permute-start.10 = (f32[64,1536]{1,0:T(8,128)S(1)}, f32[64,1536]{1,0:T(8,128)S(1)}, u32[]{:S(2)}, u32[]{:S(2)}) collective-permute-start(f32[64,1536]{1,0:T(8,128)S(1)} %add.162), channel_id=1, source_target_pairs={{0,16},{8,24},{16,0},{24,8},{32,48},{40,56},{48,32},{56,40},{1,17}... | collective-permute-start | bytes 1179656 | tf_op jit(solution)/shard_map/ppermute | solution.py:37
  65.9 34.8 %copy-start.22 = (bf16[18,512]{1,0:T(8,128)(2,1)}, bf16[18,512]{1,0:T(8,128)(2,1)S(1)}, u32[]{:S(2)}) copy-start(bf16[18,512]{1,0:T(8,128)(2,1)S(1)} %get-tuple-element.62) | copy-start | bytes 55300
  65.9 40.9 %copy-start.21 = (bf16[18,512]{1,0:T(8,128)(2,1)}, bf16[18,512]{1,0:T(8,128)(2,1)S(1)}, u32[]{:S(2)}) copy-start(bf16[18,512]{1,0:T(8,128)(2,1)S(1)} %get-tuple-element.61) | copy-start | bytes 55300
  82.2 28.2 %collective-permute-start.11 = (f32[64,1536]{1,0:T(8,128)}, f32[64,1536]{1,0:T(8,128)}, u32[]{:S(2)}, u32[]{:S(2)}) collective-permute-start(f32[64,1536]{1,0:T(8,128)} %add.163), channel_id=1, source_target_pairs={{0,32},{8,40},{16,48},{24,56},{32,0},{40,8},{48,16},{56,24},{1,33}... | collective-permute-start | bytes 1179656 | tf_op jit(solution)/shard_map/ppermute | solution.py:37
  97.0 3.6 %copy-start.24 = (s32[64]{0:T(128)S(1)}, s32[64]{0:T(128)}, u32[]{:S(2)}) copy-start(s32[64]{0:T(128)} %param.13) | copy-start | bytes 772
  110.4 2.6 copy-start.3
  113.0 6.3 %copy-start.7 = (bf16[2304,8,64]{0,2,1:T(8,128)(2,1)S(1)}, bf16[2304,8,64]{0,2,1:T(8,128)(2,1)}, u32[]{:S(2)}) copy-start(bf16[2304,8,64]{0,2,1:T(8,128)(2,1)} %reshape.244) | copy-start | bytes 7077892
  113.0 6.3 %copy-start.20 = (bf16[18,512]{0,1:T(8,128)(2,1)S(1)}, bf16[18,512]{0,1:T(8,128)(2,1)}, u32[]{:S(2)}) copy-start(bf16[18,512]{0,1:T(8,128)(2,1)} %copy.76) | copy-start | bytes 55300
  113.0 6.3 %copy-start.25 = (f32[2322]{0:T(1024)S(1)}, f32[2322]{0:T(1024)}, u32[]{:S(2)}) copy-start(f32[2322]{0:T(1024)} %constant.92.clone.1) | copy-start | bytes 27868
  114.2 43.2 %collective-permute-start.15 = (bf16[4,128,512]{2,1,0:T(8,128)(2,1)S(1)}, bf16[4,128,512]{2,1,0:T(8,128)(2,1)S(1)}, u32[]{:S(2)}, u32[]{:S(2)}) collective-permute-start(bf16[4,128,512]{2,1,0:T(8,128)(2,1)S(1)} %get-tuple-element.41), channel_id=1, source_target_pairs={{0,1},{1,2},{2,3},{3,4},{4,5},{5,6},{6,7},{7,8},{8,9},{9,10},{10,1... | collective-permute-start | bytes 1572872 | tf_op jit(solution)/shard_map/ppermute | solution.py:70
  114.2 46.0 %collective-permute-start.16 = (bf16[4,128,512]{2,1,0:T(8,128)(2,1)}, bf16[4,128,512]{2,1,0:T(8,128)(2,1)S(1)}, u32[]{:S(2)}, u32[]{:S(2)}) collective-permute-start(bf16[4,128,512]{2,1,0:T(8,128)(2,1)} %get-tuple-element.40), channel_id=1, source_target_pairs={{0,2},{1,3},{2,4},{3,5},{4,6},{5,7},{6,8},{7,9},{8,10},{9,11},{10,... | collective-permute-start | bytes 1572872 | tf_op jit(solution)/shard_map/ppermute | solution.py:70
  114.2 46.0 %collective-permute-start.17 = (bf16[4,128,512]{2,1,0:T(8,128)(2,1)}, bf16[4,128,512]{2,1,0:T(8,128)(2,1)S(1)}, u32[]{:S(2)}, u32[]{:S(2)}) collective-permute-start(bf16[4,128,512]{2,1,0:T(8,128)(2,1)} %get-tuple-element.39), channel_id=1, source_target_pairs={{0,3},{1,4},{2,5},{3,6},{4,7},{5,8},{6,9},{7,10},{8,11},{9,12},{10... | collective-permute-start | bytes 1572872 | tf_op jit(solution)/shard_map/ppermute | solution.py:70
  115.6 28.8 %collective-permute-start.12 = (bf16[4,2]{0,1:T(2,128)(2,1)S(1)}, bf16[4,2]{0,1:T(2,128)(2,1)S(1)}, u32[]{:S(2)}, u32[]{:S(2)}) collective-permute-start(bf16[4,2]{0,1:T(2,128)(2,1)S(1)} %bitcast.131), channel_id=1, source_target_pairs={{0,1},{1,2},{2,3},{3,4},{4,5},{5,6},{6,7},{7,8},{8,9},{9,10},{10,1... | collective-permute-start | bytes 56 | tf_op jit(solution)/shard_map/ppermute | solution.py:70
  115.9 29.4 %collective-permute-start.13 = (bf16[4,2]{0,1:T(2,128)(2,1)S(1)}, bf16[4,2]{0,1:T(2,128)(2,1)S(1)}, u32[]{:S(2)}, u32[]{:S(2)}) collective-permute-start(bf16[4,2]{0,1:T(2,128)(2,1)S(1)} %bitcast.130), channel_id=1, source_target_pairs={{0,2},{1,3},{2,4},{3,5},{4,6},{5,7},{6,8},{7,9},{8,10},{9,11},{10,... | collective-permute-start | bytes 56 | tf_op jit(solution)/shard_map/ppermute | solution.py:70
  120.9 2.2 copy-start.6
  120.9 2.2 copy-start.9
  120.9 2.2 copy-start.19
  144.4 4.5 %collective-permute-start.14 = (bf16[4,2]{0,1:T(2,128)(2,1)S(1)}, bf16[4,2]{0,1:T(2,128)(2,1)S(1)}, u32[]{:S(2)}, u32[]{:S(2)}) collective-permute-start(bf16[4,2]{0,1:T(2,128)(2,1)S(1)} %bitcast.133), channel_id=1, source_target_pairs={{0,3},{1,4},{2,5},{3,6},{4,7},{5,8},{6,9},{7,10},{8,11},{9,12},{10... | collective-permute-start | bytes 56 | tf_op jit(solution)/shard_map/ppermute | solution.py:70
  145.2 19.5 %collective-permute-start.18 = (bf16[4,128,512]{2,1,0:T(8,128)(2,1)}, bf16[4,128,512]{2,1,0:T(8,128)(2,1)}, u32[]{:S(2)}, u32[]{:S(2)}) collective-permute-start(bf16[4,128,512]{2,1,0:T(8,128)(2,1)} %get-tuple-element.37), channel_id=1, source_target_pairs={{0,1},{1,2},{2,3},{3,4},{4,5},{5,6},{6,7},{7,8},{8,9},{9,10},{10,1... | collective-permute-start | bytes 1572872 | tf_op jit(solution)/shard_map/ppermute | solution.py:70
  148.9 26.7 %collective-permute-start.19 = (bf16[4,128,512]{2,1,0:T(8,128)(2,1)}, bf16[4,128,512]{2,1,0:T(8,128)(2,1)}, u32[]{:S(2)}, u32[]{:S(2)}) collective-permute-start(bf16[4,128,512]{2,1,0:T(8,128)(2,1)} %get-tuple-element.36), channel_id=1, source_target_pairs={{0,2},{1,3},{2,4},{3,5},{4,6},{5,7},{6,8},{7,9},{8,10},{9,11},{10,... | collective-permute-start | bytes 1572872 | tf_op jit(solution)/shard_map/ppermute | solution.py:70
  157.4 29.1 %collective-permute-start.20 = (bf16[4,128,512]{2,1,0:T(8,128)(2,1)}, bf16[4,128,512]{2,1,0:T(8,128)(2,1)}, u32[]{:S(2)}, u32[]{:S(2)}) collective-permute-start(bf16[4,128,512]{2,1,0:T(8,128)(2,1)} %get-tuple-element.35), channel_id=1, source_target_pairs={{0,3},{1,4},{2,5},{3,6},{4,7},{5,8},{6,9},{7,10},{8,11},{9,12},{10... | collective-permute-start | bytes 1572872 | tf_op jit(solution)/shard_map/ppermute | solution.py:70
  189.4 19.3 %copy-start.10 = (bf16[64,8,32]{2,0,1:T(8,128)(2,1)S(1)}, bf16[64,8,32]{2,0,1:T(8,128)(2,1)}, u32[]{:S(2)}) copy-start(bf16[64,8,32]{2,0,1:T(8,128)(2,1)} %get-tuple-element.44) | copy-start | bytes 98308
  189.4 19.3 %copy-start.11 = (bf16[64,8,32]{2,0,1:T(8,128)(2,1)S(1)}, bf16[64,8,32]{2,0,1:T(8,128)(2,1)}, u32[]{:S(2)}) copy-start(bf16[64,8,32]{2,0,1:T(8,128)(2,1)} %get-tuple-element.45) | copy-start | bytes 98308
  189.4 19.3 %copy-start.13 = (bf16[64,8,32]{2,0,1:T(8,128)(2,1)S(1)}, bf16[64,8,32]{2,0,1:T(8,128)(2,1)}, u32[]{:S(2)}) copy-start(bf16[64,8,32]{2,0,1:T(8,128)(2,1)} %copy-done.12) | copy-start | bytes 98308
  189.4 19.3 %copy-start.15 = (bf16[64,8,32]{2,0,1:T(8,128)(2,1)S(1)}, bf16[64,8,32]{2,0,1:T(8,128)(2,1)}, u32[]{:S(2)}) copy-start(bf16[64,8,32]{2,0,1:T(8,128)(2,1)} %copy-done.14) | copy-start | bytes 98308
  189.5 1.6 collective-permute-start.21
  191.8 8.4 %collective-permute-start.22 = (f32[8,64,66]{2,1,0:T(8,128)S(1)}, f32[8,64,66]{2,1,0:T(8,128)S(1)}, u32[]{:S(2)}, u32[]{:S(2)}) collective-permute-start(f32[8,64,66]{2,1,0:T(8,128)S(1)} %pad_maximum_fusion.3), channel_id=1, source_target_pairs={{0,2},{2,0},{4,6},{6,4},{1,3},{3,1},{5,7},{7,5},{8,10},{10,8},{12,... | collective-permute-start | bytes 405512 | tf_op jit(solution)/shard_map/ppermute | solution.py:37
  201.0 14.1 %collective-permute-start.23 = (f32[8,64,66]{2,1,0:T(8,128)S(1)}, f32[8,64,66]{2,1,0:T(8,128)S(1)}, u32[]{:S(2)}, u32[]{:S(2)}) collective-permute-start(f32[8,64,66]{2,1,0:T(8,128)S(1)} %pad_maximum_fusion.4), channel_id=1, source_target_pairs={{0,4},{2,6},{4,0},{6,2},{1,5},{3,7},{5,1},{7,3},{8,12},{10,14},{12... | collective-permute-start | bytes 405512 | tf_op jit(solution)/shard_map/ppermute | solution.py:37
  215.7 7.5 %collective-permute-start.24 = (f32[8,64,66]{2,1,0:T(8,128)S(1)}, f32[8,64,66]{2,1,0:T(8,128)S(1)}, u32[]{:S(2)}, u32[]{:S(2)}) collective-permute-start(f32[8,64,66]{2,1,0:T(8,128)S(1)} %pad_maximum_fusion.5), channel_id=1, source_target_pairs={{0,8},{8,0},{16,24},{24,16},{32,40},{40,32},{48,56},{56,48},{1,9},... | collective-permute-start | bytes 405512 | tf_op jit(solution)/shard_map/ppermute | solution.py:37
  223.9 13.1 %collective-permute-start.25 = (f32[8,64,66]{2,1,0:T(8,128)S(1)}, f32[8,64,66]{2,1,0:T(8,128)S(1)}, u32[]{:S(2)}, u32[]{:S(2)}) collective-permute-start(f32[8,64,66]{2,1,0:T(8,128)S(1)} %pad_maximum_fusion.6), channel_id=1, source_target_pairs={{0,16},{8,24},{16,0},{24,8},{32,48},{40,56},{48,32},{56,40},{1,17}... | collective-permute-start | bytes 405512 | tf_op jit(solution)/shard_map/ppermute | solution.py:37
  237.8 15.1 %collective-permute-start.26 = (f32[8,64,66]{2,1,0:T(8,128)S(1)}, f32[8,64,66]{2,1,0:T(8,128)S(1)}, u32[]{:S(2)}, u32[]{:S(2)}) collective-permute-start(f32[8,64,66]{2,1,0:T(8,128)S(1)} %pad_maximum_fusion.7), channel_id=1, source_target_pairs={{0,32},{8,40},{16,48},{24,56},{32,0},{40,8},{48,16},{56,24},{1,33}... | collective-permute-start | bytes 405512 | tf_op jit(solution)/shard_map/ppermute | solution.py:37
  255.4 7.4 %collective-permute-start.27 = (f32[64,32]{0,1:T(8,128)S(1)}, f32[64,32]{0,1:T(8,128)S(1)}, u32[]{:S(2)}, u32[]{:S(2)}) collective-permute-start(f32[64,32]{0,1:T(8,128)S(1)} %fusion.59), channel_id=1, source_target_pairs={{0,64},{64,0},{128,192},{192,128},{1,65},{65,1},{129,193},{193,129... | collective-permute-start | bytes 24584 | tf_op jit(solution)/shard_map/ppermute | solution.py:37
  259.0 6.8 %copy-start.4 = (bf16[16,128,512]{2,1,0:T(8,128)(2,1)S(1)}, bf16[16,128,512]{2,1,0:T(8,128)(2,1)}, u32[]{:S(2)}) copy-start(bf16[16,128,512]{2,1,0:T(8,128)(2,1)} %gather_fusion.4) | copy-start | bytes 6291460
  262.7 7.0 %collective-permute-start.28 = (f32[64,32]{0,1:T(8,128)S(1)}, f32[64,32]{0,1:T(8,128)S(1)}, u32[]{:S(2)}, u32[]{:S(2)}) collective-permute-start(f32[64,32]{0,1:T(8,128)S(1)} %add.178), channel_id=1, source_target_pairs={{0,128},{64,192},{128,0},{192,64},{1,129},{65,193},{129,1},{193,65... | collective-permute-start | bytes 24584 | tf_op jit(solution)/shard_map/ppermute | solution.py:37
  (7 other events, 6.8 us)

commit v3 on v2

--- a/solution.py
+++ b/solution.py
@@ -110,7 +110,6 @@
     partial_value = jnp.dot(
         normed, w_qkv.reshape(w_qkv.shape[0], 3 * feat_width), preferred_element_type=jnp.float32
     )
-    proj_all = seq_sum(partial_value).reshape(requests, 3, heads_here, HDIM)
     block_ids = jnp.arange(n_blocks, dtype=jnp.int32)
     global_ids = my_index * n_blocks + block_ids
     req_ends = jnp.cumsum(req_blocks)
@@ -162,9 +161,10 @@
         axis=-1,
     )
     meta_data = meta_data.astype(jnp.float32).astype(jnp.bfloat16).reshape(HOPS, CAP, 2)
-    send_keys, send_values, meta_data, proj_all = lax.optimization_barrier(
-        (send_keys, send_values, meta_data, proj_all)
-    )
+    send_keys, send_values, meta_data, partial_value = lax.optimization_barrier(
+        (send_keys, send_values, meta_data, partial_value)
+    )
+    proj_all = seq_sum(partial_value).reshape(requests, 3, heads_here, HDIM)
     arrived = [(send_keys[0], send_values[0], meta_data[0])]
     for distance in range(1, HOPS):
         arrived.append(
@@ -187,6 +187,9 @@
     )
     packed_request = jnp.where(filled, recv_meta[picked, 1], -1)
 
+    recv_keys, recv_values, recv_meta, proj_all = lax.optimization_barrier(
+        (recv_keys, recv_values, recv_meta, proj_all)
+    )
     cos_table, sin_table = rope_tables(positions, HDIM)
     queries = rotate_half(proj_all[:, 0], cos_table, sin_table).astype(jnp.bfloat16)
     new_keys = rotate_half(proj_all[:, 1], cos_table, sin_table).astype(jnp.bfloat16)
@@ -220,9 +223,6 @@
     )
     stats = jnp.concatenate(
         [local_acc, local_sum[..., None], local_top[..., None]], axis=-1
-    )
-    recv_keys, recv_values, recv_meta, stats = lax.optimization_barrier(
-        (recv_keys, recv_values, recv_meta, stats)
     )
     stats = butterfly(stats, softmax_merge, reversed(SEQ_PARTS))
     mixture = stats[..., :HDIM]

time: 272 us -> 285 us (1.048)
  starting transfers between devices: 54.2 us -> 77.1 us
  waiting for transfers between devices: 143 us -> 129 us
    ppermute x9, starting transfers between devices: 14.4 us -> 33.6 us  [passed_along(): lax.ppermute(array, SEQ_PARTS, [(i, (i + by) % count) for i in range(coun...]
    ppermute x20, waiting for transfers between devices: 97.7 us -> 82.9 us  [butterfly(): x = merge(x, lax.ppermute(x, axis, pairs))]
    ppermute x20, starting transfers between devices: 39.9 us -> 43.5 us  [butterfly(): x = merge(x, lax.ppermute(x, axis, pairs))]
    unnamed x57 -> x49, local copies, waits for them, and re-layouts: 10.5 us -> 10.1 us
  transfers between devices with their start and end apart: 29 -> 29, of which waited for: 23 -> 20; matrix products, arithmetic and copies ran while one was open for 20% -> 19% of each run, Pallas kernels for 0% -> 0%
where the time goes in v3:
time: 285 us; the launch traced here: 281 us
  waiting for transfers between devices  129 us (45%)
  starting transfers between devices  77.1 us (27%)
  local copies, waits for them, and re-layouts  40.3 us (14%)
  other arithmetic  25.8 us (9%)
  matrix products  7.88 us (3%)
    ppermute x20, waiting for transfers between devices, butterfly(): x = merge(x, lax.ppermute(x, axis, pairs))  82.9 us
    ppermute x9, waiting for transfers between devices, passed_along(): lax.ppermute(array, SEQ_PARTS, [(i, (i + by) % count) for i in range(coun...  45.7 us
    ppermute x20, starting transfers between devices, butterfly(): x = merge(x, lax.ppermute(x, axis, pairs))  43.5 us
    ppermute x9, starting transfers between devices, passed_along(): lax.ppermute(array, SEQ_PARTS, [(i, (i + by) % count) for i in range(coun...  33.6 us
    unnamed x49, local copies, waits for them, and re-layouts  10.1 us
  transfers between devices with their start and end apart: 29, of which 20 were waited for; matrix products, arithmetic and copies ran while one was open for 19% of the time, Pallas kernels for 0%

profile of v3, /device:TPU:6, one launch (start us, length us, event | category | flops | bytes accessed | tf_op | source)
XLA Modules:
  0.0 280.9 jit_solution(2834974776524898970)
XLA Ops:
  6.0 2.6 collective-permute-done.1
  8.6 1.7 collective-permute-start.2
  11.6 2.1 collective-permute-done.2
  13.6 1.9 collective-permute-start.3
  15.7 1.5 collective-permute-done.3
  17.2 3.3 %collective-permute-start.4 = (f32[64]{0:T(128)S(1)}, f32[64]{0:T(128)S(1)}, u32[]{:S(2)}, u32[]{:S(2)}) collective-permute-start(f32[64]{0:T(128)S(1)} %add.154), channel_id=1, source_target_pairs={{0,16},{8,24},{16,0},{24,8},{32,48},{40,56},{48,32},{56,40},{1,17}... | collective-permute-start | bytes 776 | tf_op jit(solution)/shard_map/ppermute | solution.py:37
  20.5 1.5 collective-permute-done.4
  22.0 6.8 %collective-permute-start.5 = (f32[64]{0:T(128)S(1)}, f32[64]{0:T(128)S(1)}, u32[]{:S(2)}, u32[]{:S(2)}) collective-permute-start(f32[64]{0:T(128)S(1)} %add.155), channel_id=1, source_target_pairs={{0,32},{8,40},{16,48},{24,56},{32,0},{40,8},{48,16},{56,24},{1,33}... | collective-permute-start | bytes 776 | tf_op jit(solution)/shard_map/ppermute | solution.py:37
  29.7 3.7 %gather_fusion = bf16[16,128,512]{2,1,0:T(8,128)(2,1)} fusion(bf16[18,128,512]{2,1,0:T(8,128)(2,1)} %param.17, s32[1024]{0:T(1024)S(1)} %pad_clamp_fusion.1), kind=kCustom, calls=%fused_computation | custom fusion | bytes 4194368 | tf_op jit(solution)/shard_map/gather | solution.py:157
  33.4 2.0 gather_fusion.1
  35.8 1.6 collective-permute-done.15
  38.5 10.2 %collective-permute-done.16 = f32[64,1536]{1,0:T(8,128)S(1)} collective-permute-done((f32[64,1536]{1,0:T(8,128)S(1)}, f32[64,1536]{1,0:T(8,128)S(1)}, u32[]{:S(2)}, u32[]{:S(2)}) %collective-permute-start.16) | collective-permute-done | bytes 393248 | tf_op jit(solution)/shard_map/ppermute | solution.py:37
  48.8 1.5 collective-permute-start.17
  52.5 8.2 %collective-permute-done.17 = f32[64,1536]{1,0:T(8,128)S(1)} collective-permute-done((f32[64,1536]{1,0:T(8,128)S(1)}, f32[64,1536]{1,0:T(8,128)S(1)}, u32[]{:S(2)}, u32[]{:S(2)}) %collective-permute-start.17) | collective-permute-done | bytes 393248 | tf_op jit(solution)/shard_map/ppermute | solution.py:37
  64.0 3.2 %copy.78 = bf16[18,128,512]{1,0,2:T(8,128)(2,1)} copy(bf16[18,128,512]{2,1,0:T(8,128)(2,1)S(1)} %copy-done.1) | data formatting | bytes 4718592 | tf_op args[7]
  67.2 3.4 %copy.80 = bf16[18,128,512]{1,0,2:T(8,128)(2,1)S(1)} copy(bf16[18,128,512]{2,1,0:T(8,128)(2,1)} %param.18) | data formatting | bytes 4718592 | tf_op args[8]
  71.5 5.3 %reshape.244 = bf16[2304,8,64]{0,2,1:T(8,128)(2,1)} reshape(bf16[18,128,512]{1,0,2:T(8,128)(2,1)} %copy.78) | data formatting | bytes 4718592 | tf_op jit(solution)/shard_map/reshape | solution.py:198
  77.6 2.6 reshape.246
  81.1 2.4 collective-permute-start.11
  84.7 1.6 collective-permute-start.19
  86.4 2.8 fusion.55
  89.2 11.7 %collective-permute-done.6 = bf16[4,2]{0,1:T(2,128)(2,1)S(1)} collective-permute-done((bf16[4,2]{0,1:T(2,128)(2,1)S(1)}, bf16[4,2]{0,1:T(2,128)(2,1)S(1)}, u32[]{:S(2)}, u32[]{:S(2)}) %collective-permute-start.6) | collective-permute-done | bytes 48 | tf_op jit(solution)/shard_map/ppermute | solution.py:70
  100.9 22.6 %collective-permute-start.7 = (bf16[4,2]{0,1:T(2,128)(2,1)S(1)}, bf16[4,2]{0,1:T(2,128)(2,1)S(1)}, u32[]{:S(2)}, u32[]{:S(2)}) collective-permute-start(bf16[4,2]{0,1:T(2,128)(2,1)S(1)} %bitcast.131), channel_id=1, source_target_pairs={{0,2},{1,3},{2,4},{3,5},{4,6},{5,7},{6,8},{7,9},{8,10},{9,11},{10,... | collective-permute-start | bytes 56 | tf_op jit(solution)/shard_map/ppermute | solution.py:70
  124.8 4.5 %collective-permute-done.8 = bf16[4,2]{0,1:T(2,128)(2,1)S(1)} collective-permute-done((bf16[4,2]{0,1:T(2,128)(2,1)S(1)}, bf16[4,2]{0,1:T(2,128)(2,1)S(1)}, u32[]{:S(2)}, u32[]{:S(2)}) %collective-permute-start.8) | collective-permute-done | bytes 48 | tf_op jit(solution)/shard_map/ppermute | solution.py:70
  129.3 5.3 %collective-permute-start.13 = (bf16[4,128,512]{2,1,0:T(8,128)(2,1)}, bf16[4,128,512]{2,1,0:T(8,128)(2,1)}, u32[]{:S(2)}, u32[]{:S(2)}) collective-permute-start(bf16[4,128,512]{2,1,0:T(8,128)(2,1)} %get-tuple-element.36), channel_id=1, source_target_pairs={{0,2},{1,3},{2,4},{3,5},{4,6},{5,7},{6,8},{7,9},{8,10},{9,11},{10,... | collective-permute-start | bytes 1572872 | tf_op jit(solution)/shard_map/ppermute | solution.py:70
  134.6 2.3 collective-permute-start.14
  137.9 1.7 collective-permute-start.20
  140.4 1.6 pad_maximum_fusion
  142.1 6.8 %collective-permute-done.12 = bf16[4,128,512]{2,1,0:T(8,128)(2,1)} collective-permute-done((bf16[4,128,512]{2,1,0:T(8,128)(2,1)}, bf16[4,128,512]{2,1,0:T(8,128)(2,1)}, u32[]{:S(2)}, u32[]{:S(2)}) %collective-permute-start.12) | collective-permute-done | bytes 524320 | tf_op jit(solution)/shard_map/ppermute | solution.py:70
  150.2 20.1 %collective-permute-done.14 = bf16[4,128,512]{2,1,0:T(8,128)(2,1)} collective-permute-done((bf16[4,128,512]{2,1,0:T(8,128)(2,1)}, bf16[4,128,512]{2,1,0:T(8,128)(2,1)}, u32[]{:S(2)}, u32[]{:S(2)}) %collective-permute-start.14) | collective-permute-done | bytes 524320 | tf_op jit(solution)/shard_map/ppermute | solution.py:70
  170.3 2.9 %pad_maximum_fusion.1 = bf16[4,4,128,512]{3,2,1,0:T(8,128)(2,1)} fusion(bf16[1,4,128,512]{3,2,1,0:T(8,128)(2,1)} %bitcast.25, bf16[1,4,128,512]{3,2,1,0:T(8,128)(2,1)} %bitcast.23, bf16[1,4,128,512]{3,2,1,0:T(8,128)(2,1)} %bitcast.21, bf16[1,4,128,512]{3,2,1,0:T(8,128)(2,1)S(1)} %get-tuple-element.34), kind=kLoop, calls=%fused_computation.24 | loop fusion | flops 3145728 | bytes 4194304 | tf_op jit(solution)/shard_map/stack | solution.py:174
  173.2 8.9 %collective-permute-done.20 = f32[64,1536]{1,0:T(8,128)} collective-permute-done((f32[64,1536]{1,0:T(8,128)}, f32[64,1536]{1,0:T(8,128)}, u32[]{:S(2)}, u32[]{:S(2)}) %collective-permute-start.20) | collective-permute-done | bytes 393248 | tf_op jit(solution)/shard_map/ppermute | solution.py:37
  185.4 1.4 fusion.58
  189.4 4.1 %fusion.4 = f32[8,64,64]{2,1,0:T(8,128)S(1)} fusion(f32[8,64,2322]{2,1,0:T(8,128)} %copy-done.6, bf16[18,8,64]{0,2,1:T(8,128)(2,1)S(1)} %bitcast.119, bf16[2304,8,64]{0,2,1:T(8,128)(2,1)} %reshape.246, f32[8,64]{1,0:T(8,128)S(1)} %get-tuple-element.72, pred[64,2322]{1,0:T(8,128)(4,1)S(1)} %iota_compare_fusion), kind=kOutput, calls=%fused_computation.13 | convolution fusion | flops 160496640 | bytes 7414912 | tf_op jit(solution)/shard_map/hrn,nhd->hrd/dot_general | solution.py:221
  193.7 5.3 %collective-permute-start.21 = (f32[8,64,66]{2,1,0:T(8,128)S(1)}, f32[8,64,66]{2,1,0:T(8,128)S(1)}, u32[]{:S(2)}, u32[]{:S(2)}) collective-permute-start(f32[8,64,66]{2,1,0:T(8,128)S(1)} %pad_maximum_fusion.2), channel_id=1, source_target_pairs={{0,1},{1,0},{2,3},{3,2},{4,5},{5,4},{6,7},{7,6},{8,9},{9,8},{10,11... | collective-permute-start | bytes 405512 | tf_op jit(solution)/shard_map/ppermute | solution.py:37
  201.0 8.6 %collective-permute-done.22 = f32[8,64,66]{2,1,0:T(8,128)S(1)} collective-permute-done((f32[8,64,66]{2,1,0:T(8,128)S(1)}, f32[8,64,66]{2,1,0:T(8,128)S(1)}, u32[]{:S(2)}, u32[]{:S(2)}) %collective-permute-start.22) | collective-permute-done | bytes 135200 | tf_op jit(solution)/shard_map/ppermute | solution.py:37
  210.4 9.3 %collective-permute-done.23 = f32[8,64,66]{2,1,0:T(8,128)S(1)} collective-permute-done((f32[8,64,66]{2,1,0:T(8,128)S(1)}, f32[8,64,66]{2,1,0:T(8,128)S(1)}, u32[]{:S(2)}, u32[]{:S(2)}) %collective-permute-start.23) | collective-permute-done | bytes 135200 | tf_op jit(solution)/shard_map/ppermute | solution.py:37
  220.3 6.8 %collective-permute-start.24 = (f32[8,64,66]{2,1,0:T(8,128)S(1)}, f32[8,64,66]{2,1,0:T(8,128)S(1)}, u32[]{:S(2)}, u32[]{:S(2)}) collective-permute-start(f32[8,64,66]{2,1,0:T(8,128)S(1)} %pad_maximum_fusion.5), channel_id=1, source_target_pairs={{0,8},{8,0},{16,24},{24,16},{32,40},{40,32},{48,56},{56,48},{1,9},... | collective-permute-start | bytes 405512 | tf_op jit(solution)/shard_map/ppermute | solution.py:37
  227.3 5.0 %collective-permute-done.24 = f32[8,64,66]{2,1,0:T(8,128)S(1)} collective-permute-done((f32[8,64,66]{2,1,0:T(8,128)S(1)}, f32[8,64,66]{2,1,0:T(8,128)S(1)}, u32[]{:S(2)}, u32[]{:S(2)}) %collective-permute-start.24) | collective-permute-done | bytes 135200 | tf_op jit(solution)/shard_map/ppermute | solution.py:37
  233.7 3.2 %collective-permute-start.25 = (f32[8,64,66]{2,1,0:T(8,128)}, f32[8,64,66]{2,1,0:T(8,128)S(1)}, u32[]{:S(2)}, u32[]{:S(2)}) collective-permute-start(f32[8,64,66]{2,1,0:T(8,128)} %pad_maximum_fusion.6), channel_id=1, source_target_pairs={{0,16},{8,24},{16,0},{24,8},{32,48},{40,56},{48,32},{56,40},{1,17}... | collective-permute-start | bytes 405512 | tf_op jit(solution)/shard_map/ppermute | solution.py:37
  237.7 9.2 %collective-permute-done.25 = f32[8,64,66]{2,1,0:T(8,128)S(1)} collective-permute-done((f32[8,64,66]{2,1,0:T(8,128)}, f32[8,64,66]{2,1,0:T(8,128)S(1)}, u32[]{:S(2)}, u32[]{:S(2)}) %collective-permute-start.25) | collective-permute-done | bytes 135200 | tf_op jit(solution)/shard_map/ppermute | solution.py:37
  247.7 1.8 collective-permute-start.26
  250.3 13.1 %collective-permute-done.26 = f32[8,64,66]{2,1,0:T(8,128)S(1)} collective-permute-done((f32[8,64,66]{2,1,0:T(8,128)S(1)}, f32[8,64,66]{2,1,0:T(8,128)S(1)}, u32[]{:S(2)}, u32[]{:S(2)}) %collective-permute-start.26) | collective-permute-done | bytes 135200 | tf_op jit(solution)/shard_map/ppermute | solution.py:37
  265.9 1.6 collective-permute-start.27
  267.5 2.0 gather_fusion.4
  269.6 3.7 %gather_fusion.5 = bf16[16,128,512]{2,1,0:T(8,128)(2,1)} fusion(bf16[16,128,512]{2,1,0:T(8,128)(2,1)} %bitcast.113, s32[1024]{0:T(1024)S(1)} %pad_clamp_fusion), kind=kCustom, calls=%fused_computation.5 | custom fusion | bytes 4194368 | tf_op jit(solution)/shard_map/gather | solution.py:186
  273.3 3.0 %collective-permute-start.28 = (f32[64,32]{0,1:T(8,128)S(1)}, f32[64,32]{0,1:T(8,128)S(1)}, u32[]{:S(2)}, u32[]{:S(2)}) collective-permute-start(f32[64,32]{0,1:T(8,128)S(1)} %add.178), channel_id=1, source_target_pairs={{0,128},{64,192},{128,0},{192,64},{1,129},{65,193},{129,1},{193,65... | collective-permute-start | bytes 24584 | tf_op jit(solution)/shard_map/ppermute | solution.py:37
  276.3 3.9 %broadcast_select_fusion = (bf16[16,128,512]{2,1,0:T(8,128)(2,1)}, bf16[16,128,512]{2,1,0:T(8,128)(2,1)}) fusion(bf16[16,128,512]{2,1,0:T(8,128)(2,1)} %gather_fusion.5, pred[16]{0:T(512)(128)(4,1)S(1)} %fusion.38, bf16[16,128,512]{2,1,0:T(8,128)(2,1)S(1)} %copy-done.5), kind=kLoop, calls=%fused_computation.25 | loop fusion | flops 2097152 | bytes 8388624 | tf_op jit(solution)/shard_map/jit(_where)/select_n | solution.py:185
  (166 shorter events, 39.2 us)
Async XLA Ops:
  0.6 265.2 %copy-start = (bf16[512,32]{0,1:T(8,128)(2,1)S(1)}, bf16[512,32]{0,1:T(8,128)(2,1)}, u32[]{:S(2)}) copy-start(bf16[512,32]{0,1:T(8,128)(2,1)} %param.12) | copy-start | bytes 98308
  1.4 3.6 %collective-permute-start = (f32[64]{0:T(128)S(1)}, f32[64]{0:T(128)S(1)}, u32[]{:S(2)}, u32[]{:S(2)}) collective-permute-start(f32[64]{0:T(128)S(1)} %fusion.33), channel_id=1, source_target_pairs={{0,1},{1,0},{2,3},{3,2},{4,5},{5,4},{6,7},{7,6},{8,9},{9,8},{10,11... | collective-permute-start | bytes 776 | tf_op jit(solution)/shard_map/ppermute | solution.py:37
  5.0 3.6 %collective-permute-start.1 = (f32[64]{0:T(128)S(1)}, f32[64]{0:T(128)S(1)}, u32[]{:S(2)}, u32[]{:S(2)}) collective-permute-start(f32[64]{0:T(128)S(1)} %add.151), channel_id=1, source_target_pairs={{0,2},{2,0},{4,6},{6,4},{1,3},{3,1},{5,7},{7,5},{8,10},{10,8},{12,... | collective-permute-start | bytes 776 | tf_op jit(solution)/shard_map/ppermute | solution.py:37
  8.6 5.0 %collective-permute-start.2 = (f32[64]{0:T(128)S(1)}, f32[64]{0:T(128)S(1)}, u32[]{:S(2)}, u32[]{:S(2)}) collective-permute-start(f32[64]{0:T(128)S(1)} %add.152), channel_id=1, source_target_pairs={{0,4},{2,6},{4,0},{6,2},{1,5},{3,7},{5,1},{7,3},{8,12},{10,14},{12... | collective-permute-start | bytes 776 | tf_op jit(solution)/shard_map/ppermute | solution.py:37
  10.9 22.5 %copy-start.2 = (bf16[18,128,512]{2,1,0:T(8,128)(2,1)S(1)}, bf16[18,128,512]{2,1,0:T(8,128)(2,1)}, u32[]{:S(2)}) copy-start(bf16[18,128,512]{2,1,0:T(8,128)(2,1)} %param.18) | copy-start | bytes 7077892
  13.6 3.5 %collective-permute-start.3 = (f32[64]{0:T(128)S(1)}, f32[64]{0:T(128)S(1)}, u32[]{:S(2)}, u32[]{:S(2)}) collective-permute-start(f32[64]{0:T(128)S(1)} %add.153), channel_id=1, source_target_pairs={{0,8},{8,0},{16,24},{24,16},{32,40},{40,32},{48,56},{56,48},{1,9},... | collective-permute-start | bytes 776 | tf_op jit(solution)/shard_map/ppermute | solution.py:37
  17.2 4.8 %collective-permute-start.4 = (f32[64]{0:T(128)S(1)}, f32[64]{0:T(128)S(1)}, u32[]{:S(2)}, u32[]{:S(2)}) collective-permute-start(f32[64]{0:T(128)S(1)} %add.154), channel_id=1, source_target_pairs={{0,16},{8,24},{16,0},{24,8},{32,48},{40,56},{48,32},{56,40},{1,17}... | collective-permute-start | bytes 776 | tf_op jit(solution)/shard_map/ppermute | solution.py:37
  22.0 13.4 %collective-permute-start.5 = (f32[64]{0:T(128)S(1)}, f32[64]{0:T(128)S(1)}, u32[]{:S(2)}, u32[]{:S(2)}) collective-permute-start(f32[64]{0:T(128)S(1)} %add.155), channel_id=1, source_target_pairs={{0,32},{8,40},{16,48},{24,56},{32,0},{40,8},{48,16},{56,24},{1,33}... | collective-permute-start | bytes 776 | tf_op jit(solution)/shard_map/ppermute | solution.py:37
  33.4 2.0 copy-start.19
  35.4 14.9 %copy-start.3 = (bf16[18,128,512]{2,1,0:T(8,128)(2,1)S(1)}, bf16[18,128,512]{2,1,0:T(8,128)(2,1)}, u32[]{:S(2)}) copy-start(bf16[18,128,512]{2,1,0:T(8,128)(2,1)} %param.18) | copy-start | bytes 7077892
  35.4 14.9 %copy-start.18 = (f32[18,128]{1,0:T(8,128)S(1)}, f32[18,128]{1,0:T(8,128)}, u32[]{:S(2)}) copy-start(f32[18,128]{1,0:T(8,128)} %param.19) | copy-start | bytes 27652
  35.6 1.8 collective-permute-start.15
  35.8 15.6 %copy-start.1 = (bf16[18,128,512]{2,1,0:T(8,128)(2,1)S(1)}, bf16[18,128,512]{2,1,0:T(8,128)(2,1)}, u32[]{:S(2)}) copy-start(bf16[18,128,512]{2,1,0:T(8,128)(2,1)} %param.17) | copy-start | bytes 7077892
  37.5 11.2 %collective-permute-start.16 = (f32[64,1536]{1,0:T(8,128)S(1)}, f32[64,1536]{1,0:T(8,128)S(1)}, u32[]{:S(2)}, u32[]{:S(2)}) collective-permute-start(f32[64,1536]{1,0:T(8,128)S(1)} %add.160), channel_id=1, source_target_pairs={{0,2},{2,0},{4,6},{6,4},{1,3},{3,1},{5,7},{7,5},{8,10},{10,8},{12,... | collective-permute-start | bytes 1179656 | tf_op jit(solution)/shard_map/ppermute | solution.py:37
  48.8 11.9 %collective-permute-start.17 = (f32[64,1536]{1,0:T(8,128)S(1)}, f32[64,1536]{1,0:T(8,128)S(1)}, u32[]{:S(2)}, u32[]{:S(2)}) collective-permute-start(f32[64,1536]{1,0:T(8,128)S(1)} %add.161), channel_id=1, source_target_pairs={{0,4},{2,6},{4,0},{6,2},{1,5},{3,7},{5,1},{7,3},{8,12},{10,14},{12... | collective-permute-start | bytes 1179656 | tf_op jit(solution)/shard_map/ppermute | solution.py:37
  51.4 11.2 %copy-start.4 = (bf16[16,128,512]{2,1,0:T(8,128)(2,1)S(1)}, bf16[16,128,512]{2,1,0:T(8,128)(2,1)}, u32[]{:S(2)}) copy-start(bf16[16,128,512]{2,1,0:T(8,128)(2,1)} %gather_fusion) | copy-start | bytes 6291460
  61.5 22.1 %collective-permute-start.18 = (f32[64,1536]{1,0:T(8,128)}, f32[64,1536]{1,0:T(8,128)}, u32[]{:S(2)}, u32[]{:S(2)}) collective-permute-start(f32[64,1536]{1,0:T(8,128)} %add.162), channel_id=1, source_target_pairs={{0,8},{8,0},{16,24},{24,16},{32,40},{40,32},{48,56},{56,48},{1,9},... | collective-permute-start | bytes 1179656 | tf_op jit(solution)/shard_map/ppermute | solution.py:37
  62.6 8.1 %copy-start.17 = (bf16[18,512]{1,0:T(8,128)(2,1)}, bf16[18,512]{1,0:T(8,128)(2,1)S(1)}, u32[]{:S(2)}) copy-start(bf16[18,512]{1,0:T(8,128)(2,1)S(1)} %get-tuple-element.62) | copy-start | bytes 55300
  62.6 14.2 %copy-start.16 = (bf16[18,512]{1,0:T(8,128)(2,1)}, bf16[18,512]{1,0:T(8,128)(2,1)S(1)}, u32[]{:S(2)}) copy-start(bf16[18,512]{1,0:T(8,128)(2,1)S(1)} %get-tuple-element.61) | copy-start | bytes 55300
  64.0 65.3 %collective-permute-start.9 = (bf16[4,128,512]{2,1,0:T(8,128)(2,1)}, bf16[4,128,512]{2,1,0:T(8,128)(2,1)}, u32[]{:S(2)}, u32[]{:S(2)}) collective-permute-start(bf16[4,128,512]{2,1,0:T(8,128)(2,1)} %get-tuple-element.41), channel_id=1, source_target_pairs={{0,1},{1,2},{2,3},{3,4},{4,5},{5,6},{6,7},{7,8},{8,9},{9,10},{10,1... | collective-permute-start | bytes 1572872 | tf_op jit(solution)/shard_map/ppermute | solution.py:70
  67.2 3.4 %copy-start.20 = (s32[64]{0:T(128)S(1)}, s32[64]{0:T(128)}, u32[]{:S(2)}) copy-start(s32[64]{0:T(128)} %param.13) | copy-start | bytes 772
  80.2 57.7 %collective-permute-start.10 = (bf16[4,128,512]{2,1,0:T(8,128)(2,1)}, bf16[4,128,512]{2,1,0:T(8,128)(2,1)S(1)}, u32[]{:S(2)}, u32[]{:S(2)}) collective-permute-start(bf16[4,128,512]{2,1,0:T(8,128)(2,1)} %get-tuple-element.40), channel_id=1, source_target_pairs={{0,2},{1,3},{2,4},{3,5},{4,6},{5,7},{6,8},{7,9},{8,10},{9,11},{10,... | collective-permute-start | bytes 1572872 | tf_op jit(solution)/shard_map/ppermute | solution.py:70
  81.1 58.5 %collective-permute-start.11 = (bf16[4,128,512]{2,1,0:T(8,128)(2,1)}, bf16[4,128,512]{2,1,0:T(8,128)(2,1)S(1)}, u32[]{:S(2)}, u32[]{:S(2)}) collective-permute-start(bf16[4,128,512]{2,1,0:T(8,128)(2,1)} %get-tuple-element.39), channel_id=1, source_target_pairs={{0,3},{1,4},{2,5},{3,6},{4,7},{5,8},{6,9},{7,10},{8,11},{9,12},{10... | collective-permute-start | bytes 1572872 | tf_op jit(solution)/shard_map/ppermute | solution.py:70
  84.7 49.9 %collective-permute-start.19 = (f32[64,1536]{1,0:T(8,128)S(1)}, f32[64,1536]{1,0:T(8,128)S(1)}, u32[]{:S(2)}, u32[]{:S(2)}) collective-permute-start(f32[64,1536]{1,0:T(8,128)S(1)} %add.163), channel_id=1, source_target_pairs={{0,16},{8,24},{16,0},{24,8},{32,48},{40,56},{48,32},{56,40},{1,17}... | collective-permute-start | bytes 1179656 | tf_op jit(solution)/shard_map/ppermute | solution.py:37
  86.3 14.6 %collective-permute-start.6 = (bf16[4,2]{0,1:T(2,128)(2,1)S(1)}, bf16[4,2]{0,1:T(2,128)(2,1)S(1)}, u32[]{:S(2)}, u32[]{:S(2)}) collective-permute-start(bf16[4,2]{0,1:T(2,128)(2,1)S(1)} %bitcast.132), channel_id=1, source_target_pairs={{0,1},{1,2},{2,3},{3,4},{4,5},{5,6},{6,7},{7,8},{8,9},{9,10},{10,1... | collective-permute-start | bytes 56 | tf_op jit(solution)/shard_map/ppermute | solution.py:70
  86.4 54.0 %copy-start.9 = (bf16[1,4,128,512]{3,2,1,0:T(8,128)(2,1)S(1)}, bf16[1,4,128,512]{3,2,1,0:T(8,128)(2,1)}, u32[]{:S(2)}) copy-start(bf16[1,4,128,512]{3,2,1,0:T(8,128)(2,1)} %get-tuple-element.38) | copy-start | bytes 1572868
  100.9 23.9 %collective-permute-start.7 = (bf16[4,2]{0,1:T(2,128)(2,1)S(1)}, bf16[4,2]{0,1:T(2,128)(2,1)S(1)}, u32[]{:S(2)}, u32[]{:S(2)}) collective-permute-start(bf16[4,2]{0,1:T(2,128)(2,1)S(1)} %bitcast.131), channel_id=1, source_target_pairs={{0,2},{1,3},{2,4},{3,5},{4,6},{5,7},{6,8},{7,9},{8,10},{9,11},{10,... | collective-permute-start | bytes 56 | tf_op jit(solution)/shard_map/ppermute | solution.py:70
  124.8 4.5 %collective-permute-start.8 = (bf16[4,2]{0,1:T(2,128)(2,1)S(1)}, bf16[4,2]{0,1:T(2,128)(2,1)S(1)}, u32[]{:S(2)}, u32[]{:S(2)}) collective-permute-start(bf16[4,2]{0,1:T(2,128)(2,1)S(1)} %bitcast.130), channel_id=1, source_target_pairs={{0,3},{1,4},{2,5},{3,6},{4,7},{5,8},{6,9},{7,10},{8,11},{9,12},{10... | collective-permute-start | bytes 56 | tf_op jit(solution)/shard_map/ppermute | solution.py:70
  129.3 19.6 %collective-permute-start.12 = (bf16[4,128,512]{2,1,0:T(8,128)(2,1)}, bf16[4,128,512]{2,1,0:T(8,128)(2,1)}, u32[]{:S(2)}, u32[]{:S(2)}) collective-permute-start(bf16[4,128,512]{2,1,0:T(8,128)(2,1)} %get-tuple-element.37), channel_id=1, source_target_pairs={{0,1},{1,2},{2,3},{3,4},{4,5},{5,6},{6,7},{7,8},{8,9},{9,10},{10,1... | collective-permute-start | bytes 1572872 | tf_op jit(solution)/shard_map/ppermute | solution.py:70
  129.3 20.9 %collective-permute-start.13 = (bf16[4,128,512]{2,1,0:T(8,128)(2,1)}, bf16[4,128,512]{2,1,0:T(8,128)(2,1)}, u32[]{:S(2)}, u32[]{:S(2)}) collective-permute-start(bf16[4,128,512]{2,1,0:T(8,128)(2,1)} %get-tuple-element.36), channel_id=1, source_target_pairs={{0,2},{1,3},{2,4},{3,5},{4,6},{5,7},{6,8},{7,9},{8,10},{9,11},{10,... | collective-permute-start | bytes 1572872 | tf_op jit(solution)/shard_map/ppermute | solution.py:70
  134.6 35.8 %collective-permute-start.14 = (bf16[4,128,512]{2,1,0:T(8,128)(2,1)}, bf16[4,128,512]{2,1,0:T(8,128)(2,1)}, u32[]{:S(2)}, u32[]{:S(2)}) collective-permute-start(bf16[4,128,512]{2,1,0:T(8,128)(2,1)} %get-tuple-element.35), channel_id=1, source_target_pairs={{0,3},{1,4},{2,5},{3,6},{4,7},{5,8},{6,9},{7,10},{8,11},{9,12},{10... | collective-permute-start | bytes 1572872 | tf_op jit(solution)/shard_map/ppermute | solution.py:70
  137.9 44.2 %collective-permute-start.20 = (f32[64,1536]{1,0:T(8,128)}, f32[64,1536]{1,0:T(8,128)}, u32[]{:S(2)}, u32[]{:S(2)}) collective-permute-start(f32[64,1536]{1,0:T(8,128)} %add.164), channel_id=1, source_target_pairs={{0,32},{8,40},{16,48},{24,56},{32,0},{40,8},{48,16},{56,24},{1,33}... | collective-permute-start | bytes 1179656 | tf_op jit(solution)/shard_map/ppermute | solution.py:37
  183.4 1.9 copy-start.8
  183.5 1.9 copy-start.15
  183.5 1.9 copy-start.21
  184.8 2.0 copy-start.10
  186.8 2.3 copy-start.6
  186.8 2.6 copy-start.14
  193.7 6.5 %collective-permute-start.21 = (f32[8,64,66]{2,1,0:T(8,128)S(1)}, f32[8,64,66]{2,1,0:T(8,128)S(1)}, u32[]{:S(2)}, u32[]{:S(2)}) collective-permute-start(f32[8,64,66]{2,1,0:T(8,128)S(1)} %pad_maximum_fusion.2), channel_id=1, source_target_pairs={{0,1},{1,0},{2,3},{3,2},{4,5},{5,4},{6,7},{7,6},{8,9},{9,8},{10,11... | collective-permute-start | bytes 405512 | tf_op jit(solution)/shard_map/ppermute | solution.py:37
  200.9 8.7 %collective-permute-start.22 = (f32[8,64,66]{2,1,0:T(8,128)S(1)}, f32[8,64,66]{2,1,0:T(8,128)S(1)}, u32[]{:S(2)}, u32[]{:S(2)}) collective-permute-start(f32[8,64,66]{2,1,0:T(8,128)S(1)} %pad_maximum_fusion.3), channel_id=1, source_target_pairs={{0,2},{2,0},{4,6},{6,4},{1,3},{3,1},{5,7},{7,5},{8,10},{10,8},{12,... | collective-permute-start | bytes 405512 | tf_op jit(solution)/shard_map/ppermute | solution.py:37
  210.3 9.4 %collective-permute-start.23 = (f32[8,64,66]{2,1,0:T(8,128)S(1)}, f32[8,64,66]{2,1,0:T(8,128)S(1)}, u32[]{:S(2)}, u32[]{:S(2)}) collective-permute-start(f32[8,64,66]{2,1,0:T(8,128)S(1)} %pad_maximum_fusion.4), channel_id=1, source_target_pairs={{0,4},{2,6},{4,0},{6,2},{1,5},{3,7},{5,1},{7,3},{8,12},{10,14},{12... | collective-permute-start | bytes 405512 | tf_op jit(solution)/shard_map/ppermute | solution.py:37
  220.3 11.9 %collective-permute-start.24 = (f32[8,64,66]{2,1,0:T(8,128)S(1)}, f32[8,64,66]{2,1,0:T(8,128)S(1)}, u32[]{:S(2)}, u32[]{:S(2)}) collective-permute-start(f32[8,64,66]{2,1,0:T(8,128)S(1)} %pad_maximum_fusion.5), channel_id=1, source_target_pairs={{0,8},{8,0},{16,24},{24,16},{32,40},{40,32},{48,56},{56,48},{1,9},... | collective-permute-start | bytes 405512 | tf_op jit(solution)/shard_map/ppermute | solution.py:37
  232.6 17.4 %copy-start.11 = (bf16[64,8,32]{2,0,1:T(8,128)(2,1)S(1)}, bf16[64,8,32]{2,0,1:T(8,128)(2,1)}, u32[]{:S(2)}) copy-start(bf16[64,8,32]{2,0,1:T(8,128)(2,1)} %copy-done.10) | copy-start | bytes 98308
  233.7 13.3 %collective-permute-start.25 = (f32[8,64,66]{2,1,0:T(8,128)}, f32[8,64,66]{2,1,0:T(8,128)S(1)}, u32[]{:S(2)}, u32[]{:S(2)}) collective-permute-start(f32[8,64,66]{2,1,0:T(8,128)} %pad_maximum_fusion.6), channel_id=1, source_target_pairs={{0,16},{8,24},{16,0},{24,8},{32,48},{40,56},{48,32},{56,40},{1,17}... | collective-permute-start | bytes 405512 | tf_op jit(solution)/shard_map/ppermute | solution.py:37
  247.7 15.7 %collective-permute-start.26 = (f32[8,64,66]{2,1,0:T(8,128)S(1)}, f32[8,64,66]{2,1,0:T(8,128)S(1)}, u32[]{:S(2)}, u32[]{:S(2)}) collective-permute-start(f32[8,64,66]{2,1,0:T(8,128)S(1)} %pad_maximum_fusion.7), channel_id=1, source_target_pairs={{0,32},{8,40},{16,48},{24,56},{32,0},{40,8},{48,16},{56,24},{1,33}... | collective-permute-start | bytes 405512 | tf_op jit(solution)/shard_map/ppermute | solution.py:37
  265.9 7.4 %collective-permute-start.27 = (f32[64,32]{0,1:T(8,128)S(1)}, f32[64,32]{0,1:T(8,128)S(1)}, u32[]{:S(2)}, u32[]{:S(2)}) collective-permute-start(f32[64,32]{0,1:T(8,128)S(1)} %fusion.59), channel_id=1, source_target_pairs={{0,64},{64,0},{128,192},{192,128},{1,65},{65,1},{129,193},{193,129... | collective-permute-start | bytes 24584 | tf_op jit(solution)/shard_map/ppermute | solution.py:37
  269.6 6.8 %copy-start.5 = (bf16[16,128,512]{2,1,0:T(8,128)(2,1)S(1)}, bf16[16,128,512]{2,1,0:T(8,128)(2,1)}, u32[]{:S(2)}) copy-start(bf16[16,128,512]{2,1,0:T(8,128)(2,1)} %gather_fusion.4) | copy-start | bytes 6291460
  273.3 7.0 %collective-permute-start.28 = (f32[64,32]{0,1:T(8,128)S(1)}, f32[64,32]{0,1:T(8,128)S(1)}, u32[]{:S(2)}, u32[]{:S(2)}) collective-permute-start(f32[64,32]{0,1:T(8,128)S(1)} %add.178), channel_id=1, source_target_pairs={{0,128},{64,192},{128,0},{192,64},{1,129},{65,193},{129,1},{193,65... | collective-permute-start | bytes 24584 | tf_op jit(solution)/shard_map/ppermute | solution.py:37
  (3 other events, 3.4 us)

commit v4 on v1

--- a/solution.py
+++ b/solution.py
@@ -204,17 +204,26 @@
         ]
     )
     row_mask = all_req[None, :] == jnp.arange(requests, dtype=jnp.int32)[:, None]
-    scores = (
-        jnp.einsum("rhd,nhd->hrn", queries, all_keys, preferred_element_type=jnp.float32) * 0.125
-        + bias[None, None, :]
-    )
-    scores = jnp.where(row_mask[None], scores, MASKED_SCORE)
+    own_head = jnp.arange(heads_here)[:, None] == jnp.arange(heads_here)[None, :]
+    spread_queries = jnp.where(
+        own_head[None, :, :, None], queries[:, :, None, :], jnp.zeros((), jnp.bfloat16)
+    ).reshape(requests * heads_here, feat_width)
+    flat_keys = all_keys.reshape(-1, feat_width)
+    flat_values = all_values.reshape(-1, feat_width)
+    scores = lax.dot_general(
+        spread_queries, flat_keys, (((1,), (1,)), ((), ())), preferred_element_type=jnp.float32
+    ).reshape(requests, heads_here, -1)
+    scores = scores * 0.125 + bias[None, None, :]
+    scores = jnp.where(row_mask[:, None, :], scores, MASKED_SCORE)
     local_top = jnp.max(scores, axis=2)
-    expo = jnp.where(row_mask[None], jnp.exp(scores - local_top[..., None]), 0.0)
+    expo = jnp.where(row_mask[:, None, :], jnp.exp(scores - local_top[..., None]), 0.0)
     local_sum = jnp.sum(expo, axis=2)
-    local_acc = jnp.einsum(
-        "hrn,nhd->hrd", expo.astype(jnp.bfloat16), all_values, preferred_element_type=jnp.float32
-    )
+    weighted = jnp.dot(
+        expo.astype(jnp.bfloat16).reshape(requests * heads_here, -1),
+        flat_values,
+        preferred_element_type=jnp.float32,
+    ).reshape(requests, heads_here, heads_here, HDIM)
+    local_acc = jnp.sum(jnp.where(own_head[None, :, :, None], weighted, 0.0), axis=2)
     stats = jnp.concatenate(
         [local_acc, local_sum[..., None], local_top[..., None]], axis=-1
     )
@@ -223,17 +232,17 @@
     totals = stats[..., HDIM]
     top_score = stats[..., HDIM + 1]
     own_score = (
-        jnp.einsum("rhd,rhd->hr", queries, new_keys, preferred_element_type=jnp.float32) * 0.125
+        jnp.einsum("rhd,rhd->rh", queries, new_keys, preferred_element_type=jnp.float32) * 0.125
     )
     final_top = jnp.maximum(top_score, own_score)
     shrink = jnp.exp(top_score - final_top)
     own_expo = jnp.exp(own_score - final_top)
     own_prob = lax.optimization_barrier(own_expo.astype(jnp.bfloat16)).astype(jnp.float32)
     totals = totals * shrink + own_expo
-    own_values = jnp.transpose(new_values, (1, 0, 2)).astype(jnp.float32)
+    own_values = new_values.astype(jnp.float32)
     mixture = mixture * shrink[..., None] + own_prob[..., None] * own_values
     mixed = (mixture / totals[..., None]).astype(jnp.bfloat16)
-    mixed_rows = jnp.transpose(mixed, (1, 0, 2)).reshape(requests, feat_width)
+    mixed_rows = mixed.reshape(requests, feat_width)
     out_terms = jnp.dot(mixed_rows, w_out, preferred_element_type=jnp.float32)
     attn_out = butterfly(out_terms, jnp.add, ["heads"]).astype(jnp.bfloat16)
     return (packed_keys, packed_values, packed_request, folded_keys, folded_values, attn_out)

time: 261 us -> 270 us (1.034)
  local copies, waits for them, and re-layouts: 41.1 us -> 32.8 us
  waiting for transfers between devices: 116 us -> 123 us
  matrix products: 8 us -> 13.5 us
    unnamed x64 -> x35, local copies, waits for them, and re-layouts: 9.99 us -> 1.23 us
    reshape x3 -> x1, local copies, waits for them, and re-layouts: 8.28 us -> 0.14 us  [shards(): mixed_rows = mixed.reshape(requests, feat_width)]
    ppermute x20, waiting for transfers between devices: 116 us -> 123 us  [butterfly(): x = merge(x, lax.ppermute(x, axis, pairs))]
    dot_general x2, matrix products: 4.9 us -> 10.4 us  [the longest x1 5.83 us: shards(): lax.dot_general(spread_queries, flat_keys, (((1,), (1,)), ((), ())), pref...]
    ppermute x9, starting transfers between devices: 24.8 us -> 28.6 us  [passed_along(): lax.ppermute(array, SEQ_PARTS, [(i, (i + by) % count) for i in range(coun...]
    concatenate x0 -> x1, other arithmetic: none -> 3.31 us  [shards(): jnp.concatenate([row_values, folded_values.reshape(n_blocks, heads_here,...]
    exp x6 -> x0, other arithmetic: 2.8 us -> none  [the longest x5 2.79 us: softmax_merge(): scale_a = jnp.exp(top_a - top)]
    reduce_sum x1, other arithmetic: 1.14 us -> 3.92 us  [shards(): local_sum = jnp.sum(expo, axis=2)]
  transfers between devices with their start and end apart: 29 -> 29, of which waited for: 14 -> 15; matrix products, arithmetic and copies ran while one was open for 28% -> 27% of each run, Pallas kernels for 0% -> 0%
where the time goes in v4:
time: 270 us; the launch traced here: 265 us
  waiting for transfers between devices  123 us (46%)
  starting transfers between devices  66.4 us (25%)
  local copies, waits for them, and re-layouts  32.8 us (12%)
  other arithmetic  27.9 us (10%)
  matrix products  13.5 us (5%)
    ppermute x20, waiting for transfers between devices, butterfly(): x = merge(x, lax.ppermute(x, axis, pairs))  123 us
    ppermute x20, starting transfers between devices, butterfly(): x = merge(x, lax.ppermute(x, axis, pairs))  37.8 us
    ppermute x9, starting transfers between devices, passed_along(): lax.ppermute(array, SEQ_PARTS, [(i, (i + by) % count) for i in range(coun...  28.6 us
    dot_general x1, matrix products, shards(): lax.dot_general(spread_queries, flat_keys, (((1,), (1,)), ((), ())), pref...  5.83 us
  transfers between devices with their start and end apart: 29, of which 15 were waited for; matrix products, arithmetic and copies ran while one was open for 27% of the time, Pallas kernels for 0%

profile of v4, /device:TPU:6, one launch (start us, length us, event | category | flops | bytes accessed | tf_op | source)
XLA Modules:
  0.0 264.8 jit_solution(15166803474017037200)
XLA Ops:
  5.9 2.1 collective-permute-done.10
  8.0 1.7 collective-permute-start.11
  9.7 3.3 %collective-permute-done.11 = f32[64]{0:T(128)S(1)} collective-permute-done((f32[64]{0:T(128)S(1)}, f32[64]{0:T(128)S(1)}, u32[]{:S(2)}, u32[]{:S(2)}) %collective-permute-start.11) | collective-permute-done | bytes 288 | tf_op jit(solution)/shard_map/ppermute | solution.py:37
  13.0 1.9 collective-permute-start.12
  14.9 1.6 collective-permute-done.12
  16.6 3.3 %collective-permute-start.13 = (f32[64]{0:T(128)S(1)}, f32[64]{0:T(128)S(1)}, u32[]{:S(2)}, u32[]{:S(2)}) collective-permute-start(f32[64]{0:T(128)S(1)} %add.155), channel_id=1, source_target_pairs={{0,16},{8,24},{16,0},{24,8},{32,48},{40,56},{48,32},{56,40},{1,17}... | collective-permute-start | bytes 776 | tf_op jit(solution)/shard_map/ppermute | solution.py:37
  19.8 1.5 collective-permute-done.13
  21.4 6.8 %collective-permute-start.14 = (f32[64]{0:T(128)S(1)}, f32[64]{0:T(128)S(1)}, u32[]{:S(2)}, u32[]{:S(2)}) collective-permute-start(f32[64]{0:T(128)S(1)} %add.156), channel_id=1, source_target_pairs={{0,32},{8,40},{16,48},{24,56},{32,0},{40,8},{48,16},{56,24},{1,33}... | collective-permute-start | bytes 776 | tf_op jit(solution)/shard_map/ppermute | solution.py:37
  31.6 1.6 collective-permute-done.15
  34.7 1.6 collective-permute-start.1
  36.3 2.1 collective-permute-start.2
  38.5 6.0 %collective-permute-done.16 = f32[64,1536]{1,0:T(8,128)S(1)} collective-permute-done((f32[64,1536]{1,0:T(8,128)S(1)}, f32[64,1536]{1,0:T(8,128)S(1)}, u32[]{:S(2)}, u32[]{:S(2)}) %collective-permute-start.16) | collective-permute-done | bytes 393248 | tf_op jit(solution)/shard_map/ppermute | solution.py:37
  44.5 1.5 collective-permute-start.17
  46.9 1.0 fusion.43
  47.9 8.5 %collective-permute-done.17 = f32[64,1536]{1,0:T(8,128)S(1)} collective-permute-done((f32[64,1536]{1,0:T(8,128)S(1)}, f32[64,1536]{1,0:T(8,128)S(1)}, u32[]{:S(2)}, u32[]{:S(2)}) %collective-permute-start.17) | collective-permute-done | bytes 393248 | tf_op jit(solution)/shard_map/ppermute | solution.py:37
  56.5 1.1 collective-permute-start.18
  58.7 7.2 %collective-permute-done.18 = f32[64,1536]{1,0:T(8,128)S(1)} collective-permute-done((f32[64,1536]{1,0:T(8,128)S(1)}, f32[64,1536]{1,0:T(8,128)S(1)}, u32[]{:S(2)}, u32[]{:S(2)}) %collective-permute-start.18) | collective-permute-done | bytes 393248 | tf_op jit(solution)/shard_map/ppermute | solution.py:37
  66.0 1.6 collective-permute-start.19
  67.6 3.7 %gather_fusion.2 = bf16[16,128,512]{2,1,0:T(8,128)(2,1)} fusion(bf16[18,128,512]{2,1,0:T(8,128)(2,1)} %param.17, s32[1024]{0:T(1024)S(1)} %pad_clamp_fusion.1), kind=kCustom, calls=%fused_computation.2 | custom fusion | bytes 4194368 | tf_op jit(solution)/shard_map/gather | solution.py:163
  71.7 2.5 copy.164
  74.4 9.5 %collective-permute-done.19 = f32[64,1536]{1,0:T(8,128)S(1)} collective-permute-done((f32[64,1536]{1,0:T(8,128)S(1)}, f32[64,1536]{1,0:T(8,128)S(1)}, u32[]{:S(2)}, u32[]{:S(2)}) %collective-permute-start.19) | collective-permute-done | bytes 393248 | tf_op jit(solution)/shard_map/ppermute | solution.py:37
  84.0 5.5 %collective-permute-start.20 = (f32[64,1536]{1,0:T(8,128)S(1)}, f32[64,1536]{1,0:T(8,128)S(1)}, u32[]{:S(2)}, u32[]{:S(2)}) collective-permute-start(f32[64,1536]{1,0:T(8,128)S(1)} %add.164), channel_id=1, source_target_pairs={{0,32},{8,40},{16,48},{24,56},{32,0},{40,8},{48,16},{56,24},{1,33}... | collective-permute-start | bytes 1179656 | tf_op jit(solution)/shard_map/ppermute | solution.py:37
  89.4 3.3 %pad_maximum_fusion = bf16[2322,512]{0,1:T(8,128)(2,1)} fusion(bf16[18,512]{0,1:T(8,128)(2,1)S(1)} %copy.165, bf16[2304,512]{0,1:T(8,128)(2,1)} %copy.164), kind=kLoop, calls=%fused_computation.15 | loop fusion | flops 4755456 | bytes 4755456 | tf_op jit(solution)/shard_map/concatenate | solution.py:196
  92.7 14.4 %collective-permute-done.20 = f32[64,1536]{1,0:T(8,128)S(1)} collective-permute-done((f32[64,1536]{1,0:T(8,128)S(1)}, f32[64,1536]{1,0:T(8,128)S(1)}, u32[]{:S(2)}, u32[]{:S(2)}) %collective-permute-start.20) | collective-permute-done | bytes 393248 | tf_op jit(solution)/shard_map/ppermute | solution.py:37
  108.0 1.2 reshape.283
  110.3 1.4 broadcast_in_dim.192
  111.7 5.8 %fusion.57 = (f32[64,8]{1,0:T(8,128)S(1)}, f32[64,8,2322]{2,1,0:T(8,128)}) fusion(f32[2322]{0:T(1024)S(1)} %copy-done.13, bf16[18,512]{1,0:T(8,128)(2,1)S(1)} %get-tuple-element.44, bf16[2304,512]{1,0:T(8,128)(2,1)} %bitcast.136, bf16[64,8,512]{2,1,0:T(8,128)(2,1)} %broadcast_in_dim.192, pred[8,512]{1,0:T(8,128)(4,1)S(1)} %broadcast_in_dim.189, ...), kind=kOutput, calls=%fused_computation.155 | convolution fusion | flops 1227169280 | bytes 7821512 | tf_op jit(solution)/shard_map/dot_general | solution.py:213
  117.6 3.9 %fusion.2 = f32[64,8]{1,0:T(8,128)S(1)} fusion(f32[64,8,2322]{2,1,0:T(8,128)} %get-tuple-element.59, f32[64,8]{1,0:T(8,128)S(1)} %get-tuple-element.58, pred[64,2322]{1,0:T(8,128)(4,1)S(1)} %copy-done.7), kind=kLoop, calls=%fused_computation.11 | loop fusion | flops 3566080 | bytes 4908160 | tf_op jit(solution)/shard_map/reduce_sum | solution.py:220
  121.6 4.6 %select_reduce_fusion = f32[64,8,64]{2,1,0:T(8,128)S(1)} fusion(bf16[8,64,2322,1]{2,1,0,3:T(8,128)(2,1)} %bitcast.139, f32[64,8,2322]{2,1,0:T(8,128)S(1)} %copy-done.5, f32[64,8]{1,0:T(8,128)S(1)} %get-tuple-element.58, pred[64,2322]{1,0:T(8,128)(4,1)S(1)} %copy-done.7, pred[8,8]{0,1:T(8,128)(4,1)S(1)} %iota_compare_fusion.4), kind=kOutput, calls=%fused_computation.24 | convolution fusion | flops 1221454848 | bytes 7414976 | tf_op jit(solution)/shard_map/dot_general | solution.py:221
  126.9 2.9 %slice_bitcast_fusion.1 = (bf16[1,4,128,512]{3,2,1,0:T(8,128)(2,1)}, bf16[4,128,512]{2,1,0:T(8,128)(2,1)}, bf16[4,128,512]{2,1,0:T(8,128)(2,1)}, bf16[4,128,512]{2,1,0:T(8,128)(2,1)}) fusion(bf16[16,128,512]{2,1,0:T(8,128)(2,1)} %gather_fusion.2), kind=kLoop, calls=%fused_computation.29 | loop fusion | bytes 4194304 | tf_op jit(solution)/shard_map/slice | solution.py:170
  130.3 2.0 gather_fusion.4
  134.3 1.2 slice_bitcast_fusion
  138.1 6.2 %collective-permute-done.22 = f32[64,8,66]{2,1,0:T(8,128)S(1)} collective-permute-done((f32[64,8,66]{2,1,0:T(8,128)S(1)}, f32[64,8,66]{2,1,0:T(8,128)S(1)}, u32[]{:S(2)}, u32[]{:S(2)}) %collective-permute-start.22) | collective-permute-done | bytes 135200 | tf_op jit(solution)/shard_map/ppermute | solution.py:37
  145.6 7.7 %collective-permute-done.23 = f32[64,8,66]{2,1,0:T(8,128)S(1)} collective-permute-done((f32[64,8,66]{2,1,0:T(8,128)S(1)}, f32[64,8,66]{2,1,0:T(8,128)S(1)}, u32[]{:S(2)}, u32[]{:S(2)}) %collective-permute-start.23) | collective-permute-done | bytes 135200 | tf_op jit(solution)/shard_map/ppermute | solution.py:37
  155.3 15.2 %collective-permute-done.24 = f32[64,8,66]{2,1,0:T(8,128)S(1)} collective-permute-done((f32[64,8,66]{2,1,0:T(8,128)S(1)}, f32[64,8,66]{2,1,0:T(8,128)S(1)}, u32[]{:S(2)}, u32[]{:S(2)}) %collective-permute-start.24) | collective-permute-done | bytes 135200 | tf_op jit(solution)/shard_map/ppermute | solution.py:37
  171.5 4.0 %collective-permute-start.25 = (f32[64,8,66]{2,1,0:T(8,128)S(1)}, f32[64,8,66]{2,1,0:T(8,128)S(1)}, u32[]{:S(2)}, u32[]{:S(2)}) collective-permute-start(f32[64,8,66]{2,1,0:T(8,128)S(1)} %pad_maximum_fusion.7), channel_id=1, source_target_pairs={{0,16},{8,24},{16,0},{24,8},{32,48},{40,56},{48,32},{56,40},{1,17}... | collective-permute-start | bytes 405512 | tf_op jit(solution)/shard_map/ppermute | solution.py:37
  176.0 6.6 %collective-permute-done.25 = f32[64,8,66]{2,1,0:T(8,128)S(1)} collective-permute-done((f32[64,8,66]{2,1,0:T(8,128)S(1)}, f32[64,8,66]{2,1,0:T(8,128)S(1)}, u32[]{:S(2)}, u32[]{:S(2)}) %collective-permute-start.25) | collective-permute-done | bytes 135200 | tf_op jit(solution)/shard_map/ppermute | solution.py:37
  182.6 23.8 %collective-permute-start.7 = (bf16[4,128,512]{2,1,0:T(8,128)(2,1)}, bf16[4,128,512]{2,1,0:T(8,128)(2,1)}, u32[]{:S(2)}, u32[]{:S(2)}) collective-permute-start(bf16[4,128,512]{2,1,0:T(8,128)(2,1)} %get-tuple-element.21), channel_id=1, source_target_pairs={{0,2},{1,3},{2,4},{3,5},{4,6},{5,7},{6,8},{7,9},{8,10},{9,11},{10,... | collective-permute-start | bytes 1572872 | tf_op jit(solution)/shard_map/ppermute | solution.py:70
  208.2 2.7 %collective-permute-start.26 = (f32[64,8,66]{2,1,0:T(8,128)}, f32[64,8,66]{2,1,0:T(8,128)S(1)}, u32[]{:S(2)}, u32[]{:S(2)}) collective-permute-start(f32[64,8,66]{2,1,0:T(8,128)} %pad_maximum_fusion.8), channel_id=1, source_target_pairs={{0,32},{8,40},{16,48},{24,56},{32,0},{40,8},{48,16},{56,24},{1,33}... | collective-permute-start | bytes 405512 | tf_op jit(solution)/shard_map/ppermute | solution.py:37
  210.8 1.8 pad_maximum_fusion.1
  212.7 31.5 %collective-permute-done.26 = f32[64,8,66]{2,1,0:T(8,128)S(1)} collective-permute-done((f32[64,8,66]{2,1,0:T(8,128)}, f32[64,8,66]{2,1,0:T(8,128)S(1)}, u32[]{:S(2)}, u32[]{:S(2)}) %collective-permute-start.26) | collective-permute-done | bytes 135200 | tf_op jit(solution)/shard_map/ppermute | solution.py:37
  245.4 1.2 fusion.26
  246.9 1.6 collective-permute-start.27
  248.5 2.9 %pad_maximum_fusion.2 = bf16[4,4,128,512]{3,2,1,0:T(8,128)(2,1)} fusion(bf16[1,4,128,512]{3,2,1,0:T(8,128)(2,1)} %bitcast.20, bf16[1,4,128,512]{3,2,1,0:T(8,128)(2,1)} %bitcast.19, bf16[1,4,128,512]{3,2,1,0:T(8,128)(2,1)} %bitcast.18, bf16[1,4,128,512]{3,2,1,0:T(8,128)(2,1)S(1)} %get-tuple-element.20), kind=kLoop, calls=%fused_computation.23 | loop fusion | flops 3145728 | bytes 4194304 | tf_op jit(solution)/shard_map/stack | solution.py:176
  251.4 2.0 gather_fusion.3
  253.5 3.7 %gather_fusion.5 = bf16[16,128,512]{2,1,0:T(8,128)(2,1)} fusion(bf16[16,128,512]{2,1,0:T(8,128)(2,1)} %bitcast.138, s32[1024]{0:T(1024)S(1)} %pad_clamp_fusion), kind=kCustom, calls=%fused_computation.5 | custom fusion | bytes 4194368 | tf_op jit(solution)/shard_map/gather | solution.py:188
  257.2 3.0 %collective-permute-start.28 = (f32[64,32]{0,1:T(8,128)S(1)}, f32[64,32]{0,1:T(8,128)S(1)}, u32[]{:S(2)}, u32[]{:S(2)}) collective-permute-start(f32[64,32]{0,1:T(8,128)S(1)} %add.178), channel_id=1, source_target_pairs={{0,128},{64,192},{128,0},{192,64},{1,129},{65,193},{129,1},{193,65... | collective-permute-start | bytes 24584 | tf_op jit(solution)/shard_map/ppermute | solution.py:37
  260.2 3.9 %broadcast_select_fusion = (bf16[16,128,512]{2,1,0:T(8,128)(2,1)}, bf16[16,128,512]{2,1,0:T(8,128)(2,1)}) fusion(bf16[16,128,512]{2,1,0:T(8,128)(2,1)} %gather_fusion.5, pred[16]{0:T(512)(128)(4,1)S(1)} %fusion.38, bf16[16,128,512]{2,1,0:T(8,128)(2,1)S(1)} %copy-done.4), kind=kLoop, calls=%fused_computation.25 | loop fusion | flops 2097152 | bytes 8388624 | tf_op jit(solution)/shard_map/jit(_where)/select_n | solution.py:187
  (188 shorter events, 29.4 us)
Async XLA Ops:
  0.6 246.1 %copy-start = (bf16[512,32]{0,1:T(8,128)(2,1)S(1)}, bf16[512,32]{0,1:T(8,128)(2,1)}, u32[]{:S(2)}) copy-start(bf16[512,32]{0,1:T(8,128)(2,1)} %param.12) | copy-start | bytes 98308
  0.6 46.1 %copy-start.10 = (f32[18,128]{1,0:T(8,128)S(1)}, f32[18,128]{1,0:T(8,128)}, u32[]{:S(2)}) copy-start(f32[18,128]{1,0:T(8,128)} %param.19) | copy-start | bytes 27652
  0.7 46.2 %copy-start.1 = (bf16[18,128,512]{2,1,0:T(8,128)(2,1)S(1)}, bf16[18,128,512]{2,1,0:T(8,128)(2,1)}, u32[]{:S(2)}) copy-start(bf16[18,128,512]{2,1,0:T(8,128)(2,1)} %param.18) | copy-start | bytes 7077892
  1.5 2.8 %collective-permute-start.9 = (f32[64]{0:T(128)S(1)}, f32[64]{0:T(128)S(1)}, u32[]{:S(2)}, u32[]{:S(2)}) collective-permute-start(f32[64]{0:T(128)S(1)} %fusion.32), channel_id=1, source_target_pairs={{0,1},{1,0},{2,3},{3,2},{4,5},{5,4},{6,7},{7,6},{8,9},{9,8},{10,11... | collective-permute-start | bytes 776 | tf_op jit(solution)/shard_map/ppermute | solution.py:37
  4.3 3.6 %collective-permute-start.10 = (f32[64]{0:T(128)S(1)}, f32[64]{0:T(128)S(1)}, u32[]{:S(2)}, u32[]{:S(2)}) collective-permute-start(f32[64]{0:T(128)S(1)} %add.152), channel_id=1, source_target_pairs={{0,2},{2,0},{4,6},{6,4},{1,3},{3,1},{5,7},{7,5},{8,10},{10,8},{12,... | collective-permute-start | bytes 776 | tf_op jit(solution)/shard_map/ppermute | solution.py:37
  8.0 5.0 %collective-permute-start.11 = (f32[64]{0:T(128)S(1)}, f32[64]{0:T(128)S(1)}, u32[]{:S(2)}, u32[]{:S(2)}) collective-permute-start(f32[64]{0:T(128)S(1)} %add.153), channel_id=1, source_target_pairs={{0,4},{2,6},{4,0},{6,2},{1,5},{3,7},{5,1},{7,3},{8,12},{10,14},{12... | collective-permute-start | bytes 776 | tf_op jit(solution)/shard_map/ppermute | solution.py:37
  13.0 3.5 %collective-permute-start.12 = (f32[64]{0:T(128)S(1)}, f32[64]{0:T(128)S(1)}, u32[]{:S(2)}, u32[]{:S(2)}) collective-permute-start(f32[64]{0:T(128)S(1)} %add.154), channel_id=1, source_target_pairs={{0,8},{8,0},{16,24},{24,16},{32,40},{40,32},{48,56},{56,48},{1,9},... | collective-permute-start | bytes 776 | tf_op jit(solution)/shard_map/ppermute | solution.py:37
  16.6 4.8 %collective-permute-start.13 = (f32[64]{0:T(128)S(1)}, f32[64]{0:T(128)S(1)}, u32[]{:S(2)}, u32[]{:S(2)}) collective-permute-start(f32[64]{0:T(128)S(1)} %add.155), channel_id=1, source_target_pairs={{0,16},{8,24},{16,0},{24,8},{32,48},{40,56},{48,32},{56,40},{1,17}... | collective-permute-start | bytes 776 | tf_op jit(solution)/shard_map/ppermute | solution.py:37
  21.4 9.1 %collective-permute-start.14 = (f32[64]{0:T(128)S(1)}, f32[64]{0:T(128)S(1)}, u32[]{:S(2)}, u32[]{:S(2)}) collective-permute-start(f32[64]{0:T(128)S(1)} %add.156), channel_id=1, source_target_pairs={{0,32},{8,40},{16,48},{24,56},{32,0},{40,8},{48,16},{56,24},{1,33}... | collective-permute-start | bytes 776 | tf_op jit(solution)/shard_map/ppermute | solution.py:37
  31.4 1.8 collective-permute-start.15
  33.2 11.3 %collective-permute-start.16 = (f32[64,1536]{1,0:T(8,128)S(1)}, f32[64,1536]{1,0:T(8,128)S(1)}, u32[]{:S(2)}, u32[]{:S(2)}) collective-permute-start(f32[64,1536]{1,0:T(8,128)S(1)} %add.160), channel_id=1, source_target_pairs={{0,2},{2,0},{4,6},{6,4},{1,3},{3,1},{5,7},{7,5},{8,10},{10,8},{12,... | collective-permute-start | bytes 1179656 | tf_op jit(solution)/shard_map/ppermute | solution.py:37
  34.7 100.7 %collective-permute-start = (bf16[4,2]{0,1:T(2,128)(2,1)}, bf16[4,2]{0,1:T(2,128)(2,1)}, u32[]{:S(2)}, u32[]{:S(2)}) collective-permute-start(bf16[4,2]{0,1:T(2,128)(2,1)} %get-tuple-element.53), channel_id=1, source_target_pairs={{0,1},{1,2},{2,3},{3,4},{4,5},{5,6},{6,7},{7,8},{8,9},{9,10},{10,1... | collective-permute-start | bytes 56 | tf_op jit(solution)/shard_map/ppermute | solution.py:70
  34.7 101.4 %collective-permute-start.1 = (bf16[4,2]{0,1:T(2,128)(2,1)S(1)}, bf16[4,2]{0,1:T(2,128)(2,1)}, u32[]{:S(2)}, u32[]{:S(2)}) collective-permute-start(bf16[4,2]{0,1:T(2,128)(2,1)S(1)} %get-tuple-element.52), channel_id=1, source_target_pairs={{0,2},{1,3},{2,4},{3,5},{4,6},{5,7},{6,8},{7,9},{8,10},{9,11},{10,... | collective-permute-start | bytes 56 | tf_op jit(solution)/shard_map/ppermute | solution.py:70
  36.3 100.5 %collective-permute-start.2 = (bf16[4,2]{0,1:T(2,128)(2,1)S(1)}, bf16[4,2]{0,1:T(2,128)(2,1)}, u32[]{:S(2)}, u32[]{:S(2)}) collective-permute-start(bf16[4,2]{0,1:T(2,128)(2,1)S(1)} %get-tuple-element.51), channel_id=1, source_target_pairs={{0,3},{1,4},{2,5},{3,6},{4,7},{5,8},{6,9},{7,10},{8,11},{9,12},{10... | collective-permute-start | bytes 56 | tf_op jit(solution)/shard_map/ppermute | solution.py:70
  44.5 11.9 %collective-permute-start.17 = (f32[64,1536]{1,0:T(8,128)S(1)}, f32[64,1536]{1,0:T(8,128)S(1)}, u32[]{:S(2)}, u32[]{:S(2)}) collective-permute-start(f32[64,1536]{1,0:T(8,128)S(1)} %add.161), channel_id=1, source_target_pairs={{0,4},{2,6},{4,0},{6,2},{1,5},{3,7},{5,1},{7,3},{8,12},{10,14},{12... | collective-permute-start | bytes 1179656 | tf_op jit(solution)/shard_map/ppermute | solution.py:37
  46.9 10.7 %copy-start.2 = (bf16[18,128,512]{2,1,0:T(8,128)(2,1)S(1)}, bf16[18,128,512]{2,1,0:T(8,128)(2,1)}, u32[]{:S(2)}) copy-start(bf16[18,128,512]{2,1,0:T(8,128)(2,1)} %param.17) | copy-start | bytes 7077892
  56.5 9.5 %collective-permute-start.18 = (f32[64,1536]{1,0:T(8,128)S(1)}, f32[64,1536]{1,0:T(8,128)S(1)}, u32[]{:S(2)}, u32[]{:S(2)}) collective-permute-start(f32[64,1536]{1,0:T(8,128)S(1)} %add.162), channel_id=1, source_target_pairs={{0,8},{8,0},{16,24},{24,16},{32,40},{40,32},{48,56},{56,48},{1,9},... | collective-permute-start | bytes 1179656 | tf_op jit(solution)/shard_map/ppermute | solution.py:37
  58.7 12.8 %copy-start.9 = (bf16[18,512]{1,0:T(8,128)(2,1)}, bf16[18,512]{1,0:T(8,128)(2,1)S(1)}, u32[]{:S(2)}) copy-start(bf16[18,512]{1,0:T(8,128)(2,1)S(1)} %get-tuple-element.43) | copy-start | bytes 55300
  58.7 53.0 %copy-start.11 = (bf16[18,512]{1,0:T(8,128)(2,1)}, bf16[18,512]{1,0:T(8,128)(2,1)S(1)}, u32[]{:S(2)}) copy-start(bf16[18,512]{1,0:T(8,128)(2,1)S(1)} %get-tuple-element.44) | copy-start | bytes 55300
  66.0 5.2 %copy-start.12 = (s32[64]{0:T(128)S(1)}, s32[64]{0:T(128)}, u32[]{:S(2)}) copy-start(s32[64]{0:T(128)} %param.13) | copy-start | bytes 772
  66.0 17.9 %collective-permute-start.19 = (f32[64,1536]{1,0:T(8,128)S(1)}, f32[64,1536]{1,0:T(8,128)S(1)}, u32[]{:S(2)}, u32[]{:S(2)}) collective-permute-start(f32[64,1536]{1,0:T(8,128)S(1)} %add.163), channel_id=1, source_target_pairs={{0,16},{8,24},{16,0},{24,8},{32,48},{40,56},{48,32},{56,40},{1,17}... | collective-permute-start | bytes 1179656 | tf_op jit(solution)/shard_map/ppermute | solution.py:37
  84.0 23.2 %collective-permute-start.20 = (f32[64,1536]{1,0:T(8,128)S(1)}, f32[64,1536]{1,0:T(8,128)S(1)}, u32[]{:S(2)}, u32[]{:S(2)}) collective-permute-start(f32[64,1536]{1,0:T(8,128)S(1)} %add.164), channel_id=1, source_target_pairs={{0,32},{8,40},{16,48},{24,56},{32,0},{40,8},{48,16},{56,24},{1,33}... | collective-permute-start | bytes 1179656 | tf_op jit(solution)/shard_map/ppermute | solution.py:37
  109.1 0.9 copy-start.6
  109.2 2.5 copy-start.13
  111.7 5.9 %copy-start.7 = (pred[64,2322]{1,0:T(8,128)(4,1)S(1)}, pred[64,2322]{1,0:T(8,128)(4,1)}, u32[]{:S(2)}) copy-start(pred[64,2322]{1,0:T(8,128)(4,1)} %iota_compare_fusion) | copy-start | bytes 445828
  117.6 3.9 %copy-start.5 = (f32[64,8,2322]{2,1,0:T(8,128)S(1)}, f32[64,8,2322]{2,1,0:T(8,128)}, u32[]{:S(2)}) copy-start(f32[64,8,2322]{2,1,0:T(8,128)} %get-tuple-element.59) | copy-start | bytes 14266372
  126.8 5.5 %collective-permute-start.21 = (f32[64,8,66]{2,1,0:T(8,128)S(1)}, f32[64,8,66]{2,1,0:T(8,128)S(1)}, u32[]{:S(2)}, u32[]{:S(2)}) collective-permute-start(f32[64,8,66]{2,1,0:T(8,128)S(1)} %pad_maximum_fusion.3), channel_id=1, source_target_pairs={{0,1},{1,0},{2,3},{3,2},{4,5},{5,4},{6,7},{7,6},{8,9},{9,8},{10,11... | collective-permute-start | bytes 405512 | tf_op jit(solution)/shard_map/ppermute | solution.py:37
  129.8 78.4 %collective-permute-start.3 = (bf16[4,128,512]{2,1,0:T(8,128)(2,1)}, bf16[4,128,512]{2,1,0:T(8,128)(2,1)}, u32[]{:S(2)}, u32[]{:S(2)}) collective-permute-start(bf16[4,128,512]{2,1,0:T(8,128)(2,1)} %get-tuple-element.26), channel_id=1, source_target_pairs={{0,1},{1,2},{2,3},{3,4},{4,5},{5,6},{6,7},{7,8},{8,9},{9,10},{10,1... | collective-permute-start | bytes 1572872 | tf_op jit(solution)/shard_map/ppermute | solution.py:70
  132.3 2.0 copy-start.3
  133.3 11.0 %collective-permute-start.22 = (f32[64,8,66]{2,1,0:T(8,128)S(1)}, f32[64,8,66]{2,1,0:T(8,128)S(1)}, u32[]{:S(2)}, u32[]{:S(2)}) collective-permute-start(f32[64,8,66]{2,1,0:T(8,128)S(1)} %pad_maximum_fusion.4), channel_id=1, source_target_pairs={{0,2},{2,0},{4,6},{6,4},{1,3},{3,1},{5,7},{7,5},{8,10},{10,8},{12,... | collective-permute-start | bytes 405512 | tf_op jit(solution)/shard_map/ppermute | solution.py:37
  135.5 72.7 %collective-permute-start.4 = (bf16[4,128,512]{2,1,0:T(8,128)(2,1)}, bf16[4,128,512]{2,1,0:T(8,128)(2,1)S(1)}, u32[]{:S(2)}, u32[]{:S(2)}) collective-permute-start(bf16[4,128,512]{2,1,0:T(8,128)(2,1)} %get-tuple-element.25), channel_id=1, source_target_pairs={{0,2},{1,3},{2,4},{3,5},{4,6},{5,7},{6,8},{7,9},{8,10},{9,11},{10,... | collective-permute-start | bytes 1572872 | tf_op jit(solution)/shard_map/ppermute | solution.py:70
  136.2 74.7 %collective-permute-start.5 = (bf16[4,128,512]{2,1,0:T(8,128)(2,1)}, bf16[4,128,512]{2,1,0:T(8,128)(2,1)}, u32[]{:S(2)}, u32[]{:S(2)}) collective-permute-start(bf16[4,128,512]{2,1,0:T(8,128)(2,1)} %get-tuple-element.27), channel_id=1, source_target_pairs={{0,3},{1,4},{2,5},{3,6},{4,7},{5,8},{6,9},{7,10},{8,11},{9,12},{10... | collective-permute-start | bytes 1572872 | tf_op jit(solution)/shard_map/ppermute | solution.py:70
  136.8 111.7 %collective-permute-start.6 = (bf16[4,128,512]{2,1,0:T(8,128)(2,1)}, bf16[4,128,512]{2,1,0:T(8,128)(2,1)}, u32[]{:S(2)}, u32[]{:S(2)}) collective-permute-start(bf16[4,128,512]{2,1,0:T(8,128)(2,1)} %get-tuple-element.22), channel_id=1, source_target_pairs={{0,1},{1,2},{2,3},{3,4},{4,5},{5,6},{6,7},{7,8},{8,9},{9,10},{10,1... | collective-permute-start | bytes 1572872 | tf_op jit(solution)/shard_map/ppermute | solution.py:70
  145.4 8.0 %collective-permute-start.23 = (f32[64,8,66]{2,1,0:T(8,128)S(1)}, f32[64,8,66]{2,1,0:T(8,128)S(1)}, u32[]{:S(2)}, u32[]{:S(2)}) collective-permute-start(f32[64,8,66]{2,1,0:T(8,128)S(1)} %pad_maximum_fusion.5), channel_id=1, source_target_pairs={{0,4},{2,6},{4,0},{6,2},{1,5},{3,7},{5,1},{7,3},{8,12},{10,14},{12... | collective-permute-start | bytes 405512 | tf_op jit(solution)/shard_map/ppermute | solution.py:37
  154.3 16.1 %collective-permute-start.24 = (f32[64,8,66]{2,1,0:T(8,128)S(1)}, f32[64,8,66]{2,1,0:T(8,128)S(1)}, u32[]{:S(2)}, u32[]{:S(2)}) collective-permute-start(f32[64,8,66]{2,1,0:T(8,128)S(1)} %pad_maximum_fusion.6), channel_id=1, source_target_pairs={{0,8},{8,0},{16,24},{24,16},{32,40},{40,32},{48,56},{56,48},{1,9},... | collective-permute-start | bytes 405512 | tf_op jit(solution)/shard_map/ppermute | solution.py:37
  171.5 11.2 %collective-permute-start.25 = (f32[64,8,66]{2,1,0:T(8,128)S(1)}, f32[64,8,66]{2,1,0:T(8,128)S(1)}, u32[]{:S(2)}, u32[]{:S(2)}) collective-permute-start(f32[64,8,66]{2,1,0:T(8,128)S(1)} %pad_maximum_fusion.7), channel_id=1, source_target_pairs={{0,16},{8,24},{16,0},{24,8},{32,48},{40,56},{48,32},{56,40},{1,17}... | collective-permute-start | bytes 405512 | tf_op jit(solution)/shard_map/ppermute | solution.py:37
  182.6 65.9 %collective-permute-start.7 = (bf16[4,128,512]{2,1,0:T(8,128)(2,1)}, bf16[4,128,512]{2,1,0:T(8,128)(2,1)}, u32[]{:S(2)}, u32[]{:S(2)}) collective-permute-start(bf16[4,128,512]{2,1,0:T(8,128)(2,1)} %get-tuple-element.21), channel_id=1, source_target_pairs={{0,2},{1,3},{2,4},{3,5},{4,6},{5,7},{6,8},{7,9},{8,10},{9,11},{10,... | collective-permute-start | bytes 1572872 | tf_op jit(solution)/shard_map/ppermute | solution.py:70
  208.1 40.4 %collective-permute-start.8 = (bf16[4,128,512]{2,1,0:T(8,128)(2,1)}, bf16[4,128,512]{2,1,0:T(8,128)(2,1)}, u32[]{:S(2)}, u32[]{:S(2)}) collective-permute-start(bf16[4,128,512]{2,1,0:T(8,128)(2,1)} %get-tuple-element.23), channel_id=1, source_target_pairs={{0,3},{1,4},{2,5},{3,6},{4,7},{5,8},{6,9},{7,10},{8,11},{9,12},{10... | collective-permute-start | bytes 1572872 | tf_op jit(solution)/shard_map/ppermute | solution.py:70
  208.2 2.7 %copy-start.8 = (bf16[4,128,512]{2,1,0:T(8,128)(2,1)}, bf16[4,128,512]{2,1,0:T(8,128)(2,1)S(1)}, u32[]{:S(2)}) copy-start(bf16[4,128,512]{2,1,0:T(8,128)(2,1)S(1)} %collective-permute-done.4) | copy-start | bytes 1572868
  208.2 36.0 %collective-permute-start.26 = (f32[64,8,66]{2,1,0:T(8,128)}, f32[64,8,66]{2,1,0:T(8,128)S(1)}, u32[]{:S(2)}, u32[]{:S(2)}) collective-permute-start(f32[64,8,66]{2,1,0:T(8,128)} %pad_maximum_fusion.8), channel_id=1, source_target_pairs={{0,32},{8,40},{16,48},{24,56},{32,0},{40,8},{48,16},{56,24},{1,33}... | collective-permute-start | bytes 405512 | tf_op jit(solution)/shard_map/ppermute | solution.py:37
  246.9 10.3 %collective-permute-start.27 = (f32[64,32]{0,1:T(8,128)S(1)}, f32[64,32]{0,1:T(8,128)S(1)}, u32[]{:S(2)}, u32[]{:S(2)}) collective-permute-start(f32[64,32]{0,1:T(8,128)S(1)} %fusion.58), channel_id=1, source_target_pairs={{0,64},{64,0},{128,192},{192,128},{1,65},{65,1},{129,193},{193,129... | collective-permute-start | bytes 24584 | tf_op jit(solution)/shard_map/ppermute | solution.py:37
  253.5 6.7 %copy-start.4 = (bf16[16,128,512]{2,1,0:T(8,128)(2,1)S(1)}, bf16[16,128,512]{2,1,0:T(8,128)(2,1)}, u32[]{:S(2)}) copy-start(bf16[16,128,512]{2,1,0:T(8,128)(2,1)} %gather_fusion.3) | copy-start | bytes 6291460
  257.2 6.9 %collective-permute-start.28 = (f32[64,32]{0,1:T(8,128)S(1)}, f32[64,32]{0,1:T(8,128)S(1)}, u32[]{:S(2)}, u32[]{:S(2)}) collective-permute-start(f32[64,32]{0,1:T(8,128)S(1)} %add.178), channel_id=1, source_target_pairs={{0,128},{64,192},{128,0},{192,64},{1,129},{65,193},{129,1},{193,65... | collective-permute-start | bytes 24584 | tf_op jit(solution)/shard_map/ppermute | solution.py:37

commit v5 on v4

--- a/solution.py
+++ b/solution.py
@@ -110,11 +110,31 @@
     partial_value = jnp.dot(
         normed, w_qkv.reshape(w_qkv.shape[0], 3 * feat_width), preferred_element_type=jnp.float32
     )
-    proj_all = seq_sum(partial_value).reshape(requests, 3, heads_here, HDIM)
+    query_sum = partial_value[:, :feat_width]
+    key_values = partial_value[:, feat_width:]
+    own_request = jnp.zeros((), jnp.int32)
+    for axis, pairs in exchange_steps(reversed(SEQ_PARTS)):
+        bit = pairs[0][1]
+        upper_half = (lax.axis_index(axis) // bit) % 2 == 1
+        half = key_values.shape[0] // 2
+        lower, upper = key_values[:half], key_values[half:]
+        kept = jnp.where(upper_half, upper, lower)
+        given = jnp.where(upper_half, lower, upper)
+        payload = jnp.concatenate([query_sum.reshape(-1), given.reshape(-1)])
+        payload = lax.ppermute(payload, axis, pairs)
+        query_sum = query_sum + payload[: query_sum.size].reshape(query_sum.shape)
+        key_values = kept + payload[query_sum.size :].reshape(given.shape)
+        own_request = own_request + jnp.where(upper_half, half, 0)
     cos_table, sin_table = rope_tables(positions, HDIM)
-    queries = rotate_half(proj_all[:, 0], cos_table, sin_table).astype(jnp.bfloat16)
-    new_keys = rotate_half(proj_all[:, 1], cos_table, sin_table).astype(jnp.bfloat16)
-    new_values = proj_all[:, 2].astype(jnp.bfloat16)
+    queries = rotate_half(
+        query_sum.reshape(requests, heads_here, HDIM), cos_table, sin_table
+    ).astype(jnp.bfloat16)
+    own_cos = lax.dynamic_index_in_dim(cos_table, own_request, keepdims=True)
+    own_sin = lax.dynamic_index_in_dim(sin_table, own_request, keepdims=True)
+    own_key = rotate_half(
+        key_values[:, :feat_width].reshape(-1, heads_here, HDIM), own_cos[:, 0], own_sin[:, 0]
+    ).astype(jnp.bfloat16)
+    own_value = key_values[:, feat_width:].reshape(-1, heads_here, HDIM).astype(jnp.bfloat16)
 
     block_ids = jnp.arange(n_blocks, dtype=jnp.int32)
     global_ids = my_index * n_blocks + block_ids
@@ -192,15 +212,20 @@
     row_keys = key_cache.reshape(-1, heads_here, HDIM)
     row_values = value_cache.reshape(-1, heads_here, HDIM)
     row_req = jnp.repeat(jnp.where(is_kept, blk_req, -1), row_count)
-    all_keys = jnp.concatenate([row_keys, folded_keys.reshape(n_blocks, heads_here, HDIM)], axis=0)
+    all_keys = jnp.concatenate(
+        [row_keys, folded_keys.reshape(n_blocks, heads_here, HDIM), own_key], axis=0
+    )
     all_values = jnp.concatenate(
-        [row_values, folded_values.reshape(n_blocks, heads_here, HDIM)], axis=0
-    )
-    all_req = jnp.concatenate([row_req, jnp.where(is_kept, -1, blk_req)])
+        [row_values, folded_values.reshape(n_blocks, heads_here, HDIM), own_value], axis=0
+    )
+    all_req = jnp.concatenate(
+        [row_req, jnp.where(is_kept, -1, blk_req), jnp.full((own_key.shape[0],), own_request)]
+    )
     bias = jnp.concatenate(
         [
             jnp.zeros((row_req.shape[0],), jnp.float32),
             jnp.full((n_blocks,), math.log(ROWS), jnp.float32),
+            jnp.zeros((own_key.shape[0],), jnp.float32),
         ]
     )
     row_mask = all_req[None, :] == jnp.arange(requests, dtype=jnp.int32)[:, None]
@@ -230,17 +255,6 @@
     stats = butterfly(stats, softmax_merge, reversed(SEQ_PARTS))
     mixture = stats[..., :HDIM]
     totals = stats[..., HDIM]
-    top_score = stats[..., HDIM + 1]
-    own_score = (
-        jnp.einsum("rhd,rhd->rh", queries, new_keys, preferred_element_type=jnp.float32) * 0.125
-    )
-    final_top = jnp.maximum(top_score, own_score)
-    shrink = jnp.exp(top_score - final_top)
-    own_expo = jnp.exp(own_score - final_top)
-    own_prob = lax.optimization_barrier(own_expo.astype(jnp.bfloat16)).astype(jnp.float32)
-    totals = totals * shrink + own_expo
-    own_values = new_values.astype(jnp.float32)
-    mixture = mixture * shrink[..., None] + own_prob[..., None] * own_values
     mixed = (mixture / totals[..., None]).astype(jnp.bfloat16)
     mixed_rows = mixed.reshape(requests, feat_width)
     out_terms = jnp.dot(mixed_rows, w_out, preferred_element_type=jnp.float32)

time: 270 us -> 251 us (0.930)
  waiting for transfers between devices: 123 us -> 91.6 us
  local copies, waits for them, and re-layouts: 32.8 us -> 41.5 us
  matrix products: 13.5 us -> 17.5 us
  other arithmetic: 27.9 us -> 23.9 us
  starting transfers between devices: 66.4 us -> 70.3 us
    ppermute x20 -> x14, waiting for transfers between devices: 123 us -> 79.4 us  [butterfly(): x = merge(x, lax.ppermute(x, axis, pairs))]
    ppermute x0 -> x6, starting transfers between devices: none -> 13.6 us  [shards(): payload = lax.ppermute(payload, axis, pairs)]
    ppermute x0 -> x6, waiting for transfers between devices: none -> 12.1 us  [shards(): payload = lax.ppermute(payload, axis, pairs)]
    ppermute x20 -> x14, starting transfers between devices: 37.8 us -> 27.6 us  [butterfly(): x = merge(x, lax.ppermute(x, axis, pairs))]
    concatenate x0 -> x2, local copies, waits for them, and re-layouts: none -> 8.12 us  [the longest x1 8.04 us: shards(): jnp.concatenate([row_keys, folded_keys.reshape(n_blocks, heads_here, HDIM...]
    concatenate x1 -> x2, local copies, waits for them, and re-layouts: 2.55 us -> 7.29 us  [shards(): jnp.concatenate([row_values, folded_values.reshape(n_blocks, heads_here,...]
    concatenate x2 -> x8, other arithmetic: 3.32 us -> 0.27 us  [the longest x2 0.19 us: rotate_half(): jnp.concatenate([lower * cos_table - upper * sin_table, upper * cos_table...]
  transfers between devices with their start and end apart: 29 -> 29, of which waited for: 15 -> 15; matrix products, arithmetic and copies ran while one was open for 27% -> 33% of each run, Pallas kernels for 0% -> 0%
where the time goes in v5:
time: 251 us; the launch traced here: 246 us
  waiting for transfers between devices  91.6 us (36%)
  starting transfers between devices  70.3 us (28%)
  local copies, waits for them, and re-layouts  41.5 us (17%)
  other arithmetic  23.9 us (10%)
  matrix products  17.5 us (7%)
    ppermute x14, waiting for transfers between devices, butterfly(): x = merge(x, lax.ppermute(x, axis, pairs))  79.4 us
    ppermute x9, starting transfers between devices, passed_along(): lax.ppermute(array, SEQ_PARTS, [(i, (i + by) % count) for i in range(coun...  29.2 us
    ppermute x14, starting transfers between devices, butterfly(): x = merge(x, lax.ppermute(x, axis, pairs))  27.6 us
    ppermute x6, starting transfers between devices, shards(): payload = lax.ppermute(payload, axis, pairs)  13.6 us
    ppermute x6, waiting for transfers between devices, shards(): payload = lax.ppermute(payload, axis, pairs)  12.1 us
    concatenate x1, local copies, waits for them, and re-layouts, shards(): jnp.concatenate([row_keys, folded_keys.reshape(n_blocks, heads_here, HDIM...  8.04 us
    concatenate x2, local copies, waits for them, and re-layouts, shards(): jnp.concatenate([row_values, folded_values.reshape(n_blocks, heads_here,...  7.29 us
    slice x4, local copies, waits for them, and re-layouts, shards(): arrived = [(send_keys[0], send_values[0], meta_data[0])]  6.15 us
  transfers between devices with their start and end apart: 29, of which 15 were waited for; matrix products, arithmetic and copies ran while one was open for 33% of the time, Pallas kernels for 0%

profile of v5, /device:TPU:6, one launch (start us, length us, event | category | flops | bytes accessed | tf_op | source)
XLA Modules:
  0.0 246.2 jit_solution(9102675239533410766)
XLA Ops:
  7.5 1.8 collective-permute-start.1
  9.4 1.9 collective-permute-start.2
  12.9 3.0 %collective-permute-done.10 = f32[64]{0:T(128)S(1)} collective-permute-done((f32[64]{0:T(128)S(1)}, f32[64]{0:T(128)S(1)}, u32[]{:S(2)}, u32[]{:S(2)}) %collective-permute-start.10) | collective-permute-done | bytes 288 | tf_op jit(solution)/shard_map/ppermute | solution.py:37
  17.0 3.9 %collective-permute-done.11 = f32[64]{0:T(128)S(1)} collective-permute-done((f32[64]{0:T(128)S(1)}, f32[64]{0:T(128)S(1)}, u32[]{:S(2)}, u32[]{:S(2)}) %collective-permute-start.11) | collective-permute-done | bytes 288 | tf_op jit(solution)/shard_map/ppermute | solution.py:37
  21.0 1.9 collective-permute-start.12
  22.9 1.6 collective-permute-done.12
  24.5 4.4 %collective-permute-start.13 = (f32[64]{0:T(128)S(1)}, f32[64]{0:T(128)S(1)}, u32[]{:S(2)}, u32[]{:S(2)}) collective-permute-start(f32[64]{0:T(128)S(1)} %add.223), channel_id=1, source_target_pairs={{0,16},{8,24},{16,0},{24,8},{32,48},{40,56},{48,32},{56,40},{1,17}... | collective-permute-start | bytes 776 | tf_op jit(solution)/shard_map/ppermute | solution.py:37
  28.9 1.5 collective-permute-done.13
  30.4 4.8 %collective-permute-start.14 = (f32[64]{0:T(128)S(1)}, f32[64]{0:T(128)S(1)}, u32[]{:S(2)}, u32[]{:S(2)}) collective-permute-start(f32[64]{0:T(128)S(1)} %add.224), channel_id=1, source_target_pairs={{0,32},{8,40},{16,48},{24,56},{32,0},{40,8},{48,16},{56,24},{1,33}... | collective-permute-start | bytes 776 | tf_op jit(solution)/shard_map/ppermute | solution.py:37
  35.3 2.5 %collective-permute-done.14 = f32[64]{0:T(128)S(1)} collective-permute-done((f32[64]{0:T(128)S(1)}, f32[64]{0:T(128)S(1)}, u32[]{:S(2)}, u32[]{:S(2)}) %collective-permute-start.14) | collective-permute-done | bytes 288 | tf_op jit(solution)/shard_map/ppermute | solution.py:37
  41.4 3.5 %fusion.42 = f32[18,1,512]{2,1,0:T(1,128)} fusion(bf16[18,128,512]{2,1,0:T(8,128)(2,1)} %param.18, f32[18,128,1]{1,0,2:T(8,128)S(1)} %bitcast.178), kind=kOutput, calls=%fused_computation.134 | convolution fusion | flops 14155776 | bytes 2405376 | tf_op jit(solution)/shard_map/bi,bif->bf/dot_general | solution.py:153
  44.9 3.2 %collective-permute-done.16 = f32[49152]{0:T(1024)S(1)} collective-permute-done((f32[49152]{0:T(1024)S(1)}, f32[49152]{0:T(1024)S(1)}, u32[]{:S(2)}, u32[]{:S(2)}) %collective-permute-start.16) | collective-permute-done | bytes 196640 | tf_op jit(solution)/shard_map/ppermute | solution.py:124
  48.3 1.2 collective-permute-start.17
  49.5 1.6 fusion.44
  51.1 4.4 %collective-permute-done.17 = f32[40960]{0:T(1024)S(1)} collective-permute-done((f32[40960]{0:T(1024)S(1)}, f32[40960]{0:T(1024)S(1)}, u32[]{:S(2)}, u32[]{:S(2)}) %collective-permute-start.17) | collective-permute-done | bytes 163872 | tf_op jit(solution)/shard_map/ppermute | solution.py:124
  55.7 2.1 collective-permute-start.18
  59.5 1.5 collective-permute-done.18
  61.2 3.0 %collective-permute-start.19 = (f32[34816]{0:T(1024)S(1)}, f32[34816]{0:T(1024)S(1)}, u32[]{:S(2)}, u32[]{:S(2)}) collective-permute-start(f32[34816]{0:T(1024)S(1)} %pad_maximum_fusion.12), channel_id=1, source_target_pairs={{0,16},{8,24},{16,0},{24,8},{32,48},{40,56},{48,32},{56,40},{1,17}... | collective-permute-start | bytes 417800 | tf_op jit(solution)/shard_map/ppermute | solution.py:124
  64.4 2.9 %collective-permute-done.19 = f32[34816]{0:T(1024)S(1)} collective-permute-done((f32[34816]{0:T(1024)S(1)}, f32[34816]{0:T(1024)S(1)}, u32[]{:S(2)}, u32[]{:S(2)}) %collective-permute-start.19) | collective-permute-done | bytes 139296 | tf_op jit(solution)/shard_map/ppermute | solution.py:124
  67.5 6.5 %collective-permute-start.20 = (f32[33792]{0:T(1024)S(1)}, f32[33792]{0:T(1024)S(1)}, u32[]{:S(2)}, u32[]{:S(2)}) collective-permute-start(f32[33792]{0:T(1024)S(1)} %pad_maximum_fusion.13), channel_id=1, source_target_pairs={{0,32},{8,40},{16,48},{24,56},{32,0},{40,8},{48,16},{56,24},{1,33}... | collective-permute-start | bytes 405512 | tf_op jit(solution)/shard_map/ppermute | solution.py:124
  74.0 2.0 gather_fusion.2
  77.1 4.3 %copy.125 = bf16[2304,512]{0,1:T(8,128)(2,1)} copy(bf16[2304,512]{1,0:T(8,128)(2,1)} %bitcast.159) | data formatting | bytes 4718592 | tf_op jit(solution)/shard_map/concatenate | solution.py:218
  82.2 1.4 broadcast_in_dim.193
  84.1 8.0 %concatenate.82 = bf16[2323,512]{1,0:T(8,128)(2,1)} concatenate(bf16[2304,512]{1,0:T(8,128)(2,1)S(1)} %bitcast.158, bf16[18,512]{1,0:T(8,128)(2,1)S(1)} %get-tuple-element.37, bf16[1,512]{1,0:T(2,128)(2,1)S(1)} %convert_element_type.80), dimensions={0} | concatenate | bytes 4757504 | tf_op jit(solution)/shard_map/concatenate | solution.py:215
  92.2 5.7 %fusion.55 = (f32[64,8]{1,0:T(8,128)S(1)}, f32[64,8,2323]{2,1,0:T(8,128)}) fusion(f32[2323]{0:T(1024)S(1)} %copy-done.16, bf16[2323,512]{1,0:T(8,128)(2,1)} %concatenate.82, bf16[64,8,512]{2,1,0:T(8,128)(2,1)S(1)} %copy-done.6, pred[8,512]{1,0:T(8,128)(4,1)S(1)} %broadcast_in_dim.190, pred[64,2323]{1,0:T(8,128)(4,1)S(1)} %copy-done.5), kind=kOutput, calls=%fused_computation.176 | convolution fusion | flops 1222940160 | bytes 7824652 | tf_op jit(solution)/shard_map/dot_general | solution.py:238
  97.9 3.9 %fusion.2 = f32[64,8]{1,0:T(8,128)S(1)} fusion(f32[64,8,2323]{2,1,0:T(8,128)} %get-tuple-element.52, f32[64,8]{1,0:T(8,128)S(1)} %get-tuple-element.51, pred[64,2323]{1,0:T(8,128)(4,1)S(1)} %copy-done.5), kind=kLoop, calls=%fused_computation.11 | loop fusion | flops 3567616 | bytes 4910272 | tf_op jit(solution)/shard_map/reduce_sum | solution.py:245
  101.9 3.0 %concatenate.84 = bf16[2323,512]{0,1:T(8,128)(2,1)} concatenate(bf16[2304,512]{0,1:T(8,128)(2,1)S(1)} %copy-done.3, bf16[18,512]{0,1:T(8,128)(2,1)S(1)} %copy-done.7, bf16[1,512]{0,1:T(8,128)(2,1)S(1)} %copy.127), dimensions={0} | concatenate | bytes 4757504 | tf_op jit(solution)/shard_map/concatenate | solution.py:218
  104.8 5.7 %select_reduce_fusion = f32[64,8,64]{2,1,0:T(8,128)S(1)} fusion(bf16[8,64,2323,1]{2,1,0,3:T(8,128)(2,1)} %bitcast.162, f32[64,8,2323]{2,1,0:T(8,128)} %get-tuple-element.52, f32[64,8]{1,0:T(8,128)S(1)} %get-tuple-element.51, pred[64,2323]{1,0:T(8,128)(4,1)S(1)} %copy-done.5, pred[8,8]{0,1:T(8,128)(4,1)S(1)} %iota_compare_fusion.4), kind=kOutput, calls=%fused_computation.21 | convolution fusion | flops 1221980672 | bytes 7418112 | tf_op jit(solution)/shard_map/dot_general | solution.py:246
  111.5 2.8 %slice_bitcast_fusion.1 = (bf16[1,4,128,512]{3,2,1,0:T(8,128)(2,1)S(1)}, bf16[4,128,512]{2,1,0:T(8,128)(2,1)}, bf16[4,128,512]{2,1,0:T(8,128)(2,1)}, bf16[4,128,512]{2,1,0:T(8,128)(2,1)}) fusion(bf16[16,128,512]{2,1,0:T(8,128)(2,1)} %gather_fusion.2), kind=kLoop, calls=%fused_computation.26 | loop fusion | bytes 4194304 | tf_op jit(solution)/shard_map/slice | solution.py:190
  114.7 2.0 gather_fusion.4
  118.1 2.7 %slice_bitcast_fusion = (bf16[1,4,128,512]{3,2,1,0:T(8,128)(2,1)S(1)}, bf16[4,128,512]{2,1,0:T(8,128)(2,1)}, bf16[4,128,512]{2,1,0:T(8,128)(2,1)}, bf16[4,128,512]{2,1,0:T(8,128)(2,1)}) fusion(bf16[16,128,512]{2,1,0:T(8,128)(2,1)} %gather_fusion.4), kind=kLoop, calls=%fused_computation.25 | loop fusion | bytes 4194304 | tf_op jit(solution)/shard_map/slice | solution.py:190
  123.3 1.6 collective-permute-start.6
  125.6 1.5 collective-permute-done.22
  127.2 1.2 collective-permute-start.23
  128.6 6.9 %collective-permute-done.23 = f32[64,8,66]{0,1,2:T(8,128)S(1)} collective-permute-done((f32[64,8,66]{0,1,2:T(8,128)S(1)}, f32[64,8,66]{0,1,2:T(8,128)S(1)}, u32[]{:S(2)}, u32[]{:S(2)}) %collective-permute-start.23) | collective-permute-done | bytes 135200 | tf_op jit(solution)/shard_map/ppermute | solution.py:37
  137.7 18.3 %collective-permute-done.24 = f32[64,8,66]{0,1,2:T(8,128)S(1)} collective-permute-done((f32[64,8,66]{0,1,2:T(8,128)}, f32[64,8,66]{0,1,2:T(8,128)S(1)}, u32[]{:S(2)}, u32[]{:S(2)}) %collective-permute-start.24) | collective-permute-done | bytes 135200 | tf_op jit(solution)/shard_map/ppermute | solution.py:37
  156.1 3.1 %collective-permute-start.25 = (f32[64,8,66]{0,1,2:T(8,128)S(1)}, f32[64,8,66]{0,1,2:T(8,128)S(1)}, u32[]{:S(2)}, u32[]{:S(2)}) collective-permute-start(f32[64,8,66]{0,1,2:T(8,128)S(1)} %pad_maximum_fusion.6), channel_id=1, source_target_pairs={{0,16},{8,24},{16,0},{24,8},{32,48},{40,56},{48,32},{56,40},{1,17}... | collective-permute-start | bytes 405512 | tf_op jit(solution)/shard_map/ppermute | solution.py:37
  159.7 6.8 %collective-permute-done.25 = f32[64,8,66]{0,1,2:T(8,128)S(1)} collective-permute-done((f32[64,8,66]{0,1,2:T(8,128)S(1)}, f32[64,8,66]{0,1,2:T(8,128)S(1)}, u32[]{:S(2)}, u32[]{:S(2)}) %collective-permute-start.25) | collective-permute-done | bytes 135200 | tf_op jit(solution)/shard_map/ppermute | solution.py:37
  166.5 21.6 %collective-permute-start.7 = (bf16[4,128,512]{2,1,0:T(8,128)(2,1)}, bf16[4,128,512]{2,1,0:T(8,128)(2,1)}, u32[]{:S(2)}, u32[]{:S(2)}) collective-permute-start(bf16[4,128,512]{2,1,0:T(8,128)(2,1)} %get-tuple-element.17), channel_id=1, source_target_pairs={{0,2},{1,3},{2,4},{3,5},{4,6},{5,7},{6,8},{7,9},{8,10},{9,11},{10,... | collective-permute-start | bytes 1572872 | tf_op jit(solution)/shard_map/ppermute | solution.py:70
  188.3 4.6 %collective-permute-start.26 = (f32[64,8,66]{0,1,2:T(8,128)S(1)}, f32[64,8,66]{0,1,2:T(8,128)S(1)}, u32[]{:S(2)}, u32[]{:S(2)}) collective-permute-start(f32[64,8,66]{0,1,2:T(8,128)S(1)} %pad_maximum_fusion.7), channel_id=1, source_target_pairs={{0,32},{8,40},{16,48},{24,56},{32,0},{40,8},{48,16},{56,24},{1,33}... | collective-permute-start | bytes 405512 | tf_op jit(solution)/shard_map/ppermute | solution.py:37
  193.0 1.6 pad_maximum_fusion
  194.6 33.2 %collective-permute-done.26 = f32[64,8,66]{0,1,2:T(8,128)S(1)} collective-permute-done((f32[64,8,66]{0,1,2:T(8,128)S(1)}, f32[64,8,66]{0,1,2:T(8,128)S(1)}, u32[]{:S(2)}, u32[]{:S(2)}) %collective-permute-start.26) | collective-permute-done | bytes 135200 | tf_op jit(solution)/shard_map/ppermute | solution.py:37
  228.4 1.6 collective-permute-start.27
  230.0 2.9 %pad_maximum_fusion.1 = bf16[4,4,128,512]{3,2,1,0:T(8,128)(2,1)} fusion(bf16[1,4,128,512]{3,2,1,0:T(8,128)(2,1)} %bitcast.20, bf16[1,4,128,512]{3,2,1,0:T(8,128)(2,1)} %bitcast.19, bf16[1,4,128,512]{3,2,1,0:T(8,128)(2,1)} %bitcast.18, bf16[1,4,128,512]{3,2,1,0:T(8,128)(2,1)S(1)} %get-tuple-element.16), kind=kLoop, calls=%fused_computation.20 | loop fusion | flops 3145728 | bytes 4194304 | tf_op jit(solution)/shard_map/stack | solution.py:196
  232.9 2.0 gather_fusion.3
  234.9 3.7 %gather_fusion.5 = bf16[16,128,512]{2,1,0:T(8,128)(2,1)} fusion(bf16[16,128,512]{2,1,0:T(8,128)(2,1)} %bitcast.161, s32[1024]{0:T(1024)S(1)} %pad_clamp_fusion), kind=kCustom, calls=%fused_computation.5 | custom fusion | bytes 4194368 | tf_op jit(solution)/shard_map/gather | solution.py:208
  238.7 3.0 %collective-permute-start.28 = (f32[64,32]{0,1:T(8,128)S(1)}, f32[64,32]{0,1:T(8,128)S(1)}, u32[]{:S(2)}, u32[]{:S(2)}) collective-permute-start(f32[64,32]{0,1:T(8,128)S(1)} %add.251), channel_id=1, source_target_pairs={{0,128},{64,192},{128,0},{192,64},{1,129},{65,193},{129,1},{193,65... | collective-permute-start | bytes 24584 | tf_op jit(solution)/shard_map/ppermute | solution.py:37
  241.7 3.9 %broadcast_select_fusion = (bf16[16,128,512]{2,1,0:T(8,128)(2,1)}, bf16[16,128,512]{2,1,0:T(8,128)(2,1)}) fusion(bf16[16,128,512]{2,1,0:T(8,128)(2,1)} %gather_fusion.5, pred[16]{0:T(512)(128)(4,1)S(1)} %fusion.35, bf16[16,128,512]{2,1,0:T(8,128)(2,1)S(1)} %copy-done.4), kind=kLoop, calls=%fused_computation.22 | loop fusion | flops 2097152 | bytes 8388624 | tf_op jit(solution)/shard_map/jit(_where)/select_n | solution.py:207
  (218 shorter events, 27.9 us)
Async XLA Ops:
  0.6 227.6 %copy-start = (bf16[512,32]{0,1:T(8,128)(2,1)S(1)}, bf16[512,32]{0,1:T(8,128)(2,1)}, u32[]{:S(2)}) copy-start(bf16[512,32]{0,1:T(8,128)(2,1)} %param.12) | copy-start | bytes 98308
  0.6 39.1 %copy-start.13 = (f32[18,128]{1,0:T(8,128)S(1)}, f32[18,128]{1,0:T(8,128)}, u32[]{:S(2)}) copy-start(f32[18,128]{1,0:T(8,128)} %param.19) | copy-start | bytes 27652
  1.4 10.9 %collective-permute-start.9 = (f32[64]{0:T(128)S(1)}, f32[64]{0:T(128)S(1)}, u32[]{:S(2)}, u32[]{:S(2)}) collective-permute-start(f32[64]{0:T(128)S(1)} %fusion.29), channel_id=1, source_target_pairs={{0,1},{1,0},{2,3},{3,2},{4,5},{5,4},{6,7},{7,6},{8,9},{9,8},{10,11... | collective-permute-start | bytes 776 | tf_op jit(solution)/shard_map/ppermute | solution.py:37
  2.1 9.2 %copy-start.14 = (pred[18]{0:T(512)(128)(4,1)}, pred[18]{0:T(512)(128)(4,1)S(1)}, u32[]{:S(2)}) copy-start(pred[18]{0:T(512)(128)(4,1)S(1)} %broadcast_compare_fusion) | copy-start | bytes 58
  7.1 113.7 %collective-permute-start = (bf16[4,2]{0,1:T(2,128)(2,1)}, bf16[4,2]{0,1:T(2,128)(2,1)}, u32[]{:S(2)}, u32[]{:S(2)}) collective-permute-start(bf16[4,2]{0,1:T(2,128)(2,1)} %get-tuple-element.46), channel_id=1, source_target_pairs={{0,1},{1,2},{2,3},{3,4},{4,5},{5,6},{6,7},{7,8},{8,9},{9,10},{10,1... | collective-permute-start | bytes 56 | tf_op jit(solution)/shard_map/ppermute | solution.py:70
  7.5 114.2 %collective-permute-start.1 = (bf16[4,2]{0,1:T(2,128)(2,1)}, bf16[4,2]{0,1:T(2,128)(2,1)}, u32[]{:S(2)}, u32[]{:S(2)}) collective-permute-start(bf16[4,2]{0,1:T(2,128)(2,1)} %get-tuple-element.45), channel_id=1, source_target_pairs={{0,2},{1,3},{2,4},{3,5},{4,6},{5,7},{6,8},{7,9},{8,10},{9,11},{10,... | collective-permute-start | bytes 56 | tf_op jit(solution)/shard_map/ppermute | solution.py:70
  9.4 113.9 %collective-permute-start.2 = (bf16[4,2]{0,1:T(2,128)(2,1)}, bf16[4,2]{0,1:T(2,128)(2,1)}, u32[]{:S(2)}, u32[]{:S(2)}) collective-permute-start(bf16[4,2]{0,1:T(2,128)(2,1)} %get-tuple-element.44), channel_id=1, source_target_pairs={{0,3},{1,4},{2,5},{3,6},{4,7},{5,8},{6,9},{7,10},{8,11},{9,12},{10... | collective-permute-start | bytes 56 | tf_op jit(solution)/shard_map/ppermute | solution.py:70
  12.3 3.6 %collective-permute-start.10 = (f32[64]{0:T(128)S(1)}, f32[64]{0:T(128)S(1)}, u32[]{:S(2)}, u32[]{:S(2)}) collective-permute-start(f32[64]{0:T(128)S(1)} %add.220), channel_id=1, source_target_pairs={{0,2},{2,0},{4,6},{6,4},{1,3},{3,1},{5,7},{7,5},{8,10},{10,8},{12,... | collective-permute-start | bytes 776 | tf_op jit(solution)/shard_map/ppermute | solution.py:37
  15.9 5.0 %collective-permute-start.11 = (f32[64]{0:T(128)S(1)}, f32[64]{0:T(128)S(1)}, u32[]{:S(2)}, u32[]{:S(2)}) collective-permute-start(f32[64]{0:T(128)S(1)} %add.221), channel_id=1, source_target_pairs={{0,4},{2,6},{4,0},{6,2},{1,5},{3,7},{5,1},{7,3},{8,12},{10,14},{12... | collective-permute-start | bytes 776 | tf_op jit(solution)/shard_map/ppermute | solution.py:37
  21.0 3.5 %collective-permute-start.12 = (f32[64]{0:T(128)S(1)}, f32[64]{0:T(128)S(1)}, u32[]{:S(2)}, u32[]{:S(2)}) collective-permute-start(f32[64]{0:T(128)S(1)} %add.222), channel_id=1, source_target_pairs={{0,8},{8,0},{16,24},{24,16},{32,40},{40,32},{48,56},{56,48},{1,9},... | collective-permute-start | bytes 776 | tf_op jit(solution)/shard_map/ppermute | solution.py:37
  24.5 5.9 %collective-permute-start.13 = (f32[64]{0:T(128)S(1)}, f32[64]{0:T(128)S(1)}, u32[]{:S(2)}, u32[]{:S(2)}) collective-permute-start(f32[64]{0:T(128)S(1)} %add.223), channel_id=1, source_target_pairs={{0,16},{8,24},{16,0},{24,8},{32,48},{40,56},{48,32},{56,40},{1,17}... | collective-permute-start | bytes 776 | tf_op jit(solution)/shard_map/ppermute | solution.py:37
  30.4 7.4 %collective-permute-start.14 = (f32[64]{0:T(128)S(1)}, f32[64]{0:T(128)S(1)}, u32[]{:S(2)}, u32[]{:S(2)}) collective-permute-start(f32[64]{0:T(128)S(1)} %add.224), channel_id=1, source_target_pairs={{0,32},{8,40},{16,48},{24,56},{32,0},{40,8},{48,16},{56,24},{1,33}... | collective-permute-start | bytes 776 | tf_op jit(solution)/shard_map/ppermute | solution.py:37
  38.9 1.6 collective-permute-start.15
  40.8 7.2 %collective-permute-start.16 = (f32[49152]{0:T(1024)S(1)}, f32[49152]{0:T(1024)S(1)}, u32[]{:S(2)}, u32[]{:S(2)}) collective-permute-start(f32[49152]{0:T(1024)S(1)} %pad_maximum_fusion.9), channel_id=1, source_target_pairs={{0,2},{2,0},{4,6},{6,4},{1,3},{3,1},{5,7},{7,5},{8,10},{10,8},{12,... | collective-permute-start | bytes 589832 | tf_op jit(solution)/shard_map/ppermute | solution.py:124
  41.4 8.1 %copy-start.1 = (bf16[18,128,512]{2,1,0:T(8,128)(2,1)S(1)}, bf16[18,128,512]{2,1,0:T(8,128)(2,1)}, u32[]{:S(2)}) copy-start(bf16[18,128,512]{2,1,0:T(8,128)(2,1)} %param.17) | copy-start | bytes 7077892
  48.3 7.2 %collective-permute-start.17 = (f32[40960]{0:T(1024)S(1)}, f32[40960]{0:T(1024)S(1)}, u32[]{:S(2)}, u32[]{:S(2)}) collective-permute-start(f32[40960]{0:T(1024)S(1)} %pad_maximum_fusion.10), channel_id=1, source_target_pairs={{0,4},{2,6},{4,0},{6,2},{1,5},{3,7},{5,1},{7,3},{8,12},{10,14},{12... | collective-permute-start | bytes 491528 | tf_op jit(solution)/shard_map/ppermute | solution.py:124
  55.7 5.2 %collective-permute-start.18 = (f32[36864]{0:T(1024)S(1)}, f32[36864]{0:T(1024)S(1)}, u32[]{:S(2)}, u32[]{:S(2)}) collective-permute-start(f32[36864]{0:T(1024)S(1)} %pad_maximum_fusion.11), channel_id=1, source_target_pairs={{0,8},{8,0},{16,24},{24,16},{32,40},{40,32},{48,56},{56,48},{1,9},... | collective-permute-start | bytes 442376 | tf_op jit(solution)/shard_map/ppermute | solution.py:124
  58.8 17.5 %copy-start.12 = (bf16[18,512]{1,0:T(8,128)(2,1)}, bf16[18,512]{1,0:T(8,128)(2,1)S(1)}, u32[]{:S(2)}) copy-start(bf16[18,512]{1,0:T(8,128)(2,1)S(1)} %get-tuple-element.36) | copy-start | bytes 55300
  58.8 25.3 %copy-start.11 = (bf16[18,512]{1,0:T(8,128)(2,1)}, bf16[18,512]{1,0:T(8,128)(2,1)S(1)}, u32[]{:S(2)}) copy-start(bf16[18,512]{1,0:T(8,128)(2,1)S(1)} %get-tuple-element.37) | copy-start | bytes 55300
  61.2 6.1 %collective-permute-start.19 = (f32[34816]{0:T(1024)S(1)}, f32[34816]{0:T(1024)S(1)}, u32[]{:S(2)}, u32[]{:S(2)}) collective-permute-start(f32[34816]{0:T(1024)S(1)} %pad_maximum_fusion.12), channel_id=1, source_target_pairs={{0,16},{8,24},{16,0},{24,8},{32,48},{40,56},{48,32},{56,40},{1,17}... | collective-permute-start | bytes 417800 | tf_op jit(solution)/shard_map/ppermute | solution.py:124
  67.5 13.9 %collective-permute-start.20 = (f32[33792]{0:T(1024)S(1)}, f32[33792]{0:T(1024)S(1)}, u32[]{:S(2)}, u32[]{:S(2)}) collective-permute-start(f32[33792]{0:T(1024)S(1)} %pad_maximum_fusion.13), channel_id=1, source_target_pairs={{0,32},{8,40},{16,48},{24,56},{32,0},{40,8},{48,16},{56,24},{1,33}... | collective-permute-start | bytes 405512 | tf_op jit(solution)/shard_map/ppermute | solution.py:124
  84.1 8.1 %copy-start.5 = (pred[64,2323]{1,0:T(8,128)(4,1)S(1)}, pred[64,2323]{1,0:T(8,128)(4,1)}, u32[]{:S(2)}) copy-start(pred[64,2323]{1,0:T(8,128)(4,1)} %iota_compare_fusion) | copy-start | bytes 446020
  84.1 8.1 %copy-start.6 = (bf16[64,8,512]{2,1,0:T(8,128)(2,1)S(1)}, bf16[64,8,512]{2,1,0:T(8,128)(2,1)}, u32[]{:S(2)}) copy-start(bf16[64,8,512]{2,1,0:T(8,128)(2,1)} %broadcast_in_dim.193) | copy-start | bytes 1572868
  84.1 8.1 %copy-start.16 = (f32[2323]{0:T(1024)S(1)}, f32[2323]{0:T(1024)}, u32[]{:S(2)}) copy-start(f32[2323]{0:T(1024)} %constant.179.clone.1) | copy-start | bytes 27880
  97.9 3.9 %copy-start.3 = (bf16[2304,512]{0,1:T(8,128)(2,1)S(1)}, bf16[2304,512]{0,1:T(8,128)(2,1)}, u32[]{:S(2)}) copy-start(bf16[2304,512]{0,1:T(8,128)(2,1)} %copy.125) | copy-start | bytes 7077892
  97.9 3.9 %copy-start.7 = (bf16[18,512]{0,1:T(8,128)(2,1)S(1)}, bf16[18,512]{0,1:T(8,128)(2,1)}, u32[]{:S(2)}) copy-start(bf16[18,512]{0,1:T(8,128)(2,1)} %copy.126) | copy-start | bytes 55300
  111.5 3.2 %copy-start.2 = (bf16[18,128,512]{2,1,0:T(8,128)(2,1)S(1)}, bf16[18,128,512]{2,1,0:T(8,128)(2,1)}, u32[]{:S(2)}) copy-start(bf16[18,128,512]{2,1,0:T(8,128)(2,1)} %param.18) | copy-start | bytes 7077892
  111.5 5.2 %collective-permute-start.21 = (f32[64,8,66]{0,1,2:T(8,128)}, f32[64,8,66]{0,1,2:T(8,128)S(1)}, u32[]{:S(2)}, u32[]{:S(2)}) collective-permute-start(f32[64,8,66]{0,1,2:T(8,128)} %pad_maximum_fusion.2), channel_id=1, source_target_pairs={{0,1},{1,0},{2,3},{3,2},{4,5},{5,4},{6,7},{7,6},{8,9},{9,8},{10,11... | collective-permute-start | bytes 405512 | tf_op jit(solution)/shard_map/ppermute | solution.py:37
  114.4 73.9 %collective-permute-start.3 = (bf16[4,128,512]{2,1,0:T(8,128)(2,1)}, bf16[4,128,512]{2,1,0:T(8,128)(2,1)}, u32[]{:S(2)}, u32[]{:S(2)}) collective-permute-start(bf16[4,128,512]{2,1,0:T(8,128)(2,1)} %get-tuple-element.22), channel_id=1, source_target_pairs={{0,1},{1,2},{2,3},{3,4},{4,5},{5,6},{6,7},{7,8},{8,9},{9,10},{10,1... | collective-permute-start | bytes 1572872 | tf_op jit(solution)/shard_map/ppermute | solution.py:70
  117.5 3.2 %copy-start.15 = (bf16[1,4,2]{1,2,0:T(2,128)(2,1)S(1)}, bf16[1,4,2]{1,2,0:T(2,128)(2,1)}, u32[]{:S(2)}) copy-start(bf16[1,4,2]{1,2,0:T(2,128)(2,1)} %get-tuple-element.43) | copy-start | bytes 52
  117.5 3.3 %copy-start.9 = (bf16[4,128,512]{2,1,0:T(8,128)(2,1)S(1)}, bf16[4,128,512]{2,1,0:T(8,128)(2,1)}, u32[]{:S(2)}) copy-start(bf16[4,128,512]{2,1,0:T(8,128)(2,1)} %get-tuple-element.21) | copy-start | bytes 1572868
  117.5 4.2 %copy-start.8 = (bf16[4,128,512]{2,1,0:T(8,128)(2,1)S(1)}, bf16[4,128,512]{2,1,0:T(8,128)(2,1)}, u32[]{:S(2)}) copy-start(bf16[4,128,512]{2,1,0:T(8,128)(2,1)} %get-tuple-element.23) | copy-start | bytes 1572868
  117.5 9.6 %collective-permute-start.22 = (f32[64,8,66]{0,1,2:T(8,128)}, f32[64,8,66]{0,1,2:T(8,128)S(1)}, u32[]{:S(2)}, u32[]{:S(2)}) collective-permute-start(f32[64,8,66]{0,1,2:T(8,128)} %pad_maximum_fusion.3), channel_id=1, source_target_pairs={{0,2},{2,0},{4,6},{6,4},{1,3},{3,1},{5,7},{7,5},{8,10},{10,8},{12,... | collective-permute-start | bytes 405512 | tf_op jit(solution)/shard_map/ppermute | solution.py:37
  120.8 67.5 %collective-permute-start.4 = (bf16[4,128,512]{2,1,0:T(8,128)(2,1)S(1)}, bf16[4,128,512]{2,1,0:T(8,128)(2,1)S(1)}, u32[]{:S(2)}, u32[]{:S(2)}) collective-permute-start(bf16[4,128,512]{2,1,0:T(8,128)(2,1)S(1)} %copy-done.9), channel_id=1, source_target_pairs={{0,2},{1,3},{2,4},{3,5},{4,6},{5,7},{6,8},{7,9},{8,10},{9,11},{10,... | collective-permute-start | bytes 1572872 | tf_op jit(solution)/shard_map/ppermute | solution.py:70
  121.7 71.2 %collective-permute-start.5 = (bf16[4,128,512]{2,1,0:T(8,128)(2,1)S(1)}, bf16[4,128,512]{2,1,0:T(8,128)(2,1)}, u32[]{:S(2)}, u32[]{:S(2)}) collective-permute-start(bf16[4,128,512]{2,1,0:T(8,128)(2,1)S(1)} %copy-done.8), channel_id=1, source_target_pairs={{0,3},{1,4},{2,5},{3,6},{4,7},{5,8},{6,9},{7,10},{8,11},{9,12},{10... | collective-permute-start | bytes 1572872 | tf_op jit(solution)/shard_map/ppermute | solution.py:70
  123.3 106.7 %collective-permute-start.6 = (bf16[4,128,512]{2,1,0:T(8,128)(2,1)}, bf16[4,128,512]{2,1,0:T(8,128)(2,1)}, u32[]{:S(2)}, u32[]{:S(2)}) collective-permute-start(bf16[4,128,512]{2,1,0:T(8,128)(2,1)} %get-tuple-element.18), channel_id=1, source_target_pairs={{0,1},{1,2},{2,3},{3,4},{4,5},{5,6},{6,7},{7,8},{8,9},{9,10},{10,1... | collective-permute-start | bytes 1572872 | tf_op jit(solution)/shard_map/ppermute | solution.py:70
  127.2 8.3 %collective-permute-start.23 = (f32[64,8,66]{0,1,2:T(8,128)S(1)}, f32[64,8,66]{0,1,2:T(8,128)S(1)}, u32[]{:S(2)}, u32[]{:S(2)}) collective-permute-start(f32[64,8,66]{0,1,2:T(8,128)S(1)} %pad_maximum_fusion.4), channel_id=1, source_target_pairs={{0,4},{2,6},{4,0},{6,2},{1,5},{3,7},{5,1},{7,3},{8,12},{10,14},{12... | collective-permute-start | bytes 405512 | tf_op jit(solution)/shard_map/ppermute | solution.py:37
  136.3 19.7 %collective-permute-start.24 = (f32[64,8,66]{0,1,2:T(8,128)}, f32[64,8,66]{0,1,2:T(8,128)S(1)}, u32[]{:S(2)}, u32[]{:S(2)}) collective-permute-start(f32[64,8,66]{0,1,2:T(8,128)} %pad_maximum_fusion.5), channel_id=1, source_target_pairs={{0,8},{8,0},{16,24},{24,16},{32,40},{40,32},{48,56},{56,48},{1,9},... | collective-permute-start | bytes 405512 | tf_op jit(solution)/shard_map/ppermute | solution.py:37
  156.1 10.4 %collective-permute-start.25 = (f32[64,8,66]{0,1,2:T(8,128)S(1)}, f32[64,8,66]{0,1,2:T(8,128)S(1)}, u32[]{:S(2)}, u32[]{:S(2)}) collective-permute-start(f32[64,8,66]{0,1,2:T(8,128)S(1)} %pad_maximum_fusion.6), channel_id=1, source_target_pairs={{0,16},{8,24},{16,0},{24,8},{32,48},{40,56},{48,32},{56,40},{1,17}... | collective-permute-start | bytes 405512 | tf_op jit(solution)/shard_map/ppermute | solution.py:37
  166.5 63.5 %collective-permute-start.7 = (bf16[4,128,512]{2,1,0:T(8,128)(2,1)}, bf16[4,128,512]{2,1,0:T(8,128)(2,1)}, u32[]{:S(2)}, u32[]{:S(2)}) collective-permute-start(bf16[4,128,512]{2,1,0:T(8,128)(2,1)} %get-tuple-element.17), channel_id=1, source_target_pairs={{0,2},{1,3},{2,4},{3,5},{4,6},{5,7},{6,8},{7,9},{8,10},{9,11},{10,... | collective-permute-start | bytes 1572872 | tf_op jit(solution)/shard_map/ppermute | solution.py:70
  188.2 41.7 %collective-permute-start.8 = (bf16[4,128,512]{2,1,0:T(8,128)(2,1)}, bf16[4,128,512]{2,1,0:T(8,128)(2,1)}, u32[]{:S(2)}, u32[]{:S(2)}) collective-permute-start(bf16[4,128,512]{2,1,0:T(8,128)(2,1)} %get-tuple-element.19), channel_id=1, source_target_pairs={{0,3},{1,4},{2,5},{3,6},{4,7},{5,8},{6,9},{7,10},{8,11},{9,12},{10... | collective-permute-start | bytes 1572872 | tf_op jit(solution)/shard_map/ppermute | solution.py:70
  188.3 4.7 %copy-start.10 = (bf16[4,128,512]{2,1,0:T(8,128)(2,1)}, bf16[4,128,512]{2,1,0:T(8,128)(2,1)S(1)}, u32[]{:S(2)}) copy-start(bf16[4,128,512]{2,1,0:T(8,128)(2,1)S(1)} %collective-permute-done.4) | copy-start | bytes 1572868
  188.3 39.5 %collective-permute-start.26 = (f32[64,8,66]{0,1,2:T(8,128)S(1)}, f32[64,8,66]{0,1,2:T(8,128)S(1)}, u32[]{:S(2)}, u32[]{:S(2)}) collective-permute-start(f32[64,8,66]{0,1,2:T(8,128)S(1)} %pad_maximum_fusion.7), channel_id=1, source_target_pairs={{0,32},{8,40},{16,48},{24,56},{32,0},{40,8},{48,16},{56,24},{1,33}... | collective-permute-start | bytes 405512 | tf_op jit(solution)/shard_map/ppermute | solution.py:37
  228.4 10.3 %collective-permute-start.27 = (f32[64,32]{0,1:T(8,128)S(1)}, f32[64,32]{0,1:T(8,128)S(1)}, u32[]{:S(2)}, u32[]{:S(2)}) collective-permute-start(f32[64,32]{0,1:T(8,128)S(1)} %fusion.56), channel_id=1, source_target_pairs={{0,64},{64,0},{128,192},{192,128},{1,65},{65,1},{129,193},{193,129... | collective-permute-start | bytes 24584 | tf_op jit(solution)/shard_map/ppermute | solution.py:37
  234.9 6.7 %copy-start.4 = (bf16[16,128,512]{2,1,0:T(8,128)(2,1)S(1)}, bf16[16,128,512]{2,1,0:T(8,128)(2,1)}, u32[]{:S(2)}) copy-start(bf16[16,128,512]{2,1,0:T(8,128)(2,1)} %gather_fusion.3) | copy-start | bytes 6291460
  238.7 6.9 %collective-permute-start.28 = (f32[64,32]{0,1:T(8,128)S(1)}, f32[64,32]{0,1:T(8,128)S(1)}, u32[]{:S(2)}, u32[]{:S(2)}) collective-permute-start(f32[64,32]{0,1:T(8,128)S(1)} %add.251), channel_id=1, source_target_pairs={{0,128},{64,192},{128,0},{192,64},{1,129},{65,193},{129,1},{193,65... | collective-permute-start | bytes 24584 | tf_op jit(solution)/shard_map/ppermute | solution.py:37

commit v6 on v5

--- a/solution.py
+++ b/solution.py
@@ -209,45 +209,50 @@
     )
     packed_request = jnp.where(filled, recv_meta[picked, 1], -1)
 
-    row_keys = key_cache.reshape(-1, heads_here, HDIM)
-    row_values = value_cache.reshape(-1, heads_here, HDIM)
     row_req = jnp.repeat(jnp.where(is_kept, blk_req, -1), row_count)
-    all_keys = jnp.concatenate(
-        [row_keys, folded_keys.reshape(n_blocks, heads_here, HDIM), own_key], axis=0
-    )
-    all_values = jnp.concatenate(
-        [row_values, folded_values.reshape(n_blocks, heads_here, HDIM), own_value], axis=0
-    )
-    all_req = jnp.concatenate(
-        [row_req, jnp.where(is_kept, -1, blk_req), jnp.full((own_key.shape[0],), own_request)]
-    )
-    bias = jnp.concatenate(
+    extra_keys = jnp.concatenate([folded_keys, own_key.reshape(-1, feat_width)], axis=0)
+    extra_values = jnp.concatenate([folded_values, own_value.reshape(-1, feat_width)], axis=0)
+    extra_req = jnp.concatenate(
+        [jnp.where(is_kept, -1, blk_req), jnp.full((own_key.shape[0],), own_request)]
+    )
+    extra_bias = jnp.concatenate(
         [
-            jnp.zeros((row_req.shape[0],), jnp.float32),
             jnp.full((n_blocks,), math.log(ROWS), jnp.float32),
             jnp.zeros((own_key.shape[0],), jnp.float32),
         ]
     )
-    row_mask = all_req[None, :] == jnp.arange(requests, dtype=jnp.int32)[:, None]
+    request_ids = jnp.arange(requests, dtype=jnp.int32)[:, None]
+    row_mask = (row_req[None, :] == request_ids)[:, None, :]
+    extra_mask = (extra_req[None, :] == request_ids)[:, None, :]
     own_head = jnp.arange(heads_here)[:, None] == jnp.arange(heads_here)[None, :]
     spread_queries = jnp.where(
         own_head[None, :, :, None], queries[:, :, None, :], jnp.zeros((), jnp.bfloat16)
     ).reshape(requests * heads_here, feat_width)
-    flat_keys = all_keys.reshape(-1, feat_width)
-    flat_values = all_values.reshape(-1, feat_width)
-    scores = lax.dot_general(
-        spread_queries, flat_keys, (((1,), (1,)), ((), ())), preferred_element_type=jnp.float32
-    ).reshape(requests, heads_here, -1)
-    scores = scores * 0.125 + bias[None, None, :]
-    scores = jnp.where(row_mask[:, None, :], scores, MASKED_SCORE)
-    local_top = jnp.max(scores, axis=2)
-    expo = jnp.where(row_mask[:, None, :], jnp.exp(scores - local_top[..., None]), 0.0)
-    local_sum = jnp.sum(expo, axis=2)
-    weighted = jnp.dot(
-        expo.astype(jnp.bfloat16).reshape(requests * heads_here, -1),
-        flat_values,
-        preferred_element_type=jnp.float32,
-    ).reshape(requests, heads_here, heads_here, HDIM)
+
+    def scores_of(keys, mask, bias):
+        raw = lax.dot_general(
+            spread_queries, keys, (((1,), (1,)), ((), ())), preferred_element_type=jnp.float32
+        ).reshape(requests, heads_here, -1)
+        return jnp.where(mask, raw * 0.125 + bias, MASKED_SCORE)
+
+    row_scores = scores_of(key_cache.reshape(-1, feat_width), row_mask, 0.0)
+    extra_scores = scores_of(extra_keys, extra_mask, extra_bias[None, None, :])
+    local_top = jnp.maximum(jnp.max(row_scores, axis=2), jnp.max(extra_scores, axis=2))
+    row_expo = jnp.where(row_mask, jnp.exp(row_scores - local_top[..., None]), 0.0)
+    extra_expo = jnp.where(extra_mask, jnp.exp(extra_scores - local_top[..., None]), 0.0)
+    local_sum = jnp.sum(row_expo, axis=2) + jnp.sum(extra_expo, axis=2)
+
+    def weighted_of(expo, values):
+        return jnp.dot(
+            expo.astype(jnp.bfloat16).reshape(requests * heads_here, -1),
+            values,
+            preferred_element_type=jnp.float32,
+        )
+
+    weighted = weighted_of(row_expo, value_cache.reshape(-1, feat_width)) + weighted_of(
+        extra_expo, extra_values
+    )
+    weighted = weighted.reshape(requests, heads_here, heads_here, HDIM)
     local_acc = jnp.sum(jnp.where(own_head[None, :, :, None], weighted, 0.0), axis=2)
     stats = jnp.concatenate(
         [local_acc, local_sum[..., None], local_top[..., None]], axis=-1

time: 251 us -> 259 us (1.032)
  the two profiles are of different devices: /device:TPU:6 before, /device:TPU:1 now
where the time goes in v6:
time: 259 us; the launch traced here: 258 us
  waiting for transfers between devices  104 us (40%)
  starting transfers between devices  63.5 us (25%)
  local copies, waits for them, and re-layouts  36.6 us (14%)
  other arithmetic  34.5 us (13%)
  matrix products  17.2 us (7%)
    ppermute x14, waiting for transfers between devices, butterfly(): x = merge(x, lax.ppermute(x, axis, pairs))  65.5 us
    ppermute x14, starting transfers between devices, butterfly(): x = merge(x, lax.ppermute(x, axis, pairs))  38.5 us
    ppermute x9, waiting for transfers between devices, passed_along(): lax.ppermute(array, SEQ_PARTS, [(i, (i + by) % count) for i in range(coun...  29.3 us
    ppermute x6, starting transfers between devices, shards(): payload = lax.ppermute(payload, axis, pairs)  17.9 us
    ppermute x6, waiting for transfers between devices, shards(): payload = lax.ppermute(payload, axis, pairs)  9.33 us
    ppermute x9, starting transfers between devices, passed_along(): lax.ppermute(array, SEQ_PARTS, [(i, (i + by) % count) for i in range(coun...  7.12 us
    slice x4, local copies, waits for them, and re-layouts, shards(): arrived = [(send_keys[0], send_values[0], meta_data[0])]  6.26 us
    dot_general x2, matrix products, scores_of(): lax.dot_general(spread_queries, keys, (((1,), (1,)), ((), ())), preferred...  5.31 us
  transfers between devices with their start and end apart: 29, of which 14 were waited for; matrix products, arithmetic and copies ran while one was open for 33% of the time, Pallas kernels for 0%

profile of v6, /device:TPU:1, one launch (start us, length us, event | category | flops | bytes accessed | tf_op | source)
XLA Modules:
  0.0 257.6 jit_solution(6427018855032219439)
XLA Ops:
  1.5 3.3 %collective-permute-start.9 = (f32[64]{0:T(128)S(1)}, f32[64]{0:T(128)S(1)}, u32[]{:S(2)}, u32[]{:S(2)}) collective-permute-start(f32[64]{0:T(128)S(1)} %fusion.39), channel_id=1, source_target_pairs={{0,1},{1,0},{2,3},{3,2},{4,5},{5,4},{6,7},{7,6},{8,9},{9,8},{10,11... | collective-permute-start | bytes 776 | tf_op jit(solution)/shard_map/ppermute | solution.py:37
  11.6 2.0 collective-permute-start.2
  14.8 1.4 collective-permute-done.10
  16.3 2.2 collective-permute-start.11
  18.5 1.7 collective-permute-done.11
  20.2 1.6 collective-permute-start.12
  22.7 3.7 %collective-permute-start.13 = (f32[64]{0:T(128)S(1)}, f32[64]{0:T(128)S(1)}, u32[]{:S(2)}, u32[]{:S(2)}) collective-permute-start(f32[64]{0:T(128)S(1)} %add.228), channel_id=1, source_target_pairs={{0,16},{8,24},{16,0},{24,8},{32,48},{40,56},{48,32},{56,40},{1,17}... | collective-permute-start | bytes 776 | tf_op jit(solution)/shard_map/ppermute | solution.py:37
  27.3 5.4 %collective-permute-start.14 = (f32[64]{0:T(128)S(1)}, f32[64]{0:T(128)S(1)}, u32[]{:S(2)}, u32[]{:S(2)}) collective-permute-start(f32[64]{0:T(128)S(1)} %add.229), channel_id=1, source_target_pairs={{0,32},{8,40},{16,48},{24,56},{32,0},{40,8},{48,16},{56,24},{1,33}... | collective-permute-start | bytes 776 | tf_op jit(solution)/shard_map/ppermute | solution.py:37
  35.2 4.5 %collective-permute-start.15 = (f32[65536]{0:T(1024)S(1)}, f32[65536]{0:T(1024)S(1)}, u32[]{:S(2)}, u32[]{:S(2)}) collective-permute-start(f32[65536]{0:T(1024)S(1)} %pad_maximum_fusion.8), channel_id=1, source_target_pairs={{0,1},{1,0},{2,3},{3,2},{4,5},{5,4},{6,7},{7,6},{8,9},{9,8},{10,11... | collective-permute-start | bytes 786440 | tf_op jit(solution)/shard_map/ppermute | solution.py:124
  39.7 3.3 %fusion.52 = f32[18,1,512]{2,1,0:T(1,128)} fusion(bf16[18,128,512]{2,1,0:T(8,128)(2,1)} %param.18, f32[18,128,1]{1,0,2:T(8,128)S(1)} %bitcast.177), kind=kOutput, calls=%fused_computation.151 | convolution fusion | flops 14155776 | bytes 2405376 | tf_op jit(solution)/shard_map/bi,bif->bf/dot_general | solution.py:153
  43.2 1.8 collective-permute-start.16
  45.0 2.3 fusion.54
  47.4 2.9 %collective-permute-done.16 = f32[49152]{0:T(1024)S(1)} collective-permute-done((f32[49152]{0:T(1024)S(1)}, f32[49152]{0:T(1024)S(1)}, u32[]{:S(2)}, u32[]{:S(2)}) %collective-permute-start.16) | collective-permute-done | bytes 196640 | tf_op jit(solution)/shard_map/ppermute | solution.py:124
  51.1 1.4 pad_maximum_fusion.10
  52.5 2.8 %collective-permute-start.17 = (f32[40960]{0:T(1024)}, f32[40960]{0:T(1024)S(1)}, u32[]{:S(2)}, u32[]{:S(2)}) collective-permute-start(f32[40960]{0:T(1024)} %pad_maximum_fusion.10), channel_id=1, source_target_pairs={{0,4},{2,6},{4,0},{6,2},{1,5},{3,7},{5,1},{7,3},{8,12},{10,14},{12... | collective-permute-start | bytes 491528 | tf_op jit(solution)/shard_map/ppermute | solution.py:124
  55.3 1.5 fusion.31
  61.1 1.8 collective-permute-start.18
  65.7 2.7 %collective-permute-start.19 = (f32[34816]{0:T(1024)S(1)}, f32[34816]{0:T(1024)S(1)}, u32[]{:S(2)}, u32[]{:S(2)}) collective-permute-start(f32[34816]{0:T(1024)S(1)} %pad_maximum_fusion.12), channel_id=1, source_target_pairs={{0,16},{8,24},{16,0},{24,8},{32,48},{40,56},{48,32},{56,40},{1,17}... | collective-permute-start | bytes 417800 | tf_op jit(solution)/shard_map/ppermute | solution.py:124
  69.0 3.8 %collective-permute-done.19 = f32[34816]{0:T(1024)S(1)} collective-permute-done((f32[34816]{0:T(1024)S(1)}, f32[34816]{0:T(1024)S(1)}, u32[]{:S(2)}, u32[]{:S(2)}) %collective-permute-start.19) | collective-permute-done | bytes 139296 | tf_op jit(solution)/shard_map/ppermute | solution.py:124
  73.0 4.2 %collective-permute-start.20 = (f32[33792]{0:T(1024)S(1)}, f32[33792]{0:T(1024)S(1)}, u32[]{:S(2)}, u32[]{:S(2)}) collective-permute-start(f32[33792]{0:T(1024)S(1)} %pad_maximum_fusion.13), channel_id=1, source_target_pairs={{0,32},{8,40},{16,48},{24,56},{32,0},{40,8},{48,16},{56,24},{1,33}... | collective-permute-start | bytes 405512 | tf_op jit(solution)/shard_map/ppermute | solution.py:124
  77.2 2.1 gather_fusion.2
  84.5 1.4 broadcast_in_dim.215
  85.9 2.6 select_n.320
  88.5 5.0 %fusion.68 = (f32[64,8]{1,0:T(8,128)S(1)}, f32[64,8,2304]{2,1,0:T(8,128)}) fusion(bf16[64,8,512]{2,1,0:T(8,128)(2,1)} %select_n.320, bf16[2304,512,1]{1,0,2:T(8,128)(2,1)S(1)} %bitcast.158, pred[64,2304]{1,0:T(8,128)(4,1)S(1)} %iota_compare_fusion), kind=kOutput, calls=%fused_computation.197 | convolution fusion | flops 1211497984 | bytes 7751680 | tf_op jit(solution)/shard_map/dot_general | solution.py:233
  94.0 3.8 %fusion.1 = f32[64,8]{1,0:T(8,128)S(1)} fusion(f32[64,8,2304]{2,1,0:T(8,128)} %get-tuple-element.52, f32[64,8]{1,0:T(8,128)S(1)} %max.32, pred[64,2304]{1,0:T(8,128)(4,1)} %copy-done.4), kind=kLoop, calls=%fused_computation.10 | loop fusion | flops 3538432 | bytes 4870144 | tf_op jit(solution)/shard_map/reduce_sum | solution.py:243
  97.8 3.8 %fusion.4 = f32[512,512]{1,0:T(8,128)S(1)} fusion(bf16[2304,512]{1,0:T(8,128)(2,1)S(1)} %bitcast.159, f32[64,8,2304]{2,1,0:T(8,128)} %get-tuple-element.52, f32[64,8]{1,0:T(8,128)S(1)} %max.32, pred[64,2304]{1,0:T(8,128)(4,1)S(1)} %copy-done.5), kind=kOutput, calls=%fused_computation.13 | convolution fusion | flops 1211498496 | bytes 8275968 | tf_op jit(solution)/shard_map/dot_general | solution.py:246
  103.2 1.7 reshape.525
  104.9 2.3 select_reduce_fusion
  107.6 4.5 %collective-permute-start.21 = (f32[64,8,66]{0,1,2:T(8,128)S(1)}, f32[64,8,66]{0,1,2:T(8,128)S(1)}, u32[]{:S(2)}, u32[]{:S(2)}) collective-permute-start(f32[64,8,66]{0,1,2:T(8,128)S(1)} %pad_maximum_fusion.2), channel_id=1, source_target_pairs={{0,1},{1,0},{2,3},{3,2},{4,5},{5,4},{6,7},{7,6},{8,9},{9,8},{10,11... | collective-permute-start | bytes 405512 | tf_op jit(solution)/shard_map/ppermute | solution.py:37
  112.0 2.9 %slice_bitcast_fusion.1 = (bf16[1,4,128,512]{3,2,1,0:T(8,128)(2,1)}, bf16[4,128,512]{2,1,0:T(8,128)(2,1)}, bf16[4,128,512]{2,1,0:T(8,128)(2,1)}, bf16[4,128,512]{2,1,0:T(8,128)(2,1)}) fusion(bf16[16,128,512]{2,1,0:T(8,128)(2,1)} %gather_fusion.2), kind=kLoop, calls=%fused_computation.29 | loop fusion | bytes 4194304 | tf_op jit(solution)/shard_map/slice | solution.py:190
  115.9 3.8 %gather_fusion.4 = bf16[16,128,512]{2,1,0:T(8,128)(2,1)} fusion(bf16[18,128,512]{2,1,0:T(8,128)(2,1)} %param.18, s32[1024]{0:T(1024)} %copy-done.14), kind=kCustom, calls=%fused_computation.4 | custom fusion | bytes 4194368 | tf_op jit(solution)/shard_map/gather | solution.py:184
  121.7 2.7 %slice_bitcast_fusion = (bf16[1,4,128,512]{3,2,1,0:T(8,128)(2,1)S(1)}, bf16[4,128,512]{2,1,0:T(8,128)(2,1)}, bf16[4,128,512]{2,1,0:T(8,128)(2,1)}, bf16[4,128,512]{2,1,0:T(8,128)(2,1)}) fusion(bf16[16,128,512]{2,1,0:T(8,128)(2,1)} %gather_fusion.4), kind=kLoop, calls=%fused_computation.28 | loop fusion | bytes 4194304 | tf_op jit(solution)/shard_map/slice | solution.py:190
  125.6 2.6 %collective-permute-start.5 = (bf16[4,128,512]{2,1,0:T(8,128)(2,1)}, bf16[4,128,512]{2,1,0:T(8,128)(2,1)}, u32[]{:S(2)}, u32[]{:S(2)}) collective-permute-start(bf16[4,128,512]{2,1,0:T(8,128)(2,1)} %get-tuple-element.23), channel_id=1, source_target_pairs={{0,3},{1,4},{2,5},{3,6},{4,7},{5,8},{6,9},{7,10},{8,11},{9,12},{10... | collective-permute-start | bytes 1572872 | tf_op jit(solution)/shard_map/ppermute | solution.py:70
  130.0 2.8 %collective-permute-start.23 = (f32[64,8,66]{0,1,2:T(8,128)S(1)}, f32[64,8,66]{0,1,2:T(8,128)S(1)}, u32[]{:S(2)}, u32[]{:S(2)}) collective-permute-start(f32[64,8,66]{0,1,2:T(8,128)S(1)} %pad_maximum_fusion.4), channel_id=1, source_target_pairs={{0,4},{2,6},{4,0},{6,2},{1,5},{3,7},{5,1},{7,3},{8,12},{10,14},{12... | collective-permute-start | bytes 405512 | tf_op jit(solution)/shard_map/ppermute | solution.py:37
  132.9 37.2 %collective-permute-done.23 = f32[64,8,66]{0,1,2:T(8,128)S(1)} collective-permute-done((f32[64,8,66]{0,1,2:T(8,128)S(1)}, f32[64,8,66]{0,1,2:T(8,128)S(1)}, u32[]{:S(2)}, u32[]{:S(2)}) %collective-permute-start.23) | collective-permute-done | bytes 135200 | tf_op jit(solution)/shard_map/ppermute | solution.py:37
  172.9 6.1 %collective-permute-done.24 = f32[64,8,66]{0,1,2:T(8,128)S(1)} collective-permute-done((f32[64,8,66]{0,1,2:T(8,128)}, f32[64,8,66]{0,1,2:T(8,128)S(1)}, u32[]{:S(2)}, u32[]{:S(2)}) %collective-permute-start.24) | collective-permute-done | bytes 135200 | tf_op jit(solution)/shard_map/ppermute | solution.py:37
  179.0 2.0 collective-permute-start.25
  181.5 12.3 %collective-permute-done.25 = f32[64,8,66]{0,1,2:T(8,128)S(1)} collective-permute-done((f32[64,8,66]{0,1,2:T(8,128)S(1)}, f32[64,8,66]{0,1,2:T(8,128)S(1)}, u32[]{:S(2)}, u32[]{:S(2)}) %collective-permute-start.25) | collective-permute-done | bytes 135200 | tf_op jit(solution)/shard_map/ppermute | solution.py:37
  194.0 5.3 %collective-permute-start.26 = (f32[64,8,66]{0,1,2:T(8,128)S(1)}, f32[64,8,66]{0,1,2:T(8,128)S(1)}, u32[]{:S(2)}, u32[]{:S(2)}) collective-permute-start(f32[64,8,66]{0,1,2:T(8,128)S(1)} %pad_maximum_fusion.7), channel_id=1, source_target_pairs={{0,32},{8,40},{16,48},{24,56},{32,0},{40,8},{48,16},{56,24},{1,33}... | collective-permute-start | bytes 405512 | tf_op jit(solution)/shard_map/ppermute | solution.py:37
  199.4 2.9 %pad_maximum_fusion = bf16[4,4,128,512]{3,2,1,0:T(8,128)(2,1)} fusion(bf16[1,4,128,512]{3,2,1,0:T(8,128)(2,1)} %bitcast.13, bf16[1,4,128,512]{3,2,1,0:T(8,128)(2,1)} %bitcast.12, bf16[1,4,128,512]{3,2,1,0:T(8,128)(2,1)} %bitcast.11, bf16[1,4,128,512]{3,2,1,0:T(8,128)(2,1)S(1)} %copy-done.2), kind=kLoop, calls=%fused_computation.17 | loop fusion | flops 3145728 | bytes 4194304 | tf_op jit(solution)/shard_map/stack | solution.py:195
  202.3 5.8 %collective-permute-done.26 = f32[64,8,66]{0,1,2:T(8,128)S(1)} collective-permute-done((f32[64,8,66]{0,1,2:T(8,128)S(1)}, f32[64,8,66]{0,1,2:T(8,128)S(1)}, u32[]{:S(2)}, u32[]{:S(2)}) %collective-permute-start.26) | collective-permute-done | bytes 135200 | tf_op jit(solution)/shard_map/ppermute | solution.py:37
  210.0 5.3 %collective-permute-done.7 = bf16[4,128,512]{2,1,0:T(8,128)(2,1)} collective-permute-done((bf16[4,128,512]{2,1,0:T(8,128)(2,1)}, bf16[4,128,512]{2,1,0:T(8,128)(2,1)}, u32[]{:S(2)}, u32[]{:S(2)}) %collective-permute-start.7) | collective-permute-done | bytes 524320 | tf_op jit(solution)/shard_map/ppermute | solution.py:70
  215.4 23.9 %collective-permute-done.8 = bf16[4,128,512]{2,1,0:T(8,128)(2,1)} collective-permute-done((bf16[4,128,512]{2,1,0:T(8,128)(2,1)}, bf16[4,128,512]{2,1,0:T(8,128)(2,1)}, u32[]{:S(2)}, u32[]{:S(2)}) %collective-permute-start.8) | collective-permute-done | bytes 524320 | tf_op jit(solution)/shard_map/ppermute | solution.py:70
  239.3 2.9 %pad_maximum_fusion.1 = bf16[4,4,128,512]{3,2,1,0:T(8,128)(2,1)} fusion(bf16[1,4,128,512]{3,2,1,0:T(8,128)(2,1)} %bitcast.20, bf16[1,4,128,512]{3,2,1,0:T(8,128)(2,1)} %bitcast.19, bf16[1,4,128,512]{3,2,1,0:T(8,128)(2,1)} %bitcast.18, bf16[1,4,128,512]{3,2,1,0:T(8,128)(2,1)S(1)} %get-tuple-element.16), kind=kLoop, calls=%fused_computation.18 | loop fusion | flops 3145728 | bytes 4194304 | tf_op jit(solution)/shard_map/stack | solution.py:196
  242.3 3.6 %gather_fusion.3 = bf16[16,128,512]{2,1,0:T(8,128)(2,1)} fusion(bf16[16,128,512]{2,1,0:T(8,128)(2,1)} %bitcast.160, s32[1024]{0:T(1024)S(1)} %pad_clamp_fusion), kind=kCustom, calls=%fused_computation.3 | custom fusion | bytes 4194368 | tf_op jit(solution)/shard_map/gather | solution.py:206
  245.9 3.6 %gather_fusion.5 = bf16[16,128,512]{2,1,0:T(8,128)(2,1)} fusion(bf16[16,128,512]{2,1,0:T(8,128)(2,1)} %bitcast.161, s32[1024]{0:T(1024)S(1)} %pad_clamp_fusion), kind=kCustom, calls=%fused_computation.5 | custom fusion | bytes 4194368 | tf_op jit(solution)/shard_map/gather | solution.py:208
  249.5 3.0 %collective-permute-start.28 = (f32[64,32]{0,1:T(8,128)S(1)}, f32[64,32]{0,1:T(8,128)S(1)}, u32[]{:S(2)}, u32[]{:S(2)}) collective-permute-start(f32[64,32]{0,1:T(8,128)S(1)} %add.270), channel_id=1, source_target_pairs={{0,128},{64,192},{128,0},{192,64},{1,129},{65,193},{129,1},{193,65... | collective-permute-start | bytes 24584 | tf_op jit(solution)/shard_map/ppermute | solution.py:37
  252.4 4.6 %broadcast_select_fusion = (bf16[16,128,512]{2,1,0:T(8,128)(2,1)}, bf16[16,128,512]{2,1,0:T(8,128)(2,1)}) fusion(bf16[16,128,512]{2,1,0:T(8,128)(2,1)} %gather_fusion.5, pred[16]{0:T(512)(128)(4,1)S(1)} %fusion.45, bf16[16,128,512]{2,1,0:T(8,128)(2,1)} %gather_fusion.3), kind=kLoop, calls=%fused_computation.20 | loop fusion | flops 2097152 | bytes 8388624 | tf_op jit(solution)/shard_map/jit(_where)/select_n | solution.py:207
  (234 shorter events, 40.9 us)
Async XLA Ops:
  0.6 44.4 %copy-start = (bf16[18,128,512]{2,1,0:T(8,128)(2,1)S(1)}, bf16[18,128,512]{2,1,0:T(8,128)(2,1)}, u32[]{:S(2)}) copy-start(bf16[18,128,512]{2,1,0:T(8,128)(2,1)} %param.17) | copy-start | bytes 7077892
  1.5 12.2 %collective-permute-start.9 = (f32[64]{0:T(128)S(1)}, f32[64]{0:T(128)S(1)}, u32[]{:S(2)}, u32[]{:S(2)}) collective-permute-start(f32[64]{0:T(128)S(1)} %fusion.39), channel_id=1, source_target_pairs={{0,1},{1,0},{2,3},{3,2},{4,5},{5,4},{6,7},{7,6},{8,9},{9,8},{10,11... | collective-permute-start | bytes 776 | tf_op jit(solution)/shard_map/ppermute | solution.py:37
  5.5 28.6 %copy-start.18 = (pred[18]{0:T(512)(128)(4,1)}, pred[18]{0:T(512)(128)(4,1)S(1)}, u32[]{:S(2)}) copy-start(pred[18]{0:T(512)(128)(4,1)S(1)} %broadcast_compare_fusion) | copy-start | bytes 58
  8.9 25.2 %copy-start.14 = (s32[1024]{0:T(1024)}, s32[1024]{0:T(1024)S(1)}, u32[]{:S(2)}) copy-start(s32[1024]{0:T(1024)S(1)} %pad_clamp_fusion.1) | copy-start | bytes 12292
  11.0 113.4 %collective-permute-start = (bf16[4,2]{0,1:T(2,128)(2,1)}, bf16[4,2]{0,1:T(2,128)(2,1)}, u32[]{:S(2)}, u32[]{:S(2)}) collective-permute-start(bf16[4,2]{0,1:T(2,128)(2,1)} %get-tuple-element.46), channel_id=1, source_target_pairs={{0,1},{1,2},{2,3},{3,4},{4,5},{5,6},{6,7},{7,8},{8,9},{9,10},{10,1... | collective-permute-start | bytes 56 | tf_op jit(solution)/shard_map/ppermute | solution.py:70
  11.0 114.6 %collective-permute-start.1 = (bf16[4,2]{0,1:T(2,128)(2,1)}, bf16[4,2]{0,1:T(2,128)(2,1)}, u32[]{:S(2)}, u32[]{:S(2)}) collective-permute-start(bf16[4,2]{0,1:T(2,128)(2,1)} %get-tuple-element.45), channel_id=1, source_target_pairs={{0,2},{1,3},{2,4},{3,5},{4,6},{5,7},{6,8},{7,9},{8,10},{9,11},{10,... | collective-permute-start | bytes 56 | tf_op jit(solution)/shard_map/ppermute | solution.py:70
  11.6 117.3 %collective-permute-start.2 = (bf16[4,2]{0,1:T(2,128)(2,1)}, bf16[4,2]{0,1:T(2,128)(2,1)}, u32[]{:S(2)}, u32[]{:S(2)}) collective-permute-start(bf16[4,2]{0,1:T(2,128)(2,1)} %get-tuple-element.44), channel_id=1, source_target_pairs={{0,3},{1,4},{2,5},{3,6},{4,7},{5,8},{6,9},{7,10},{8,11},{9,12},{10... | collective-permute-start | bytes 56 | tf_op jit(solution)/shard_map/ppermute | solution.py:70
  13.7 74.7 %copy-start.4 = (pred[64,2304]{1,0:T(8,128)(4,1)}, pred[64,2304]{1,0:T(8,128)(4,1)S(1)}, u32[]{:S(2)}) copy-start(pred[64,2304]{1,0:T(8,128)(4,1)S(1)} %iota_compare_fusion) | copy-start | bytes 442372
  13.8 2.5 collective-permute-start.10
  16.3 3.9 %collective-permute-start.11 = (f32[64]{0:T(128)S(1)}, f32[64]{0:T(128)S(1)}, u32[]{:S(2)}, u32[]{:S(2)}) collective-permute-start(f32[64]{0:T(128)S(1)} %add.226), channel_id=1, source_target_pairs={{0,4},{2,6},{4,0},{6,2},{1,5},{3,7},{5,1},{7,3},{8,12},{10,14},{12... | collective-permute-start | bytes 776 | tf_op jit(solution)/shard_map/ppermute | solution.py:37
  20.2 2.6 collective-permute-start.12
  22.7 4.6 %collective-permute-start.13 = (f32[64]{0:T(128)S(1)}, f32[64]{0:T(128)S(1)}, u32[]{:S(2)}, u32[]{:S(2)}) collective-permute-start(f32[64]{0:T(128)S(1)} %add.228), channel_id=1, source_target_pairs={{0,16},{8,24},{16,0},{24,8},{32,48},{40,56},{48,32},{56,40},{1,17}... | collective-permute-start | bytes 776 | tf_op jit(solution)/shard_map/ppermute | solution.py:37
  27.3 6.7 %collective-permute-start.14 = (f32[64]{0:T(128)S(1)}, f32[64]{0:T(128)S(1)}, u32[]{:S(2)}, u32[]{:S(2)}) collective-permute-start(f32[64]{0:T(128)S(1)} %add.229), channel_id=1, source_target_pairs={{0,32},{8,40},{16,48},{24,56},{32,0},{40,8},{48,16},{56,24},{1,33}... | collective-permute-start | bytes 776 | tf_op jit(solution)/shard_map/ppermute | solution.py:37
  34.1 5.6 %copy-start.9 = (f32[18,128]{1,0:T(8,128)S(1)}, f32[18,128]{1,0:T(8,128)}, u32[]{:S(2)}) copy-start(f32[18,128]{1,0:T(8,128)} %param.19) | copy-start | bytes 27652
  35.2 7.8 %collective-permute-start.15 = (f32[65536]{0:T(1024)S(1)}, f32[65536]{0:T(1024)S(1)}, u32[]{:S(2)}, u32[]{:S(2)}) collective-permute-start(f32[65536]{0:T(1024)S(1)} %pad_maximum_fusion.8), channel_id=1, source_target_pairs={{0,1},{1,0},{2,3},{3,2},{4,5},{5,4},{6,7},{7,6},{8,9},{9,8},{10,11... | collective-permute-start | bytes 786440 | tf_op jit(solution)/shard_map/ppermute | solution.py:124
  43.2 7.0 %collective-permute-start.16 = (f32[49152]{0:T(1024)S(1)}, f32[49152]{0:T(1024)S(1)}, u32[]{:S(2)}, u32[]{:S(2)}) collective-permute-start(f32[49152]{0:T(1024)S(1)} %pad_maximum_fusion.9), channel_id=1, source_target_pairs={{0,2},{2,0},{4,6},{6,4},{1,3},{3,1},{5,7},{7,5},{8,10},{10,8},{12,... | collective-permute-start | bytes 589832 | tf_op jit(solution)/shard_map/ppermute | solution.py:124
  52.5 6.8 %collective-permute-start.17 = (f32[40960]{0:T(1024)}, f32[40960]{0:T(1024)S(1)}, u32[]{:S(2)}, u32[]{:S(2)}) collective-permute-start(f32[40960]{0:T(1024)} %pad_maximum_fusion.10), channel_id=1, source_target_pairs={{0,4},{2,6},{4,0},{6,2},{1,5},{3,7},{5,1},{7,3},{8,12},{10,14},{12... | collective-permute-start | bytes 491528 | tf_op jit(solution)/shard_map/ppermute | solution.py:124
  61.1 4.4 %collective-permute-start.18 = (f32[36864]{0:T(1024)S(1)}, f32[36864]{0:T(1024)S(1)}, u32[]{:S(2)}, u32[]{:S(2)}) collective-permute-start(f32[36864]{0:T(1024)S(1)} %pad_maximum_fusion.11), channel_id=1, source_target_pairs={{0,8},{8,0},{16,24},{24,16},{32,40},{40,32},{48,56},{56,48},{1,9},... | collective-permute-start | bytes 442376 | tf_op jit(solution)/shard_map/ppermute | solution.py:124
  65.7 7.1 %collective-permute-start.19 = (f32[34816]{0:T(1024)S(1)}, f32[34816]{0:T(1024)S(1)}, u32[]{:S(2)}, u32[]{:S(2)}) collective-permute-start(f32[34816]{0:T(1024)S(1)} %pad_maximum_fusion.12), channel_id=1, source_target_pairs={{0,16},{8,24},{16,0},{24,8},{32,48},{40,56},{48,32},{56,40},{1,17}... | collective-permute-start | bytes 417800 | tf_op jit(solution)/shard_map/ppermute | solution.py:124
  73.0 8.1 %collective-permute-start.20 = (f32[33792]{0:T(1024)S(1)}, f32[33792]{0:T(1024)S(1)}, u32[]{:S(2)}, u32[]{:S(2)}) collective-permute-start(f32[33792]{0:T(1024)S(1)} %pad_maximum_fusion.13), channel_id=1, source_target_pairs={{0,32},{8,40},{16,48},{24,56},{32,0},{40,8},{48,16},{56,24},{1,33}... | collective-permute-start | bytes 405512 | tf_op jit(solution)/shard_map/ppermute | solution.py:124
  77.2 5.8 %copy-start.15 = (pred[8,8]{1,0:T(8,128)(4,1)}, pred[8,8]{1,0:T(8,128)(4,1)S(1)}, u32[]{:S(2)}) copy-start(pred[8,8]{1,0:T(8,128)(4,1)S(1)} %iota_compare_fusion.5) | copy-start | bytes 196
  88.5 5.0 %copy-start.6 = (bf16[64,8,512]{2,1,0:T(8,128)(2,1)S(1)}, bf16[64,8,512]{2,1,0:T(8,128)(2,1)}, u32[]{:S(2)}) copy-start(bf16[64,8,512]{2,1,0:T(8,128)(2,1)} %broadcast_in_dim.215) | copy-start | bytes 1572868
  88.5 5.0 %copy-start.10 = (pred[64,19]{1,0:T(8,128)(4,1)S(1)}, pred[64,19]{1,0:T(8,128)(4,1)}, u32[]{:S(2)}) copy-start(pred[64,19]{1,0:T(8,128)(4,1)} %iota_compare_fusion.1) | copy-start | bytes 3652
  88.5 5.0 %copy-start.13 = (bf16[18,512]{1,0:T(8,128)(2,1)S(1)}, bf16[18,512]{1,0:T(8,128)(2,1)}, u32[]{:S(2)}) copy-start(bf16[18,512]{1,0:T(8,128)(2,1)} %get-tuple-element.37) | copy-start | bytes 55300
  88.5 5.0 %copy-start.19 = (pred[8,512]{1,0:T(8,128)(4,1)S(1)}, pred[8,512]{1,0:T(8,128)(4,1)}, u32[]{:S(2)}) copy-start(pred[8,512]{1,0:T(8,128)(4,1)} %broadcast_in_dim.213) | copy-start | bytes 12292
  88.5 5.0 %copy-start.20 = (bf16[1,512]{1,0:T(2,128)(2,1)S(1)}, bf16[1,512]{1,0:T(2,128)(2,1)}, u32[]{:S(2)}) copy-start(bf16[1,512]{1,0:T(2,128)(2,1)} %convert_element_type.83) | copy-start | bytes 3076
  88.5 5.0 %copy-start.22 = (f32[19]{0:T(128)S(1)}, f32[19]{0:T(128)}, u32[]{:S(2)}) copy-start(f32[19]{0:T(128)} %constant.182.clone.1) | copy-start | bytes 232
  93.9 7.7 %copy-start.3 = (f32[64,8,19]{2,1,0:T(8,128)}, f32[64,8,19]{2,1,0:T(8,128)S(1)}, u32[]{:S(2)}) copy-start(f32[64,8,19]{2,1,0:T(8,128)S(1)} %get-tuple-element.54) | copy-start | bytes 116740
  97.7 4.1 %copy-start.8 = (bf16[18,512]{1,0:T(8,128)(2,1)S(1)}, bf16[18,512]{1,0:T(8,128)(2,1)}, u32[]{:S(2)}) copy-start(bf16[18,512]{1,0:T(8,128)(2,1)} %get-tuple-element.36) | copy-start | bytes 55300
  97.7 4.1 %copy-start.11 = (pred[64,19]{1,0:T(8,128)(4,1)S(1)}, pred[64,19]{1,0:T(8,128)(4,1)}, u32[]{:S(2)}) copy-start(pred[64,19]{1,0:T(8,128)(4,1)} %iota_compare_fusion.1) | copy-start | bytes 3652
  97.8 4.1 %copy-start.17 = (bf16[1,512]{1,0:T(2,128)(2,1)S(1)}, bf16[1,512]{1,0:T(2,128)(2,1)}, u32[]{:S(2)}) copy-start(bf16[1,512]{1,0:T(2,128)(2,1)} %slice.527) | copy-start | bytes 3076
  107.6 12.1 %collective-permute-start.21 = (f32[64,8,66]{0,1,2:T(8,128)S(1)}, f32[64,8,66]{0,1,2:T(8,128)S(1)}, u32[]{:S(2)}, u32[]{:S(2)}) collective-permute-start(f32[64,8,66]{0,1,2:T(8,128)S(1)} %pad_maximum_fusion.2), channel_id=1, source_target_pairs={{0,1},{1,0},{2,3},{3,2},{4,5},{5,4},{6,7},{7,6},{8,9},{9,8},{10,11... | collective-permute-start | bytes 405512 | tf_op jit(solution)/shard_map/ppermute | solution.py:37
  114.9 79.0 %collective-permute-start.3 = (bf16[4,128,512]{2,1,0:T(8,128)(2,1)}, bf16[4,128,512]{2,1,0:T(8,128)(2,1)}, u32[]{:S(2)}, u32[]{:S(2)}) collective-permute-start(bf16[4,128,512]{2,1,0:T(8,128)(2,1)} %get-tuple-element.22), channel_id=1, source_target_pairs={{0,1},{1,2},{2,3},{3,4},{4,5},{5,6},{6,7},{7,8},{8,9},{9,10},{10,1... | collective-permute-start | bytes 1572872 | tf_op jit(solution)/shard_map/ppermute | solution.py:70
  120.5 3.9 %copy-start.21 = (bf16[1,4,2]{1,2,0:T(2,128)(2,1)S(1)}, bf16[1,4,2]{1,2,0:T(2,128)(2,1)}, u32[]{:S(2)}) copy-start(bf16[1,4,2]{1,2,0:T(2,128)(2,1)} %get-tuple-element.43) | copy-start | bytes 52
  120.5 9.4 %collective-permute-start.22 = (f32[64,8,66]{0,1,2:T(8,128)}, f32[64,8,66]{0,1,2:T(8,128)S(1)}, u32[]{:S(2)}, u32[]{:S(2)}) collective-permute-start(f32[64,8,66]{0,1,2:T(8,128)} %pad_maximum_fusion.3), channel_id=1, source_target_pairs={{0,2},{2,0},{4,6},{6,4},{1,3},{3,1},{5,7},{7,5},{8,10},{10,8},{12,... | collective-permute-start | bytes 405512 | tf_op jit(solution)/shard_map/ppermute | solution.py:37
  124.4 69.6 %collective-permute-start.4 = (bf16[4,128,512]{2,1,0:T(8,128)(2,1)}, bf16[4,128,512]{2,1,0:T(8,128)(2,1)}, u32[]{:S(2)}, u32[]{:S(2)}) collective-permute-start(bf16[4,128,512]{2,1,0:T(8,128)(2,1)} %get-tuple-element.21), channel_id=1, source_target_pairs={{0,2},{1,3},{2,4},{3,5},{4,6},{5,7},{6,8},{7,9},{8,10},{9,11},{10,... | collective-permute-start | bytes 1572872 | tf_op jit(solution)/shard_map/ppermute | solution.py:70
  125.6 73.8 %collective-permute-start.5 = (bf16[4,128,512]{2,1,0:T(8,128)(2,1)}, bf16[4,128,512]{2,1,0:T(8,128)(2,1)}, u32[]{:S(2)}, u32[]{:S(2)}) collective-permute-start(bf16[4,128,512]{2,1,0:T(8,128)(2,1)} %get-tuple-element.23), channel_id=1, source_target_pairs={{0,3},{1,4},{2,5},{3,6},{4,7},{5,8},{6,9},{7,10},{8,11},{9,12},{10... | collective-permute-start | bytes 1572872 | tf_op jit(solution)/shard_map/ppermute | solution.py:70
  128.8 81.2 %collective-permute-start.6 = (bf16[4,128,512]{2,1,0:T(8,128)(2,1)}, bf16[4,128,512]{2,1,0:T(8,128)(2,1)}, u32[]{:S(2)}, u32[]{:S(2)}) collective-permute-start(bf16[4,128,512]{2,1,0:T(8,128)(2,1)} %get-tuple-element.18), channel_id=1, source_target_pairs={{0,1},{1,2},{2,3},{3,4},{4,5},{5,6},{6,7},{7,8},{8,9},{9,10},{10,1... | collective-permute-start | bytes 1572872 | tf_op jit(solution)/shard_map/ppermute | solution.py:70
  130.0 40.1 %collective-permute-start.23 = (f32[64,8,66]{0,1,2:T(8,128)S(1)}, f32[64,8,66]{0,1,2:T(8,128)S(1)}, u32[]{:S(2)}, u32[]{:S(2)}) collective-permute-start(f32[64,8,66]{0,1,2:T(8,128)S(1)} %pad_maximum_fusion.4), channel_id=1, source_target_pairs={{0,4},{2,6},{4,0},{6,2},{1,5},{3,7},{5,1},{7,3},{8,12},{10,14},{12... | collective-permute-start | bytes 405512 | tf_op jit(solution)/shard_map/ppermute | solution.py:37
  170.9 8.1 %collective-permute-start.24 = (f32[64,8,66]{0,1,2:T(8,128)}, f32[64,8,66]{0,1,2:T(8,128)S(1)}, u32[]{:S(2)}, u32[]{:S(2)}) collective-permute-start(f32[64,8,66]{0,1,2:T(8,128)} %pad_maximum_fusion.5), channel_id=1, source_target_pairs={{0,8},{8,0},{16,24},{24,16},{32,40},{40,32},{48,56},{56,48},{1,9},... | collective-permute-start | bytes 405512 | tf_op jit(solution)/shard_map/ppermute | solution.py:37
  172.8 26.6 %copy-start.2 = (bf16[1,4,128,512]{3,2,1,0:T(8,128)(2,1)S(1)}, bf16[1,4,128,512]{3,2,1,0:T(8,128)(2,1)}, u32[]{:S(2)}) copy-start(bf16[1,4,128,512]{3,2,1,0:T(8,128)(2,1)} %get-tuple-element.20) | copy-start | bytes 1572868
  179.0 14.8 %collective-permute-start.25 = (f32[64,8,66]{0,1,2:T(8,128)S(1)}, f32[64,8,66]{0,1,2:T(8,128)S(1)}, u32[]{:S(2)}, u32[]{:S(2)}) collective-permute-start(f32[64,8,66]{0,1,2:T(8,128)S(1)} %pad_maximum_fusion.6), channel_id=1, source_target_pairs={{0,16},{8,24},{16,0},{24,8},{32,48},{40,56},{48,32},{56,40},{1,17}... | collective-permute-start | bytes 405512 | tf_op jit(solution)/shard_map/ppermute | solution.py:37
  193.8 21.6 %collective-permute-start.7 = (bf16[4,128,512]{2,1,0:T(8,128)(2,1)}, bf16[4,128,512]{2,1,0:T(8,128)(2,1)}, u32[]{:S(2)}, u32[]{:S(2)}) collective-permute-start(bf16[4,128,512]{2,1,0:T(8,128)(2,1)} %get-tuple-element.17), channel_id=1, source_target_pairs={{0,2},{1,3},{2,4},{3,5},{4,6},{5,7},{6,8},{7,9},{8,10},{9,11},{10,... | collective-permute-start | bytes 1572872 | tf_op jit(solution)/shard_map/ppermute | solution.py:70
  193.9 45.4 %collective-permute-start.8 = (bf16[4,128,512]{2,1,0:T(8,128)(2,1)}, bf16[4,128,512]{2,1,0:T(8,128)(2,1)}, u32[]{:S(2)}, u32[]{:S(2)}) collective-permute-start(bf16[4,128,512]{2,1,0:T(8,128)(2,1)} %get-tuple-element.19), channel_id=1, source_target_pairs={{0,3},{1,4},{2,5},{3,6},{4,7},{5,8},{6,9},{7,10},{8,11},{9,12},{10... | collective-permute-start | bytes 1572872 | tf_op jit(solution)/shard_map/ppermute | solution.py:70
  194.0 14.1 %collective-permute-start.26 = (f32[64,8,66]{0,1,2:T(8,128)S(1)}, f32[64,8,66]{0,1,2:T(8,128)S(1)}, u32[]{:S(2)}, u32[]{:S(2)}) collective-permute-start(f32[64,8,66]{0,1,2:T(8,128)S(1)} %pad_maximum_fusion.7), channel_id=1, source_target_pairs={{0,32},{8,40},{16,48},{24,56},{32,0},{40,8},{48,16},{56,24},{1,33}... | collective-permute-start | bytes 405512 | tf_op jit(solution)/shard_map/ppermute | solution.py:37
  199.3 9.2 %copy-start.12 = (bf16[512,32]{0,1:T(8,128)(2,1)S(1)}, bf16[512,32]{0,1:T(8,128)(2,1)}, u32[]{:S(2)}) copy-start(bf16[512,32]{0,1:T(8,128)(2,1)} %param.12) | copy-start | bytes 98308
  208.7 40.8 %collective-permute-start.27 = (f32[64,32]{0,1:T(8,128)S(1)}, f32[64,32]{0,1:T(8,128)S(1)}, u32[]{:S(2)}, u32[]{:S(2)}) collective-permute-start(f32[64,32]{0,1:T(8,128)S(1)} %fusion.70), channel_id=1, source_target_pairs={{0,64},{64,0},{128,192},{192,128},{1,65},{65,1},{129,193},{193,129... | collective-permute-start | bytes 24584 | tf_op jit(solution)/shard_map/ppermute | solution.py:37
  249.5 7.5 %collective-permute-start.28 = (f32[64,32]{0,1:T(8,128)S(1)}, f32[64,32]{0,1:T(8,128)S(1)}, u32[]{:S(2)}, u32[]{:S(2)}) collective-permute-start(f32[64,32]{0,1:T(8,128)S(1)} %add.270), channel_id=1, source_target_pairs={{0,128},{64,192},{128,0},{192,64},{1,129},{65,193},{129,1},{193,65... | collective-permute-start | bytes 24584 | tf_op jit(solution)/shard_map/ppermute | solution.py:37
  (4 other events, 10.0 us)

commit v7 on v6

--- a/solution.py
+++ b/solution.py
@@ -257,7 +257,7 @@
     stats = jnp.concatenate(
         [local_acc, local_sum[..., None], local_top[..., None]], axis=-1
     )
-    stats = butterfly(stats, softmax_merge, reversed(SEQ_PARTS))
+    stats = butterfly(stats, softmax_merge, ["z", "core", "x"])
     mixture = stats[..., :HDIM]
     totals = stats[..., HDIM]
     mixed = (mixture / totals[..., None]).astype(jnp.bfloat16)

time: 259 us -> 239 us (0.923)
  the two profiles are of different devices: /device:TPU:1 before, /device:TPU:97 now
where the time goes in v7:
time: 239 us; the launch traced here: 238 us
  waiting for transfers between devices  97.7 us (41%)
  starting transfers between devices  50.4 us (21%)
  local copies, waits for them, and re-layouts  36.6 us (15%)
  other arithmetic  34.5 us (14%)
  matrix products  17.2 us (7%)
    ppermute x14, waiting for transfers between devices, butterfly(): x = merge(x, lax.ppermute(x, axis, pairs))  53.8 us
    ppermute x9, waiting for transfers between devices, passed_along(): lax.ppermute(array, SEQ_PARTS, [(i, (i + by) % count) for i in range(coun...  27.1 us
    ppermute x9, starting transfers between devices, passed_along(): lax.ppermute(array, SEQ_PARTS, [(i, (i + by) % count) for i in range(coun...  20.9 us
    ppermute x14, starting transfers between devices, butterfly(): x = merge(x, lax.ppermute(x, axis, pairs))  17.7 us
    ppermute x6, waiting for transfers between devices, shards(): payload = lax.ppermute(payload, axis, pairs)  16.7 us
    ppermute x6, starting transfers between devices, shards(): payload = lax.ppermute(payload, axis, pairs)  11.9 us
    slice x4, local copies, waits for them, and re-layouts, shards(): arrived = [(send_keys[0], send_values[0], meta_data[0])]  6.26 us
    dot_general x2, matrix products, scores_of(): lax.dot_general(spread_queries, keys, (((1,), (1,)), ((), ())), preferred...  5.31 us
  transfers between devices with their start and end apart: 29, of which 17 were waited for; matrix products, arithmetic and copies ran while one was open for 36% of the time, Pallas kernels for 0%

profile of v7, /device:TPU:97, one launch (start us, length us, event | category | flops | bytes accessed | tf_op | source)
XLA Modules:
  0.0 238.0 jit_solution(15706017346866228267)
XLA Ops:
  10.7 2.0 collective-permute-start.2
  12.9 2.2 collective-permute-start.10
  16.1 2.7 %collective-permute-start.11 = (f32[64]{0:T(128)S(1)}, f32[64]{0:T(128)S(1)}, u32[]{:S(2)}, u32[]{:S(2)}) collective-permute-start(f32[64]{0:T(128)S(1)} %add.226), channel_id=1, source_target_pairs={{0,4},{2,6},{4,0},{6,2},{1,5},{3,7},{5,1},{7,3},{8,12},{10,14},{12... | collective-permute-start | bytes 776 | tf_op jit(solution)/shard_map/ppermute | solution.py:37
  20.0 2.4 %collective-permute-done.12 = f32[64]{0:T(128)S(1)} collective-permute-done((f32[64]{0:T(128)S(1)}, f32[64]{0:T(128)S(1)}, u32[]{:S(2)}, u32[]{:S(2)}) %collective-permute-start.12) | collective-permute-done | bytes 288 | tf_op jit(solution)/shard_map/ppermute | solution.py:37
  23.3 2.4 %collective-permute-done.13 = f32[64]{0:T(128)S(1)} collective-permute-done((f32[64]{0:T(128)S(1)}, f32[64]{0:T(128)S(1)}, u32[]{:S(2)}, u32[]{:S(2)}) %collective-permute-start.13) | collective-permute-done | bytes 288 | tf_op jit(solution)/shard_map/ppermute | solution.py:37
  25.7 3.5 %collective-permute-start.14 = (f32[64]{0:T(128)S(1)}, f32[64]{0:T(128)S(1)}, u32[]{:S(2)}, u32[]{:S(2)}) collective-permute-start(f32[64]{0:T(128)S(1)} %add.229), channel_id=1, source_target_pairs={{0,32},{8,40},{16,48},{24,56},{32,0},{40,8},{48,16},{56,24},{1,33}... | collective-permute-start | bytes 776 | tf_op jit(solution)/shard_map/ppermute | solution.py:37
  29.2 1.3 reduce_sum.91
  30.6 1.4 collective-permute-done.14
  33.1 5.5 %collective-permute-start.15 = (f32[65536]{0:T(1024)S(1)}, f32[65536]{0:T(1024)S(1)}, u32[]{:S(2)}, u32[]{:S(2)}) collective-permute-start(f32[65536]{0:T(1024)S(1)} %pad_maximum_fusion.8), channel_id=1, source_target_pairs={{0,1},{1,0},{2,3},{3,2},{4,5},{5,4},{6,7},{7,6},{8,9},{9,8},{10,11... | collective-permute-start | bytes 786440 | tf_op jit(solution)/shard_map/ppermute | solution.py:124
  38.6 3.3 %fusion.52 = f32[18,1,512]{2,1,0:T(1,128)} fusion(bf16[18,128,512]{2,1,0:T(8,128)(2,1)} %param.18, f32[18,128,1]{1,0,2:T(8,128)S(1)} %bitcast.177), kind=kOutput, calls=%fused_computation.151 | convolution fusion | flops 14155776 | bytes 2405376 | tf_op jit(solution)/shard_map/bi,bif->bf/dot_general | solution.py:153
  42.2 1.8 collective-permute-start.16
  44.0 2.3 fusion.54
  46.3 2.9 %collective-permute-done.16 = f32[49152]{0:T(1024)S(1)} collective-permute-done((f32[49152]{0:T(1024)S(1)}, f32[49152]{0:T(1024)S(1)}, u32[]{:S(2)}, u32[]{:S(2)}) %collective-permute-start.16) | collective-permute-done | bytes 196640 | tf_op jit(solution)/shard_map/ppermute | solution.py:124
  50.0 1.4 pad_maximum_fusion.10
  51.4 2.8 %collective-permute-start.17 = (f32[40960]{0:T(1024)}, f32[40960]{0:T(1024)S(1)}, u32[]{:S(2)}, u32[]{:S(2)}) collective-permute-start(f32[40960]{0:T(1024)} %pad_maximum_fusion.10), channel_id=1, source_target_pairs={{0,4},{2,6},{4,0},{6,2},{1,5},{3,7},{5,1},{7,3},{8,12},{10,14},{12... | collective-permute-start | bytes 491528 | tf_op jit(solution)/shard_map/ppermute | solution.py:124
  54.2 1.5 fusion.31
  61.8 2.3 collective-permute-done.18
  65.0 6.9 %collective-permute-done.19 = f32[34816]{0:T(1024)S(1)} collective-permute-done((f32[34816]{0:T(1024)S(1)}, f32[34816]{0:T(1024)S(1)}, u32[]{:S(2)}, u32[]{:S(2)}) %collective-permute-start.19) | collective-permute-done | bytes 139296 | tf_op jit(solution)/shard_map/ppermute | solution.py:124
  72.1 1.6 collective-permute-start.20
  73.7 2.1 gather_fusion.2
  76.6 3.8 %collective-permute-done.20 = f32[33792]{0:T(1024)S(1)} collective-permute-done((f32[33792]{0:T(1024)S(1)}, f32[33792]{0:T(1024)S(1)}, u32[]{:S(2)}, u32[]{:S(2)}) %collective-permute-start.20) | collective-permute-done | bytes 135200 | tf_op jit(solution)/shard_map/ppermute | solution.py:124
  83.8 1.4 broadcast_in_dim.215
  85.2 2.6 %select_n.320 = bf16[64,8,512]{2,1,0:T(8,128)(2,1)} reshape(bf16[64,8,8,64]{3,2,1,0:T(8,128)(2,1)} %broadcast_select_fusion.2) | data formatting | bytes 1048576 | tf_op jit(solution)/shard_map/jit(_where)/select_n | solution.py:228
  87.8 5.0 %fusion.68 = (f32[64,8]{1,0:T(8,128)S(1)}, f32[64,8,2304]{2,1,0:T(8,128)}) fusion(bf16[64,8,512]{2,1,0:T(8,128)(2,1)} %select_n.320, bf16[2304,512,1]{1,0,2:T(8,128)(2,1)S(1)} %bitcast.158, pred[64,2304]{1,0:T(8,128)(4,1)S(1)} %iota_compare_fusion), kind=kOutput, calls=%fused_computation.197 | convolution fusion | flops 1211497984 | bytes 7751680 | tf_op jit(solution)/shard_map/dot_general | solution.py:233
  93.3 3.8 %fusion.1 = f32[64,8]{1,0:T(8,128)S(1)} fusion(f32[64,8,2304]{2,1,0:T(8,128)} %get-tuple-element.52, f32[64,8]{1,0:T(8,128)S(1)} %max.32, pred[64,2304]{1,0:T(8,128)(4,1)} %copy-done.4), kind=kLoop, calls=%fused_computation.10 | loop fusion | flops 3538432 | bytes 4870144 | tf_op jit(solution)/shard_map/reduce_sum | solution.py:243
  97.1 3.8 %fusion.4 = f32[512,512]{1,0:T(8,128)S(1)} fusion(bf16[2304,512]{1,0:T(8,128)(2,1)S(1)} %bitcast.159, f32[64,8,2304]{2,1,0:T(8,128)} %get-tuple-element.52, f32[64,8]{1,0:T(8,128)S(1)} %max.32, pred[64,2304]{1,0:T(8,128)(4,1)S(1)} %copy-done.5), kind=kOutput, calls=%fused_computation.13 | convolution fusion | flops 1211498496 | bytes 8275968 | tf_op jit(solution)/shard_map/dot_general | solution.py:246
  102.5 1.7 reshape.525
  104.3 2.3 select_reduce_fusion
  107.0 2.9 %slice_bitcast_fusion.1 = (bf16[1,4,128,512]{3,2,1,0:T(8,128)(2,1)}, bf16[4,128,512]{2,1,0:T(8,128)(2,1)}, bf16[4,128,512]{2,1,0:T(8,128)(2,1)}, bf16[4,128,512]{2,1,0:T(8,128)(2,1)}) fusion(bf16[16,128,512]{2,1,0:T(8,128)(2,1)} %gather_fusion.2), kind=kLoop, calls=%fused_computation.29 | loop fusion | bytes 4194304 | tf_op jit(solution)/shard_map/slice | solution.py:190
  109.9 5.5 %collective-permute-start.3 = (bf16[4,128,512]{2,1,0:T(8,128)(2,1)}, bf16[4,128,512]{2,1,0:T(8,128)(2,1)}, u32[]{:S(2)}, u32[]{:S(2)}) collective-permute-start(bf16[4,128,512]{2,1,0:T(8,128)(2,1)} %get-tuple-element.22), channel_id=1, source_target_pairs={{0,1},{1,2},{2,3},{3,4},{4,5},{5,6},{6,7},{7,8},{8,9},{9,10},{10,1... | collective-permute-start | bytes 1572872 | tf_op jit(solution)/shard_map/ppermute | solution.py:70
  115.4 3.8 %gather_fusion.4 = bf16[16,128,512]{2,1,0:T(8,128)(2,1)} fusion(bf16[18,128,512]{2,1,0:T(8,128)(2,1)} %param.18, s32[1024]{0:T(1024)} %copy-done.14), kind=kCustom, calls=%fused_computation.4 | custom fusion | bytes 4194368 | tf_op jit(solution)/shard_map/gather | solution.py:184
  120.0 2.7 %slice_bitcast_fusion = (bf16[1,4,128,512]{3,2,1,0:T(8,128)(2,1)S(1)}, bf16[4,128,512]{2,1,0:T(8,128)(2,1)}, bf16[4,128,512]{2,1,0:T(8,128)(2,1)}, bf16[4,128,512]{2,1,0:T(8,128)(2,1)}) fusion(bf16[16,128,512]{2,1,0:T(8,128)(2,1)} %gather_fusion.4), kind=kLoop, calls=%fused_computation.28 | loop fusion | bytes 4194304 | tf_op jit(solution)/shard_map/slice | solution.py:190
  124.2 2.0 collective-permute-start.5
  126.9 2.7 %collective-permute-start.6 = (bf16[4,128,512]{2,1,0:T(8,128)(2,1)}, bf16[4,128,512]{2,1,0:T(8,128)(2,1)}, u32[]{:S(2)}, u32[]{:S(2)}) collective-permute-start(bf16[4,128,512]{2,1,0:T(8,128)(2,1)} %get-tuple-element.18), channel_id=1, source_target_pairs={{0,1},{1,2},{2,3},{3,4},{4,5},{5,6},{6,7},{7,8},{8,9},{9,10},{10,1... | collective-permute-start | bytes 1572872 | tf_op jit(solution)/shard_map/ppermute | solution.py:70
  130.3 4.6 %collective-permute-done.22 = f32[64,8,66]{0,1,2:T(8,128)S(1)} collective-permute-done((f32[64,8,66]{0,1,2:T(8,128)}, f32[64,8,66]{0,1,2:T(8,128)S(1)}, u32[]{:S(2)}, u32[]{:S(2)}) %collective-permute-start.22) | collective-permute-done | bytes 135200 | tf_op jit(solution)/shard_map/ppermute | solution.py:37
  135.0 2.2 collective-permute-start.23
  137.4 15.0 %collective-permute-done.23 = f32[64,8,66]{0,1,2:T(8,128)S(1)} collective-permute-done((f32[64,8,66]{0,1,2:T(8,128)S(1)}, f32[64,8,66]{0,1,2:T(8,128)S(1)}, u32[]{:S(2)}, u32[]{:S(2)}) %collective-permute-start.23) | collective-permute-done | bytes 135200 | tf_op jit(solution)/shard_map/ppermute | solution.py:37
  156.3 6.6 %collective-permute-done.25 = f32[64,8,66]{0,1,2:T(8,128)S(1)} collective-permute-done((f32[64,8,66]{0,1,2:T(8,128)S(1)}, f32[64,8,66]{0,1,2:T(8,128)S(1)}, u32[]{:S(2)}, u32[]{:S(2)}) %collective-permute-start.25) | collective-permute-done | bytes 135200 | tf_op jit(solution)/shard_map/ppermute | solution.py:37
  163.5 4.9 %collective-permute-start.8 = (bf16[4,128,512]{2,1,0:T(8,128)(2,1)}, bf16[4,128,512]{2,1,0:T(8,128)(2,1)}, u32[]{:S(2)}, u32[]{:S(2)}) collective-permute-start(bf16[4,128,512]{2,1,0:T(8,128)(2,1)} %get-tuple-element.19), channel_id=1, source_target_pairs={{0,3},{1,4},{2,5},{3,6},{4,7},{5,8},{6,9},{7,10},{8,11},{9,12},{10... | collective-permute-start | bytes 1572872 | tf_op jit(solution)/shard_map/ppermute | solution.py:70
  169.0 2.9 %pad_maximum_fusion = bf16[4,4,128,512]{3,2,1,0:T(8,128)(2,1)} fusion(bf16[1,4,128,512]{3,2,1,0:T(8,128)(2,1)} %bitcast.13, bf16[1,4,128,512]{3,2,1,0:T(8,128)(2,1)} %bitcast.12, bf16[1,4,128,512]{3,2,1,0:T(8,128)(2,1)} %bitcast.11, bf16[1,4,128,512]{3,2,1,0:T(8,128)(2,1)S(1)} %copy-done.2), kind=kLoop, calls=%fused_computation.17 | loop fusion | flops 3145728 | bytes 4194304 | tf_op jit(solution)/shard_map/stack | solution.py:195
  172.0 18.7 %collective-permute-done.26 = f32[64,8,66]{0,1,2:T(8,128)S(1)} collective-permute-done((f32[64,8,66]{0,1,2:T(8,128)S(1)}, f32[64,8,66]{0,1,2:T(8,128)S(1)}, u32[]{:S(2)}, u32[]{:S(2)}) %collective-permute-start.26) | collective-permute-done | bytes 135200 | tf_op jit(solution)/shard_map/ppermute | solution.py:37
  192.6 15.0 %collective-permute-done.7 = bf16[4,128,512]{2,1,0:T(8,128)(2,1)} collective-permute-done((bf16[4,128,512]{2,1,0:T(8,128)(2,1)}, bf16[4,128,512]{2,1,0:T(8,128)(2,1)}, u32[]{:S(2)}, u32[]{:S(2)}) %collective-permute-start.7) | collective-permute-done | bytes 524320 | tf_op jit(solution)/shard_map/ppermute | solution.py:70
  207.6 12.1 %collective-permute-done.8 = bf16[4,128,512]{2,1,0:T(8,128)(2,1)} collective-permute-done((bf16[4,128,512]{2,1,0:T(8,128)(2,1)}, bf16[4,128,512]{2,1,0:T(8,128)(2,1)}, u32[]{:S(2)}, u32[]{:S(2)}) %collective-permute-start.8) | collective-permute-done | bytes 524320 | tf_op jit(solution)/shard_map/ppermute | solution.py:70
  219.7 2.9 %pad_maximum_fusion.1 = bf16[4,4,128,512]{3,2,1,0:T(8,128)(2,1)} fusion(bf16[1,4,128,512]{3,2,1,0:T(8,128)(2,1)} %bitcast.20, bf16[1,4,128,512]{3,2,1,0:T(8,128)(2,1)} %bitcast.19, bf16[1,4,128,512]{3,2,1,0:T(8,128)(2,1)} %bitcast.18, bf16[1,4,128,512]{3,2,1,0:T(8,128)(2,1)S(1)} %get-tuple-element.16), kind=kLoop, calls=%fused_computation.18 | loop fusion | flops 3145728 | bytes 4194304 | tf_op jit(solution)/shard_map/stack | solution.py:196
  222.6 3.6 %gather_fusion.3 = bf16[16,128,512]{2,1,0:T(8,128)(2,1)} fusion(bf16[16,128,512]{2,1,0:T(8,128)(2,1)} %bitcast.160, s32[1024]{0:T(1024)S(1)} %pad_clamp_fusion), kind=kCustom, calls=%fused_computation.3 | custom fusion | bytes 4194368 | tf_op jit(solution)/shard_map/gather | solution.py:206
  226.2 3.6 %gather_fusion.5 = bf16[16,128,512]{2,1,0:T(8,128)(2,1)} fusion(bf16[16,128,512]{2,1,0:T(8,128)(2,1)} %bitcast.161, s32[1024]{0:T(1024)S(1)} %pad_clamp_fusion), kind=kCustom, calls=%fused_computation.5 | custom fusion | bytes 4194368 | tf_op jit(solution)/shard_map/gather | solution.py:208
  229.8 3.0 %collective-permute-start.28 = (f32[64,32]{0,1:T(8,128)S(1)}, f32[64,32]{0,1:T(8,128)S(1)}, u32[]{:S(2)}, u32[]{:S(2)}) collective-permute-start(f32[64,32]{0,1:T(8,128)S(1)} %add.270), channel_id=1, source_target_pairs={{0,128},{64,192},{128,0},{192,64},{1,129},{65,193},{129,1},{193,65... | collective-permute-start | bytes 24584 | tf_op jit(solution)/shard_map/ppermute | solution.py:37
  232.8 4.6 %broadcast_select_fusion = (bf16[16,128,512]{2,1,0:T(8,128)(2,1)}, bf16[16,128,512]{2,1,0:T(8,128)(2,1)}) fusion(bf16[16,128,512]{2,1,0:T(8,128)(2,1)} %gather_fusion.5, pred[16]{0:T(512)(128)(4,1)S(1)} %fusion.45, bf16[16,128,512]{2,1,0:T(8,128)(2,1)} %gather_fusion.3), kind=kLoop, calls=%fused_computation.20 | loop fusion | flops 2097152 | bytes 8388624 | tf_op jit(solution)/shard_map/jit(_where)/select_n | solution.py:207
  (234 shorter events, 40.0 us)
Async XLA Ops:
  0.6 43.3 %copy-start = (bf16[18,128,512]{2,1,0:T(8,128)(2,1)S(1)}, bf16[18,128,512]{2,1,0:T(8,128)(2,1)}, u32[]{:S(2)}) copy-start(bf16[18,128,512]{2,1,0:T(8,128)(2,1)} %param.17) | copy-start | bytes 7077892
  1.5 11.4 %collective-permute-start.9 = (f32[64]{0:T(128)S(1)}, f32[64]{0:T(128)S(1)}, u32[]{:S(2)}, u32[]{:S(2)}) collective-permute-start(f32[64]{0:T(128)S(1)} %fusion.39), channel_id=1, source_target_pairs={{0,1},{1,0},{2,3},{3,2},{4,5},{5,4},{6,7},{7,6},{8,9},{9,8},{10,11... | collective-permute-start | bytes 776 | tf_op jit(solution)/shard_map/ppermute | solution.py:37
  2.9 29.1 %copy-start.18 = (pred[18]{0:T(512)(128)(4,1)}, pred[18]{0:T(512)(128)(4,1)S(1)}, u32[]{:S(2)}) copy-start(pred[18]{0:T(512)(128)(4,1)S(1)} %broadcast_compare_fusion) | copy-start | bytes 58
  6.4 25.7 %copy-start.14 = (s32[1024]{0:T(1024)}, s32[1024]{0:T(1024)S(1)}, u32[]{:S(2)}) copy-start(s32[1024]{0:T(1024)S(1)} %pad_clamp_fusion.1) | copy-start | bytes 12292
  8.4 114.3 %collective-permute-start = (bf16[4,2]{0,1:T(2,128)(2,1)}, bf16[4,2]{0,1:T(2,128)(2,1)}, u32[]{:S(2)}, u32[]{:S(2)}) collective-permute-start(bf16[4,2]{0,1:T(2,128)(2,1)} %get-tuple-element.46), channel_id=1, source_target_pairs={{0,1},{1,2},{2,3},{3,4},{4,5},{5,6},{6,7},{7,8},{8,9},{9,10},{10,1... | collective-permute-start | bytes 56 | tf_op jit(solution)/shard_map/ppermute | solution.py:70
  9.5 114.7 %collective-permute-start.1 = (bf16[4,2]{0,1:T(2,128)(2,1)}, bf16[4,2]{0,1:T(2,128)(2,1)}, u32[]{:S(2)}, u32[]{:S(2)}) collective-permute-start(bf16[4,2]{0,1:T(2,128)(2,1)} %get-tuple-element.45), channel_id=1, source_target_pairs={{0,2},{1,3},{2,4},{3,5},{4,6},{5,7},{6,8},{7,9},{8,10},{9,11},{10,... | collective-permute-start | bytes 56 | tf_op jit(solution)/shard_map/ppermute | solution.py:70
  10.7 116.2 %collective-permute-start.2 = (bf16[4,2]{0,1:T(2,128)(2,1)}, bf16[4,2]{0,1:T(2,128)(2,1)}, u32[]{:S(2)}, u32[]{:S(2)}) collective-permute-start(bf16[4,2]{0,1:T(2,128)(2,1)} %get-tuple-element.44), channel_id=1, source_target_pairs={{0,3},{1,4},{2,5},{3,6},{4,7},{5,8},{6,9},{7,10},{8,11},{9,12},{10... | collective-permute-start | bytes 56 | tf_op jit(solution)/shard_map/ppermute | solution.py:70
  12.9 74.9 %copy-start.4 = (pred[64,2304]{1,0:T(8,128)(4,1)}, pred[64,2304]{1,0:T(8,128)(4,1)S(1)}, u32[]{:S(2)}) copy-start(pred[64,2304]{1,0:T(8,128)(4,1)S(1)} %iota_compare_fusion) | copy-start | bytes 442372
  12.9 3.2 %collective-permute-start.10 = (f32[64]{0:T(128)S(1)}, f32[64]{0:T(128)S(1)}, u32[]{:S(2)}, u32[]{:S(2)}) collective-permute-start(f32[64]{0:T(128)S(1)} %add.225), channel_id=1, source_target_pairs={{0,2},{2,0},{4,6},{6,4},{1,3},{3,1},{5,7},{7,5},{8,10},{10,8},{12,... | collective-permute-start | bytes 776 | tf_op jit(solution)/shard_map/ppermute | solution.py:37
  16.1 3.9 %collective-permute-start.11 = (f32[64]{0:T(128)S(1)}, f32[64]{0:T(128)S(1)}, u32[]{:S(2)}, u32[]{:S(2)}) collective-permute-start(f32[64]{0:T(128)S(1)} %add.226), channel_id=1, source_target_pairs={{0,4},{2,6},{4,0},{6,2},{1,5},{3,7},{5,1},{7,3},{8,12},{10,14},{12... | collective-permute-start | bytes 776 | tf_op jit(solution)/shard_map/ppermute | solution.py:37
  20.0 2.4 %collective-permute-start.12 = (f32[64]{0:T(128)S(1)}, f32[64]{0:T(128)S(1)}, u32[]{:S(2)}, u32[]{:S(2)}) collective-permute-start(f32[64]{0:T(128)S(1)} %add.227), channel_id=1, source_target_pairs={{0,8},{8,0},{16,24},{24,16},{32,40},{40,32},{48,56},{56,48},{1,9},... | collective-permute-start | bytes 776 | tf_op jit(solution)/shard_map/ppermute | solution.py:37
  22.4 3.3 %collective-permute-start.13 = (f32[64]{0:T(128)S(1)}, f32[64]{0:T(128)S(1)}, u32[]{:S(2)}, u32[]{:S(2)}) collective-permute-start(f32[64]{0:T(128)S(1)} %add.228), channel_id=1, source_target_pairs={{0,16},{8,24},{16,0},{24,8},{32,48},{40,56},{48,32},{56,40},{1,17}... | collective-permute-start | bytes 776 | tf_op jit(solution)/shard_map/ppermute | solution.py:37
  25.7 6.3 %collective-permute-start.14 = (f32[64]{0:T(128)S(1)}, f32[64]{0:T(128)S(1)}, u32[]{:S(2)}, u32[]{:S(2)}) collective-permute-start(f32[64]{0:T(128)S(1)} %add.229), channel_id=1, source_target_pairs={{0,32},{8,40},{16,48},{24,56},{32,0},{40,8},{48,16},{56,24},{1,33}... | collective-permute-start | bytes 776 | tf_op jit(solution)/shard_map/ppermute | solution.py:37
  30.6 8.0 %copy-start.9 = (f32[18,128]{1,0:T(8,128)S(1)}, f32[18,128]{1,0:T(8,128)}, u32[]{:S(2)}) copy-start(f32[18,128]{1,0:T(8,128)} %param.19) | copy-start | bytes 27652
  33.1 8.8 %collective-permute-start.15 = (f32[65536]{0:T(1024)S(1)}, f32[65536]{0:T(1024)S(1)}, u32[]{:S(2)}, u32[]{:S(2)}) collective-permute-start(f32[65536]{0:T(1024)S(1)} %pad_maximum_fusion.8), channel_id=1, source_target_pairs={{0,1},{1,0},{2,3},{3,2},{4,5},{5,4},{6,7},{7,6},{8,9},{9,8},{10,11... | collective-permute-start | bytes 786440 | tf_op jit(solution)/shard_map/ppermute | solution.py:124
  42.2 7.0 %collective-permute-start.16 = (f32[49152]{0:T(1024)S(1)}, f32[49152]{0:T(1024)S(1)}, u32[]{:S(2)}, u32[]{:S(2)}) collective-permute-start(f32[49152]{0:T(1024)S(1)} %pad_maximum_fusion.9), channel_id=1, source_target_pairs={{0,2},{2,0},{4,6},{6,4},{1,3},{3,1},{5,7},{7,5},{8,10},{10,8},{12,... | collective-permute-start | bytes 589832 | tf_op jit(solution)/shard_map/ppermute | solution.py:124
  51.4 6.8 %collective-permute-start.17 = (f32[40960]{0:T(1024)}, f32[40960]{0:T(1024)S(1)}, u32[]{:S(2)}, u32[]{:S(2)}) collective-permute-start(f32[40960]{0:T(1024)} %pad_maximum_fusion.10), channel_id=1, source_target_pairs={{0,4},{2,6},{4,0},{6,2},{1,5},{3,7},{5,1},{7,3},{8,12},{10,14},{12... | collective-permute-start | bytes 491528 | tf_op jit(solution)/shard_map/ppermute | solution.py:124
  60.0 4.1 %collective-permute-start.18 = (f32[36864]{0:T(1024)S(1)}, f32[36864]{0:T(1024)S(1)}, u32[]{:S(2)}, u32[]{:S(2)}) collective-permute-start(f32[36864]{0:T(1024)S(1)} %pad_maximum_fusion.11), channel_id=1, source_target_pairs={{0,8},{8,0},{16,24},{24,16},{32,40},{40,32},{48,56},{56,48},{1,9},... | collective-permute-start | bytes 442376 | tf_op jit(solution)/shard_map/ppermute | solution.py:124
  64.3 7.6 %collective-permute-start.19 = (f32[34816]{0:T(1024)S(1)}, f32[34816]{0:T(1024)S(1)}, u32[]{:S(2)}, u32[]{:S(2)}) collective-permute-start(f32[34816]{0:T(1024)S(1)} %pad_maximum_fusion.12), channel_id=1, source_target_pairs={{0,16},{8,24},{16,0},{24,8},{32,48},{40,56},{48,32},{56,40},{1,17}... | collective-permute-start | bytes 417800 | tf_op jit(solution)/shard_map/ppermute | solution.py:124
  72.1 8.3 %collective-permute-start.20 = (f32[33792]{0:T(1024)S(1)}, f32[33792]{0:T(1024)S(1)}, u32[]{:S(2)}, u32[]{:S(2)}) collective-permute-start(f32[33792]{0:T(1024)S(1)} %pad_maximum_fusion.13), channel_id=1, source_target_pairs={{0,32},{8,40},{16,48},{24,56},{32,0},{40,8},{48,16},{56,24},{1,33}... | collective-permute-start | bytes 405512 | tf_op jit(solution)/shard_map/ppermute | solution.py:124
  73.7 8.7 %copy-start.15 = (pred[8,8]{1,0:T(8,128)(4,1)}, pred[8,8]{1,0:T(8,128)(4,1)S(1)}, u32[]{:S(2)}) copy-start(pred[8,8]{1,0:T(8,128)(4,1)S(1)} %iota_compare_fusion.5) | copy-start | bytes 196
  87.8 5.0 %copy-start.6 = (bf16[64,8,512]{2,1,0:T(8,128)(2,1)S(1)}, bf16[64,8,512]{2,1,0:T(8,128)(2,1)}, u32[]{:S(2)}) copy-start(bf16[64,8,512]{2,1,0:T(8,128)(2,1)} %broadcast_in_dim.215) | copy-start | bytes 1572868
  87.8 5.0 %copy-start.10 = (pred[64,19]{1,0:T(8,128)(4,1)S(1)}, pred[64,19]{1,0:T(8,128)(4,1)}, u32[]{:S(2)}) copy-start(pred[64,19]{1,0:T(8,128)(4,1)} %iota_compare_fusion.1) | copy-start | bytes 3652
  87.8 5.0 %copy-start.13 = (bf16[18,512]{1,0:T(8,128)(2,1)S(1)}, bf16[18,512]{1,0:T(8,128)(2,1)}, u32[]{:S(2)}) copy-start(bf16[18,512]{1,0:T(8,128)(2,1)} %get-tuple-element.37) | copy-start | bytes 55300
  87.8 5.0 %copy-start.19 = (pred[8,512]{1,0:T(8,128)(4,1)S(1)}, pred[8,512]{1,0:T(8,128)(4,1)}, u32[]{:S(2)}) copy-start(pred[8,512]{1,0:T(8,128)(4,1)} %broadcast_in_dim.213) | copy-start | bytes 12292
  87.8 5.0 %copy-start.20 = (bf16[1,512]{1,0:T(2,128)(2,1)S(1)}, bf16[1,512]{1,0:T(2,128)(2,1)}, u32[]{:S(2)}) copy-start(bf16[1,512]{1,0:T(2,128)(2,1)} %convert_element_type.83) | copy-start | bytes 3076
  87.8 5.0 %copy-start.22 = (f32[19]{0:T(128)S(1)}, f32[19]{0:T(128)}, u32[]{:S(2)}) copy-start(f32[19]{0:T(128)} %constant.182.clone.1) | copy-start | bytes 232
  93.2 7.7 %copy-start.3 = (f32[64,8,19]{2,1,0:T(8,128)}, f32[64,8,19]{2,1,0:T(8,128)S(1)}, u32[]{:S(2)}) copy-start(f32[64,8,19]{2,1,0:T(8,128)S(1)} %get-tuple-element.54) | copy-start | bytes 116740
  93.3 3.8 %copy-start.5 = (pred[64,2304]{1,0:T(8,128)(4,1)S(1)}, pred[64,2304]{1,0:T(8,128)(4,1)}, u32[]{:S(2)}) copy-start(pred[64,2304]{1,0:T(8,128)(4,1)} %copy-done.4) | copy-start | bytes 442372
  97.0 4.1 %copy-start.8 = (bf16[18,512]{1,0:T(8,128)(2,1)S(1)}, bf16[18,512]{1,0:T(8,128)(2,1)}, u32[]{:S(2)}) copy-start(bf16[18,512]{1,0:T(8,128)(2,1)} %get-tuple-element.36) | copy-start | bytes 55300
  97.1 4.1 %copy-start.11 = (pred[64,19]{1,0:T(8,128)(4,1)S(1)}, pred[64,19]{1,0:T(8,128)(4,1)}, u32[]{:S(2)}) copy-start(pred[64,19]{1,0:T(8,128)(4,1)} %iota_compare_fusion.1) | copy-start | bytes 3652
  97.1 4.1 %copy-start.17 = (bf16[1,512]{1,0:T(2,128)(2,1)S(1)}, bf16[1,512]{1,0:T(2,128)(2,1)}, u32[]{:S(2)}) copy-start(bf16[1,512]{1,0:T(2,128)(2,1)} %slice.527) | copy-start | bytes 3076
  106.9 12.3 %collective-permute-start.21 = (f32[64,8,66]{0,1,2:T(8,128)S(1)}, f32[64,8,66]{0,1,2:T(8,128)S(1)}, u32[]{:S(2)}, u32[]{:S(2)}) collective-permute-start(f32[64,8,66]{0,1,2:T(8,128)S(1)} %pad_maximum_fusion.2), channel_id=1, source_target_pairs={{0,8},{8,0},{16,24},{24,16},{32,40},{40,32},{48,56},{56,48},{1,9},... | collective-permute-start | bytes 405512 | tf_op jit(solution)/shard_map/ppermute | solution.py:37
  109.9 53.7 %collective-permute-start.3 = (bf16[4,128,512]{2,1,0:T(8,128)(2,1)}, bf16[4,128,512]{2,1,0:T(8,128)(2,1)}, u32[]{:S(2)}, u32[]{:S(2)}) collective-permute-start(bf16[4,128,512]{2,1,0:T(8,128)(2,1)} %get-tuple-element.22), channel_id=1, source_target_pairs={{0,1},{1,2},{2,3},{3,4},{4,5},{5,6},{6,7},{7,8},{8,9},{9,10},{10,1... | collective-permute-start | bytes 1572872 | tf_op jit(solution)/shard_map/ppermute | solution.py:70
  120.0 15.0 %collective-permute-start.22 = (f32[64,8,66]{0,1,2:T(8,128)}, f32[64,8,66]{0,1,2:T(8,128)S(1)}, u32[]{:S(2)}, u32[]{:S(2)}) collective-permute-start(f32[64,8,66]{0,1,2:T(8,128)} %pad_maximum_fusion.3), channel_id=1, source_target_pairs={{0,16},{8,24},{16,0},{24,8},{32,48},{40,56},{48,32},{56,40},{1,17}... | collective-permute-start | bytes 405512 | tf_op jit(solution)/shard_map/ppermute | solution.py:37
  122.7 45.7 %collective-permute-start.4 = (bf16[4,128,512]{2,1,0:T(8,128)(2,1)}, bf16[4,128,512]{2,1,0:T(8,128)(2,1)}, u32[]{:S(2)}, u32[]{:S(2)}) collective-permute-start(bf16[4,128,512]{2,1,0:T(8,128)(2,1)} %get-tuple-element.21), channel_id=1, source_target_pairs={{0,2},{1,3},{2,4},{3,5},{4,6},{5,7},{6,8},{7,9},{8,10},{9,11},{10,... | collective-permute-start | bytes 1572872 | tf_op jit(solution)/shard_map/ppermute | solution.py:70
  124.2 44.8 %collective-permute-start.5 = (bf16[4,128,512]{2,1,0:T(8,128)(2,1)}, bf16[4,128,512]{2,1,0:T(8,128)(2,1)}, u32[]{:S(2)}, u32[]{:S(2)}) collective-permute-start(bf16[4,128,512]{2,1,0:T(8,128)(2,1)} %get-tuple-element.23), channel_id=1, source_target_pairs={{0,3},{1,4},{2,5},{3,6},{4,7},{5,8},{6,9},{7,10},{8,11},{9,12},{10... | collective-permute-start | bytes 1572872 | tf_op jit(solution)/shard_map/ppermute | solution.py:70
  126.9 65.7 %collective-permute-start.6 = (bf16[4,128,512]{2,1,0:T(8,128)(2,1)}, bf16[4,128,512]{2,1,0:T(8,128)(2,1)}, u32[]{:S(2)}, u32[]{:S(2)}) collective-permute-start(bf16[4,128,512]{2,1,0:T(8,128)(2,1)} %get-tuple-element.18), channel_id=1, source_target_pairs={{0,1},{1,2},{2,3},{3,4},{4,5},{5,6},{6,7},{7,8},{8,9},{9,10},{10,1... | collective-permute-start | bytes 1572872 | tf_op jit(solution)/shard_map/ppermute | solution.py:70
  135.0 17.3 %collective-permute-start.23 = (f32[64,8,66]{0,1,2:T(8,128)S(1)}, f32[64,8,66]{0,1,2:T(8,128)S(1)}, u32[]{:S(2)}, u32[]{:S(2)}) collective-permute-start(f32[64,8,66]{0,1,2:T(8,128)S(1)} %pad_maximum_fusion.4), channel_id=1, source_target_pairs={{0,32},{8,40},{16,48},{24,56},{32,0},{40,8},{48,16},{56,24},{1,33}... | collective-permute-start | bytes 405512 | tf_op jit(solution)/shard_map/ppermute | solution.py:37
  153.1 1.8 collective-permute-start.24
  154.2 14.8 %copy-start.2 = (bf16[1,4,128,512]{3,2,1,0:T(8,128)(2,1)S(1)}, bf16[1,4,128,512]{3,2,1,0:T(8,128)(2,1)}, u32[]{:S(2)}) copy-start(bf16[1,4,128,512]{3,2,1,0:T(8,128)(2,1)} %get-tuple-element.20) | copy-start | bytes 1572868
  155.0 7.9 %collective-permute-start.25 = (f32[64,8,66]{0,1,2:T(8,128)S(1)}, f32[64,8,66]{0,1,2:T(8,128)S(1)}, u32[]{:S(2)}, u32[]{:S(2)}) collective-permute-start(f32[64,8,66]{0,1,2:T(8,128)S(1)} %pad_maximum_fusion.6), channel_id=1, source_target_pairs={{0,2},{2,0},{4,6},{6,4},{1,3},{3,1},{5,7},{7,5},{8,10},{10,8},{12,... | collective-permute-start | bytes 405512 | tf_op jit(solution)/shard_map/ppermute | solution.py:37
  162.9 44.7 %collective-permute-start.7 = (bf16[4,128,512]{2,1,0:T(8,128)(2,1)}, bf16[4,128,512]{2,1,0:T(8,128)(2,1)}, u32[]{:S(2)}, u32[]{:S(2)}) collective-permute-start(bf16[4,128,512]{2,1,0:T(8,128)(2,1)} %get-tuple-element.17), channel_id=1, source_target_pairs={{0,2},{1,3},{2,4},{3,5},{4,6},{5,7},{6,8},{7,9},{8,10},{9,11},{10,... | collective-permute-start | bytes 1572872 | tf_op jit(solution)/shard_map/ppermute | solution.py:70
  163.5 56.2 %collective-permute-start.8 = (bf16[4,128,512]{2,1,0:T(8,128)(2,1)}, bf16[4,128,512]{2,1,0:T(8,128)(2,1)}, u32[]{:S(2)}, u32[]{:S(2)}) collective-permute-start(bf16[4,128,512]{2,1,0:T(8,128)(2,1)} %get-tuple-element.19), channel_id=1, source_target_pairs={{0,3},{1,4},{2,5},{3,6},{4,7},{5,8},{6,9},{7,10},{8,11},{9,12},{10... | collective-permute-start | bytes 1572872 | tf_op jit(solution)/shard_map/ppermute | solution.py:70
  168.4 22.3 %collective-permute-start.26 = (f32[64,8,66]{0,1,2:T(8,128)S(1)}, f32[64,8,66]{0,1,2:T(8,128)S(1)}, u32[]{:S(2)}, u32[]{:S(2)}) collective-permute-start(f32[64,8,66]{0,1,2:T(8,128)S(1)} %pad_maximum_fusion.7), channel_id=1, source_target_pairs={{0,4},{2,6},{4,0},{6,2},{1,5},{3,7},{5,1},{7,3},{8,12},{10,14},{12... | collective-permute-start | bytes 405512 | tf_op jit(solution)/shard_map/ppermute | solution.py:37
  169.0 22.1 %copy-start.12 = (bf16[512,32]{0,1:T(8,128)(2,1)S(1)}, bf16[512,32]{0,1:T(8,128)(2,1)}, u32[]{:S(2)}) copy-start(bf16[512,32]{0,1:T(8,128)(2,1)} %param.12) | copy-start | bytes 98308
  191.3 38.6 %collective-permute-start.27 = (f32[64,32]{0,1:T(8,128)S(1)}, f32[64,32]{0,1:T(8,128)S(1)}, u32[]{:S(2)}, u32[]{:S(2)}) collective-permute-start(f32[64,32]{0,1:T(8,128)S(1)} %fusion.70), channel_id=1, source_target_pairs={{0,64},{64,0},{128,192},{192,128},{1,65},{65,1},{129,193},{193,129... | collective-permute-start | bytes 24584 | tf_op jit(solution)/shard_map/ppermute | solution.py:37
  229.8 7.6 %collective-permute-start.28 = (f32[64,32]{0,1:T(8,128)S(1)}, f32[64,32]{0,1:T(8,128)S(1)}, u32[]{:S(2)}, u32[]{:S(2)}) collective-permute-start(f32[64,32]{0,1:T(8,128)S(1)} %add.270), channel_id=1, source_target_pairs={{0,128},{64,192},{128,0},{192,64},{1,129},{65,193},{129,1},{193,65... | collective-permute-start | bytes 24584 | tf_op jit(solution)/shard_map/ppermute | solution.py:37
  (4 other events, 8.9 us)

commit v8 on v7

--- a/solution.py
+++ b/solution.py
@@ -180,33 +180,31 @@
     hit_table = send_pos[None, :] == targets[:, None]
     has_block = jnp.any(hit_table, axis=1)
     source = jnp.sum(jnp.where(hit_table, block_ids[None, :], 0), axis=1)
-    send_keys = key_cache[source].reshape(HOPS, CAP, row_count, feat_width)
-    send_values = value_cache[source].reshape(HOPS, CAP, row_count, feat_width)
+    send_blocks = jnp.stack([key_cache[source], value_cache[source]], axis=1).reshape(
+        HOPS, CAP, 2, row_count, feat_width
+    )
     meta_data = jnp.stack(
         [jnp.where(has_block, local_slot[source], -1), jnp.where(has_block, blk_req[source], -1)],
         axis=-1,
     )
     meta_data = meta_data.astype(jnp.float32).astype(jnp.bfloat16).reshape(HOPS, CAP, 2)
-    arrived = [(send_keys[0], send_values[0], meta_data[0])]
+    arrived = [(send_blocks[0], meta_data[0])]
     for distance in range(1, HOPS):
-        arrived.append(
-            passed_along((send_keys[distance], send_values[distance], meta_data[distance]), distance)
-        )
-    recv_keys = jnp.stack([entry[0] for entry in arrived])
-    recv_values = jnp.stack([entry[1] for entry in arrived])
-    recv_meta = jnp.stack([entry[2] for entry in arrived])
-    recv_keys = recv_keys.reshape(arrivals, row_count, feat_width)
-    recv_values = recv_values.reshape(arrivals, row_count, feat_width)
+        arrived.append(passed_along((send_blocks[distance], meta_data[distance]), distance))
+    recv_blocks = jnp.stack([entry[0] for entry in arrived])
+    recv_meta = jnp.stack([entry[1] for entry in arrived])
+    recv_blocks = recv_blocks.reshape(arrivals, 2, row_count, feat_width)
     recv_meta = recv_meta.reshape(arrivals, 2).astype(jnp.float32).astype(jnp.int32)
     match_table = recv_meta[None, :, 0] == jnp.arange(SLOT_DEV, dtype=jnp.int32)[:, None]
     filled = jnp.any(match_table, axis=1)
     picked = jnp.sum(
         jnp.where(match_table, jnp.arange(arrivals, dtype=jnp.int32)[None, :], 0), axis=1
     )
-    packed_keys = jnp.where(filled[:, None, None], recv_keys[picked], jnp.zeros((), jnp.bfloat16))
-    packed_values = jnp.where(
-        filled[:, None, None], recv_values[picked], jnp.zeros((), jnp.bfloat16)
-    )
+    packed_blocks = jnp.where(
+        filled[:, None, None, None], recv_blocks[picked], jnp.zeros((), jnp.bfloat16)
+    )
+    packed_keys = packed_blocks[:, 0]
+    packed_values = packed_blocks[:, 1]
     packed_request = jnp.where(filled, recv_meta[picked, 1], -1)
 
     row_req = jnp.repeat(jnp.where(is_kept, blk_req, -1), row_count)

time: 239 us -> 251 us (1.050)
  the two profiles are of different devices: /device:TPU:97 before, /device:TPU:6 now
where the time goes in v8:
time: 251 us
  waiting for transfers between devices  117 us (47%)
  starting transfers between devices  49.4 us (20%)
  other arithmetic  40.9 us (16%)
  local copies, waits for them, and re-layouts  27.3 us (11%)
  matrix products  14.4 us (6%)
    ppermute x14, waiting for transfers between devices, butterfly(): x = merge(x, lax.ppermute(x, axis, pairs))  87.9 us
    ppermute x14, starting transfers between devices, butterfly(): x = merge(x, lax.ppermute(x, axis, pairs))  32.8 us
    ppermute x6, waiting for transfers between devices, shards(): payload = lax.ppermute(payload, axis, pairs)  20.5 us
    ppermute x6, starting transfers between devices, shards(): payload = lax.ppermute(payload, axis, pairs)  9.51 us
    ppermute x6, waiting for transfers between devices, passed_along(): lax.ppermute(array, SEQ_PARTS, [(i, (i + by) % count) for i in range(coun...  8.7 us
    ppermute x6, starting transfers between devices, passed_along(): lax.ppermute(array, SEQ_PARTS, [(i, (i + by) % count) for i in range(coun...  7.15 us
    dot_general x2, matrix products, scores_of(): lax.dot_general(spread_queries, keys, (((1,), (1,)), ((), ())), preferred...  5.17 us
    dot_general x2, matrix products, weighted_of(): jnp.dot(expo.astype(jnp.bfloat16).reshape(requests * heads_here, -1), val...  5.16 us
  transfers between devices with their start and end apart: 26, of which 16 were waited for; matrix products, arithmetic and copies ran while one was open for 31% of the time, Pallas kernels for 0%

profile of v8, /device:TPU:6, one launch (start us, length us, event | category | flops | bytes accessed | tf_op | source)
XLA Modules:
  0.0 250.7 jit_solution(18144765108960267317)
XLA Ops:
  4.3 1.2 broadcast_select_fusion.5
  5.6 2.0 gather_fusion.2
  7.6 3.7 %gather_fusion.3 = bf16[16,128,512]{2,1,0:T(8,128)(2,1)} fusion(bf16[18,128,512]{2,1,0:T(8,128)(2,1)} %param.18, s32[1024]{0:T(1024)S(1)} %pad_clamp_fusion.1), kind=kCustom, calls=%fused_computation.3 | custom fusion | bytes 4194368 | tf_op jit(solution)/shard_map/gather | solution.py:183
  11.3 3.6 %fusion.13 = (bf16[1,4,2,128,512]{4,3,2,1,0:T(8,128)(2,1)}, bf16[4,2,128,512]{3,2,1,0:T(8,128)(2,1)}, bf16[4,2,128,512]{3,2,1,0:T(8,128)(2,1)}, bf16[4,2,128,512]{3,2,1,0:T(8,128)(2,1)}) fusion(bf16[16,1,128,512]{3,2,1,0:T(8,128)(2,1)} %bitcast.161, bf16[16,1,128,512]{3,2,1,0:T(8,128)(2,1)} %bitcast.162), kind=kLoop, calls=%fused_computation.33 | loop fusion | flops 2097152 | bytes 8388608 | tf_op jit(solution)/shard_map/slice | solution.py:191
  15.5 1.8 collective-permute-start.4
  17.3 1.9 collective-permute-start.5
  20.6 53.8 %collective-permute-done.7 = f32[64]{0:T(128)S(1)} collective-permute-done((f32[64]{0:T(128)S(1)}, f32[64]{0:T(128)S(1)}, u32[]{:S(2)}, u32[]{:S(2)}) %collective-permute-start.7) | collective-permute-done | bytes 288 | tf_op jit(solution)/shard_map/ppermute | solution.py:37
  74.3 5.0 %collective-permute-done.8 = f32[64]{0:T(128)S(1)} collective-permute-done((f32[64]{0:T(128)S(1)}, f32[64]{0:T(128)S(1)}, u32[]{:S(2)}, u32[]{:S(2)}) %collective-permute-start.8) | collective-permute-done | bytes 288 | tf_op jit(solution)/shard_map/ppermute | solution.py:37
  79.4 1.9 collective-permute-start.9
  81.3 1.6 collective-permute-done.9
  82.9 3.3 %collective-permute-start.10 = (f32[64]{0:T(128)S(1)}, f32[64]{0:T(128)S(1)}, u32[]{:S(2)}, u32[]{:S(2)}) collective-permute-start(f32[64]{0:T(128)S(1)} %add.227), channel_id=1, source_target_pairs={{0,16},{8,24},{16,0},{24,8},{32,48},{40,56},{48,32},{56,40},{1,17}... | collective-permute-start | bytes 776 | tf_op jit(solution)/shard_map/ppermute | solution.py:37
  86.2 1.5 collective-permute-done.10
  87.7 6.8 %collective-permute-start.11 = (f32[64]{0:T(128)S(1)}, f32[64]{0:T(128)S(1)}, u32[]{:S(2)}, u32[]{:S(2)}) collective-permute-start(f32[64]{0:T(128)S(1)} %add.228), channel_id=1, source_target_pairs={{0,32},{8,40},{16,48},{24,56},{32,0},{40,8},{48,16},{56,24},{1,33}... | collective-permute-start | bytes 776 | tf_op jit(solution)/shard_map/ppermute | solution.py:37
  96.6 2.7 %fusion.56 = f32[18,1,512]{2,1,0:T(1,128)S(1)} fusion(bf16[18,128,512]{2,1,0:T(8,128)(2,1)} %param.18, f32[18,128,1]{1,0,2:T(8,128)S(1)} %bitcast.177), kind=kOutput, calls=%fused_computation.159 | convolution fusion | flops 14155776 | bytes 2405376 | tf_op jit(solution)/shard_map/bi,bif->bf/dot_general | solution.py:153
  100.7 6.3 %collective-permute-done.13 = f32[49152]{0:T(1024)S(1)} collective-permute-done((f32[49152]{0:T(1024)S(1)}, f32[49152]{0:T(1024)S(1)}, u32[]{:S(2)}, u32[]{:S(2)}) %collective-permute-start.13) | collective-permute-done | bytes 196640 | tf_op jit(solution)/shard_map/ppermute | solution.py:124
  107.8 1.4 fusion.35
  109.8 5.5 %collective-permute-done.14 = f32[40960]{0:T(1024)S(1)} collective-permute-done((f32[40960]{0:T(1024)}, f32[40960]{0:T(1024)S(1)}, u32[]{:S(2)}, u32[]{:S(2)}) %collective-permute-start.14) | collective-permute-done | bytes 163872 | tf_op jit(solution)/shard_map/ppermute | solution.py:124
  117.5 3.3 %collective-permute-done.15 = f32[36864]{0:T(1024)S(1)} collective-permute-done((f32[36864]{0:T(1024)S(1)}, f32[36864]{0:T(1024)S(1)}, u32[]{:S(2)}, u32[]{:S(2)}) %collective-permute-start.15) | collective-permute-done | bytes 147488 | tf_op jit(solution)/shard_map/ppermute | solution.py:124
  121.0 2.3 collective-permute-start.16
  123.3 5.4 %collective-permute-done.16 = f32[34816]{0:T(1024)S(1)} collective-permute-done((f32[34816]{0:T(1024)S(1)}, f32[34816]{0:T(1024)S(1)}, u32[]{:S(2)}, u32[]{:S(2)}) %collective-permute-start.16) | collective-permute-done | bytes 139296 | tf_op jit(solution)/shard_map/ppermute | solution.py:124
  128.9 6.1 %collective-permute-start.17 = (f32[33792]{0:T(1024)S(1)}, f32[33792]{0:T(1024)S(1)}, u32[]{:S(2)}, u32[]{:S(2)}) collective-permute-start(f32[33792]{0:T(1024)S(1)} %pad_maximum_fusion.13), channel_id=1, source_target_pairs={{0,32},{8,40},{16,48},{24,56},{32,0},{40,8},{48,16},{56,24},{1,33}... | collective-permute-start | bytes 405512 | tf_op jit(solution)/shard_map/ppermute | solution.py:124
  135.0 1.4 gather_fusion.1
  136.6 1.3 gather_fusion
  137.9 1.3 fusion.50
  142.0 1.4 broadcast_in_dim.209
  143.4 1.9 select_n.315
  145.4 4.8 %fusion.72 = (f32[64,8]{1,0:T(8,128)S(1)}, f32[64,8,2304]{2,1,0:T(8,128)}) fusion(bf16[64,8,512]{2,1,0:T(8,128)(2,1)S(1)} %select_n.315, bf16[2304,512,1]{1,0,2:T(8,128)(2,1)S(1)} %bitcast.158, pred[64,2304]{1,0:T(8,128)(4,1)} %iota_compare_fusion), kind=kOutput, calls=%fused_computation.205 | convolution fusion | flops 1211497984 | bytes 7751680 | tf_op jit(solution)/shard_map/dot_general | solution.py:231
  150.6 3.8 %fusion.1 = f32[64,8]{1,0:T(8,128)S(1)} fusion(f32[64,8,2304]{2,1,0:T(8,128)} %get-tuple-element.48, f32[64,8]{1,0:T(8,128)S(1)} %max.32, pred[64,2304]{1,0:T(8,128)(4,1)S(1)} %copy-done.8), kind=kLoop, calls=%fused_computation.17 | loop fusion | flops 3538432 | bytes 4870144 | tf_op jit(solution)/shard_map/reduce_sum | solution.py:241
  154.4 3.9 %fusion.4 = f32[512,512]{1,0:T(8,128)S(1)} fusion(bf16[2304,512]{1,0:T(8,128)(2,1)S(1)} %bitcast.160, f32[64,8,2304]{2,1,0:T(8,128)} %get-tuple-element.48, f32[64,8]{1,0:T(8,128)S(1)} %max.32, pred[64,2304]{1,0:T(8,128)(4,1)S(1)} %copy-done.8), kind=kOutput, calls=%fused_computation.20 | convolution fusion | flops 1211498496 | bytes 8275968 | tf_op jit(solution)/shard_map/dot_general | solution.py:244
  158.6 1.3 convolution_add_fusion
  159.9 1.7 reshape.513
  161.6 2.4 select_reduce_fusion
  166.7 5.8 %collective-permute-done.18 = f32[64,8,66]{0,1,2:T(8,128)S(1)} collective-permute-done((f32[64,8,66]{0,1,2:T(8,128)S(1)}, f32[64,8,66]{0,1,2:T(8,128)S(1)}, u32[]{:S(2)}, u32[]{:S(2)}) %collective-permute-start.18) | collective-permute-done | bytes 135200 | tf_op jit(solution)/shard_map/ppermute | solution.py:37
  174.4 3.1 %collective-permute-start.19 = (f32[64,8,66]{0,1,2:T(8,128)}, f32[64,8,66]{0,1,2:T(8,128)}, u32[]{:S(2)}, u32[]{:S(2)}) collective-permute-start(f32[64,8,66]{0,1,2:T(8,128)} %pad_maximum_fusion.3), channel_id=1, source_target_pairs={{0,16},{8,24},{16,0},{24,8},{32,48},{40,56},{48,32},{56,40},{1,17}... | collective-permute-start | bytes 405512 | tf_op jit(solution)/shard_map/ppermute | solution.py:37
  177.6 2.9 %collective-permute-done = bf16[4,2]{0,1:T(2,128)(2,1)S(1)} collective-permute-done((bf16[4,2]{0,1:T(2,128)(2,1)S(1)}, bf16[4,2]{0,1:T(2,128)(2,1)S(1)}, u32[]{:S(2)}, u32[]{:S(2)}) %collective-permute-start) | collective-permute-done | bytes 48 | tf_op jit(solution)/shard_map/ppermute | solution.py:70
  180.5 2.8 %collective-permute-start.1 = (bf16[4,2]{0,1:T(2,128)(2,1)S(1)}, bf16[4,2]{0,1:T(2,128)(2,1)S(1)}, u32[]{:S(2)}, u32[]{:S(2)}) collective-permute-start(bf16[4,2]{0,1:T(2,128)(2,1)S(1)} %get-tuple-element.41), channel_id=1, source_target_pairs={{0,2},{1,3},{2,4},{3,5},{4,6},{5,7},{6,8},{7,9},{8,10},{9,11},{10,... | collective-permute-start | bytes 56 | tf_op jit(solution)/shard_map/ppermute | solution.py:70
  183.3 1.3 collective-permute-done.1
  184.6 4.5 %collective-permute-done.2 = bf16[4,2]{0,1:T(2,128)(2,1)S(1)} collective-permute-done((bf16[4,2]{0,1:T(2,128)(2,1)S(1)}, bf16[4,2]{0,1:T(2,128)(2,1)S(1)}, u32[]{:S(2)}, u32[]{:S(2)}) %collective-permute-start.2) | collective-permute-done | bytes 48 | tf_op jit(solution)/shard_map/ppermute | solution.py:70
  191.7 5.2 %collective-permute-start.20 = (f32[64,8,66]{0,1,2:T(8,128)S(1)}, f32[64,8,66]{0,1,2:T(8,128)S(1)}, u32[]{:S(2)}, u32[]{:S(2)}) collective-permute-start(f32[64,8,66]{0,1,2:T(8,128)S(1)} %pad_maximum_fusion.4), channel_id=1, source_target_pairs={{0,32},{8,40},{16,48},{24,56},{32,0},{40,8},{48,16},{56,24},{1,33}... | collective-permute-start | bytes 405512 | tf_op jit(solution)/shard_map/ppermute | solution.py:37
  197.0 10.9 %collective-permute-done.20 = f32[64,8,66]{0,1,2:T(8,128)S(1)} collective-permute-done((f32[64,8,66]{0,1,2:T(8,128)S(1)}, f32[64,8,66]{0,1,2:T(8,128)S(1)}, u32[]{:S(2)}, u32[]{:S(2)}) %collective-permute-start.20) | collective-permute-done | bytes 135200 | tf_op jit(solution)/shard_map/ppermute | solution.py:37
  215.2 7.3 %collective-permute-done.22 = f32[64,8,66]{0,1,2:T(8,128)S(1)} collective-permute-done((f32[64,8,66]{0,1,2:T(8,128)S(1)}, f32[64,8,66]{0,1,2:T(8,128)S(1)}, u32[]{:S(2)}, u32[]{:S(2)}) %collective-permute-start.22) | collective-permute-done | bytes 135200 | tf_op jit(solution)/shard_map/ppermute | solution.py:37
  223.9 5.7 %collective-permute-start.23 = (f32[64,8,66]{0,1,2:T(8,128)}, f32[64,8,66]{0,1,2:T(8,128)}, u32[]{:S(2)}, u32[]{:S(2)}) collective-permute-start(f32[64,8,66]{0,1,2:T(8,128)} %pad_maximum_fusion.7), channel_id=1, source_target_pairs={{0,4},{2,6},{4,0},{6,2},{1,5},{3,7},{5,1},{7,3},{8,12},{10,14},{12... | collective-permute-start | bytes 405512 | tf_op jit(solution)/shard_map/ppermute | solution.py:37
  229.6 3.6 %pad_maximum_fusion = bf16[4,4,2,128,512]{4,3,2,1,0:T(8,128)(2,1)} fusion(bf16[1,4,2,128,512]{4,3,2,1,0:T(8,128)(2,1)} %bitcast.15, bf16[1,4,2,128,512]{4,3,2,1,0:T(8,128)(2,1)} %bitcast.14, bf16[1,4,2,128,512]{4,3,2,1,0:T(8,128)(2,1)} %bitcast.13, bf16[1,4,2,128,512]{4,3,2,1,0:T(8,128)(2,1)S(1)} %copy-done.2), kind=kLoop, calls=%fused_computation.15 | loop fusion | flops 6291456 | bytes 8388608 | tf_op jit(solution)/shard_map/stack | solution.py:194
  233.2 5.1 %gather_fusion.4 = bf16[16,2,128,512]{3,2,1,0:T(8,128)(2,1)} fusion(bf16[16,2,128,512]{3,2,1,0:T(8,128)(2,1)} %bitcast.159, s32[1024]{0:T(1024)S(1)} %pad_clamp_fusion), kind=kCustom, calls=%fused_computation.4 | custom fusion | bytes 8388672 | tf_op jit(solution)/shard_map/gather | solution.py:204
  240.5 1.6 collective-permute-start.24
  242.1 2.5 %broadcast_select_fusion = bf16[16,2,128,512]{3,2,1,0:T(8,128)(2,1)S(1)} fusion(bf16[16,2,128,512]{3,2,1,0:T(8,128)(2,1)} %gather_fusion.4, pred[16]{0:T(512)(128)(4,1)S(1)} %fusion.49), kind=kLoop, calls=%fused_computation.16 | loop fusion | flops 2097152 | bytes 8388624 | tf_op jit(solution)/shard_map/jit(_where)/select_n | solution.py:203
  244.6 3.0 %collective-permute-start.25 = (f32[64,32]{0,1:T(8,128)S(1)}, f32[64,32]{0,1:T(8,128)S(1)}, u32[]{:S(2)}, u32[]{:S(2)}) collective-permute-start(f32[64,32]{0,1:T(8,128)S(1)} %add.269), channel_id=1, source_target_pairs={{0,128},{64,192},{128,0},{192,64},{1,129},{65,193},{129,1},{193,65... | collective-permute-start | bytes 24584 | tf_op jit(solution)/shard_map/ppermute | solution.py:37
  247.6 2.5 slice_bitcast_fusion
  (228 shorter events, 35.1 us)
Async XLA Ops:
  0.6 5.0 %copy-start = (bf16[18,128,512]{2,1,0:T(8,128)(2,1)S(1)}, bf16[18,128,512]{2,1,0:T(8,128)(2,1)}, u32[]{:S(2)}) copy-start(bf16[18,128,512]{2,1,0:T(8,128)(2,1)} %param.17) | copy-start | bytes 7077892
  1.5 18.5 %collective-permute-start.6 = (f32[64]{0:T(128)S(1)}, f32[64]{0:T(128)S(1)}, u32[]{:S(2)}, u32[]{:S(2)}) collective-permute-start(f32[64]{0:T(128)S(1)} %fusion.43), channel_id=1, source_target_pairs={{0,1},{1,0},{2,3},{3,2},{4,5},{5,4},{6,7},{7,6},{8,9},{9,8},{10,11... | collective-permute-start | bytes 776 | tf_op jit(solution)/shard_map/ppermute | solution.py:37
  2.3 1.6 copy-start.18
  5.5 5.8 %copy-start.21 = (s32[18]{0:T(128)}, s32[18]{0:T(128)S(1)}, u32[]{:S(2)}) copy-start(s32[18]{0:T(128)S(1)} %get-tuple-element.36) | copy-start | bytes 220
  5.6 5.7 %copy-start.16 = (s32[1024]{0:T(1024)}, s32[1024]{0:T(1024)S(1)}, u32[]{:S(2)}) copy-start(s32[1024]{0:T(1024)S(1)} %pad_clamp_fusion.1) | copy-start | bytes 12292
  11.3 74.9 %copy-start.11 = (bf16[32,3,512]{2,0,1:T(8,128)(2,1)S(1)}, bf16[32,3,512]{2,0,1:T(8,128)(2,1)}, u32[]{:S(2)}) copy-start(bf16[32,3,512]{2,0,1:T(8,128)(2,1)} %param.11) | copy-start | bytes 294916
  11.3 83.3 %copy-start.12 = (f32[18,128]{1,0:T(8,128)S(1)}, f32[18,128]{1,0:T(8,128)}, u32[]{:S(2)}) copy-start(f32[18,128]{1,0:T(8,128)} %param.19) | copy-start | bytes 27652
  11.3 84.8 %copy-start.13 = (bf16[64,32]{0,1:T(8,128)(2,1)S(1)}, bf16[64,32]{0,1:T(8,128)(2,1)}, u32[]{:S(2)}) copy-start(bf16[64,32]{0,1:T(8,128)(2,1)} %param.10) | copy-start | bytes 12292
  14.9 214.7 %collective-permute-start.3 = (bf16[4,2,128,512]{3,2,1,0:T(8,128)(2,1)}, bf16[4,2,128,512]{3,2,1,0:T(8,128)(2,1)}, u32[]{:S(2)}, u32[]{:S(2)}) collective-permute-start(bf16[4,2,128,512]{3,2,1,0:T(8,128)(2,1)} %get-tuple-element.19), channel_id=1, source_target_pairs={{0,1},{1,2},{2,3},{3,4},{4,5},{5,6},{6,7},{7,8},{8,9},{9,10},{10,1... | collective-permute-start | bytes 3145736 | tf_op jit(solution)/shard_map/ppermute | solution.py:70
  15.5 214.1 %collective-permute-start.4 = (bf16[4,2,128,512]{3,2,1,0:T(8,128)(2,1)}, bf16[4,2,128,512]{3,2,1,0:T(8,128)(2,1)}, u32[]{:S(2)}, u32[]{:S(2)}) collective-permute-start(bf16[4,2,128,512]{3,2,1,0:T(8,128)(2,1)} %get-tuple-element.21), channel_id=1, source_target_pairs={{0,2},{1,3},{2,4},{3,5},{4,6},{5,7},{6,8},{7,9},{8,10},{9,11},{10,... | collective-permute-start | bytes 3145736 | tf_op jit(solution)/shard_map/ppermute | solution.py:70
  17.3 212.3 %collective-permute-start.5 = (bf16[4,2,128,512]{3,2,1,0:T(8,128)(2,1)}, bf16[4,2,128,512]{3,2,1,0:T(8,128)(2,1)}, u32[]{:S(2)}, u32[]{:S(2)}) collective-permute-start(bf16[4,2,128,512]{3,2,1,0:T(8,128)(2,1)} %get-tuple-element.20), channel_id=1, source_target_pairs={{0,3},{1,4},{2,5},{3,6},{4,7},{5,8},{6,9},{7,10},{8,11},{9,12},{10... | collective-permute-start | bytes 3145736 | tf_op jit(solution)/shard_map/ppermute | solution.py:70
  20.0 54.3 %collective-permute-start.7 = (f32[64]{0:T(128)S(1)}, f32[64]{0:T(128)S(1)}, u32[]{:S(2)}, u32[]{:S(2)}) collective-permute-start(f32[64]{0:T(128)S(1)} %add.224), channel_id=1, source_target_pairs={{0,2},{2,0},{4,6},{6,4},{1,3},{3,1},{5,7},{7,5},{8,10},{10,8},{12,... | collective-permute-start | bytes 776 | tf_op jit(solution)/shard_map/ppermute | solution.py:37
  74.3 5.0 %collective-permute-start.8 = (f32[64]{0:T(128)S(1)}, f32[64]{0:T(128)S(1)}, u32[]{:S(2)}, u32[]{:S(2)}) collective-permute-start(f32[64]{0:T(128)S(1)} %add.225), channel_id=1, source_target_pairs={{0,4},{2,6},{4,0},{6,2},{1,5},{3,7},{5,1},{7,3},{8,12},{10,14},{12... | collective-permute-start | bytes 776 | tf_op jit(solution)/shard_map/ppermute | solution.py:37
  79.4 3.5 %collective-permute-start.9 = (f32[64]{0:T(128)S(1)}, f32[64]{0:T(128)S(1)}, u32[]{:S(2)}, u32[]{:S(2)}) collective-permute-start(f32[64]{0:T(128)S(1)} %add.226), channel_id=1, source_target_pairs={{0,8},{8,0},{16,24},{24,16},{32,40},{40,32},{48,56},{56,48},{1,9},... | collective-permute-start | bytes 776 | tf_op jit(solution)/shard_map/ppermute | solution.py:37
  82.9 4.8 %collective-permute-start.10 = (f32[64]{0:T(128)S(1)}, f32[64]{0:T(128)S(1)}, u32[]{:S(2)}, u32[]{:S(2)}) collective-permute-start(f32[64]{0:T(128)S(1)} %add.227), channel_id=1, source_target_pairs={{0,16},{8,24},{16,0},{24,8},{32,48},{40,56},{48,32},{56,40},{1,17}... | collective-permute-start | bytes 776 | tf_op jit(solution)/shard_map/ppermute | solution.py:37
  87.7 8.4 %collective-permute-start.11 = (f32[64]{0:T(128)S(1)}, f32[64]{0:T(128)S(1)}, u32[]{:S(2)}, u32[]{:S(2)}) collective-permute-start(f32[64]{0:T(128)S(1)} %add.228), channel_id=1, source_target_pairs={{0,32},{8,40},{16,48},{24,56},{32,0},{40,8},{48,16},{56,24},{1,33}... | collective-permute-start | bytes 776 | tf_op jit(solution)/shard_map/ppermute | solution.py:37
  96.5 2.8 %collective-permute-start.12 = (f32[65536]{0:T(1024)S(1)}, f32[65536]{0:T(1024)S(1)}, u32[]{:S(2)}, u32[]{:S(2)}) collective-permute-start(f32[65536]{0:T(1024)S(1)} %pad_maximum_fusion.8), channel_id=1, source_target_pairs={{0,1},{1,0},{2,3},{3,2},{4,5},{5,4},{6,7},{7,6},{8,9},{9,8},{10,11... | collective-permute-start | bytes 786440 | tf_op jit(solution)/shard_map/ppermute | solution.py:124
  99.5 7.4 %collective-permute-start.13 = (f32[49152]{0:T(1024)S(1)}, f32[49152]{0:T(1024)S(1)}, u32[]{:S(2)}, u32[]{:S(2)}) collective-permute-start(f32[49152]{0:T(1024)S(1)} %pad_maximum_fusion.9), channel_id=1, source_target_pairs={{0,2},{2,0},{4,6},{6,4},{1,3},{3,1},{5,7},{7,5},{8,10},{10,8},{12,... | collective-permute-start | bytes 589832 | tf_op jit(solution)/shard_map/ppermute | solution.py:124
  107.8 7.5 %collective-permute-start.14 = (f32[40960]{0:T(1024)}, f32[40960]{0:T(1024)S(1)}, u32[]{:S(2)}, u32[]{:S(2)}) collective-permute-start(f32[40960]{0:T(1024)} %pad_maximum_fusion.10), channel_id=1, source_target_pairs={{0,4},{2,6},{4,0},{6,2},{1,5},{3,7},{5,1},{7,3},{8,12},{10,14},{12... | collective-permute-start | bytes 491528 | tf_op jit(solution)/shard_map/ppermute | solution.py:124
  115.6 5.2 %collective-permute-start.15 = (f32[36864]{0:T(1024)S(1)}, f32[36864]{0:T(1024)S(1)}, u32[]{:S(2)}, u32[]{:S(2)}) collective-permute-start(f32[36864]{0:T(1024)S(1)} %pad_maximum_fusion.11), channel_id=1, source_target_pairs={{0,8},{8,0},{16,24},{24,16},{32,40},{40,32},{48,56},{56,48},{1,9},... | collective-permute-start | bytes 442376 | tf_op jit(solution)/shard_map/ppermute | solution.py:124
  121.0 7.7 %collective-permute-start.16 = (f32[34816]{0:T(1024)S(1)}, f32[34816]{0:T(1024)S(1)}, u32[]{:S(2)}, u32[]{:S(2)}) collective-permute-start(f32[34816]{0:T(1024)S(1)} %pad_maximum_fusion.12), channel_id=1, source_target_pairs={{0,16},{8,24},{16,0},{24,8},{32,48},{40,56},{48,32},{56,40},{1,17}... | collective-permute-start | bytes 417800 | tf_op jit(solution)/shard_map/ppermute | solution.py:124
  128.9 10.3 %collective-permute-start.17 = (f32[33792]{0:T(1024)S(1)}, f32[33792]{0:T(1024)S(1)}, u32[]{:S(2)}, u32[]{:S(2)}) collective-permute-start(f32[33792]{0:T(1024)S(1)} %pad_maximum_fusion.13), channel_id=1, source_target_pairs={{0,32},{8,40},{16,48},{24,56},{32,0},{40,8},{48,16},{56,24},{1,33}... | collective-permute-start | bytes 405512 | tf_op jit(solution)/shard_map/ppermute | solution.py:124
  145.3 4.9 %copy-start.9 = (bf16[64,8,512]{2,1,0:T(8,128)(2,1)S(1)}, bf16[64,8,512]{2,1,0:T(8,128)(2,1)}, u32[]{:S(2)}) copy-start(bf16[64,8,512]{2,1,0:T(8,128)(2,1)} %broadcast_in_dim.209) | copy-start | bytes 1572868
  145.3 4.9 %copy-start.15 = (bf16[18,512]{1,0:T(8,128)(2,1)S(1)}, bf16[18,512]{1,0:T(8,128)(2,1)}, u32[]{:S(2)}) copy-start(bf16[18,512]{1,0:T(8,128)(2,1)} %get-tuple-element.35) | copy-start | bytes 55300
  145.3 4.8 %copy-start.23 = (f32[19]{0:T(128)S(1)}, f32[19]{0:T(128)}, u32[]{:S(2)}) copy-start(f32[19]{0:T(128)} %constant.182.clone.1) | copy-start | bytes 232
  145.4 5.3 %copy-start.8 = (pred[64,2304]{1,0:T(8,128)(4,1)S(1)}, pred[64,2304]{1,0:T(8,128)(4,1)}, u32[]{:S(2)}) copy-start(pred[64,2304]{1,0:T(8,128)(4,1)} %iota_compare_fusion) | copy-start | bytes 442372
  150.5 7.7 %copy-start.7 = (f32[64,8,19]{2,1,0:T(8,128)}, f32[64,8,19]{2,1,0:T(8,128)S(1)}, u32[]{:S(2)}) copy-start(f32[64,8,19]{2,1,0:T(8,128)S(1)} %get-tuple-element.50) | copy-start | bytes 116740
  150.6 3.8 %copy-start.1 = (bf16[18,128,512]{2,1,0:T(8,128)(2,1)S(1)}, bf16[18,128,512]{2,1,0:T(8,128)(2,1)}, u32[]{:S(2)}) copy-start(bf16[18,128,512]{2,1,0:T(8,128)(2,1)} %param.18) | copy-start | bytes 7077892
  154.4 4.1 %copy-start.10 = (bf16[18,512]{1,0:T(8,128)(2,1)S(1)}, bf16[18,512]{1,0:T(8,128)(2,1)}, u32[]{:S(2)}) copy-start(bf16[18,512]{1,0:T(8,128)(2,1)} %get-tuple-element.34) | copy-start | bytes 55300
  154.4 4.1 %copy-start.17 = (bf16[1,512]{1,0:T(2,128)(2,1)S(1)}, bf16[1,512]{1,0:T(2,128)(2,1)}, u32[]{:S(2)}) copy-start(bf16[1,512]{1,0:T(2,128)(2,1)} %slice.530) | copy-start | bytes 3076
  158.5 8.1 %copy-start.19 = (s32[16]{0:T(128)S(1)}, s32[16]{0:T(128)}, u32[]{:S(2)}) copy-start(s32[16]{0:T(128)} %gather_fusion.1) | copy-start | bytes 196
  159.9 6.8 %copy-start.20 = (s32[16]{0:T(128)S(1)}, s32[16]{0:T(128)}, u32[]{:S(2)}) copy-start(s32[16]{0:T(128)} %gather_fusion) | copy-start | bytes 196
  159.9 6.8 %copy-start.22 = (pred[16]{0:T(512)(128)(4,1)S(1)}, pred[16]{0:T(512)(128)(4,1)}, u32[]{:S(2)}) copy-start(pred[16]{0:T(512)(128)(4,1)} %fusion.50) | copy-start | bytes 52
  164.9 64.7 %copy-start.2 = (bf16[1,4,2,128,512]{4,3,2,1,0:T(8,128)(2,1)S(1)}, bf16[1,4,2,128,512]{4,3,2,1,0:T(8,128)(2,1)}, u32[]{:S(2)}) copy-start(bf16[1,4,2,128,512]{4,3,2,1,0:T(8,128)(2,1)} %get-tuple-element.18) | copy-start | bytes 3145732
  166.0 6.5 %collective-permute-start.18 = (f32[64,8,66]{0,1,2:T(8,128)S(1)}, f32[64,8,66]{0,1,2:T(8,128)S(1)}, u32[]{:S(2)}, u32[]{:S(2)}) collective-permute-start(f32[64,8,66]{0,1,2:T(8,128)S(1)} %pad_maximum_fusion.2), channel_id=1, source_target_pairs={{0,8},{8,0},{16,24},{24,16},{32,40},{40,32},{48,56},{56,48},{1,9},... | collective-permute-start | bytes 405512 | tf_op jit(solution)/shard_map/ppermute | solution.py:37
  173.6 15.5 %copy-start.3 = (f32[64,8,65]{0,1,2:T(8,128)}, f32[64,8,65]{0,1,2:T(8,128)S(1)}, u32[]{:S(2)}) copy-start(f32[64,8,65]{0,1,2:T(8,128)S(1)} %fusion.22) | copy-start | bytes 399364
  174.4 14.8 %collective-permute-start.19 = (f32[64,8,66]{0,1,2:T(8,128)}, f32[64,8,66]{0,1,2:T(8,128)}, u32[]{:S(2)}, u32[]{:S(2)}) collective-permute-start(f32[64,8,66]{0,1,2:T(8,128)} %pad_maximum_fusion.3), channel_id=1, source_target_pairs={{0,16},{8,24},{16,0},{24,8},{32,48},{40,56},{48,32},{56,40},{1,17}... | collective-permute-start | bytes 405512 | tf_op jit(solution)/shard_map/ppermute | solution.py:37
  177.5 3.0 %collective-permute-start = (bf16[4,2]{0,1:T(2,128)(2,1)S(1)}, bf16[4,2]{0,1:T(2,128)(2,1)S(1)}, u32[]{:S(2)}, u32[]{:S(2)}) collective-permute-start(bf16[4,2]{0,1:T(2,128)(2,1)S(1)} %get-tuple-element.42), channel_id=1, source_target_pairs={{0,1},{1,2},{2,3},{3,4},{4,5},{5,6},{6,7},{7,8},{8,9},{9,10},{10,1... | collective-permute-start | bytes 56 | tf_op jit(solution)/shard_map/ppermute | solution.py:70
  180.5 4.1 %collective-permute-start.1 = (bf16[4,2]{0,1:T(2,128)(2,1)S(1)}, bf16[4,2]{0,1:T(2,128)(2,1)S(1)}, u32[]{:S(2)}, u32[]{:S(2)}) collective-permute-start(bf16[4,2]{0,1:T(2,128)(2,1)S(1)} %get-tuple-element.41), channel_id=1, source_target_pairs={{0,2},{1,3},{2,4},{3,5},{4,6},{5,7},{6,8},{7,9},{8,10},{9,11},{10,... | collective-permute-start | bytes 56 | tf_op jit(solution)/shard_map/ppermute | solution.py:70
  184.6 4.5 %collective-permute-start.2 = (bf16[4,2]{0,1:T(2,128)(2,1)S(1)}, bf16[4,2]{0,1:T(2,128)(2,1)S(1)}, u32[]{:S(2)}, u32[]{:S(2)}) collective-permute-start(bf16[4,2]{0,1:T(2,128)(2,1)S(1)} %get-tuple-element.40), channel_id=1, source_target_pairs={{0,3},{1,4},{2,5},{3,6},{4,7},{5,8},{6,9},{7,10},{8,11},{9,12},{10... | collective-permute-start | bytes 56 | tf_op jit(solution)/shard_map/ppermute | solution.py:70
  191.7 16.3 %collective-permute-start.20 = (f32[64,8,66]{0,1,2:T(8,128)S(1)}, f32[64,8,66]{0,1,2:T(8,128)S(1)}, u32[]{:S(2)}, u32[]{:S(2)}) collective-permute-start(f32[64,8,66]{0,1,2:T(8,128)S(1)} %pad_maximum_fusion.4), channel_id=1, source_target_pairs={{0,32},{8,40},{16,48},{24,56},{32,0},{40,8},{48,16},{56,24},{1,33}... | collective-permute-start | bytes 405512 | tf_op jit(solution)/shard_map/ppermute | solution.py:37
  209.4 1.9 collective-permute-start.21
  213.8 8.6 %collective-permute-start.22 = (f32[64,8,66]{0,1,2:T(8,128)S(1)}, f32[64,8,66]{0,1,2:T(8,128)S(1)}, u32[]{:S(2)}, u32[]{:S(2)}) collective-permute-start(f32[64,8,66]{0,1,2:T(8,128)S(1)} %pad_maximum_fusion.6), channel_id=1, source_target_pairs={{0,2},{2,0},{4,6},{6,4},{1,3},{3,1},{5,7},{7,5},{8,10},{10,8},{12,... | collective-permute-start | bytes 405512 | tf_op jit(solution)/shard_map/ppermute | solution.py:37
  223.9 14.4 %collective-permute-start.23 = (f32[64,8,66]{0,1,2:T(8,128)}, f32[64,8,66]{0,1,2:T(8,128)}, u32[]{:S(2)}, u32[]{:S(2)}) collective-permute-start(f32[64,8,66]{0,1,2:T(8,128)} %pad_maximum_fusion.7), channel_id=1, source_target_pairs={{0,4},{2,6},{4,0},{6,2},{1,5},{3,7},{5,1},{7,3},{8,12},{10,14},{12... | collective-permute-start | bytes 405512 | tf_op jit(solution)/shard_map/ppermute | solution.py:37
  233.2 5.8 %copy-start.5 = (f32[64,8,65]{0,1,2:T(8,128)S(1)}, f32[64,8,65]{0,1,2:T(8,128)}, u32[]{:S(2)}) copy-start(f32[64,8,65]{0,1,2:T(8,128)} %copy-done.4) | copy-start | bytes 399364
  233.2 7.1 %copy-start.14 = (bf16[512,32]{0,1:T(8,128)(2,1)S(1)}, bf16[512,32]{0,1:T(8,128)(2,1)}, u32[]{:S(2)}) copy-start(bf16[512,32]{0,1:T(8,128)(2,1)} %param.12) | copy-start | bytes 98308
  240.5 4.1 %collective-permute-start.24 = (f32[64,32]{0,1:T(8,128)S(1)}, f32[64,32]{0,1:T(8,128)S(1)}, u32[]{:S(2)}, u32[]{:S(2)}) collective-permute-start(f32[64,32]{0,1:T(8,128)S(1)} %fusion.74), channel_id=1, source_target_pairs={{0,64},{64,0},{128,192},{192,128},{1,65},{65,1},{129,193},{193,129... | collective-permute-start | bytes 24584 | tf_op jit(solution)/shard_map/ppermute | solution.py:37
  244.6 5.5 %collective-permute-start.25 = (f32[64,32]{0,1:T(8,128)S(1)}, f32[64,32]{0,1:T(8,128)S(1)}, u32[]{:S(2)}, u32[]{:S(2)}) collective-permute-start(f32[64,32]{0,1:T(8,128)S(1)} %add.269), channel_id=1, source_target_pairs={{0,128},{64,192},{128,0},{192,64},{1,129},{65,193},{129,1},{193,65... | collective-permute-start | bytes 24584 | tf_op jit(solution)/shard_map/ppermute | solution.py:37
  (2 other events, 1.4 us)

commit v9 on v7

--- a/solution.py
+++ b/solution.py
@@ -257,7 +257,11 @@
     stats = jnp.concatenate(
         [local_acc, local_sum[..., None], local_top[..., None]], axis=-1
     )
-    stats = butterfly(stats, softmax_merge, ["z", "core", "x"])
+    stats = butterfly(stats, softmax_merge, ["z", "core"])
+    recv_keys, recv_values, recv_meta, stats = lax.optimization_barrier(
+        (recv_keys, recv_values, recv_meta, stats)
+    )
+    stats = butterfly(stats, softmax_merge, ["x"])
     mixture = stats[..., :HDIM]
     totals = stats[..., HDIM]
     mixed = (mixture / totals[..., None]).astype(jnp.bfloat16)

time: 239 us -> 244 us (1.021)
  the two profiles are of different devices: /device:TPU:97 before, /device:TPU:6 now
where the time goes in v9:
time: 244 us; the launch traced here: 240 us
  waiting for transfers between devices  97 us (40%)
  starting transfers between devices  56.3 us (23%)
  local copies, waits for them, and re-layouts  36 us (15%)
  other arithmetic  32.8 us (13%)
  matrix products  16.5 us (7%)
    ppermute x14, waiting for transfers between devices, butterfly(): x = merge(x, lax.ppermute(x, axis, pairs))  85.2 us
    ppermute x14, starting transfers between devices, butterfly(): x = merge(x, lax.ppermute(x, axis, pairs))  36.4 us
    ppermute x6, starting transfers between devices, shards(): payload = lax.ppermute(payload, axis, pairs)  12.2 us
    ppermute x6, waiting for transfers between devices, shards(): payload = lax.ppermute(payload, axis, pairs)  11.8 us
    ppermute x9, starting transfers between devices, passed_along(): lax.ppermute(array, SEQ_PARTS, [(i, (i + by) % count) for i in range(coun...  7.67 us
    slice x4, local copies, waits for them, and re-layouts, shards(): arrived = [(send_keys[0], send_values[0], meta_data[0])]  6.46 us
    dot_general x2, matrix products, scores_of(): lax.dot_general(spread_queries, keys, (((1,), (1,)), ((), ())), preferred...  5.33 us
    dot_general x2, matrix products, weighted_of(): jnp.dot(expo.astype(jnp.bfloat16).reshape(requests * heads_here, -1), val...  5.14 us
  transfers between devices with their start and end apart: 29, of which 13 were waited for; matrix products, arithmetic and copies ran while one was open for 34% of the time, Pallas kernels for 0%

profile of v9, /device:TPU:6, one launch (start us, length us, event | category | flops | bytes accessed | tf_op | source)
XLA Modules:
  0.0 240.4 jit_solution(15363871831322270216)
XLA Ops:
  8.2 1.8 collective-permute-start.1
  10.1 1.9 collective-permute-start.2
  12.0 2.0 gather_fusion.2
  14.0 2.9 %slice_bitcast_fusion.1 = (bf16[1,4,128,512]{3,2,1,0:T(8,128)(2,1)}, bf16[4,128,512]{2,1,0:T(8,128)(2,1)}, bf16[4,128,512]{2,1,0:T(8,128)(2,1)}, bf16[4,128,512]{2,1,0:T(8,128)(2,1)}) fusion(bf16[16,128,512]{2,1,0:T(8,128)(2,1)} %gather_fusion.2), kind=kLoop, calls=%fused_computation.29 | loop fusion | bytes 4194304 | tf_op jit(solution)/shard_map/slice | solution.py:190
  17.9 3.5 %collective-permute-done.10 = f32[64]{0:T(128)S(1)} collective-permute-done((f32[64]{0:T(128)S(1)}, f32[64]{0:T(128)S(1)}, u32[]{:S(2)}, u32[]{:S(2)}) %collective-permute-start.10) | collective-permute-done | bytes 288 | tf_op jit(solution)/shard_map/ppermute | solution.py:37
  22.5 3.9 %collective-permute-done.11 = f32[64]{0:T(128)S(1)} collective-permute-done((f32[64]{0:T(128)S(1)}, f32[64]{0:T(128)S(1)}, u32[]{:S(2)}, u32[]{:S(2)}) %collective-permute-start.11) | collective-permute-done | bytes 288 | tf_op jit(solution)/shard_map/ppermute | solution.py:37
  26.5 1.9 collective-permute-start.12
  28.4 1.6 collective-permute-done.12
  30.0 4.4 %collective-permute-start.13 = (f32[64]{0:T(128)S(1)}, f32[64]{0:T(128)S(1)}, u32[]{:S(2)}, u32[]{:S(2)}) collective-permute-start(f32[64]{0:T(128)S(1)} %add.228), channel_id=1, source_target_pairs={{0,16},{8,24},{16,0},{24,8},{32,48},{40,56},{48,32},{56,40},{1,17}... | collective-permute-start | bytes 776 | tf_op jit(solution)/shard_map/ppermute | solution.py:37
  34.4 1.5 collective-permute-done.13
  35.9 4.8 %collective-permute-start.14 = (f32[64]{0:T(128)S(1)}, f32[64]{0:T(128)S(1)}, u32[]{:S(2)}, u32[]{:S(2)}) collective-permute-start(f32[64]{0:T(128)S(1)} %add.229), channel_id=1, source_target_pairs={{0,32},{8,40},{16,48},{24,56},{32,0},{40,8},{48,16},{56,24},{1,33}... | collective-permute-start | bytes 776 | tf_op jit(solution)/shard_map/ppermute | solution.py:37
  41.4 2.0 collective-permute-done.14
  44.4 2.3 fusion.54
  47.0 3.3 %fusion.52 = f32[18,1,512]{2,1,0:T(1,128)} fusion(bf16[18,128,512]{2,1,0:T(8,128)(2,1)} %param.18, f32[18,128,1]{1,0,2:T(8,128)} %bitcast.179), kind=kOutput, calls=%fused_computation.151 | convolution fusion | flops 14155776 | bytes 2405376 | tf_op jit(solution)/shard_map/bi,bif->bf/dot_general | solution.py:153
  50.4 3.5 %collective-permute-done.16 = f32[49152]{0:T(1024)S(1)} collective-permute-done((f32[49152]{0:T(1024)S(1)}, f32[49152]{0:T(1024)S(1)}, u32[]{:S(2)}, u32[]{:S(2)}) %collective-permute-start.16) | collective-permute-done | bytes 196640 | tf_op jit(solution)/shard_map/ppermute | solution.py:124
  54.7 1.4 pad_maximum_fusion.10
  57.2 1.5 fusion.31
  60.4 2.7 %collective-permute-done.17 = f32[40960]{0:T(1024)S(1)} collective-permute-done((f32[40960]{0:T(1024)}, f32[40960]{0:T(1024)S(1)}, u32[]{:S(2)}, u32[]{:S(2)}) %collective-permute-start.17) | collective-permute-done | bytes 163872 | tf_op jit(solution)/shard_map/ppermute | solution.py:124
  64.9 2.5 %collective-permute-start.18 = (f32[36864]{0:T(1024)S(1)}, f32[36864]{0:T(1024)S(1)}, u32[]{:S(2)}, u32[]{:S(2)}) collective-permute-start(f32[36864]{0:T(1024)S(1)} %pad_maximum_fusion.11), channel_id=1, source_target_pairs={{0,8},{8,0},{16,24},{24,16},{32,40},{40,32},{48,56},{56,48},{1,9},... | collective-permute-start | bytes 442376 | tf_op jit(solution)/shard_map/ppermute | solution.py:124
  69.1 1.4 collective-permute-done.18
  70.7 3.3 %collective-permute-start.19 = (f32[34816]{0:T(1024)S(1)}, f32[34816]{0:T(1024)S(1)}, u32[]{:S(2)}, u32[]{:S(2)}) collective-permute-start(f32[34816]{0:T(1024)S(1)} %pad_maximum_fusion.12), channel_id=1, source_target_pairs={{0,16},{8,24},{16,0},{24,8},{32,48},{40,56},{48,32},{56,40},{1,17}... | collective-permute-start | bytes 417800 | tf_op jit(solution)/shard_map/ppermute | solution.py:124
  74.6 4.2 %collective-permute-done.19 = f32[34816]{0:T(1024)S(1)} collective-permute-done((f32[34816]{0:T(1024)S(1)}, f32[34816]{0:T(1024)S(1)}, u32[]{:S(2)}, u32[]{:S(2)}) %collective-permute-start.19) | collective-permute-done | bytes 139296 | tf_op jit(solution)/shard_map/ppermute | solution.py:124
  79.0 4.7 %collective-permute-start.20 = (f32[33792]{0:T(1024)S(1)}, f32[33792]{0:T(1024)S(1)}, u32[]{:S(2)}, u32[]{:S(2)}) collective-permute-start(f32[33792]{0:T(1024)S(1)} %pad_maximum_fusion.13), channel_id=1, source_target_pairs={{0,32},{8,40},{16,48},{24,56},{32,0},{40,8},{48,16},{56,24},{1,33}... | collective-permute-start | bytes 405512 | tf_op jit(solution)/shard_map/ppermute | solution.py:124
  83.7 3.8 %gather_fusion.4 = bf16[16,128,512]{2,1,0:T(8,128)(2,1)} fusion(bf16[18,128,512]{2,1,0:T(8,128)(2,1)} %param.18, s32[1024]{0:T(1024)} %copy-done.18), kind=kCustom, calls=%fused_computation.4 | custom fusion | bytes 4194368 | tf_op jit(solution)/shard_map/gather | solution.py:184
  93.1 2.5 %select_n.320 = bf16[64,8,512]{2,1,0:T(8,128)(2,1)} reshape(bf16[64,8,8,64]{3,2,1,0:T(8,128)(2,1)} %broadcast_select_fusion.2) | data formatting | bytes 1048576 | tf_op jit(solution)/shard_map/jit(_where)/select_n | solution.py:228
  95.7 5.0 %fusion.68 = (f32[64,8]{1,0:T(8,128)S(1)}, f32[64,8,2304]{2,1,0:T(8,128)}) fusion(bf16[64,8,512]{2,1,0:T(8,128)(2,1)} %select_n.320, bf16[2304,512,1]{1,0,2:T(8,128)(2,1)S(1)} %bitcast.158, pred[64,2304]{1,0:T(8,128)(4,1)S(1)} %iota_compare_fusion), kind=kOutput, calls=%fused_computation.197 | convolution fusion | flops 1211497984 | bytes 7751680 | tf_op jit(solution)/shard_map/dot_general | solution.py:233
  101.1 3.8 %fusion.1 = f32[64,8]{1,0:T(8,128)S(1)} fusion(f32[64,8,2304]{2,1,0:T(8,128)} %get-tuple-element.54, f32[64,8]{1,0:T(8,128)S(1)} %max.32, pred[64,2304]{1,0:T(8,128)(4,1)} %copy-done.5), kind=kLoop, calls=%fused_computation.10 | loop fusion | flops 3538432 | bytes 4870144 | tf_op jit(solution)/shard_map/reduce_sum | solution.py:243
  104.9 3.8 %fusion.4 = f32[512,512]{1,0:T(8,128)S(1)} fusion(bf16[2304,512]{1,0:T(8,128)(2,1)S(1)} %bitcast.159, f32[64,8,2304]{2,1,0:T(8,128)} %get-tuple-element.54, f32[64,8]{1,0:T(8,128)S(1)} %max.32, pred[64,2304]{1,0:T(8,128)(4,1)S(1)} %copy-done.6), kind=kOutput, calls=%fused_computation.13 | convolution fusion | flops 1211498496 | bytes 8275968 | tf_op jit(solution)/shard_map/dot_general | solution.py:246
  110.4 1.7 reshape.525
  112.1 2.3 select_reduce_fusion
  115.5 1.8 collective-permute-start.21
  117.3 2.9 %slice_bitcast_fusion = (bf16[1,4,128,512]{3,2,1,0:T(8,128)(2,1)}, bf16[4,128,512]{2,1,0:T(8,128)(2,1)}, bf16[4,128,512]{2,1,0:T(8,128)(2,1)}, bf16[4,128,512]{2,1,0:T(8,128)(2,1)}) fusion(bf16[16,128,512]{2,1,0:T(8,128)(2,1)} %gather_fusion.4), kind=kLoop, calls=%fused_computation.28 | loop fusion | bytes 4194304 | tf_op jit(solution)/shard_map/slice | solution.py:190
  120.2 1.6 collective-permute-start.4
  125.1 3.4 %collective-permute-start.22 = (f32[64,8,66]{0,1,2:T(8,128)S(1)}, f32[64,8,66]{0,1,2:T(8,128)S(1)}, u32[]{:S(2)}, u32[]{:S(2)}) collective-permute-start(f32[64,8,66]{0,1,2:T(8,128)S(1)} %pad_maximum_fusion.3), channel_id=1, source_target_pairs={{0,16},{8,24},{16,0},{24,8},{32,48},{40,56},{48,32},{56,40},{1,17}... | collective-permute-start | bytes 405512 | tf_op jit(solution)/shard_map/ppermute | solution.py:37
  128.6 28.1 %collective-permute-done.22 = f32[64,8,66]{0,1,2:T(8,128)S(1)} collective-permute-done((f32[64,8,66]{0,1,2:T(8,128)S(1)}, f32[64,8,66]{0,1,2:T(8,128)S(1)}, u32[]{:S(2)}, u32[]{:S(2)}) %collective-permute-start.22) | collective-permute-done | bytes 135200 | tf_op jit(solution)/shard_map/ppermute | solution.py:37
  156.9 3.0 %collective-permute-start.23 = (f32[64,8,66]{0,1,2:T(8,128)S(1)}, f32[64,8,66]{0,1,2:T(8,128)S(1)}, u32[]{:S(2)}, u32[]{:S(2)}) collective-permute-start(f32[64,8,66]{0,1,2:T(8,128)S(1)} %pad_maximum_fusion.4), channel_id=1, source_target_pairs={{0,32},{8,40},{16,48},{24,56},{32,0},{40,8},{48,16},{56,24},{1,33}... | collective-permute-start | bytes 405512 | tf_op jit(solution)/shard_map/ppermute | solution.py:37
  159.9 3.0 %pad_maximum_fusion = bf16[4,4,128,512]{3,2,1,0:T(8,128)(2,1)} fusion(bf16[1,4,128,512]{3,2,1,0:T(8,128)(2,1)} %bitcast.13, bf16[1,4,128,512]{3,2,1,0:T(8,128)(2,1)} %bitcast.12, bf16[1,4,128,512]{3,2,1,0:T(8,128)(2,1)} %bitcast.11, bf16[1,4,128,512]{3,2,1,0:T(8,128)(2,1)S(1)} %copy-done.2), kind=kLoop, calls=%fused_computation.17 | loop fusion | flops 3145728 | bytes 4194304 | tf_op jit(solution)/shard_map/stack | solution.py:195
  162.9 31.7 %collective-permute-done.23 = f32[64,8,66]{0,1,2:T(8,128)S(1)} collective-permute-done((f32[64,8,66]{0,1,2:T(8,128)S(1)}, f32[64,8,66]{0,1,2:T(8,128)S(1)}, u32[]{:S(2)}, u32[]{:S(2)}) %collective-permute-start.23) | collective-permute-done | bytes 135200 | tf_op jit(solution)/shard_map/ppermute | solution.py:37
  194.6 1.4 collective-permute-start.24
  196.1 2.6 %pad_maximum_fusion.1 = bf16[4,4,128,512]{3,2,1,0:T(8,128)(2,1)} fusion(bf16[1,4,128,512]{3,2,1,0:T(8,128)(2,1)S(1)} %bitcast.173, bf16[1,4,128,512]{3,2,1,0:T(8,128)(2,1)S(1)} %bitcast.172, bf16[1,4,128,512]{3,2,1,0:T(8,128)(2,1)} %bitcast.18, bf16[1,4,128,512]{3,2,1,0:T(8,128)(2,1)S(1)} %copy-done.3), kind=kLoop, calls=%fused_computation.18 | loop fusion | flops 3145728 | bytes 4194304 | tf_op jit(solution)/shard_map/stack | solution.py:196
  199.7 7.6 %collective-permute-done.25 = f32[64,8,66]{0,1,2:T(8,128)S(1)} collective-permute-done((f32[64,8,66]{0,1,2:T(8,128)S(1)}, f32[64,8,66]{0,1,2:T(8,128)S(1)}, u32[]{:S(2)}, u32[]{:S(2)}) %collective-permute-start.25) | collective-permute-done | bytes 135200 | tf_op jit(solution)/shard_map/ppermute | solution.py:37
  207.4 9.7 %collective-permute-start.26 = (f32[64,8,66]{0,1,2:T(8,128)S(1)}, f32[64,8,66]{0,1,2:T(8,128)S(1)}, u32[]{:S(2)}, u32[]{:S(2)}) collective-permute-start(f32[64,8,66]{0,1,2:T(8,128)S(1)} %pad_maximum_fusion.7), channel_id=1, source_target_pairs={{0,4},{2,6},{4,0},{6,2},{1,5},{3,7},{5,1},{7,3},{8,12},{10,14},{12... | collective-permute-start | bytes 405512 | tf_op jit(solution)/shard_map/ppermute | solution.py:37
  217.6 5.2 %collective-permute-done.26 = f32[64,8,66]{0,1,2:T(8,128)S(1)} collective-permute-done((f32[64,8,66]{0,1,2:T(8,128)S(1)}, f32[64,8,66]{0,1,2:T(8,128)S(1)}, u32[]{:S(2)}, u32[]{:S(2)}) %collective-permute-start.26) | collective-permute-done | bytes 135200 | tf_op jit(solution)/shard_map/ppermute | solution.py:37
  223.4 1.6 collective-permute-start.27
  225.0 3.6 %gather_fusion.3 = bf16[16,128,512]{2,1,0:T(8,128)(2,1)} fusion(bf16[16,128,512]{2,1,0:T(8,128)(2,1)} %bitcast.160, s32[1024]{0:T(1024)S(1)} %pad_clamp_fusion), kind=kCustom, calls=%fused_computation.3 | custom fusion | bytes 4194368 | tf_op jit(solution)/shard_map/gather | solution.py:206
  228.6 3.6 %gather_fusion.5 = bf16[16,128,512]{2,1,0:T(8,128)(2,1)} fusion(bf16[16,128,512]{2,1,0:T(8,128)(2,1)} %bitcast.161, s32[1024]{0:T(1024)S(1)} %pad_clamp_fusion), kind=kCustom, calls=%fused_computation.5 | custom fusion | bytes 4194368 | tf_op jit(solution)/shard_map/gather | solution.py:208
  232.2 3.0 %collective-permute-start.28 = (f32[64,32]{0,1:T(8,128)S(1)}, f32[64,32]{0,1:T(8,128)S(1)}, u32[]{:S(2)}, u32[]{:S(2)}) collective-permute-start(f32[64,32]{0,1:T(8,128)S(1)} %add.270), channel_id=1, source_target_pairs={{0,128},{64,192},{128,0},{192,64},{1,129},{65,193},{129,1},{193,65... | collective-permute-start | bytes 24584 | tf_op jit(solution)/shard_map/ppermute | solution.py:37
  235.2 4.6 %broadcast_select_fusion = (bf16[16,128,512]{2,1,0:T(8,128)(2,1)}, bf16[16,128,512]{2,1,0:T(8,128)(2,1)}) fusion(bf16[16,128,512]{2,1,0:T(8,128)(2,1)} %gather_fusion.5, pred[16]{0:T(512)(128)(4,1)S(1)} %fusion.45, bf16[16,128,512]{2,1,0:T(8,128)(2,1)} %gather_fusion.3), kind=kLoop, calls=%fused_computation.20 | loop fusion | flops 2097152 | bytes 8388624 | tf_op jit(solution)/shard_map/jit(_where)/select_n | solution.py:207
  (242 shorter events, 34.1 us)
Async XLA Ops:
  0.6 11.4 %copy-start = (bf16[18,128,512]{2,1,0:T(8,128)(2,1)S(1)}, bf16[18,128,512]{2,1,0:T(8,128)(2,1)}, u32[]{:S(2)}) copy-start(bf16[18,128,512]{2,1,0:T(8,128)(2,1)} %param.17) | copy-start | bytes 7077892
  1.5 16.2 %collective-permute-start.9 = (f32[64]{0:T(128)S(1)}, f32[64]{0:T(128)S(1)}, u32[]{:S(2)}, u32[]{:S(2)}) collective-permute-start(f32[64]{0:T(128)S(1)} %fusion.39), channel_id=1, source_target_pairs={{0,1},{1,0},{2,3},{3,2},{4,5},{5,4},{6,7},{7,6},{8,9},{9,8},{10,11... | collective-permute-start | bytes 776 | tf_op jit(solution)/shard_map/ppermute | solution.py:37
  2.3 9.7 %copy-start.22 = (pred[18]{0:T(512)(128)(4,1)}, pred[18]{0:T(512)(128)(4,1)S(1)}, u32[]{:S(2)}) copy-start(pred[18]{0:T(512)(128)(4,1)S(1)} %broadcast_compare_fusion) | copy-start | bytes 58
  5.7 6.3 %copy-start.18 = (s32[1024]{0:T(1024)}, s32[1024]{0:T(1024)S(1)}, u32[]{:S(2)}) copy-start(s32[1024]{0:T(1024)S(1)} %pad_clamp_fusion.1) | copy-start | bytes 12292
  7.7 112.4 %collective-permute-start = (bf16[4,2]{0,1:T(2,128)(2,1)}, bf16[4,2]{0,1:T(2,128)(2,1)}, u32[]{:S(2)}, u32[]{:S(2)}) collective-permute-start(bf16[4,2]{0,1:T(2,128)(2,1)} %get-tuple-element.48), channel_id=1, source_target_pairs={{0,1},{1,2},{2,3},{3,4},{4,5},{5,6},{6,7},{7,8},{8,9},{9,10},{10,1... | collective-permute-start | bytes 56 | tf_op jit(solution)/shard_map/ppermute | solution.py:70
  8.2 114.2 %collective-permute-start.1 = (bf16[4,2]{0,1:T(2,128)(2,1)}, bf16[4,2]{0,1:T(2,128)(2,1)}, u32[]{:S(2)}, u32[]{:S(2)}) collective-permute-start(bf16[4,2]{0,1:T(2,128)(2,1)} %get-tuple-element.47), channel_id=1, source_target_pairs={{0,2},{1,3},{2,4},{3,5},{4,6},{5,7},{6,8},{7,9},{8,10},{9,11},{10,... | collective-permute-start | bytes 56 | tf_op jit(solution)/shard_map/ppermute | solution.py:70
  10.1 113.0 %collective-permute-start.2 = (bf16[4,2]{0,1:T(2,128)(2,1)}, bf16[4,2]{0,1:T(2,128)(2,1)}, u32[]{:S(2)}, u32[]{:S(2)}) collective-permute-start(bf16[4,2]{0,1:T(2,128)(2,1)} %get-tuple-element.46), channel_id=1, source_target_pairs={{0,3},{1,4},{2,5},{3,6},{4,7},{5,8},{6,9},{7,10},{8,11},{9,12},{10... | collective-permute-start | bytes 56 | tf_op jit(solution)/shard_map/ppermute | solution.py:70
  14.0 20.4 %copy-start.11 = (bf16[32,3,512]{2,0,1:T(8,128)(2,1)S(1)}, bf16[32,3,512]{2,0,1:T(8,128)(2,1)}, u32[]{:S(2)}) copy-start(bf16[32,3,512]{2,0,1:T(8,128)(2,1)} %param.11) | copy-start | bytes 294916
  14.0 26.7 %copy-start.12 = (f32[18,128]{1,0:T(8,128)S(1)}, f32[18,128]{1,0:T(8,128)}, u32[]{:S(2)}) copy-start(f32[18,128]{1,0:T(8,128)} %param.19) | copy-start | bytes 27652
  14.0 29.4 %copy-start.15 = (bf16[64,32]{0,1:T(8,128)(2,1)S(1)}, bf16[64,32]{0,1:T(8,128)(2,1)}, u32[]{:S(2)}) copy-start(bf16[64,32]{0,1:T(8,128)(2,1)} %param.10) | copy-start | bytes 12292
  16.9 139.8 %collective-permute-start.3 = (bf16[4,128,512]{2,1,0:T(8,128)(2,1)}, bf16[4,128,512]{2,1,0:T(8,128)(2,1)}, u32[]{:S(2)}, u32[]{:S(2)}) collective-permute-start(bf16[4,128,512]{2,1,0:T(8,128)(2,1)} %get-tuple-element.24), channel_id=1, source_target_pairs={{0,1},{1,2},{2,3},{3,4},{4,5},{5,6},{6,7},{7,8},{8,9},{9,10},{10,1... | collective-permute-start | bytes 1572872 | tf_op jit(solution)/shard_map/ppermute | solution.py:70
  17.7 77.9 %copy-start.5 = (pred[64,2304]{1,0:T(8,128)(4,1)}, pred[64,2304]{1,0:T(8,128)(4,1)S(1)}, u32[]{:S(2)}) copy-start(pred[64,2304]{1,0:T(8,128)(4,1)S(1)} %iota_compare_fusion) | copy-start | bytes 442372
  17.7 3.7 %collective-permute-start.10 = (f32[64]{0:T(128)S(1)}, f32[64]{0:T(128)S(1)}, u32[]{:S(2)}, u32[]{:S(2)}) collective-permute-start(f32[64]{0:T(128)S(1)} %add.225), channel_id=1, source_target_pairs={{0,2},{2,0},{4,6},{6,4},{1,3},{3,1},{5,7},{7,5},{8,10},{10,8},{12,... | collective-permute-start | bytes 776 | tf_op jit(solution)/shard_map/ppermute | solution.py:37
  21.4 5.0 %collective-permute-start.11 = (f32[64]{0:T(128)S(1)}, f32[64]{0:T(128)S(1)}, u32[]{:S(2)}, u32[]{:S(2)}) collective-permute-start(f32[64]{0:T(128)S(1)} %add.226), channel_id=1, source_target_pairs={{0,4},{2,6},{4,0},{6,2},{1,5},{3,7},{5,1},{7,3},{8,12},{10,14},{12... | collective-permute-start | bytes 776 | tf_op jit(solution)/shard_map/ppermute | solution.py:37
  26.5 3.5 %collective-permute-start.12 = (f32[64]{0:T(128)S(1)}, f32[64]{0:T(128)S(1)}, u32[]{:S(2)}, u32[]{:S(2)}) collective-permute-start(f32[64]{0:T(128)S(1)} %add.227), channel_id=1, source_target_pairs={{0,8},{8,0},{16,24},{24,16},{32,40},{40,32},{48,56},{56,48},{1,9},... | collective-permute-start | bytes 776 | tf_op jit(solution)/shard_map/ppermute | solution.py:37
  30.0 5.9 %collective-permute-start.13 = (f32[64]{0:T(128)S(1)}, f32[64]{0:T(128)S(1)}, u32[]{:S(2)}, u32[]{:S(2)}) collective-permute-start(f32[64]{0:T(128)S(1)} %add.228), channel_id=1, source_target_pairs={{0,16},{8,24},{16,0},{24,8},{32,48},{40,56},{48,32},{56,40},{1,17}... | collective-permute-start | bytes 776 | tf_op jit(solution)/shard_map/ppermute | solution.py:37
  35.9 7.4 %collective-permute-start.14 = (f32[64]{0:T(128)S(1)}, f32[64]{0:T(128)S(1)}, u32[]{:S(2)}, u32[]{:S(2)}) collective-permute-start(f32[64]{0:T(128)S(1)} %add.229), channel_id=1, source_target_pairs={{0,32},{8,40},{16,48},{24,56},{32,0},{40,8},{48,16},{56,24},{1,33}... | collective-permute-start | bytes 776 | tf_op jit(solution)/shard_map/ppermute | solution.py:37
  43.7 3.0 %collective-permute-start.15 = (f32[65536]{0:T(1024)S(1)}, f32[65536]{0:T(1024)S(1)}, u32[]{:S(2)}, u32[]{:S(2)}) collective-permute-start(f32[65536]{0:T(1024)S(1)} %pad_maximum_fusion.8), channel_id=1, source_target_pairs={{0,1},{1,0},{2,3},{3,2},{4,5},{5,4},{6,7},{7,6},{8,9},{9,8},{10,11... | collective-permute-start | bytes 786440 | tf_op jit(solution)/shard_map/ppermute | solution.py:124
  46.9 6.9 %collective-permute-start.16 = (f32[49152]{0:T(1024)S(1)}, f32[49152]{0:T(1024)S(1)}, u32[]{:S(2)}, u32[]{:S(2)}) collective-permute-start(f32[49152]{0:T(1024)S(1)} %pad_maximum_fusion.9), channel_id=1, source_target_pairs={{0,2},{2,0},{4,6},{6,4},{1,3},{3,1},{5,7},{7,5},{8,10},{10,8},{12,... | collective-permute-start | bytes 589832 | tf_op jit(solution)/shard_map/ppermute | solution.py:124
  56.1 7.0 %collective-permute-start.17 = (f32[40960]{0:T(1024)}, f32[40960]{0:T(1024)S(1)}, u32[]{:S(2)}, u32[]{:S(2)}) collective-permute-start(f32[40960]{0:T(1024)} %pad_maximum_fusion.10), channel_id=1, source_target_pairs={{0,4},{2,6},{4,0},{6,2},{1,5},{3,7},{5,1},{7,3},{8,12},{10,14},{12... | collective-permute-start | bytes 491528 | tf_op jit(solution)/shard_map/ppermute | solution.py:124
  64.9 5.6 %collective-permute-start.18 = (f32[36864]{0:T(1024)S(1)}, f32[36864]{0:T(1024)S(1)}, u32[]{:S(2)}, u32[]{:S(2)}) collective-permute-start(f32[36864]{0:T(1024)S(1)} %pad_maximum_fusion.11), channel_id=1, source_target_pairs={{0,8},{8,0},{16,24},{24,16},{32,40},{40,32},{48,56},{56,48},{1,9},... | collective-permute-start | bytes 442376 | tf_op jit(solution)/shard_map/ppermute | solution.py:124
  70.7 8.1 %collective-permute-start.19 = (f32[34816]{0:T(1024)S(1)}, f32[34816]{0:T(1024)S(1)}, u32[]{:S(2)}, u32[]{:S(2)}) collective-permute-start(f32[34816]{0:T(1024)S(1)} %pad_maximum_fusion.12), channel_id=1, source_target_pairs={{0,16},{8,24},{16,0},{24,8},{32,48},{40,56},{48,32},{56,40},{1,17}... | collective-permute-start | bytes 417800 | tf_op jit(solution)/shard_map/ppermute | solution.py:124
  79.0 9.2 %collective-permute-start.20 = (f32[33792]{0:T(1024)S(1)}, f32[33792]{0:T(1024)S(1)}, u32[]{:S(2)}, u32[]{:S(2)}) collective-permute-start(f32[33792]{0:T(1024)S(1)} %pad_maximum_fusion.13), channel_id=1, source_target_pairs={{0,32},{8,40},{16,48},{24,56},{32,0},{40,8},{48,16},{56,24},{1,33}... | collective-permute-start | bytes 405512 | tf_op jit(solution)/shard_map/ppermute | solution.py:124
  83.7 6.6 %copy-start.19 = (pred[8,8]{1,0:T(8,128)(4,1)}, pred[8,8]{1,0:T(8,128)(4,1)S(1)}, u32[]{:S(2)}) copy-start(pred[8,8]{1,0:T(8,128)(4,1)S(1)} %iota_compare_fusion.5) | copy-start | bytes 196
  95.6 5.0 %copy-start.7 = (bf16[64,8,512]{2,1,0:T(8,128)(2,1)S(1)}, bf16[64,8,512]{2,1,0:T(8,128)(2,1)}, u32[]{:S(2)}) copy-start(bf16[64,8,512]{2,1,0:T(8,128)(2,1)} %broadcast_in_dim.215) | copy-start | bytes 1572868
  95.6 5.0 %copy-start.13 = (pred[64,19]{1,0:T(8,128)(4,1)S(1)}, pred[64,19]{1,0:T(8,128)(4,1)}, u32[]{:S(2)}) copy-start(pred[64,19]{1,0:T(8,128)(4,1)} %iota_compare_fusion.1) | copy-start | bytes 3652
  95.6 5.0 %copy-start.17 = (bf16[18,512]{1,0:T(8,128)(2,1)S(1)}, bf16[18,512]{1,0:T(8,128)(2,1)}, u32[]{:S(2)}) copy-start(bf16[18,512]{1,0:T(8,128)(2,1)} %get-tuple-element.39) | copy-start | bytes 55300
  95.6 5.0 %copy-start.23 = (pred[8,512]{1,0:T(8,128)(4,1)S(1)}, pred[8,512]{1,0:T(8,128)(4,1)}, u32[]{:S(2)}) copy-start(pred[8,512]{1,0:T(8,128)(4,1)} %broadcast_in_dim.213) | copy-start | bytes 12292
  95.7 5.0 %copy-start.24 = (bf16[1,512]{1,0:T(2,128)(2,1)S(1)}, bf16[1,512]{1,0:T(2,128)(2,1)}, u32[]{:S(2)}) copy-start(bf16[1,512]{1,0:T(2,128)(2,1)} %convert_element_type.83) | copy-start | bytes 3076
  95.7 5.0 %copy-start.26 = (f32[19]{0:T(128)S(1)}, f32[19]{0:T(128)}, u32[]{:S(2)}) copy-start(f32[19]{0:T(128)} %constant.182.clone.1) | copy-start | bytes 232
  101.1 7.7 %copy-start.4 = (f32[64,8,19]{2,1,0:T(8,128)}, f32[64,8,19]{2,1,0:T(8,128)S(1)}, u32[]{:S(2)}) copy-start(f32[64,8,19]{2,1,0:T(8,128)S(1)} %get-tuple-element.56) | copy-start | bytes 116740
  115.5 9.5 %collective-permute-start.21 = (f32[64,8,66]{0,1,2:T(8,128)}, f32[64,8,66]{0,1,2:T(8,128)S(1)}, u32[]{:S(2)}, u32[]{:S(2)}) collective-permute-start(f32[64,8,66]{0,1,2:T(8,128)} %pad_maximum_fusion.2), channel_id=1, source_target_pairs={{0,8},{8,0},{16,24},{24,16},{32,40},{40,32},{48,56},{56,48},{1,9},... | collective-permute-start | bytes 405512 | tf_op jit(solution)/shard_map/ppermute | solution.py:37
  120.2 39.7 %copy-start.2 = (bf16[1,4,128,512]{3,2,1,0:T(8,128)(2,1)S(1)}, bf16[1,4,128,512]{3,2,1,0:T(8,128)(2,1)}, u32[]{:S(2)}) copy-start(bf16[1,4,128,512]{3,2,1,0:T(8,128)(2,1)} %get-tuple-element.22) | copy-start | bytes 1572868
  120.2 36.7 %collective-permute-start.4 = (bf16[4,128,512]{2,1,0:T(8,128)(2,1)}, bf16[4,128,512]{2,1,0:T(8,128)(2,1)}, u32[]{:S(2)}, u32[]{:S(2)}) collective-permute-start(bf16[4,128,512]{2,1,0:T(8,128)(2,1)} %get-tuple-element.23), channel_id=1, source_target_pairs={{0,2},{1,3},{2,4},{3,5},{4,6},{5,7},{6,8},{7,9},{8,10},{9,11},{10,... | collective-permute-start | bytes 1572872 | tf_op jit(solution)/shard_map/ppermute | solution.py:70
  122.4 37.4 %collective-permute-start.5 = (bf16[4,128,512]{2,1,0:T(8,128)(2,1)}, bf16[4,128,512]{2,1,0:T(8,128)(2,1)}, u32[]{:S(2)}, u32[]{:S(2)}) collective-permute-start(bf16[4,128,512]{2,1,0:T(8,128)(2,1)} %get-tuple-element.25), channel_id=1, source_target_pairs={{0,3},{1,4},{2,5},{3,6},{4,7},{5,8},{6,9},{7,10},{8,11},{9,12},{10... | collective-permute-start | bytes 1572872 | tf_op jit(solution)/shard_map/ppermute | solution.py:70
  123.1 73.0 %collective-permute-start.6 = (bf16[4,128,512]{2,1,0:T(8,128)(2,1)}, bf16[4,128,512]{2,1,0:T(8,128)(2,1)}, u32[]{:S(2)}, u32[]{:S(2)}) collective-permute-start(bf16[4,128,512]{2,1,0:T(8,128)(2,1)} %get-tuple-element.20), channel_id=1, source_target_pairs={{0,1},{1,2},{2,3},{3,4},{4,5},{5,6},{6,7},{7,8},{8,9},{9,10},{10,1... | collective-permute-start | bytes 1572872 | tf_op jit(solution)/shard_map/ppermute | solution.py:70
  125.0 31.8 %copy-start.8 = (bf16[4,128,512]{2,1,0:T(8,128)(2,1)S(1)}, bf16[4,128,512]{2,1,0:T(8,128)(2,1)}, u32[]{:S(2)}) copy-start(bf16[4,128,512]{2,1,0:T(8,128)(2,1)} %get-tuple-element.21) | copy-start | bytes 1572868
  125.1 31.6 %collective-permute-start.22 = (f32[64,8,66]{0,1,2:T(8,128)S(1)}, f32[64,8,66]{0,1,2:T(8,128)S(1)}, u32[]{:S(2)}, u32[]{:S(2)}) collective-permute-start(f32[64,8,66]{0,1,2:T(8,128)S(1)} %pad_maximum_fusion.3), channel_id=1, source_target_pairs={{0,16},{8,24},{16,0},{24,8},{32,48},{40,56},{48,32},{56,40},{1,17}... | collective-permute-start | bytes 405512 | tf_op jit(solution)/shard_map/ppermute | solution.py:37
  156.7 39.4 %collective-permute-start.7 = (bf16[4,128,512]{2,1,0:T(8,128)(2,1)}, bf16[4,128,512]{2,1,0:T(8,128)(2,1)S(1)}, u32[]{:S(2)}, u32[]{:S(2)}) collective-permute-start(bf16[4,128,512]{2,1,0:T(8,128)(2,1)} %get-tuple-element.19), channel_id=1, source_target_pairs={{0,2},{1,3},{2,4},{3,5},{4,6},{5,7},{6,8},{7,9},{8,10},{9,11},{10,... | collective-permute-start | bytes 1572872 | tf_op jit(solution)/shard_map/ppermute | solution.py:70
  156.8 39.3 %collective-permute-start.8 = (bf16[4,128,512]{2,1,0:T(8,128)(2,1)S(1)}, bf16[4,128,512]{2,1,0:T(8,128)(2,1)S(1)}, u32[]{:S(2)}, u32[]{:S(2)}) collective-permute-start(bf16[4,128,512]{2,1,0:T(8,128)(2,1)S(1)} %copy-done.8), channel_id=1, source_target_pairs={{0,3},{1,4},{2,5},{3,6},{4,7},{5,8},{6,9},{7,10},{8,11},{9,12},{10... | collective-permute-start | bytes 1572872 | tf_op jit(solution)/shard_map/ppermute | solution.py:70
  156.9 37.6 %collective-permute-start.23 = (f32[64,8,66]{0,1,2:T(8,128)S(1)}, f32[64,8,66]{0,1,2:T(8,128)S(1)}, u32[]{:S(2)}, u32[]{:S(2)}) collective-permute-start(f32[64,8,66]{0,1,2:T(8,128)S(1)} %pad_maximum_fusion.4), channel_id=1, source_target_pairs={{0,32},{8,40},{16,48},{24,56},{32,0},{40,8},{48,16},{56,24},{1,33}... | collective-permute-start | bytes 405512 | tf_op jit(solution)/shard_map/ppermute | solution.py:37
  159.9 36.2 %copy-start.3 = (bf16[1,4,128,512]{3,2,1,0:T(8,128)(2,1)S(1)}, bf16[1,4,128,512]{3,2,1,0:T(8,128)(2,1)}, u32[]{:S(2)}) copy-start(bf16[1,4,128,512]{3,2,1,0:T(8,128)(2,1)} %get-tuple-element.18) | copy-start | bytes 1572868
  194.6 4.1 %collective-permute-start.24 = (f32[64,8,66]{0,1,2:T(8,128)S(1)}, f32[64,8,66]{0,1,2:T(8,128)S(1)}, u32[]{:S(2)}, u32[]{:S(2)}) collective-permute-start(f32[64,8,66]{0,1,2:T(8,128)S(1)} %pad_maximum_fusion.5), channel_id=1, source_target_pairs={{0,1},{1,0},{2,3},{3,2},{4,5},{5,4},{6,7},{7,6},{8,9},{9,8},{10,11... | collective-permute-start | bytes 405512 | tf_op jit(solution)/shard_map/ppermute | solution.py:37
  198.8 24.5 %copy-start.16 = (bf16[512,32]{0,1:T(8,128)(2,1)S(1)}, bf16[512,32]{0,1:T(8,128)(2,1)}, u32[]{:S(2)}) copy-start(bf16[512,32]{0,1:T(8,128)(2,1)} %param.12) | copy-start | bytes 98308
  198.8 8.5 %collective-permute-start.25 = (f32[64,8,66]{0,1,2:T(8,128)S(1)}, f32[64,8,66]{0,1,2:T(8,128)S(1)}, u32[]{:S(2)}, u32[]{:S(2)}) collective-permute-start(f32[64,8,66]{0,1,2:T(8,128)S(1)} %pad_maximum_fusion.6), channel_id=1, source_target_pairs={{0,2},{2,0},{4,6},{6,4},{1,3},{3,1},{5,7},{7,5},{8,10},{10,8},{12,... | collective-permute-start | bytes 405512 | tf_op jit(solution)/shard_map/ppermute | solution.py:37
  207.4 15.5 %collective-permute-start.26 = (f32[64,8,66]{0,1,2:T(8,128)S(1)}, f32[64,8,66]{0,1,2:T(8,128)S(1)}, u32[]{:S(2)}, u32[]{:S(2)}) collective-permute-start(f32[64,8,66]{0,1,2:T(8,128)S(1)} %pad_maximum_fusion.7), channel_id=1, source_target_pairs={{0,4},{2,6},{4,0},{6,2},{1,5},{3,7},{5,1},{7,3},{8,12},{10,14},{12... | collective-permute-start | bytes 405512 | tf_op jit(solution)/shard_map/ppermute | solution.py:37
  223.4 8.8 %collective-permute-start.27 = (f32[64,32]{0,1:T(8,128)S(1)}, f32[64,32]{0,1:T(8,128)S(1)}, u32[]{:S(2)}, u32[]{:S(2)}) collective-permute-start(f32[64,32]{0,1:T(8,128)S(1)} %fusion.70), channel_id=1, source_target_pairs={{0,64},{64,0},{128,192},{192,128},{1,65},{65,1},{129,193},{193,129... | collective-permute-start | bytes 24584 | tf_op jit(solution)/shard_map/ppermute | solution.py:37
  232.2 7.5 %collective-permute-start.28 = (f32[64,32]{0,1:T(8,128)S(1)}, f32[64,32]{0,1:T(8,128)S(1)}, u32[]{:S(2)}, u32[]{:S(2)}) collective-permute-start(f32[64,32]{0,1:T(8,128)S(1)} %add.270), channel_id=1, source_target_pairs={{0,128},{64,192},{128,0},{192,64},{1,129},{65,193},{129,1},{193,65... | collective-permute-start | bytes 24584 | tf_op jit(solution)/shard_map/ppermute | solution.py:37
  (8 other events, 27.0 us)

commit v10 on v7

--- a/solution.py
+++ b/solution.py
@@ -109,6 +109,60 @@
     normed = (widened * lax.rsqrt(total_sq / D + NORM_EPSILON)[:, None]).astype(jnp.bfloat16)
     partial_value = jnp.dot(
         normed, w_qkv.reshape(w_qkv.shape[0], 3 * feat_width), preferred_element_type=jnp.float32
+    )
+    block_ids = jnp.arange(n_blocks, dtype=jnp.int32)
+    global_ids = my_index * n_blocks + block_ids
+    req_ends = jnp.cumsum(req_blocks)
+    blk_req = jnp.sum((global_ids[:, None] >= req_ends[None, :]).astype(jnp.int32), axis=1)
+    is_kept = keep_list == 1
+
+    weight_sum = jnp.sum(fold_weight, axis=1)
+    fold_keys = jnp.einsum(
+        "bi,bif->bf",
+        fold_weight,
+        key_cache,
+        preferred_element_type=jnp.float32,
+        precision=lax.Precision.HIGHEST,
+    )
+    fold_values = jnp.einsum(
+        "bi,bif->bf",
+        fold_weight,
+        value_cache,
+        preferred_element_type=jnp.float32,
+        precision=lax.Precision.HIGHEST,
+    )
+    folded_keys = jnp.where(is_kept[:, None], 0.0, fold_keys / weight_sum[:, None]).astype(
+        jnp.bfloat16
+    )
+    folded_values = jnp.where(is_kept[:, None], 0.0, fold_values / weight_sum[:, None]).astype(
+        jnp.bfloat16
+    )
+
+    owners = dest_slot // SLOT_DEV
+    local_slot = dest_slot % SLOT_DEV
+    hop_of = (owners - my_index) % seq_count
+    earlier = (
+        is_kept[None, :]
+        & is_kept[:, None]
+        & (hop_of[None, :] == hop_of[:, None])
+        & (block_ids[None, :] < block_ids[:, None])
+    )
+    placed = jnp.sum(earlier.astype(jnp.int32), axis=1)
+    arrivals = HOPS * CAP
+    send_pos = jnp.where(is_kept, hop_of * CAP + placed, arrivals)
+    targets = jnp.arange(arrivals, dtype=jnp.int32)
+    hit_table = send_pos[None, :] == targets[:, None]
+    has_block = jnp.any(hit_table, axis=1)
+    source = jnp.sum(jnp.where(hit_table, block_ids[None, :], 0), axis=1)
+    send_keys = key_cache[source].reshape(HOPS, CAP, row_count, feat_width)
+    send_values = value_cache[source].reshape(HOPS, CAP, row_count, feat_width)
+    meta_data = jnp.stack(
+        [jnp.where(has_block, local_slot[source], -1), jnp.where(has_block, blk_req[source], -1)],
+        axis=-1,
+    )
+    meta_data = meta_data.astype(jnp.float32).astype(jnp.bfloat16).reshape(HOPS, CAP, 2)
+    send_keys, send_values, meta_data, partial_value = lax.optimization_barrier(
+        (send_keys, send_values, meta_data, partial_value)
     )
     query_sum = partial_value[:, :feat_width]
     key_values = partial_value[:, feat_width:]
@@ -136,57 +190,6 @@
     ).astype(jnp.bfloat16)
     own_value = key_values[:, feat_width:].reshape(-1, heads_here, HDIM).astype(jnp.bfloat16)
 
-    block_ids = jnp.arange(n_blocks, dtype=jnp.int32)
-    global_ids = my_index * n_blocks + block_ids
-    req_ends = jnp.cumsum(req_blocks)
-    blk_req = jnp.sum((global_ids[:, None] >= req_ends[None, :]).astype(jnp.int32), axis=1)
-    is_kept = keep_list == 1
-
-    weight_sum = jnp.sum(fold_weight, axis=1)
-    fold_keys = jnp.einsum(
-        "bi,bif->bf",
-        fold_weight,
-        key_cache,
-        preferred_element_type=jnp.float32,
-        precision=lax.Precision.HIGHEST,
-    )
-    fold_values = jnp.einsum(
-        "bi,bif->bf",
-        fold_weight,
-        value_cache,
-        preferred_element_type=jnp.float32,
-        precision=lax.Precision.HIGHEST,
-    )
-    folded_keys = jnp.where(is_kept[:, None], 0.0, fold_keys / weight_sum[:, None]).astype(
-        jnp.bfloat16
-    )
-    folded_values = jnp.where(is_kept[:, None], 0.0, fold_values / weight_sum[:, None]).astype(
-        jnp.bfloat16
-    )
-
-    owners = dest_slot // SLOT_DEV
-    local_slot = dest_slot % SLOT_DEV
-    hop_of = (owners - my_index) % seq_count
-    earlier = (
-        is_kept[None, :]
-        & is_kept[:, None]
-        & (hop_of[None, :] == hop_of[:, None])
-        & (block_ids[None, :] < block_ids[:, None])
-    )
-    placed = jnp.sum(earlier.astype(jnp.int32), axis=1)
-    arrivals = HOPS * CAP
-    send_pos = jnp.where(is_kept, hop_of * CAP + placed, arrivals)
-    targets = jnp.arange(arrivals, dtype=jnp.int32)
-    hit_table = send_pos[None, :] == targets[:, None]
-    has_block = jnp.any(hit_table, axis=1)
-    source = jnp.sum(jnp.where(hit_table, block_ids[None, :], 0), axis=1)
-    send_keys = key_cache[source].reshape(HOPS, CAP, row_count, feat_width)
-    send_values = value_cache[source].reshape(HOPS, CAP, row_count, feat_width)
-    meta_data = jnp.stack(
-        [jnp.where(has_block, local_slot[source], -1), jnp.where(has_block, blk_req[source], -1)],
-        axis=-1,
-    )
-    meta_data = meta_data.astype(jnp.float32).astype(jnp.bfloat16).reshape(HOPS, CAP, 2)
     arrived = [(send_keys[0], send_values[0], meta_data[0])]
     for distance in range(1, HOPS):
         arrived.append(

time: 239 us -> 235 us (0.983)
  the two profiles are of different devices: /device:TPU:97 before, /device:TPU:65 now
where the time goes in v10:
time: 235 us
  starting transfers between devices  91.3 us (39%)
  waiting for transfers between devices  61.8 us (26%)
  local copies, waits for them, and re-layouts  32.4 us (14%)
  other arithmetic  32 us (14%)
  matrix products  15.9 us (7%)
    ppermute x14, waiting for transfers between devices, butterfly(): x = merge(x, lax.ppermute(x, axis, pairs))  48.6 us
    ppermute x9, starting transfers between devices, passed_along(): lax.ppermute(array, SEQ_PARTS, [(i, (i + by) % count) for i in range(coun...  47.6 us
    ppermute x14, starting transfers between devices, butterfly(): x = merge(x, lax.ppermute(x, axis, pairs))  30.3 us
    ppermute x6, starting transfers between devices, shards(): payload = lax.ppermute(payload, axis, pairs)  13.4 us
    ppermute x6, waiting for transfers between devices, shards(): payload = lax.ppermute(payload, axis, pairs)  13.2 us
    dot_general x2, matrix products, weighted_of(): jnp.dot(expo.astype(jnp.bfloat16).reshape(requests * heads_here, -1), val...  6.5 us
    dot_general x2, matrix products, scores_of(): lax.dot_general(spread_queries, keys, (((1,), (1,)), ((), ())), preferred...  5.34 us
  transfers between devices with their start and end apart: 29, of which 14 were waited for; matrix products, arithmetic and copies ran while one was open for 33% of the time, Pallas kernels for 0%

profile of v10, /device:TPU:65, one launch (start us, length us, event | category | flops | bytes accessed | tf_op | source)
XLA Modules:
  0.0 234.8 jit_solution(12665312442856969673)
XLA Ops:
  9.2 2.7 %fusion.53 = f32[18,1,512]{2,1,0:T(1,128)S(1)} fusion(bf16[18,128,512]{2,1,0:T(8,128)(2,1)} %param.18, f32[18,128,1]{1,0,2:T(8,128)} %bitcast.191), kind=kOutput, calls=%fused_computation.157 | convolution fusion | flops 14155776 | bytes 2405376 | tf_op jit(solution)/shard_map/bi,bif->bf/dot_general | solution.py:127
  14.4 2.7 %collective-permute-start.2 = (f32[64]{0:T(128)S(1)}, f32[64]{0:T(128)S(1)}, u32[]{:S(2)}, u32[]{:S(2)}) collective-permute-start(f32[64]{0:T(128)S(1)} %add.225), channel_id=1, source_target_pairs={{0,4},{2,6},{4,0},{6,2},{1,5},{3,7},{5,1},{7,3},{8,12},{10,14},{12... | collective-permute-start | bytes 776 | tf_op jit(solution)/shard_map/ppermute | solution.py:37
  17.2 3.7 %gather_fusion.1 = bf16[16,128,512]{2,1,0:T(8,128)(2,1)} fusion(bf16[18,128,512]{2,1,0:T(8,128)(2,1)} %param.18, s32[1024]{0:T(1024)S(1)} %pad_clamp_fusion.1), kind=kCustom, calls=%fused_computation.1 | custom fusion | bytes 4194368 | tf_op jit(solution)/shard_map/gather | solution.py:158
  20.9 1.6 collective-permute-start.3
  24.7 2.1 collective-permute-done.4
  26.7 4.9 %collective-permute-start.5 = (f32[64]{0:T(128)S(1)}, f32[64]{0:T(128)S(1)}, u32[]{:S(2)}, u32[]{:S(2)}) collective-permute-start(f32[64]{0:T(128)S(1)} %add.228), channel_id=1, source_target_pairs={{0,32},{8,40},{16,48},{24,56},{32,0},{40,8},{48,16},{56,24},{1,33}... | collective-permute-start | bytes 776 | tf_op jit(solution)/shard_map/ppermute | solution.py:37
  31.7 2.0 gather_fusion
  34.1 4.1 %collective-permute-start.15 = (f32[65536]{0:T(1024)S(1)}, f32[65536]{0:T(1024)S(1)}, u32[]{:S(2)}, u32[]{:S(2)}) collective-permute-start(f32[65536]{0:T(1024)S(1)} %pad_maximum_fusion.8), channel_id=1, source_target_pairs={{0,1},{1,0},{2,3},{3,2},{4,5},{5,4},{6,7},{7,6},{8,9},{9,8},{10,11... | collective-permute-start | bytes 786440 | tf_op jit(solution)/shard_map/ppermute | solution.py:178
  40.1 1.4 fusion.31
  41.4 4.4 %collective-permute-done.16 = f32[49152]{0:T(1024)S(1)} collective-permute-done((f32[49152]{0:T(1024)S(1)}, f32[49152]{0:T(1024)S(1)}, u32[]{:S(2)}, u32[]{:S(2)}) %collective-permute-start.16) | collective-permute-done | bytes 196640 | tf_op jit(solution)/shard_map/ppermute | solution.py:178
  47.8 1.5 multiply_cosine_fusion
  50.0 2.9 %collective-permute-done.17 = f32[40960]{0:T(1024)S(1)} collective-permute-done((f32[40960]{0:T(1024)}, f32[40960]{0:T(1024)S(1)}, u32[]{:S(2)}, u32[]{:S(2)}) %collective-permute-start.17) | collective-permute-done | bytes 163872 | tf_op jit(solution)/shard_map/ppermute | solution.py:178
  53.2 1.7 collective-permute-start.18
  54.9 2.5 %collective-permute-done.18 = f32[36864]{0:T(1024)S(1)} collective-permute-done((f32[36864]{0:T(1024)S(1)}, f32[36864]{0:T(1024)S(1)}, u32[]{:S(2)}, u32[]{:S(2)}) %collective-permute-start.18) | collective-permute-done | bytes 147488 | tf_op jit(solution)/shard_map/ppermute | solution.py:178
  59.5 3.1 %collective-permute-done.19 = f32[34816]{0:T(1024)S(1)} collective-permute-done((f32[34816]{0:T(1024)S(1)}, f32[34816]{0:T(1024)S(1)}, u32[]{:S(2)}, u32[]{:S(2)}) %collective-permute-start.19) | collective-permute-done | bytes 139296 | tf_op jit(solution)/shard_map/ppermute | solution.py:178
  62.8 5.0 %collective-permute-start.20 = (f32[33792]{0:T(1024)S(1)}, f32[33792]{0:T(1024)S(1)}, u32[]{:S(2)}, u32[]{:S(2)}) collective-permute-start(f32[33792]{0:T(1024)S(1)} %pad_maximum_fusion.13), channel_id=1, source_target_pairs={{0,32},{8,40},{16,48},{24,56},{32,0},{40,8},{48,16},{56,24},{1,33}... | collective-permute-start | bytes 405512 | tf_op jit(solution)/shard_map/ppermute | solution.py:178
  70.1 4.9 %collective-permute-start.6 = (bf16[4,2]{0,1:T(2,128)(2,1)}, bf16[4,2]{0,1:T(2,128)(2,1)}, u32[]{:S(2)}, u32[]{:S(2)}) collective-permute-start(bf16[4,2]{0,1:T(2,128)(2,1)} %bitcast.170), channel_id=1, source_target_pairs={{0,1},{1,2},{2,3},{3,4},{4,5},{5,6},{6,7},{7,8},{8,9},{9,10},{10,1... | collective-permute-start | bytes 56 | tf_op jit(solution)/shard_map/ppermute | solution.py:70
  75.4 1.6 collective-permute-start.8
  79.2 1.4 select_n.322
  80.8 1.4 broadcast_in_dim.215
  82.3 5.0 %fusion.71 = (f32[64,8]{1,0:T(8,128)S(1)}, f32[64,8,2304]{2,1,0:T(8,128)}) fusion(bf16[64,8,512]{2,1,0:T(8,128)(2,1)} %select_n.322, bf16[2304,512,1]{1,0,2:T(8,128)(2,1)S(1)} %bitcast.171, pred[64,2304]{1,0:T(8,128)(4,1)} %iota_compare_fusion), kind=kOutput, calls=%fused_computation.206 | convolution fusion | flops 1211497984 | bytes 7751680 | tf_op jit(solution)/shard_map/dot_general | solution.py:236
  88.0 3.8 %fusion.1 = f32[64,8]{1,0:T(8,128)S(1)} fusion(f32[64,8,2304]{2,1,0:T(8,128)} %get-tuple-element.60, f32[64,8]{1,0:T(8,128)S(1)} %max.32, pred[64,2304]{1,0:T(8,128)(4,1)S(1)} %copy-done.5), kind=kLoop, calls=%fused_computation.10 | loop fusion | flops 3538432 | bytes 4870144 | tf_op jit(solution)/shard_map/reduce_sum | solution.py:246
  91.8 4.8 %fusion.4 = f32[512,512]{1,0:T(8,128)} fusion(bf16[2304,512]{1,0:T(8,128)(2,1)S(1)} %bitcast.172, f32[64,8,2304]{2,1,0:T(8,128)} %get-tuple-element.60, f32[64,8]{1,0:T(8,128)S(1)} %max.32, pred[64,2304]{1,0:T(8,128)(4,1)S(1)} %copy-done.5), kind=kOutput, calls=%fused_computation.13 | convolution fusion | flops 1211498496 | bytes 8275968 | tf_op jit(solution)/shard_map/dot_general | solution.py:249
  96.7 1.7 convolution_add_fusion
  98.4 1.7 reshape.524
  100.1 2.3 select_reduce_fusion
  102.7 3.7 %collective-permute-start.21 = (f32[64,8,66]{0,1,2:T(8,128)S(1)}, f32[64,8,66]{0,1,2:T(8,128)S(1)}, u32[]{:S(2)}, u32[]{:S(2)}) collective-permute-start(f32[64,8,66]{0,1,2:T(8,128)S(1)} %pad_maximum_fusion.2), channel_id=1, source_target_pairs={{0,8},{8,0},{16,24},{24,16},{32,40},{40,32},{48,56},{56,48},{1,9},... | collective-permute-start | bytes 405512 | tf_op jit(solution)/shard_map/ppermute | solution.py:37
  106.3 2.9 %fusion.68 = (bf16[1,4,128,512]{3,2,1,0:T(8,128)(2,1)}, bf16[4,128,512]{2,1,0:T(8,128)(2,1)}, bf16[4,128,512]{2,1,0:T(8,128)(2,1)}, bf16[4,128,512]{2,1,0:T(8,128)(2,1)}) fusion(bf16[4,4,128,512]{3,2,1,0:T(8,128)(2,1)} %bitcast.174), kind=kLoop, calls=%fused_computation.203 | loop fusion | bytes 4194304 | tf_op jit(solution)/shard_map/slice | solution.py:193
  109.2 1.9 collective-permute-start.11
  111.1 2.1 collective-permute-done.21
  115.6 1.4 collective-permute-start.10
  117.6 1.3 collective-permute-start.9
  121.3 4.6 %collective-permute-done.22 = f32[64,8,66]{0,1,2:T(8,128)S(1)} collective-permute-done((f32[64,8,66]{0,1,2:T(8,128)}, f32[64,8,66]{0,1,2:T(8,128)S(1)}, u32[]{:S(2)}, u32[]{:S(2)}) %collective-permute-start.22) | collective-permute-done | bytes 135200 | tf_op jit(solution)/shard_map/ppermute | solution.py:37
  126.1 1.7 collective-permute-start.23
  127.9 9.0 %collective-permute-done.23 = f32[64,8,66]{0,1,2:T(8,128)S(1)} collective-permute-done((f32[64,8,66]{0,1,2:T(8,128)S(1)}, f32[64,8,66]{0,1,2:T(8,128)S(1)}, u32[]{:S(2)}, u32[]{:S(2)}) %collective-permute-start.23) | collective-permute-done | bytes 135200 | tf_op jit(solution)/shard_map/ppermute | solution.py:37
  137.7 3.1 %collective-permute-start.24 = (f32[64,8,66]{0,1,2:T(8,128)}, f32[64,8,66]{0,1,2:T(8,128)S(1)}, u32[]{:S(2)}, u32[]{:S(2)}) collective-permute-start(f32[64,8,66]{0,1,2:T(8,128)} %pad_maximum_fusion.5), channel_id=1, source_target_pairs={{0,1},{1,0},{2,3},{3,2},{4,5},{5,4},{6,7},{7,6},{8,9},{9,8},{10,11... | collective-permute-start | bytes 405512 | tf_op jit(solution)/shard_map/ppermute | solution.py:37
  142.2 6.1 %collective-permute-start.25 = (f32[64,8,66]{0,1,2:T(8,128)S(1)}, f32[64,8,66]{0,1,2:T(8,128)S(1)}, u32[]{:S(2)}, u32[]{:S(2)}) collective-permute-start(f32[64,8,66]{0,1,2:T(8,128)S(1)} %pad_maximum_fusion.6), channel_id=1, source_target_pairs={{0,2},{2,0},{4,6},{6,4},{1,3},{3,1},{5,7},{7,5},{8,10},{10,8},{12,... | collective-permute-start | bytes 405512 | tf_op jit(solution)/shard_map/ppermute | solution.py:37
  148.8 7.9 %collective-permute-done.25 = f32[64,8,66]{0,1,2:T(8,128)S(1)} collective-permute-done((f32[64,8,66]{0,1,2:T(8,128)S(1)}, f32[64,8,66]{0,1,2:T(8,128)S(1)}, u32[]{:S(2)}, u32[]{:S(2)}) %collective-permute-start.25) | collective-permute-done | bytes 135200 | tf_op jit(solution)/shard_map/ppermute | solution.py:37
  156.7 1.9 collective-permute-start.13
  158.7 33.0 %collective-permute-start.12 = (bf16[4,128,512]{2,1,0:T(8,128)(2,1)}, bf16[4,128,512]{2,1,0:T(8,128)(2,1)}, u32[]{:S(2)}, u32[]{:S(2)}) collective-permute-start(bf16[4,128,512]{2,1,0:T(8,128)(2,1)} %get-tuple-element.27), channel_id=1, source_target_pairs={{0,1},{1,2},{2,3},{3,4},{4,5},{5,6},{6,7},{7,8},{8,9},{9,10},{10,1... | collective-permute-start | bytes 1572872 | tf_op jit(solution)/shard_map/ppermute | solution.py:70
  191.7 2.9 %pad_maximum_fusion = bf16[4,4,128,512]{3,2,1,0:T(8,128)(2,1)} fusion(bf16[1,4,128,512]{3,2,1,0:T(8,128)(2,1)} %bitcast.14, bf16[1,4,128,512]{3,2,1,0:T(8,128)(2,1)} %bitcast.12, bf16[1,4,128,512]{3,2,1,0:T(8,128)(2,1)} %bitcast.10, bf16[1,4,128,512]{3,2,1,0:T(8,128)(2,1)S(1)} %copy-done.3), kind=kLoop, calls=%fused_computation.17 | loop fusion | flops 3145728 | bytes 4194304 | tf_op jit(solution)/shard_map/stack | solution.py:198
  194.6 20.3 %collective-permute-done.26 = f32[64,8,66]{0,1,2:T(8,128)S(1)} collective-permute-done((f32[64,8,66]{0,1,2:T(8,128)S(1)}, f32[64,8,66]{0,1,2:T(8,128)S(1)}, u32[]{:S(2)}, u32[]{:S(2)}) %collective-permute-start.26) | collective-permute-done | bytes 135200 | tf_op jit(solution)/shard_map/ppermute | solution.py:37
  215.4 1.3 collective-permute-start.27
  216.8 2.9 %pad_maximum_fusion.1 = bf16[4,4,128,512]{3,2,1,0:T(8,128)(2,1)} fusion(bf16[1,4,128,512]{3,2,1,0:T(8,128)(2,1)} %bitcast.23, bf16[1,4,128,512]{3,2,1,0:T(8,128)(2,1)} %bitcast.21, bf16[1,4,128,512]{3,2,1,0:T(8,128)(2,1)} %bitcast.19, bf16[1,4,128,512]{3,2,1,0:T(8,128)(2,1)S(1)} %get-tuple-element.24), kind=kLoop, calls=%fused_computation.18 | loop fusion | flops 3145728 | bytes 4194304 | tf_op jit(solution)/shard_map/stack | solution.py:199
  219.7 3.6 %gather_fusion.4 = bf16[16,128,512]{2,1,0:T(8,128)(2,1)} fusion(bf16[16,128,512]{2,1,0:T(8,128)(2,1)} %bitcast.175, s32[1024]{0:T(1024)S(1)} %pad_clamp_fusion), kind=kCustom, calls=%fused_computation.4 | custom fusion | bytes 4194368 | tf_op jit(solution)/shard_map/gather | solution.py:209
  223.3 3.6 %gather_fusion.5 = bf16[16,128,512]{2,1,0:T(8,128)(2,1)} fusion(bf16[16,128,512]{2,1,0:T(8,128)(2,1)} %bitcast.176, s32[1024]{0:T(1024)S(1)} %pad_clamp_fusion), kind=kCustom, calls=%fused_computation.5 | custom fusion | bytes 4194368 | tf_op jit(solution)/shard_map/gather | solution.py:211
  226.9 2.7 %collective-permute-start.28 = (f32[64,32]{0,1:T(8,128)S(1)}, f32[64,32]{0,1:T(8,128)S(1)}, u32[]{:S(2)}, u32[]{:S(2)}) collective-permute-start(f32[64,32]{0,1:T(8,128)S(1)} %add.270), channel_id=1, source_target_pairs={{0,128},{64,192},{128,0},{192,64},{1,129},{65,193},{129,1},{193,65... | collective-permute-start | bytes 24584 | tf_op jit(solution)/shard_map/ppermute | solution.py:37
  229.6 4.6 %broadcast_select_fusion = (bf16[16,128,512]{2,1,0:T(8,128)(2,1)}, bf16[16,128,512]{2,1,0:T(8,128)(2,1)}) fusion(bf16[16,128,512]{2,1,0:T(8,128)(2,1)} %gather_fusion.5, pred[16]{0:T(512)(128)(4,1)S(1)} %fusion.44, bf16[16,128,512]{2,1,0:T(8,128)(2,1)} %gather_fusion.4), kind=kLoop, calls=%fused_computation.20 | loop fusion | flops 2097152 | bytes 8388624 | tf_op jit(solution)/shard_map/jit(_where)/select_n | solution.py:210
  (232 shorter events, 35.7 us)
Async XLA Ops:
  0.6 31.1 %copy-start = (bf16[18,128,512]{2,1,0:T(8,128)(2,1)S(1)}, bf16[18,128,512]{2,1,0:T(8,128)(2,1)}, u32[]{:S(2)}) copy-start(bf16[18,128,512]{2,1,0:T(8,128)(2,1)} %param.17) | copy-start | bytes 7077892
  1.5 10.4 %collective-permute-start = (f32[64]{0:T(128)S(1)}, f32[64]{0:T(128)S(1)}, u32[]{:S(2)}, u32[]{:S(2)}) collective-permute-start(f32[64]{0:T(128)S(1)} %fusion.39), channel_id=1, source_target_pairs={{0,1},{1,0},{2,3},{3,2},{4,5},{5,4},{6,7},{7,6},{8,9},{9,8},{10,11... | collective-permute-start | bytes 776 | tf_op jit(solution)/shard_map/ppermute | solution.py:37
  11.9 2.5 %collective-permute-start.1 = (f32[64]{0:T(128)S(1)}, f32[64]{0:T(128)S(1)}, u32[]{:S(2)}, u32[]{:S(2)}) collective-permute-start(f32[64]{0:T(128)S(1)} %add.224), channel_id=1, source_target_pairs={{0,2},{2,0},{4,6},{6,4},{1,3},{3,1},{5,7},{7,5},{8,10},{10,8},{12,... | collective-permute-start | bytes 776 | tf_op jit(solution)/shard_map/ppermute | solution.py:37
  14.4 6.5 %collective-permute-start.2 = (f32[64]{0:T(128)S(1)}, f32[64]{0:T(128)S(1)}, u32[]{:S(2)}, u32[]{:S(2)}) collective-permute-start(f32[64]{0:T(128)S(1)} %add.225), channel_id=1, source_target_pairs={{0,4},{2,6},{4,0},{6,2},{1,5},{3,7},{5,1},{7,3},{8,12},{10,14},{12... | collective-permute-start | bytes 776 | tf_op jit(solution)/shard_map/ppermute | solution.py:37
  17.2 6.3 %copy-start.18 = (s32[64]{0:T(128)S(1)}, s32[64]{0:T(128)}, u32[]{:S(2)}) copy-start(s32[64]{0:T(128)} %param.13) | copy-start | bytes 772
  17.2 6.9 %copy-start.10 = (f32[18,128]{1,0:T(8,128)S(1)}, f32[18,128]{1,0:T(8,128)}, u32[]{:S(2)}) copy-start(f32[18,128]{1,0:T(8,128)} %param.19) | copy-start | bytes 27652
  17.2 14.5 %copy-start.9 = (bf16[32,3,512]{2,0,1:T(8,128)(2,1)S(1)}, bf16[32,3,512]{2,0,1:T(8,128)(2,1)}, u32[]{:S(2)}) copy-start(bf16[32,3,512]{2,0,1:T(8,128)(2,1)} %param.11) | copy-start | bytes 294916
  20.9 2.6 %collective-permute-start.3 = (f32[64]{0:T(128)S(1)}, f32[64]{0:T(128)S(1)}, u32[]{:S(2)}, u32[]{:S(2)}) collective-permute-start(f32[64]{0:T(128)S(1)} %add.226), channel_id=1, source_target_pairs={{0,8},{8,0},{16,24},{24,16},{32,40},{40,32},{48,56},{56,48},{1,9},... | collective-permute-start | bytes 776 | tf_op jit(solution)/shard_map/ppermute | solution.py:37
  23.4 3.3 %collective-permute-start.4 = (f32[64]{0:T(128)S(1)}, f32[64]{0:T(128)S(1)}, u32[]{:S(2)}, u32[]{:S(2)}) collective-permute-start(f32[64]{0:T(128)S(1)} %add.227), channel_id=1, source_target_pairs={{0,16},{8,24},{16,0},{24,8},{32,48},{40,56},{48,32},{56,40},{1,17}... | collective-permute-start | bytes 776 | tf_op jit(solution)/shard_map/ppermute | solution.py:37
  26.7 7.0 %collective-permute-start.5 = (f32[64]{0:T(128)S(1)}, f32[64]{0:T(128)S(1)}, u32[]{:S(2)}, u32[]{:S(2)}) collective-permute-start(f32[64]{0:T(128)S(1)} %add.228), channel_id=1, source_target_pairs={{0,32},{8,40},{16,48},{24,56},{32,0},{40,8},{48,16},{56,24},{1,33}... | collective-permute-start | bytes 776 | tf_op jit(solution)/shard_map/ppermute | solution.py:37
  34.1 5.3 %collective-permute-start.15 = (f32[65536]{0:T(1024)S(1)}, f32[65536]{0:T(1024)S(1)}, u32[]{:S(2)}, u32[]{:S(2)}) collective-permute-start(f32[65536]{0:T(1024)S(1)} %pad_maximum_fusion.8), channel_id=1, source_target_pairs={{0,1},{1,0},{2,3},{3,2},{4,5},{5,4},{6,7},{7,6},{8,9},{9,8},{10,11... | collective-permute-start | bytes 786440 | tf_op jit(solution)/shard_map/ppermute | solution.py:178
  39.7 6.2 %collective-permute-start.16 = (f32[49152]{0:T(1024)S(1)}, f32[49152]{0:T(1024)S(1)}, u32[]{:S(2)}, u32[]{:S(2)}) collective-permute-start(f32[49152]{0:T(1024)S(1)} %pad_maximum_fusion.9), channel_id=1, source_target_pairs={{0,2},{2,0},{4,6},{6,4},{1,3},{3,1},{5,7},{7,5},{8,10},{10,8},{12,... | collective-permute-start | bytes 589832 | tf_op jit(solution)/shard_map/ppermute | solution.py:178
  46.8 6.2 %collective-permute-start.17 = (f32[40960]{0:T(1024)}, f32[40960]{0:T(1024)S(1)}, u32[]{:S(2)}, u32[]{:S(2)}) collective-permute-start(f32[40960]{0:T(1024)} %pad_maximum_fusion.10), channel_id=1, source_target_pairs={{0,4},{2,6},{4,0},{6,2},{1,5},{3,7},{5,1},{7,3},{8,12},{10,14},{12... | collective-permute-start | bytes 491528 | tf_op jit(solution)/shard_map/ppermute | solution.py:178
  53.0 6.5 %copy-start.7 = (f32[64,32]{1,0:T(8,128)S(1)}, f32[64,32]{1,0:T(8,128)}, u32[]{:S(2)}) copy-start(f32[64,32]{1,0:T(8,128)} %get-tuple-element.47) | copy-start | bytes 24580
  53.2 4.3 %collective-permute-start.18 = (f32[36864]{0:T(1024)S(1)}, f32[36864]{0:T(1024)S(1)}, u32[]{:S(2)}, u32[]{:S(2)}) collective-permute-start(f32[36864]{0:T(1024)S(1)} %pad_maximum_fusion.11), channel_id=1, source_target_pairs={{0,8},{8,0},{16,24},{24,16},{32,40},{40,32},{48,56},{56,48},{1,9},... | collective-permute-start | bytes 442376 | tf_op jit(solution)/shard_map/ppermute | solution.py:178
  57.7 5.0 %collective-permute-start.19 = (f32[34816]{0:T(1024)S(1)}, f32[34816]{0:T(1024)S(1)}, u32[]{:S(2)}, u32[]{:S(2)}) collective-permute-start(f32[34816]{0:T(1024)S(1)} %pad_maximum_fusion.12), channel_id=1, source_target_pairs={{0,16},{8,24},{16,0},{24,8},{32,48},{40,56},{48,32},{56,40},{1,17}... | collective-permute-start | bytes 417800 | tf_op jit(solution)/shard_map/ppermute | solution.py:178
  62.8 14.2 %collective-permute-start.20 = (f32[33792]{0:T(1024)S(1)}, f32[33792]{0:T(1024)S(1)}, u32[]{:S(2)}, u32[]{:S(2)}) collective-permute-start(f32[33792]{0:T(1024)S(1)} %pad_maximum_fusion.13), channel_id=1, source_target_pairs={{0,32},{8,40},{16,48},{24,56},{32,0},{40,8},{48,16},{56,24},{1,33}... | collective-permute-start | bytes 405512 | tf_op jit(solution)/shard_map/ppermute | solution.py:178
  70.1 45.5 %collective-permute-start.6 = (bf16[4,2]{0,1:T(2,128)(2,1)}, bf16[4,2]{0,1:T(2,128)(2,1)}, u32[]{:S(2)}, u32[]{:S(2)}) collective-permute-start(bf16[4,2]{0,1:T(2,128)(2,1)} %bitcast.170), channel_id=1, source_target_pairs={{0,1},{1,2},{2,3},{3,4},{4,5},{5,6},{6,7},{7,8},{8,9},{9,10},{10,1... | collective-permute-start | bytes 56 | tf_op jit(solution)/shard_map/ppermute | solution.py:70
  75.0 42.6 %collective-permute-start.7 = (bf16[4,2]{0,1:T(2,128)(2,1)}, bf16[4,2]{0,1:T(2,128)(2,1)}, u32[]{:S(2)}, u32[]{:S(2)}) collective-permute-start(bf16[4,2]{0,1:T(2,128)(2,1)} %bitcast.169), channel_id=1, source_target_pairs={{0,2},{1,3},{2,4},{3,5},{4,6},{5,7},{6,8},{7,9},{8,10},{9,11},{10,... | collective-permute-start | bytes 56 | tf_op jit(solution)/shard_map/ppermute | solution.py:70
  75.4 44.2 %collective-permute-start.8 = (bf16[4,2]{0,1:T(2,128)(2,1)}, bf16[4,2]{0,1:T(2,128)(2,1)}, u32[]{:S(2)}, u32[]{:S(2)}) collective-permute-start(bf16[4,2]{0,1:T(2,128)(2,1)} %bitcast.168), channel_id=1, source_target_pairs={{0,3},{1,4},{2,5},{3,6},{4,7},{5,8},{6,9},{7,10},{8,11},{9,12},{10... | collective-permute-start | bytes 56 | tf_op jit(solution)/shard_map/ppermute | solution.py:70
  82.2 5.0 %copy-start.6 = (bf16[64,8,512]{2,1,0:T(8,128)(2,1)S(1)}, bf16[64,8,512]{2,1,0:T(8,128)(2,1)}, u32[]{:S(2)}) copy-start(bf16[64,8,512]{2,1,0:T(8,128)(2,1)} %broadcast_in_dim.215) | copy-start | bytes 1572868
  82.2 5.0 %copy-start.13 = (bf16[18,512]{1,0:T(8,128)(2,1)S(1)}, bf16[18,512]{1,0:T(8,128)(2,1)}, u32[]{:S(2)}) copy-start(bf16[18,512]{1,0:T(8,128)(2,1)} %get-tuple-element.49) | copy-start | bytes 55300
  82.2 5.0 %copy-start.15 = (pred[8,512]{1,0:T(8,128)(4,1)S(1)}, pred[8,512]{1,0:T(8,128)(4,1)}, u32[]{:S(2)}) copy-start(pred[8,512]{1,0:T(8,128)(4,1)} %broadcast_in_dim.213) | copy-start | bytes 12292
  82.3 5.0 %copy-start.17 = (bf16[1,512]{1,0:T(2,128)(2,1)S(1)}, bf16[1,512]{1,0:T(2,128)(2,1)}, u32[]{:S(2)}) copy-start(bf16[1,512]{1,0:T(2,128)(2,1)} %convert_element_type.85) | copy-start | bytes 3076
  82.3 5.0 %copy-start.19 = (f32[19]{0:T(128)S(1)}, f32[19]{0:T(128)}, u32[]{:S(2)}) copy-start(f32[19]{0:T(128)} %constant.182.clone.1) | copy-start | bytes 232
  82.3 5.7 %copy-start.5 = (pred[64,2304]{1,0:T(8,128)(4,1)S(1)}, pred[64,2304]{1,0:T(8,128)(4,1)}, u32[]{:S(2)}) copy-start(pred[64,2304]{1,0:T(8,128)(4,1)} %iota_compare_fusion) | copy-start | bytes 442372
  87.7 4.1 %copy-start.4 = (f32[64,8,19]{2,1,0:T(8,128)}, f32[64,8,19]{2,1,0:T(8,128)S(1)}, u32[]{:S(2)}) copy-start(f32[64,8,19]{2,1,0:T(8,128)S(1)} %get-tuple-element.62) | copy-start | bytes 116740
  88.0 3.8 %copy-start.1 = (bf16[18,128,512]{2,1,0:T(8,128)(2,1)S(1)}, bf16[18,128,512]{2,1,0:T(8,128)(2,1)}, u32[]{:S(2)}) copy-start(bf16[18,128,512]{2,1,0:T(8,128)(2,1)} %param.18) | copy-start | bytes 7077892
  91.8 4.9 %copy-start.8 = (bf16[18,512]{1,0:T(8,128)(2,1)S(1)}, bf16[18,512]{1,0:T(8,128)(2,1)}, u32[]{:S(2)}) copy-start(bf16[18,512]{1,0:T(8,128)(2,1)} %get-tuple-element.48) | copy-start | bytes 55300
  91.8 4.9 %copy-start.14 = (bf16[1,512]{1,0:T(2,128)(2,1)S(1)}, bf16[1,512]{1,0:T(2,128)(2,1)}, u32[]{:S(2)}) copy-start(bf16[1,512]{1,0:T(2,128)(2,1)} %slice.498) | copy-start | bytes 3076
  102.7 11.8 %copy-start.2 = (bf16[16,128,512]{2,1,0:T(8,128)(2,1)S(1)}, bf16[16,128,512]{2,1,0:T(8,128)(2,1)}, u32[]{:S(2)}) copy-start(bf16[16,128,512]{2,1,0:T(8,128)(2,1)} %gather_fusion.1) | copy-start | bytes 6291460
  102.7 10.6 %collective-permute-start.21 = (f32[64,8,66]{0,1,2:T(8,128)S(1)}, f32[64,8,66]{0,1,2:T(8,128)S(1)}, u32[]{:S(2)}, u32[]{:S(2)}) collective-permute-start(f32[64,8,66]{0,1,2:T(8,128)S(1)} %pad_maximum_fusion.2), channel_id=1, source_target_pairs={{0,8},{8,0},{16,24},{24,16},{32,40},{40,32},{48,56},{56,48},{1,9},... | collective-permute-start | bytes 405512 | tf_op jit(solution)/shard_map/ppermute | solution.py:37
  109.2 49.5 %collective-permute-start.11 = (bf16[4,128,512]{2,1,0:T(8,128)(2,1)}, bf16[4,128,512]{2,1,0:T(8,128)(2,1)}, u32[]{:S(2)}, u32[]{:S(2)}) collective-permute-start(bf16[4,128,512]{2,1,0:T(8,128)(2,1)} %get-tuple-element.29), channel_id=1, source_target_pairs={{0,3},{1,4},{2,5},{3,6},{4,7},{5,8},{6,9},{7,10},{8,11},{9,12},{10... | collective-permute-start | bytes 1572872 | tf_op jit(solution)/shard_map/ppermute | solution.py:70
  114.0 7.2 %copy-start.16 = (bf16[1,4,2]{1,0,2:T(2,128)(2,1)S(1)}, bf16[1,4,2]{1,0,2:T(2,128)(2,1)}, u32[]{:S(2)}) copy-start(bf16[1,4,2]{1,0,2:T(2,128)(2,1)} %get-tuple-element.40) | copy-start | bytes 52
  114.0 11.9 %collective-permute-start.22 = (f32[64,8,66]{0,1,2:T(8,128)}, f32[64,8,66]{0,1,2:T(8,128)S(1)}, u32[]{:S(2)}, u32[]{:S(2)}) collective-permute-start(f32[64,8,66]{0,1,2:T(8,128)} %pad_maximum_fusion.3), channel_id=1, source_target_pairs={{0,16},{8,24},{16,0},{24,8},{32,48},{40,56},{48,32},{56,40},{1,17}... | collective-permute-start | bytes 405512 | tf_op jit(solution)/shard_map/ppermute | solution.py:37
  115.6 76.1 %collective-permute-start.10 = (bf16[4,128,512]{2,1,0:T(8,128)(2,1)}, bf16[4,128,512]{2,1,0:T(8,128)(2,1)}, u32[]{:S(2)}, u32[]{:S(2)}) collective-permute-start(bf16[4,128,512]{2,1,0:T(8,128)(2,1)} %get-tuple-element.30), channel_id=1, source_target_pairs={{0,2},{1,3},{2,4},{3,5},{4,6},{5,7},{6,8},{7,9},{8,10},{9,11},{10,... | collective-permute-start | bytes 1572872 | tf_op jit(solution)/shard_map/ppermute | solution.py:70
  117.6 74.1 %collective-permute-start.9 = (bf16[4,128,512]{2,1,0:T(8,128)(2,1)}, bf16[4,128,512]{2,1,0:T(8,128)(2,1)}, u32[]{:S(2)}, u32[]{:S(2)}) collective-permute-start(bf16[4,128,512]{2,1,0:T(8,128)(2,1)} %get-tuple-element.31), channel_id=1, source_target_pairs={{0,1},{1,2},{2,3},{3,4},{4,5},{5,6},{6,7},{7,8},{8,9},{9,10},{10,1... | collective-permute-start | bytes 1572872 | tf_op jit(solution)/shard_map/ppermute | solution.py:70
  119.5 97.2 %collective-permute-start.14 = (bf16[4,128,512]{2,1,0:T(8,128)(2,1)}, bf16[4,128,512]{2,1,0:T(8,128)(2,1)}, u32[]{:S(2)}, u32[]{:S(2)}) collective-permute-start(bf16[4,128,512]{2,1,0:T(8,128)(2,1)} %get-tuple-element.25), channel_id=1, source_target_pairs={{0,3},{1,4},{2,5},{3,6},{4,7},{5,8},{6,9},{7,10},{8,11},{9,12},{10... | collective-permute-start | bytes 1572872 | tf_op jit(solution)/shard_map/ppermute | solution.py:70
  126.1 10.8 %collective-permute-start.23 = (f32[64,8,66]{0,1,2:T(8,128)S(1)}, f32[64,8,66]{0,1,2:T(8,128)S(1)}, u32[]{:S(2)}, u32[]{:S(2)}) collective-permute-start(f32[64,8,66]{0,1,2:T(8,128)S(1)} %pad_maximum_fusion.4), channel_id=1, source_target_pairs={{0,32},{8,40},{16,48},{24,56},{32,0},{40,8},{48,16},{56,24},{1,33}... | collective-permute-start | bytes 405512 | tf_op jit(solution)/shard_map/ppermute | solution.py:37
  137.7 4.5 %collective-permute-start.24 = (f32[64,8,66]{0,1,2:T(8,128)}, f32[64,8,66]{0,1,2:T(8,128)S(1)}, u32[]{:S(2)}, u32[]{:S(2)}) collective-permute-start(f32[64,8,66]{0,1,2:T(8,128)} %pad_maximum_fusion.5), channel_id=1, source_target_pairs={{0,1},{1,0},{2,3},{3,2},{4,5},{5,4},{6,7},{7,6},{8,9},{9,8},{10,11... | collective-permute-start | bytes 405512 | tf_op jit(solution)/shard_map/ppermute | solution.py:37
  141.4 50.3 %copy-start.3 = (bf16[1,4,128,512]{3,2,1,0:T(8,128)(2,1)S(1)}, bf16[1,4,128,512]{3,2,1,0:T(8,128)(2,1)}, u32[]{:S(2)}) copy-start(bf16[1,4,128,512]{3,2,1,0:T(8,128)(2,1)} %get-tuple-element.28) | copy-start | bytes 1572868
  142.2 14.5 %collective-permute-start.25 = (f32[64,8,66]{0,1,2:T(8,128)S(1)}, f32[64,8,66]{0,1,2:T(8,128)S(1)}, u32[]{:S(2)}, u32[]{:S(2)}) collective-permute-start(f32[64,8,66]{0,1,2:T(8,128)S(1)} %pad_maximum_fusion.6), channel_id=1, source_target_pairs={{0,2},{2,0},{4,6},{6,4},{1,3},{3,1},{5,7},{7,5},{8,10},{10,8},{12,... | collective-permute-start | bytes 405512 | tf_op jit(solution)/shard_map/ppermute | solution.py:37
  156.7 60.1 %collective-permute-start.13 = (bf16[4,128,512]{2,1,0:T(8,128)(2,1)}, bf16[4,128,512]{2,1,0:T(8,128)(2,1)}, u32[]{:S(2)}, u32[]{:S(2)}) collective-permute-start(bf16[4,128,512]{2,1,0:T(8,128)(2,1)} %get-tuple-element.26), channel_id=1, source_target_pairs={{0,2},{1,3},{2,4},{3,5},{4,6},{5,7},{6,8},{7,9},{8,10},{9,11},{10,... | collective-permute-start | bytes 1572872 | tf_op jit(solution)/shard_map/ppermute | solution.py:70
  158.7 58.1 %collective-permute-start.12 = (bf16[4,128,512]{2,1,0:T(8,128)(2,1)}, bf16[4,128,512]{2,1,0:T(8,128)(2,1)}, u32[]{:S(2)}, u32[]{:S(2)}) collective-permute-start(bf16[4,128,512]{2,1,0:T(8,128)(2,1)} %get-tuple-element.27), channel_id=1, source_target_pairs={{0,1},{1,2},{2,3},{3,4},{4,5},{5,6},{6,7},{7,8},{8,9},{9,10},{10,1... | collective-permute-start | bytes 1572872 | tf_op jit(solution)/shard_map/ppermute | solution.py:70
  191.7 23.2 %collective-permute-start.26 = (f32[64,8,66]{0,1,2:T(8,128)S(1)}, f32[64,8,66]{0,1,2:T(8,128)S(1)}, u32[]{:S(2)}, u32[]{:S(2)}) collective-permute-start(f32[64,8,66]{0,1,2:T(8,128)S(1)} %pad_maximum_fusion.7), channel_id=1, source_target_pairs={{0,4},{2,6},{4,0},{6,2},{1,5},{3,7},{5,1},{7,3},{8,12},{10,14},{12... | collective-permute-start | bytes 405512 | tf_op jit(solution)/shard_map/ppermute | solution.py:37
  191.7 23.6 %copy-start.12 = (bf16[512,32]{0,1:T(8,128)(2,1)S(1)}, bf16[512,32]{0,1:T(8,128)(2,1)}, u32[]{:S(2)}) copy-start(bf16[512,32]{0,1:T(8,128)(2,1)} %param.12) | copy-start | bytes 98308
  215.4 11.5 %collective-permute-start.27 = (f32[64,32]{0,1:T(8,128)S(1)}, f32[64,32]{0,1:T(8,128)S(1)}, u32[]{:S(2)}, u32[]{:S(2)}) collective-permute-start(f32[64,32]{0,1:T(8,128)S(1)} %fusion.73), channel_id=1, source_target_pairs={{0,64},{64,0},{128,192},{192,128},{1,65},{65,1},{129,193},{193,129... | collective-permute-start | bytes 24584 | tf_op jit(solution)/shard_map/ppermute | solution.py:37
  226.9 7.3 %collective-permute-start.28 = (f32[64,32]{0,1:T(8,128)S(1)}, f32[64,32]{0,1:T(8,128)S(1)}, u32[]{:S(2)}, u32[]{:S(2)}) collective-permute-start(f32[64,32]{0,1:T(8,128)S(1)} %add.270), channel_id=1, source_target_pairs={{0,128},{64,192},{128,0},{192,64},{1,129},{65,193},{129,1},{193,65... | collective-permute-start | bytes 24584 | tf_op jit(solution)/shard_map/ppermute | solution.py:37
  (1 other events, 2.0 us)

commit v11 on v10

--- a/solution.py
+++ b/solution.py
@@ -260,7 +260,7 @@
     stats = jnp.concatenate(
         [local_acc, local_sum[..., None], local_top[..., None]], axis=-1
     )
-    stats = butterfly(stats, softmax_merge, ["z", "core", "x"])
+    stats = butterfly(stats, softmax_merge, ["core", "z", "x"])
     mixture = stats[..., :HDIM]
     totals = stats[..., HDIM]
     mixed = (mixture / totals[..., None]).astype(jnp.bfloat16)

time: 235 us -> 234 us (level)
  the two profiles are of different devices: /device:TPU:65 before, /device:TPU:97 now
where the time goes in v11:
time: 234 us; the launch traced here: 233 us
  starting transfers between devices  79 us (34%)
  waiting for transfers between devices  72.3 us (31%)
  local copies, waits for them, and re-layouts  32.5 us (14%)
  other arithmetic  32 us (14%)
  matrix products  15.9 us (7%)
    ppermute x14, waiting for transfers between devices, butterfly(): x = merge(x, lax.ppermute(x, axis, pairs))  55.8 us
    ppermute x14, starting transfers between devices, butterfly(): x = merge(x, lax.ppermute(x, axis, pairs))  38.8 us
    ppermute x9, starting transfers between devices, passed_along(): lax.ppermute(array, SEQ_PARTS, [(i, (i + by) % count) for i in range(coun...  28.7 us
    ppermute x6, waiting for transfers between devices, shards(): payload = lax.ppermute(payload, axis, pairs)  16.5 us
    ppermute x6, starting transfers between devices, shards(): payload = lax.ppermute(payload, axis, pairs)  11.5 us
    dot_general x2, matrix products, weighted_of(): jnp.dot(expo.astype(jnp.bfloat16).reshape(requests * heads_here, -1), val...  6.5 us
    dot_general x2, matrix products, scores_of(): lax.dot_general(spread_queries, keys, (((1,), (1,)), ((), ())), preferred...  5.35 us
    slice x3, local copies, waits for them, and re-layouts, shards(): arrived = [(send_keys[0], send_values[0], meta_data[0])]  4.74 us
  transfers between devices with their start and end apart: 29, of which 14 were waited for; matrix products, arithmetic and copies ran while one was open for 33% of the time, Pallas kernels for 0%

profile of v11, /device:TPU:97, one launch (start us, length us, event | category | flops | bytes accessed | tf_op | source)
XLA Modules:
  0.0 233.2 jit_solution(16668389323177502952)
XLA Ops:
  5.4 1.2 broadcast_select_fusion.8
  9.2 2.7 %fusion.53 = f32[18,1,512]{2,1,0:T(1,128)S(1)} fusion(bf16[18,128,512]{2,1,0:T(8,128)(2,1)} %param.18, f32[18,128,1]{1,0,2:T(8,128)} %bitcast.191), kind=kOutput, calls=%fused_computation.157 | convolution fusion | flops 14155776 | bytes 2405376 | tf_op jit(solution)/shard_map/bi,bif->bf/dot_general | solution.py:127
  11.9 1.3 collective-permute-start.1
  13.2 1.2 collective-permute-done.1
  14.4 2.7 %collective-permute-start.2 = (f32[64]{0:T(128)S(1)}, f32[64]{0:T(128)S(1)}, u32[]{:S(2)}, u32[]{:S(2)}) collective-permute-start(f32[64]{0:T(128)S(1)} %add.225), channel_id=1, source_target_pairs={{0,4},{2,6},{4,0},{6,2},{1,5},{3,7},{5,1},{7,3},{8,12},{10,14},{12... | collective-permute-start | bytes 776 | tf_op jit(solution)/shard_map/ppermute | solution.py:37
  17.2 3.7 %gather_fusion.1 = bf16[16,128,512]{2,1,0:T(8,128)(2,1)} fusion(bf16[18,128,512]{2,1,0:T(8,128)(2,1)} %param.18, s32[1024]{0:T(1024)S(1)} %pad_clamp_fusion.1), kind=kCustom, calls=%fused_computation.1 | custom fusion | bytes 4194368 | tf_op jit(solution)/shard_map/gather | solution.py:158
  20.9 2.4 %collective-permute-done.3 = f32[64]{0:T(128)S(1)} collective-permute-done((f32[64]{0:T(128)S(1)}, f32[64]{0:T(128)S(1)}, u32[]{:S(2)}, u32[]{:S(2)}) %collective-permute-start.3) | collective-permute-done | bytes 288 | tf_op jit(solution)/shard_map/ppermute | solution.py:37
  24.5 2.1 collective-permute-done.4
  26.6 4.2 %collective-permute-start.5 = (f32[64]{0:T(128)S(1)}, f32[64]{0:T(128)S(1)}, u32[]{:S(2)}, u32[]{:S(2)}) collective-permute-start(f32[64]{0:T(128)S(1)} %add.228), channel_id=1, source_target_pairs={{0,32},{8,40},{16,48},{24,56},{32,0},{40,8},{48,16},{56,24},{1,33}... | collective-permute-start | bytes 776 | tf_op jit(solution)/shard_map/ppermute | solution.py:37
  30.8 2.0 gather_fusion
  33.3 5.0 %collective-permute-start.15 = (f32[65536]{0:T(1024)S(1)}, f32[65536]{0:T(1024)S(1)}, u32[]{:S(2)}, u32[]{:S(2)}) collective-permute-start(f32[65536]{0:T(1024)S(1)} %pad_maximum_fusion.8), channel_id=1, source_target_pairs={{0,1},{1,0},{2,3},{3,2},{4,5},{5,4},{6,7},{7,6},{8,9},{9,8},{10,11... | collective-permute-start | bytes 786440 | tf_op jit(solution)/shard_map/ppermute | solution.py:178
  40.1 1.4 fusion.31
  41.4 4.4 %collective-permute-done.16 = f32[49152]{0:T(1024)S(1)} collective-permute-done((f32[49152]{0:T(1024)S(1)}, f32[49152]{0:T(1024)S(1)}, u32[]{:S(2)}, u32[]{:S(2)}) %collective-permute-start.16) | collective-permute-done | bytes 196640 | tf_op jit(solution)/shard_map/ppermute | solution.py:178
  47.8 1.5 multiply_cosine_fusion
  50.0 2.9 %collective-permute-done.17 = f32[40960]{0:T(1024)S(1)} collective-permute-done((f32[40960]{0:T(1024)}, f32[40960]{0:T(1024)S(1)}, u32[]{:S(2)}, u32[]{:S(2)}) %collective-permute-start.17) | collective-permute-done | bytes 163872 | tf_op jit(solution)/shard_map/ppermute | solution.py:178
  53.3 4.0 %collective-permute-done.18 = f32[36864]{0:T(1024)S(1)} collective-permute-done((f32[36864]{0:T(1024)S(1)}, f32[36864]{0:T(1024)S(1)}, u32[]{:S(2)}, u32[]{:S(2)}) %collective-permute-start.18) | collective-permute-done | bytes 147488 | tf_op jit(solution)/shard_map/ppermute | solution.py:178
  58.6 5.0 %collective-permute-done.19 = f32[34816]{0:T(1024)S(1)} collective-permute-done((f32[34816]{0:T(1024)S(1)}, f32[34816]{0:T(1024)S(1)}, u32[]{:S(2)}, u32[]{:S(2)}) %collective-permute-start.19) | collective-permute-done | bytes 139296 | tf_op jit(solution)/shard_map/ppermute | solution.py:178
  63.8 4.6 %collective-permute-start.20 = (f32[33792]{0:T(1024)S(1)}, f32[33792]{0:T(1024)S(1)}, u32[]{:S(2)}, u32[]{:S(2)}) collective-permute-start(f32[33792]{0:T(1024)S(1)} %pad_maximum_fusion.13), channel_id=1, source_target_pairs={{0,32},{8,40},{16,48},{24,56},{32,0},{40,8},{48,16},{56,24},{1,33}... | collective-permute-start | bytes 405512 | tf_op jit(solution)/shard_map/ppermute | solution.py:178
  70.5 6.3 %collective-permute-start.6 = (bf16[4,2]{0,1:T(2,128)(2,1)}, bf16[4,2]{0,1:T(2,128)(2,1)}, u32[]{:S(2)}, u32[]{:S(2)}) collective-permute-start(bf16[4,2]{0,1:T(2,128)(2,1)} %bitcast.170), channel_id=1, source_target_pairs={{0,1},{1,2},{2,3},{3,4},{4,5},{5,6},{6,7},{7,8},{8,9},{9,10},{10,1... | collective-permute-start | bytes 56 | tf_op jit(solution)/shard_map/ppermute | solution.py:70
  77.3 1.6 collective-permute-start.8
  81.1 1.4 select_n.322
  82.8 1.4 broadcast_in_dim.215
  84.2 5.0 %fusion.71 = (f32[64,8]{1,0:T(8,128)S(1)}, f32[64,8,2304]{2,1,0:T(8,128)}) fusion(bf16[64,8,512]{2,1,0:T(8,128)(2,1)} %select_n.322, bf16[2304,512,1]{1,0,2:T(8,128)(2,1)S(1)} %bitcast.171, pred[64,2304]{1,0:T(8,128)(4,1)} %iota_compare_fusion), kind=kOutput, calls=%fused_computation.206 | convolution fusion | flops 1211497984 | bytes 7751680 | tf_op jit(solution)/shard_map/dot_general | solution.py:236
  89.9 3.8 %fusion.1 = f32[64,8]{1,0:T(8,128)S(1)} fusion(f32[64,8,2304]{2,1,0:T(8,128)} %get-tuple-element.60, f32[64,8]{1,0:T(8,128)S(1)} %max.32, pred[64,2304]{1,0:T(8,128)(4,1)S(1)} %copy-done.5), kind=kLoop, calls=%fused_computation.10 | loop fusion | flops 3538432 | bytes 4870144 | tf_op jit(solution)/shard_map/reduce_sum | solution.py:246
  93.7 4.8 %fusion.4 = f32[512,512]{1,0:T(8,128)} fusion(bf16[2304,512]{1,0:T(8,128)(2,1)S(1)} %bitcast.172, f32[64,8,2304]{2,1,0:T(8,128)} %get-tuple-element.60, f32[64,8]{1,0:T(8,128)S(1)} %max.32, pred[64,2304]{1,0:T(8,128)(4,1)S(1)} %copy-done.5), kind=kOutput, calls=%fused_computation.13 | convolution fusion | flops 1211498496 | bytes 8275968 | tf_op jit(solution)/shard_map/dot_general | solution.py:249
  98.6 1.7 convolution_add_fusion
  100.3 1.7 reshape.524
  102.0 2.3 %select_reduce_fusion = f32[64,8,64]{2,1,0:T(8,128)S(1)} fusion(f32[64,8,8,64]{3,2,1,0:T(8,128)} %reshape.524, pred[8,8]{1,0:T(8,128)(4,1)S(1)} %iota_compare_fusion.5), kind=kLoop, calls=%fused_computation.19 | loop fusion | flops 491520 | bytes 1179712 | tf_op jit(solution)/shard_map/reduce_sum | solution.py:259
  104.7 3.0 %fusion.68 = (bf16[1,4,128,512]{3,2,1,0:T(8,128)(2,1)}, bf16[4,128,512]{2,1,0:T(8,128)(2,1)}, bf16[4,128,512]{2,1,0:T(8,128)(2,1)}, bf16[4,128,512]{2,1,0:T(8,128)(2,1)}) fusion(bf16[4,4,128,512]{3,2,1,0:T(8,128)(2,1)} %bitcast.174), kind=kLoop, calls=%fused_computation.203 | loop fusion | bytes 4194304 | tf_op jit(solution)/shard_map/slice | solution.py:193
  108.6 3.2 %collective-permute-start.22 = (f32[64,8,66]{0,1,2:T(8,128)}, f32[64,8,66]{0,1,2:T(8,128)S(1)}, u32[]{:S(2)}, u32[]{:S(2)}) collective-permute-start(f32[64,8,66]{0,1,2:T(8,128)} %pad_maximum_fusion.3), channel_id=1, source_target_pairs={{0,8},{8,0},{16,24},{24,16},{32,40},{40,32},{48,56},{56,48},{1,9},... | collective-permute-start | bytes 405512 | tf_op jit(solution)/shard_map/ppermute | solution.py:37
  111.8 1.2 fusion.67
  113.6 1.1 collective-permute-start.9
  115.3 1.5 collective-permute-start.14
  117.6 1.5 collective-permute-done.22
  119.6 14.1 %collective-permute-done.23 = f32[64,8,66]{0,1,2:T(8,128)S(1)} collective-permute-done((f32[64,8,66]{0,1,2:T(8,128)S(1)}, f32[64,8,66]{0,1,2:T(8,128)S(1)}, u32[]{:S(2)}, u32[]{:S(2)}) %collective-permute-start.23) | collective-permute-done | bytes 135200 | tf_op jit(solution)/shard_map/ppermute | solution.py:37
  134.5 3.7 %collective-permute-start.24 = (f32[64,8,66]{0,1,2:T(8,128)}, f32[64,8,66]{0,1,2:T(8,128)S(1)}, u32[]{:S(2)}, u32[]{:S(2)}) collective-permute-start(f32[64,8,66]{0,1,2:T(8,128)} %pad_maximum_fusion.5), channel_id=1, source_target_pairs={{0,32},{8,40},{16,48},{24,56},{32,0},{40,8},{48,16},{56,24},{1,33}... | collective-permute-start | bytes 405512 | tf_op jit(solution)/shard_map/ppermute | solution.py:37
  139.0 13.2 %collective-permute-done.24 = f32[64,8,66]{0,1,2:T(8,128)S(1)} collective-permute-done((f32[64,8,66]{0,1,2:T(8,128)}, f32[64,8,66]{0,1,2:T(8,128)S(1)}, u32[]{:S(2)}, u32[]{:S(2)}) %collective-permute-start.24) | collective-permute-done | bytes 135200 | tf_op jit(solution)/shard_map/ppermute | solution.py:37
  153.0 6.4 %collective-permute-done.25 = f32[64,8,66]{0,1,2:T(8,128)S(1)} collective-permute-done((f32[64,8,66]{0,1,2:T(8,128)S(1)}, f32[64,8,66]{0,1,2:T(8,128)S(1)}, u32[]{:S(2)}, u32[]{:S(2)}) %collective-permute-start.25) | collective-permute-done | bytes 135200 | tf_op jit(solution)/shard_map/ppermute | solution.py:37
  159.9 17.2 %collective-permute-start.12 = (bf16[4,128,512]{2,1,0:T(8,128)(2,1)}, bf16[4,128,512]{2,1,0:T(8,128)(2,1)}, u32[]{:S(2)}, u32[]{:S(2)}) collective-permute-start(bf16[4,128,512]{2,1,0:T(8,128)(2,1)} %get-tuple-element.27), channel_id=1, source_target_pairs={{0,1},{1,2},{2,3},{3,4},{4,5},{5,6},{6,7},{7,8},{8,9},{9,10},{10,1... | collective-permute-start | bytes 1572872 | tf_op jit(solution)/shard_map/ppermute | solution.py:70
  177.1 18.3 %collective-permute-start.26 = (f32[64,8,66]{0,1,2:T(8,128)S(1)}, f32[64,8,66]{0,1,2:T(8,128)S(1)}, u32[]{:S(2)}, u32[]{:S(2)}) collective-permute-start(f32[64,8,66]{0,1,2:T(8,128)S(1)} %pad_maximum_fusion.7), channel_id=1, source_target_pairs={{0,4},{2,6},{4,0},{6,2},{1,5},{3,7},{5,1},{7,3},{8,12},{10,14},{12... | collective-permute-start | bytes 405512 | tf_op jit(solution)/shard_map/ppermute | solution.py:37
  195.4 2.9 %pad_maximum_fusion = bf16[4,4,128,512]{3,2,1,0:T(8,128)(2,1)} fusion(bf16[1,4,128,512]{3,2,1,0:T(8,128)(2,1)} %bitcast.14, bf16[1,4,128,512]{3,2,1,0:T(8,128)(2,1)} %bitcast.12, bf16[1,4,128,512]{3,2,1,0:T(8,128)(2,1)} %bitcast.10, bf16[1,4,128,512]{3,2,1,0:T(8,128)(2,1)S(1)} %copy-done.3), kind=kLoop, calls=%fused_computation.17 | loop fusion | flops 3145728 | bytes 4194304 | tf_op jit(solution)/shard_map/stack | solution.py:198
  198.4 14.9 %collective-permute-done.26 = f32[64,8,66]{0,1,2:T(8,128)S(1)} collective-permute-done((f32[64,8,66]{0,1,2:T(8,128)S(1)}, f32[64,8,66]{0,1,2:T(8,128)S(1)}, u32[]{:S(2)}, u32[]{:S(2)}) %collective-permute-start.26) | collective-permute-done | bytes 135200 | tf_op jit(solution)/shard_map/ppermute | solution.py:37
  213.9 1.3 collective-permute-start.27
  215.2 2.9 %pad_maximum_fusion.1 = bf16[4,4,128,512]{3,2,1,0:T(8,128)(2,1)} fusion(bf16[1,4,128,512]{3,2,1,0:T(8,128)(2,1)} %bitcast.23, bf16[1,4,128,512]{3,2,1,0:T(8,128)(2,1)} %bitcast.21, bf16[1,4,128,512]{3,2,1,0:T(8,128)(2,1)} %bitcast.19, bf16[1,4,128,512]{3,2,1,0:T(8,128)(2,1)S(1)} %get-tuple-element.24), kind=kLoop, calls=%fused_computation.18 | loop fusion | flops 3145728 | bytes 4194304 | tf_op jit(solution)/shard_map/stack | solution.py:199
  218.1 3.6 %gather_fusion.4 = bf16[16,128,512]{2,1,0:T(8,128)(2,1)} fusion(bf16[16,128,512]{2,1,0:T(8,128)(2,1)} %bitcast.175, s32[1024]{0:T(1024)S(1)} %pad_clamp_fusion), kind=kCustom, calls=%fused_computation.4 | custom fusion | bytes 4194368 | tf_op jit(solution)/shard_map/gather | solution.py:209
  221.7 3.6 %gather_fusion.5 = bf16[16,128,512]{2,1,0:T(8,128)(2,1)} fusion(bf16[16,128,512]{2,1,0:T(8,128)(2,1)} %bitcast.176, s32[1024]{0:T(1024)S(1)} %pad_clamp_fusion), kind=kCustom, calls=%fused_computation.5 | custom fusion | bytes 4194368 | tf_op jit(solution)/shard_map/gather | solution.py:211
  225.3 2.7 %collective-permute-start.28 = (f32[64,32]{0,1:T(8,128)S(1)}, f32[64,32]{0,1:T(8,128)S(1)}, u32[]{:S(2)}, u32[]{:S(2)}) collective-permute-start(f32[64,32]{0,1:T(8,128)S(1)} %add.270), channel_id=1, source_target_pairs={{0,128},{64,192},{128,0},{192,64},{1,129},{65,193},{129,1},{193,65... | collective-permute-start | bytes 24584 | tf_op jit(solution)/shard_map/ppermute | solution.py:37
  228.1 4.6 %broadcast_select_fusion = (bf16[16,128,512]{2,1,0:T(8,128)(2,1)}, bf16[16,128,512]{2,1,0:T(8,128)(2,1)}) fusion(bf16[16,128,512]{2,1,0:T(8,128)(2,1)} %gather_fusion.5, pred[16]{0:T(512)(128)(4,1)S(1)} %fusion.44, bf16[16,128,512]{2,1,0:T(8,128)(2,1)} %gather_fusion.4), kind=kLoop, calls=%fused_computation.20 | loop fusion | flops 2097152 | bytes 8388624 | tf_op jit(solution)/shard_map/jit(_where)/select_n | solution.py:210
  (232 shorter events, 28.4 us)
Async XLA Ops:
  0.6 30.2 %copy-start = (bf16[18,128,512]{2,1,0:T(8,128)(2,1)S(1)}, bf16[18,128,512]{2,1,0:T(8,128)(2,1)}, u32[]{:S(2)}) copy-start(bf16[18,128,512]{2,1,0:T(8,128)(2,1)} %param.17) | copy-start | bytes 7077892
  1.5 10.4 %collective-permute-start = (f32[64]{0:T(128)S(1)}, f32[64]{0:T(128)S(1)}, u32[]{:S(2)}, u32[]{:S(2)}) collective-permute-start(f32[64]{0:T(128)S(1)} %fusion.39), channel_id=1, source_target_pairs={{0,1},{1,0},{2,3},{3,2},{4,5},{5,4},{6,7},{7,6},{8,9},{9,8},{10,11... | collective-permute-start | bytes 776 | tf_op jit(solution)/shard_map/ppermute | solution.py:37
  11.9 2.5 %collective-permute-start.1 = (f32[64]{0:T(128)S(1)}, f32[64]{0:T(128)S(1)}, u32[]{:S(2)}, u32[]{:S(2)}) collective-permute-start(f32[64]{0:T(128)S(1)} %add.224), channel_id=1, source_target_pairs={{0,2},{2,0},{4,6},{6,4},{1,3},{3,1},{5,7},{7,5},{8,10},{10,8},{12,... | collective-permute-start | bytes 776 | tf_op jit(solution)/shard_map/ppermute | solution.py:37
  14.4 6.5 %collective-permute-start.2 = (f32[64]{0:T(128)S(1)}, f32[64]{0:T(128)S(1)}, u32[]{:S(2)}, u32[]{:S(2)}) collective-permute-start(f32[64]{0:T(128)S(1)} %add.225), channel_id=1, source_target_pairs={{0,4},{2,6},{4,0},{6,2},{1,5},{3,7},{5,1},{7,3},{8,12},{10,14},{12... | collective-permute-start | bytes 776 | tf_op jit(solution)/shard_map/ppermute | solution.py:37
  17.2 6.1 %copy-start.18 = (s32[64]{0:T(128)S(1)}, s32[64]{0:T(128)}, u32[]{:S(2)}) copy-start(s32[64]{0:T(128)} %param.13) | copy-start | bytes 772
  17.2 6.7 %copy-start.10 = (f32[18,128]{1,0:T(8,128)S(1)}, f32[18,128]{1,0:T(8,128)}, u32[]{:S(2)}) copy-start(f32[18,128]{1,0:T(8,128)} %param.19) | copy-start | bytes 27652
  17.2 13.6 %copy-start.9 = (bf16[32,3,512]{2,0,1:T(8,128)(2,1)S(1)}, bf16[32,3,512]{2,0,1:T(8,128)(2,1)}, u32[]{:S(2)}) copy-start(bf16[32,3,512]{2,0,1:T(8,128)(2,1)} %param.11) | copy-start | bytes 294916
  20.9 2.4 %collective-permute-start.3 = (f32[64]{0:T(128)S(1)}, f32[64]{0:T(128)S(1)}, u32[]{:S(2)}, u32[]{:S(2)}) collective-permute-start(f32[64]{0:T(128)S(1)} %add.226), channel_id=1, source_target_pairs={{0,8},{8,0},{16,24},{24,16},{32,40},{40,32},{48,56},{56,48},{1,9},... | collective-permute-start | bytes 776 | tf_op jit(solution)/shard_map/ppermute | solution.py:37
  23.3 3.3 %collective-permute-start.4 = (f32[64]{0:T(128)S(1)}, f32[64]{0:T(128)S(1)}, u32[]{:S(2)}, u32[]{:S(2)}) collective-permute-start(f32[64]{0:T(128)S(1)} %add.227), channel_id=1, source_target_pairs={{0,16},{8,24},{16,0},{24,8},{32,48},{40,56},{48,32},{56,40},{1,17}... | collective-permute-start | bytes 776 | tf_op jit(solution)/shard_map/ppermute | solution.py:37
  26.6 6.3 %collective-permute-start.5 = (f32[64]{0:T(128)S(1)}, f32[64]{0:T(128)S(1)}, u32[]{:S(2)}, u32[]{:S(2)}) collective-permute-start(f32[64]{0:T(128)S(1)} %add.228), channel_id=1, source_target_pairs={{0,32},{8,40},{16,48},{24,56},{32,0},{40,8},{48,16},{56,24},{1,33}... | collective-permute-start | bytes 776 | tf_op jit(solution)/shard_map/ppermute | solution.py:37
  33.3 6.2 %collective-permute-start.15 = (f32[65536]{0:T(1024)S(1)}, f32[65536]{0:T(1024)S(1)}, u32[]{:S(2)}, u32[]{:S(2)}) collective-permute-start(f32[65536]{0:T(1024)S(1)} %pad_maximum_fusion.8), channel_id=1, source_target_pairs={{0,1},{1,0},{2,3},{3,2},{4,5},{5,4},{6,7},{7,6},{8,9},{9,8},{10,11... | collective-permute-start | bytes 786440 | tf_op jit(solution)/shard_map/ppermute | solution.py:178
  39.7 6.2 %collective-permute-start.16 = (f32[49152]{0:T(1024)S(1)}, f32[49152]{0:T(1024)S(1)}, u32[]{:S(2)}, u32[]{:S(2)}) collective-permute-start(f32[49152]{0:T(1024)S(1)} %pad_maximum_fusion.9), channel_id=1, source_target_pairs={{0,2},{2,0},{4,6},{6,4},{1,3},{3,1},{5,7},{7,5},{8,10},{10,8},{12,... | collective-permute-start | bytes 589832 | tf_op jit(solution)/shard_map/ppermute | solution.py:178
  46.7 6.2 %collective-permute-start.17 = (f32[40960]{0:T(1024)}, f32[40960]{0:T(1024)S(1)}, u32[]{:S(2)}, u32[]{:S(2)}) collective-permute-start(f32[40960]{0:T(1024)} %pad_maximum_fusion.10), channel_id=1, source_target_pairs={{0,4},{2,6},{4,0},{6,2},{1,5},{3,7},{5,1},{7,3},{8,12},{10,14},{12... | collective-permute-start | bytes 491528 | tf_op jit(solution)/shard_map/ppermute | solution.py:178
  53.0 5.6 %copy-start.7 = (f32[64,32]{1,0:T(8,128)S(1)}, f32[64,32]{1,0:T(8,128)}, u32[]{:S(2)}) copy-start(f32[64,32]{1,0:T(8,128)} %get-tuple-element.47) | copy-start | bytes 24580
  53.2 4.1 %collective-permute-start.18 = (f32[36864]{0:T(1024)S(1)}, f32[36864]{0:T(1024)S(1)}, u32[]{:S(2)}, u32[]{:S(2)}) collective-permute-start(f32[36864]{0:T(1024)S(1)} %pad_maximum_fusion.11), channel_id=1, source_target_pairs={{0,8},{8,0},{16,24},{24,16},{32,40},{40,32},{48,56},{56,48},{1,9},... | collective-permute-start | bytes 442376 | tf_op jit(solution)/shard_map/ppermute | solution.py:178
  57.5 6.1 %collective-permute-start.19 = (f32[34816]{0:T(1024)S(1)}, f32[34816]{0:T(1024)S(1)}, u32[]{:S(2)}, u32[]{:S(2)}) collective-permute-start(f32[34816]{0:T(1024)S(1)} %pad_maximum_fusion.12), channel_id=1, source_target_pairs={{0,16},{8,24},{16,0},{24,8},{32,48},{40,56},{48,32},{56,40},{1,17}... | collective-permute-start | bytes 417800 | tf_op jit(solution)/shard_map/ppermute | solution.py:178
  63.8 15.2 %collective-permute-start.20 = (f32[33792]{0:T(1024)S(1)}, f32[33792]{0:T(1024)S(1)}, u32[]{:S(2)}, u32[]{:S(2)}) collective-permute-start(f32[33792]{0:T(1024)S(1)} %pad_maximum_fusion.13), channel_id=1, source_target_pairs={{0,32},{8,40},{16,48},{24,56},{32,0},{40,8},{48,16},{56,24},{1,33}... | collective-permute-start | bytes 405512 | tf_op jit(solution)/shard_map/ppermute | solution.py:178
  70.5 42.4 %collective-permute-start.6 = (bf16[4,2]{0,1:T(2,128)(2,1)}, bf16[4,2]{0,1:T(2,128)(2,1)}, u32[]{:S(2)}, u32[]{:S(2)}) collective-permute-start(bf16[4,2]{0,1:T(2,128)(2,1)} %bitcast.170), channel_id=1, source_target_pairs={{0,1},{1,2},{2,3},{3,4},{4,5},{5,6},{6,7},{7,8},{8,9},{9,10},{10,1... | collective-permute-start | bytes 56 | tf_op jit(solution)/shard_map/ppermute | solution.py:70
  76.9 36.7 %collective-permute-start.7 = (bf16[4,2]{0,1:T(2,128)(2,1)}, bf16[4,2]{0,1:T(2,128)(2,1)}, u32[]{:S(2)}, u32[]{:S(2)}) collective-permute-start(bf16[4,2]{0,1:T(2,128)(2,1)} %bitcast.169), channel_id=1, source_target_pairs={{0,2},{1,3},{2,4},{3,5},{4,6},{5,7},{6,8},{7,9},{8,10},{9,11},{10,... | collective-permute-start | bytes 56 | tf_op jit(solution)/shard_map/ppermute | solution.py:70
  77.3 38.0 %collective-permute-start.8 = (bf16[4,2]{0,1:T(2,128)(2,1)}, bf16[4,2]{0,1:T(2,128)(2,1)}, u32[]{:S(2)}, u32[]{:S(2)}) collective-permute-start(bf16[4,2]{0,1:T(2,128)(2,1)} %bitcast.168), channel_id=1, source_target_pairs={{0,3},{1,4},{2,5},{3,6},{4,7},{5,8},{6,9},{7,10},{8,11},{9,12},{10... | collective-permute-start | bytes 56 | tf_op jit(solution)/shard_map/ppermute | solution.py:70
  84.2 5.0 %copy-start.6 = (bf16[64,8,512]{2,1,0:T(8,128)(2,1)S(1)}, bf16[64,8,512]{2,1,0:T(8,128)(2,1)}, u32[]{:S(2)}) copy-start(bf16[64,8,512]{2,1,0:T(8,128)(2,1)} %broadcast_in_dim.215) | copy-start | bytes 1572868
  84.2 5.0 %copy-start.13 = (bf16[18,512]{1,0:T(8,128)(2,1)S(1)}, bf16[18,512]{1,0:T(8,128)(2,1)}, u32[]{:S(2)}) copy-start(bf16[18,512]{1,0:T(8,128)(2,1)} %get-tuple-element.49) | copy-start | bytes 55300
  84.2 5.0 %copy-start.15 = (pred[8,512]{1,0:T(8,128)(4,1)S(1)}, pred[8,512]{1,0:T(8,128)(4,1)}, u32[]{:S(2)}) copy-start(pred[8,512]{1,0:T(8,128)(4,1)} %broadcast_in_dim.213) | copy-start | bytes 12292
  84.2 5.0 %copy-start.17 = (bf16[1,512]{1,0:T(2,128)(2,1)S(1)}, bf16[1,512]{1,0:T(2,128)(2,1)}, u32[]{:S(2)}) copy-start(bf16[1,512]{1,0:T(2,128)(2,1)} %convert_element_type.85) | copy-start | bytes 3076
  84.2 5.0 %copy-start.19 = (f32[19]{0:T(128)S(1)}, f32[19]{0:T(128)}, u32[]{:S(2)}) copy-start(f32[19]{0:T(128)} %constant.182.clone.1) | copy-start | bytes 232
  84.2 5.7 %copy-start.5 = (pred[64,2304]{1,0:T(8,128)(4,1)S(1)}, pred[64,2304]{1,0:T(8,128)(4,1)}, u32[]{:S(2)}) copy-start(pred[64,2304]{1,0:T(8,128)(4,1)} %iota_compare_fusion) | copy-start | bytes 442372
  89.6 4.1 %copy-start.4 = (f32[64,8,19]{2,1,0:T(8,128)}, f32[64,8,19]{2,1,0:T(8,128)S(1)}, u32[]{:S(2)}) copy-start(f32[64,8,19]{2,1,0:T(8,128)S(1)} %get-tuple-element.62) | copy-start | bytes 116740
  89.9 3.8 %copy-start.1 = (bf16[18,128,512]{2,1,0:T(8,128)(2,1)S(1)}, bf16[18,128,512]{2,1,0:T(8,128)(2,1)}, u32[]{:S(2)}) copy-start(bf16[18,128,512]{2,1,0:T(8,128)(2,1)} %param.18) | copy-start | bytes 7077892
  93.7 4.9 %copy-start.8 = (bf16[18,512]{1,0:T(8,128)(2,1)S(1)}, bf16[18,512]{1,0:T(8,128)(2,1)}, u32[]{:S(2)}) copy-start(bf16[18,512]{1,0:T(8,128)(2,1)} %get-tuple-element.48) | copy-start | bytes 55300
  93.7 4.9 %copy-start.14 = (bf16[1,512]{1,0:T(2,128)(2,1)S(1)}, bf16[1,512]{1,0:T(2,128)(2,1)}, u32[]{:S(2)}) copy-start(bf16[1,512]{1,0:T(2,128)(2,1)} %slice.498) | copy-start | bytes 3076
  104.6 7.2 %copy-start.2 = (bf16[16,128,512]{2,1,0:T(8,128)(2,1)S(1)}, bf16[16,128,512]{2,1,0:T(8,128)(2,1)}, u32[]{:S(2)}) copy-start(bf16[16,128,512]{2,1,0:T(8,128)(2,1)} %gather_fusion.1) | copy-start | bytes 6291460
  104.6 3.2 %collective-permute-start.21 = (f32[64,8,66]{0,1,2:T(8,128)S(1)}, f32[64,8,66]{0,1,2:T(8,128)S(1)}, u32[]{:S(2)}, u32[]{:S(2)}) collective-permute-start(f32[64,8,66]{0,1,2:T(8,128)S(1)} %pad_maximum_fusion.2), channel_id=1, source_target_pairs={{0,1},{1,0},{2,3},{3,2},{4,5},{5,4},{6,7},{7,6},{8,9},{9,8},{10,11... | collective-permute-start | bytes 405512 | tf_op jit(solution)/shard_map/ppermute | solution.py:37
  107.7 52.2 %collective-permute-start.11 = (bf16[4,128,512]{2,1,0:T(8,128)(2,1)}, bf16[4,128,512]{2,1,0:T(8,128)(2,1)}, u32[]{:S(2)}, u32[]{:S(2)}) collective-permute-start(bf16[4,128,512]{2,1,0:T(8,128)(2,1)} %get-tuple-element.29), channel_id=1, source_target_pairs={{0,3},{1,4},{2,5},{3,6},{4,7},{5,8},{6,9},{7,10},{8,11},{9,12},{10... | collective-permute-start | bytes 1572872 | tf_op jit(solution)/shard_map/ppermute | solution.py:70
  108.6 8.9 %copy-start.16 = (bf16[1,4,2]{1,0,2:T(2,128)(2,1)S(1)}, bf16[1,4,2]{1,0,2:T(2,128)(2,1)}, u32[]{:S(2)}) copy-start(bf16[1,4,2]{1,0,2:T(2,128)(2,1)} %get-tuple-element.40) | copy-start | bytes 52
  108.6 10.5 %collective-permute-start.22 = (f32[64,8,66]{0,1,2:T(8,128)}, f32[64,8,66]{0,1,2:T(8,128)S(1)}, u32[]{:S(2)}, u32[]{:S(2)}) collective-permute-start(f32[64,8,66]{0,1,2:T(8,128)} %pad_maximum_fusion.3), channel_id=1, source_target_pairs={{0,8},{8,0},{16,24},{24,16},{32,40},{40,32},{48,56},{56,48},{1,9},... | collective-permute-start | bytes 405512 | tf_op jit(solution)/shard_map/ppermute | solution.py:37
  113.0 64.2 %collective-permute-start.10 = (bf16[4,128,512]{2,1,0:T(8,128)(2,1)}, bf16[4,128,512]{2,1,0:T(8,128)(2,1)}, u32[]{:S(2)}, u32[]{:S(2)}) collective-permute-start(bf16[4,128,512]{2,1,0:T(8,128)(2,1)} %get-tuple-element.30), channel_id=1, source_target_pairs={{0,2},{1,3},{2,4},{3,5},{4,6},{5,7},{6,8},{7,9},{8,10},{9,11},{10,... | collective-permute-start | bytes 1572872 | tf_op jit(solution)/shard_map/ppermute | solution.py:70
  113.6 81.9 %collective-permute-start.9 = (bf16[4,128,512]{2,1,0:T(8,128)(2,1)}, bf16[4,128,512]{2,1,0:T(8,128)(2,1)}, u32[]{:S(2)}, u32[]{:S(2)}) collective-permute-start(bf16[4,128,512]{2,1,0:T(8,128)(2,1)} %get-tuple-element.31), channel_id=1, source_target_pairs={{0,1},{1,2},{2,3},{3,4},{4,5},{5,6},{6,7},{7,8},{8,9},{9,10},{10,1... | collective-permute-start | bytes 1572872 | tf_op jit(solution)/shard_map/ppermute | solution.py:70
  115.3 99.9 %collective-permute-start.14 = (bf16[4,128,512]{2,1,0:T(8,128)(2,1)}, bf16[4,128,512]{2,1,0:T(8,128)(2,1)}, u32[]{:S(2)}, u32[]{:S(2)}) collective-permute-start(bf16[4,128,512]{2,1,0:T(8,128)(2,1)} %get-tuple-element.25), channel_id=1, source_target_pairs={{0,3},{1,4},{2,5},{3,6},{4,7},{5,8},{6,9},{7,10},{8,11},{9,12},{10... | collective-permute-start | bytes 1572872 | tf_op jit(solution)/shard_map/ppermute | solution.py:70
  119.2 14.6 %collective-permute-start.23 = (f32[64,8,66]{0,1,2:T(8,128)S(1)}, f32[64,8,66]{0,1,2:T(8,128)S(1)}, u32[]{:S(2)}, u32[]{:S(2)}) collective-permute-start(f32[64,8,66]{0,1,2:T(8,128)S(1)} %pad_maximum_fusion.4), channel_id=1, source_target_pairs={{0,16},{8,24},{16,0},{24,8},{32,48},{40,56},{48,32},{56,40},{1,17}... | collective-permute-start | bytes 405512 | tf_op jit(solution)/shard_map/ppermute | solution.py:37
  134.5 17.7 %collective-permute-start.24 = (f32[64,8,66]{0,1,2:T(8,128)}, f32[64,8,66]{0,1,2:T(8,128)S(1)}, u32[]{:S(2)}, u32[]{:S(2)}) collective-permute-start(f32[64,8,66]{0,1,2:T(8,128)} %pad_maximum_fusion.5), channel_id=1, source_target_pairs={{0,32},{8,40},{16,48},{24,56},{32,0},{40,8},{48,16},{56,24},{1,33}... | collective-permute-start | bytes 405512 | tf_op jit(solution)/shard_map/ppermute | solution.py:37
  138.9 56.5 %copy-start.3 = (bf16[1,4,128,512]{3,2,1,0:T(8,128)(2,1)S(1)}, bf16[1,4,128,512]{3,2,1,0:T(8,128)(2,1)}, u32[]{:S(2)}) copy-start(bf16[1,4,128,512]{3,2,1,0:T(8,128)(2,1)} %get-tuple-element.28) | copy-start | bytes 1572868
  152.3 7.0 %collective-permute-start.25 = (f32[64,8,66]{0,1,2:T(8,128)S(1)}, f32[64,8,66]{0,1,2:T(8,128)S(1)}, u32[]{:S(2)}, u32[]{:S(2)}) collective-permute-start(f32[64,8,66]{0,1,2:T(8,128)S(1)} %pad_maximum_fusion.6), channel_id=1, source_target_pairs={{0,2},{2,0},{4,6},{6,4},{1,3},{3,1},{5,7},{7,5},{8,10},{10,8},{12,... | collective-permute-start | bytes 405512 | tf_op jit(solution)/shard_map/ppermute | solution.py:37
  159.4 55.8 %collective-permute-start.13 = (bf16[4,128,512]{2,1,0:T(8,128)(2,1)}, bf16[4,128,512]{2,1,0:T(8,128)(2,1)}, u32[]{:S(2)}, u32[]{:S(2)}) collective-permute-start(bf16[4,128,512]{2,1,0:T(8,128)(2,1)} %get-tuple-element.26), channel_id=1, source_target_pairs={{0,2},{1,3},{2,4},{3,5},{4,6},{5,7},{6,8},{7,9},{8,10},{9,11},{10,... | collective-permute-start | bytes 1572872 | tf_op jit(solution)/shard_map/ppermute | solution.py:70
  159.9 55.3 %collective-permute-start.12 = (bf16[4,128,512]{2,1,0:T(8,128)(2,1)}, bf16[4,128,512]{2,1,0:T(8,128)(2,1)}, u32[]{:S(2)}, u32[]{:S(2)}) collective-permute-start(bf16[4,128,512]{2,1,0:T(8,128)(2,1)} %get-tuple-element.27), channel_id=1, source_target_pairs={{0,1},{1,2},{2,3},{3,4},{4,5},{5,6},{6,7},{7,8},{8,9},{9,10},{10,1... | collective-permute-start | bytes 1572872 | tf_op jit(solution)/shard_map/ppermute | solution.py:70
  177.1 36.2 %collective-permute-start.26 = (f32[64,8,66]{0,1,2:T(8,128)S(1)}, f32[64,8,66]{0,1,2:T(8,128)S(1)}, u32[]{:S(2)}, u32[]{:S(2)}) collective-permute-start(f32[64,8,66]{0,1,2:T(8,128)S(1)} %pad_maximum_fusion.7), channel_id=1, source_target_pairs={{0,4},{2,6},{4,0},{6,2},{1,5},{3,7},{5,1},{7,3},{8,12},{10,14},{12... | collective-permute-start | bytes 405512 | tf_op jit(solution)/shard_map/ppermute | solution.py:37
  195.4 18.3 %copy-start.12 = (bf16[512,32]{0,1:T(8,128)(2,1)S(1)}, bf16[512,32]{0,1:T(8,128)(2,1)}, u32[]{:S(2)}) copy-start(bf16[512,32]{0,1:T(8,128)(2,1)} %param.12) | copy-start | bytes 98308
  213.9 11.4 %collective-permute-start.27 = (f32[64,32]{0,1:T(8,128)S(1)}, f32[64,32]{0,1:T(8,128)S(1)}, u32[]{:S(2)}, u32[]{:S(2)}) collective-permute-start(f32[64,32]{0,1:T(8,128)S(1)} %fusion.73), channel_id=1, source_target_pairs={{0,64},{64,0},{128,192},{192,128},{1,65},{65,1},{129,193},{193,129... | collective-permute-start | bytes 24584 | tf_op jit(solution)/shard_map/ppermute | solution.py:37
  225.3 7.3 %collective-permute-start.28 = (f32[64,32]{0,1:T(8,128)S(1)}, f32[64,32]{0,1:T(8,128)S(1)}, u32[]{:S(2)}, u32[]{:S(2)}) collective-permute-start(f32[64,32]{0,1:T(8,128)S(1)} %add.270), channel_id=1, source_target_pairs={{0,128},{64,192},{128,0},{192,64},{1,129},{65,193},{129,1},{193,65... | collective-permute-start | bytes 24584 | tf_op jit(solution)/shard_map/ppermute | solution.py:37
  (1 other events, 2.1 us)
